TPU v7x, 512 devices: a whole 4x8x8 slice. The times are simulated.
512 devices in a mesh: rows: 128 (over y_hi, x, z), rep: 4 (over y_lo, core).
Axes of the slice: x: 4, y: 8 (y_hi: 4, y_lo: 2; y = y_hi * 2 + y_lo), z: 8, core: 2. Of those that a mesh axis runs over, the one named last changes fastest.
Arguments:
- features: bfloat16 [65536, 256], P(('rows', 'rep')), may hold values from -6 to 6
- weight: bfloat16 [256, 256], replicated, may hold values from -0.375 to 0.375
- bias_terms: float32 [256], replicated, may hold values from -3 to 3
- tile_data: bfloat16 [128, 4, 8, 128, 128], P('rows'), may hold values from -0.1875 to 0.1875
- tile_row: int32 [128, 4, 8], P('rows'), may hold values from 0 to 3
- tile_col: int32 [128, 4, 8], P('rows'), may hold values from 0 to 127
- tile_count: int32 [128, 4], P('rows'), may hold values from 1 to 8, as said below
- grad_out: bfloat16 [65536, 256], P(('rows', 'rep')), may hold values from -6 to 6
Outputs:
- layer_out: bfloat16 [65536, 256], P(('rows', 'rep'))
- weight_grad: float32 [256, 256], replicated
- bias_grad: float32 [256], replicated
Inputs may be any that keep to these rules, and one draw needn't show every extreme that they name: `tile_count`: some group's stripe has all 8 slots live in every draw.
All inputs are finite; a program needn't handle non-finite values.
Results may differ from a plain program's by a relative error of at most 0.015.
Values may be sent and summed in bfloat16 or wider, within the bound.
No kernel may reach another device: no remote copies, remote signals or barrier semaphores. Data moves between devices by JAX's collectives and lax.ppermute only.
A program may use at most 64 MiB of HBM per device.

v0:
```python
import jax
import jax.numpy as jnp
from jax import lax
from jax.sharding import PartitionSpec as P


def slots_wide(tile_set, row_set, col_set, live_set, blocks, row_count):
    picked = jnp.take(blocks, col_set, axis=0)
    product = jnp.einsum("tij,tjf->tif", tile_set, picked, preferred_element_type=jnp.float32)
    local_ids = jnp.arange(row_count, dtype=jnp.int32)
    select = ((row_set[None, :] == local_ids[:, None]) & live_set[None, :]).astype(jnp.float32)
    return jnp.einsum("bt,tif->bif", select, product)


def propagate(tile_set, row_set, col_set, count_set, blocks, row_count, slot_fn):
    stripes, capacity = row_set.shape
    block_size = tile_set.shape[-1]
    slot_ids = jnp.arange(capacity, dtype=jnp.int32)
    live_set = slot_ids[None, :] < count_set[:, None]
    accumulated = slot_fn(
        tile_set.reshape(-1, block_size, block_size),
        row_set.reshape(-1),
        col_set.reshape(-1),
        live_set.reshape(-1),
        blocks,
        row_count,
    )
    return accumulated


def shards(features, weight, bias_terms, tile_data, tile_row, tile_col, tile_count, grad_out):
    block_size = tile_data.shape[-1]
    feature_width = features.shape[1]
    row_count = lax.axis_size("rep")
    rep_index = lax.axis_index("rep")
    own_tiles = lax.dynamic_slice_in_dim(tile_data[0], rep_index, 1, 0)
    own_rows = lax.dynamic_slice_in_dim(tile_row[0], rep_index, 1, 0)
    own_cols = lax.dynamic_slice_in_dim(tile_col[0], rep_index, 1, 0)
    own_count = lax.dynamic_slice_in_dim(tile_count[0], rep_index, 1, 0)
    stripe_nodes = lax.all_gather(features, "rows", axis=0, tiled=True)
    blocks = stripe_nodes.reshape(-1, block_size, feature_width)
    partial_value = propagate(
        own_tiles, own_rows, own_cols, own_count, blocks, row_count, slots_wide
    )
    partial_value = partial_value.reshape(row_count * block_size, feature_width)
    propagated = lax.psum_scatter(partial_value, "rep", scatter_dimension=0, tiled=True).astype(
        jnp.bfloat16
    )
    preact = jnp.dot(propagated, weight, preferred_element_type=jnp.float32) + bias_terms
    sigma = jax.nn.sigmoid(preact)
    layer_out = (preact * sigma).astype(jnp.bfloat16)
    slope = sigma * (1.0 + preact * (1.0 - sigma))
    grad_pre = (grad_out.astype(jnp.float32) * slope).astype(jnp.bfloat16)
    weight_term = lax.dot_general(
        propagated, grad_pre, (((0,), (0,)), ((), ())), preferred_element_type=jnp.float32
    )
    bias_term = jnp.sum(grad_pre.astype(jnp.float32), axis=0)
    weight_grad, bias_grad = lax.psum((weight_term, bias_term), ("rows", "rep"))
    return (layer_out, weight_grad, bias_grad)


def solution(mesh):
    placed = (
        P(("rows", "rep"), None),
        P(),
        P(),
        P("rows", None, None, None, None),
        P("rows", None, None),
        P("rows", None, None),
        P("rows", None),
        P(("rows", "rep"), None),
    )
    return jax.shard_map(
        shards,
        mesh=mesh,
        in_specs=placed,
        out_specs=(P(("rows", "rep"), None), P(), P()),
        check_vma=False,
    )
```

profile of v0, /device:TPU:1, one launch (start us, length us, event | category | flops | bytes accessed | tf_op | source)
XLA Modules:
  0.0 482.7 jit_solution(15143895187925583589)
XLA Ops:
  7.2 0.0 copy-start
  7.2 0.0 all-gather.2.cloned.1.call-start
  7.2 0.7 all-gather.2.cloned.1.call-update
  7.9 0.0 reduce-scatter.2.cloned.1.call-start
  8.0 1.2 constant_dynamic-slice_fusion.1
  9.2 0.7 fusion.18
  9.9 0.7 compare_and_fusion
  10.6 0.6 iota_compare_fusion.1
  11.2 0.7 fusion.17
  11.9 157.0 %all-gather.2.cloned.1.call-done = bf16[16384,256]{1,0:T(8,128)(2,1)} async-done(((bf16[128,256]{1,0:T(8,128)(2,1)}), bf16[16384,256]{1,0:T(8,128)(2,1)}) %all-gather.2.cloned.1.call-update) | async-done | bytes 8388624 | tf_op jit(solution)/shard_map/all_gather | solution.py:40
  168.9 4.0 gather_fusion
  172.9 0.0 copy-done
  172.9 0.4 fusion.2
  173.3 0.4 fusion
  173.7 0.9 copy.11
  174.6 0.0 reduce-scatter.2.cloned.1.call-update
  174.6 0.0 all-reduce.2.cloned.1.call-start
  174.6 22.8 %reduce-scatter.2.cloned.1.call-done = f32[128,256]{1,0:T(8,128)} async-done(((f32[512,256]{1,0:T(8,128)}), f32[128,256]{1,0:T(8,128)}) %reduce-scatter.2.cloned.1.call-update) | async-done | bytes 131088 | tf_op jit(solution)/shard_map/reduce_scatter | solution.py:46
  197.4 1.8 convert_reduce_fusion
  199.2 1.8 fusion.8
  201.0 0.0 all-reduce.2.cloned.1.call-update
  201.1 100.3 %psum.15 = f32[256]{0:T(256)} all-reduce(f32[256]{0:T(256)S(1)} %get-tuple-element.3), channel_id=1, replica_groups=mesh['rows'=128,'rep'=4] {'rows','rep'}, use_global_device_ids=true, to_apply=%region_3.4 | all-reduce | flops 256 | bytes 2048 | tf_op jit(solution)/shard_map/psum | solution.py:58
  301.3 173.2 %all-reduce.2.cloned.1.call-done = f32[256,256]{1,0:T(8,128)} async-done(((f32[256,256]{1,0:T(8,128)}), f32[256,256]{1,0:T(8,128)}) %all-reduce.2.cloned.1.call-update) | async-done | bytes 262160 | tf_op jit(solution)/shard_map/psum | solution.py:58
  474.5 1.7 copy.16
  (1 shorter events, 0.0 us)
Async XLA Ops:
  7.2 165.7 %copy-start = (bf16[1,4,8,128,128]{4,3,2,1,0:T(8,128)(2,1)S(1)}, bf16[1,4,8,128,128]{4,3,2,1,0:T(8,128)(2,1)}, u32[]{:S(2)}) copy-start(bf16[1,4,8,128,128]{4,3,2,1,0:T(8,128)(2,1)} %param.11) | copy-start | bytes 3145732
  7.2 161.7 %all-gather.2.cloned.1.call-start = ((), (), s32[]{:S(2)}) async-start(), calls=%async_computation.1 | async-start | bytes 8454144 | tf_op jit(solution)/shard_map/all_gather | solution.py:40
  7.9 189.5 %reduce-scatter.2.cloned.1.call-start = ((), (), s32[]{:S(2)}) async-start(), calls=%async_computation.2 | async-start | bytes 655360 | tf_op jit(solution)/shard_map/reduce_scatter | solution.py:46
  174.6 299.9 %all-reduce.2.cloned.1.call-start = ((), (), s32[]{:S(2)}) async-start(), calls=%async_computation.3 | async-start | bytes 524288 | tf_op jit(solution)/shard_map/psum | solution.py:58
Sparse Core Ops, SparseCore 0:
  12.5 156.3 all-gather.1
  174.7 22.6 reduce-scatter.1
  203.0 271.5 all-reduce.1
where the time goes:
time: 483 us
  waiting for transfers between devices  354 us (73%)
  blocking collectives  100 us (21%)
  between operations  13.8 us (3%)
  local copies, waits for them, and re-layouts  8.46 us (2%)
    psum x1, waiting for transfers between devices, shards(): weight_grad, bias_grad = lax.psum((weight_term, bias_term), ('rows', 'rep'))  173 us
    all_gather x1, waiting for transfers between devices, shards(): stripe_nodes = lax.all_gather(features, 'rows', axis=0, tiled=True)  157 us
    psum x1, blocking collectives, shards(): weight_grad, bias_grad = lax.psum((weight_term, bias_term), ('rows', 'rep'))  100 us
    reduce_scatter x1, waiting for transfers between devices, shards(): lax.psum_scatter(partial_value, 'rep', scatter_dimension=0, tiled=True)  22.8 us
  transfers between devices with their start and end apart: 3, of which 3 were waited for; matrix products, arithmetic and copies ran while one was open for 1% of the time, Pallas kernels for 0%

commit v1 on v0

v1 whole, which is shorter than its diff:
```python
import jax
import jax.numpy as jnp
from jax import lax
from jax.sharding import Mesh
from jax.sharding import PartitionSpec as P

ROW_AXES = ("y_hi", "x", "z")
REP_AXES = ("y_lo", "core")
ALL_AXES = ROW_AXES + REP_AXES


def physical_mesh(mesh):
    rows, rep = mesh.devices.shape
    y_hi, x, y_lo = 4, 4, 2
    return Mesh(mesh.devices.reshape(y_hi, x, rows // (y_hi * x), y_lo, rep // y_lo), ALL_AXES)


def ring_gather(piece, axis):
    n = lax.axis_size(axis)
    fwd = [(i, (i + 1) % n) for i in range(n)]
    bwd = [(i, (i - 1) % n) for i in range(n)]
    pieces = {0: piece}
    left = piece
    right = piece
    for k in range(1, n // 2 + 1):
        left = lax.ppermute(left, axis, fwd)
        pieces[-k] = left
        if k < n - k:
            right = lax.ppermute(right, axis, bwd)
            pieces[k] = right
    return jnp.stack([pieces[d] for d in range(-(n // 2), n - n // 2)])


def gather_blocks(features, cols):
    order = ("y_hi", "x", "z")
    stack = features
    for a in order:
        stack = ring_gather(stack, a)
    blocks = stack.reshape(-1, features.shape[0], features.shape[1])
    return jnp.take(blocks, nested_slot(cols, order), axis=0)


def nested_slot(cols, order):
    sizes = {a: lax.axis_size(a) for a in ROW_AXES}
    coords = {}
    rest = cols
    for a in reversed(ROW_AXES):
        coords[a] = rest % sizes[a]
        rest = rest // sizes[a]
    flat = jnp.zeros_like(cols)
    for a in reversed(order):
        k = (coords[a] - lax.axis_index(a) + sizes[a] // 2) % sizes[a]
        flat = flat * sizes[a] + k
    return flat


def halving_steps(axes):
    steps = []
    for a in axes:
        n = lax.axis_size(a)
        for b in reversed(range(n.bit_length() - 1)):
            steps.append((a, b, [(i, i ^ (1 << b)) for i in range(n)]))
    return steps


def reduce_scatter_flat(flat, steps):
    for a, b, perm in steps:
        upper = (lax.axis_index(a) >> b) & 1
        half = flat.shape[0] // 2
        lower_half, upper_half = flat[:half], flat[half:]
        send = jnp.where(upper == 1, lower_half, upper_half)
        keep = jnp.where(upper == 1, upper_half, lower_half)
        flat = keep + lax.ppermute(send, a, perm)
    return flat


def all_gather_flat(flat, steps):
    for a, b, perm in reversed(steps):
        upper = (lax.axis_index(a) >> b) & 1
        other = lax.ppermute(flat, a, perm)
        flat = jnp.where(
            upper == 1, jnp.concatenate([other, flat]), jnp.concatenate([flat, other])
        )
    return flat


def reduce_all(packed):
    for a, b, perm in halving_steps(("core", "y_lo", "z", "x", "y_hi")):
        packed = packed + lax.ppermute(packed, a, perm)
    return packed


def reduce_over_rep(partial_value):
    steps = halving_steps(("y_lo", "core"))
    rows, width = partial_value.shape
    flat = reduce_scatter_flat(partial_value.reshape(-1), steps)
    return flat.reshape(rows // lax.axis_size(REP_AXES), width)


def shards(features, weight, bias_terms, tile_data, tile_row, tile_col, tile_count, grad_out):
    block_size = tile_data.shape[-1]
    feature_width = features.shape[1]
    row_count = lax.axis_size(REP_AXES)
    rep_index = lax.axis_index(REP_AXES)
    own_tiles = lax.dynamic_index_in_dim(tile_data[0], rep_index, 0, keepdims=False)
    own_rows = lax.dynamic_index_in_dim(tile_row[0], rep_index, 0, keepdims=False)
    own_cols = lax.dynamic_index_in_dim(tile_col[0], rep_index, 0, keepdims=False)
    own_count = lax.dynamic_index_in_dim(tile_count[0], rep_index, 0, keepdims=False)
    capacity = own_rows.shape[0]
    stripe_nodes = lax.all_gather(features, ROW_AXES, axis=0, tiled=True)
    picked = jnp.take(stripe_nodes.reshape(-1, block_size, feature_width), own_cols, axis=0)
    product = jnp.einsum("tij,tjf->tif", own_tiles, picked, preferred_element_type=jnp.float32)
    live = jnp.arange(capacity, dtype=jnp.int32) < own_count
    local_ids = jnp.arange(row_count, dtype=jnp.int32)
    select = ((own_rows[None, :] == local_ids[:, None]) & live[None, :]).astype(jnp.float32)
    partial_value = jnp.einsum("bt,tif->bif", select, product)
    partial_value = partial_value.reshape(row_count * block_size, feature_width)
    propagated = lax.psum_scatter(partial_value, REP_AXES, scatter_dimension=0, tiled=True).astype(
        jnp.bfloat16
    )
    preact = jnp.dot(propagated, weight, preferred_element_type=jnp.float32) + bias_terms
    sigma = jax.nn.sigmoid(preact)
    layer_out = (preact * sigma).astype(jnp.bfloat16)
    slope = sigma * (1.0 + preact * (1.0 - sigma))
    grad_pre = (grad_out.astype(jnp.float32) * slope).astype(jnp.bfloat16)
    weight_term = lax.dot_general(
        propagated, grad_pre, (((0,), (0,)), ((), ())), preferred_element_type=jnp.float32
    )
    bias_term = jnp.sum(grad_pre.astype(jnp.float32), axis=0)
    pad_rows = (-(feature_width + 1)) % 8
    packed = jnp.concatenate(
        [weight_term, bias_term[None, :], jnp.zeros((pad_rows, feature_width), jnp.float32)], axis=0
    )
    packed = reduce_all(packed)
    weight_grad = packed[:feature_width]
    bias_grad = packed[feature_width]
    return (layer_out, weight_grad, bias_grad)


def solution(mesh):
    flat = P(ALL_AXES, None)
    placed = (
        flat,
        P(),
        P(),
        P(ROW_AXES, None, None, None, None),
        P(ROW_AXES, None, None),
        P(ROW_AXES, None, None),
        P(ROW_AXES, None),
        flat,
    )
    return jax.shard_map(
        shards,
        mesh=physical_mesh(mesh),
        in_specs=placed,
        out_specs=(flat, P(), P()),
        check_vma=False,
    )
```

time: 483 us -> 316 us (0.65)
  waiting for transfers between devices: 354 us -> 249 us
  blocking collectives: 100 us -> 0 us
  starting transfers between devices: 0.12 us -> 36.6 us
    psum x1 -> x0, waiting for transfers between devices: 173 us -> none  [shards(): weight_grad, bias_grad = lax.psum((weight_term, bias_term), ('rows', 'rep'))]
    psum x1 -> x0, blocking collectives: 100 us -> none  [shards(): weight_grad, bias_grad = lax.psum((weight_term, bias_term), ('rows', 'rep'))]
    ppermute x0 -> x9, waiting for transfers between devices: none -> 68.2 us  [reduce_all(): packed = packed + lax.ppermute(packed, a, perm)]
    ppermute x0 -> x9, starting transfers between devices: none -> 36.5 us  [reduce_all(): packed = packed + lax.ppermute(packed, a, perm)]
  transfers between devices with their start and end apart: 3 -> 11, of which waited for: 3 -> 11; matrix products, arithmetic and copies ran while one was open for 1% -> 1% of each run, Pallas kernels for 0% -> 0%
where the time goes in v1:
time: 316 us; the launch traced here: 314 us
  waiting for transfers between devices  249 us (79%)
  starting transfers between devices  36.6 us (12%)
  between operations  14.2 us (4%)
  local copies, waits for them, and re-layouts  8.15 us (3%)
  matrix products  3.71 us (1%)
    all_gather x1, waiting for transfers between devices, shards(): stripe_nodes = lax.all_gather(features, ROW_AXES, axis=0, tiled=True)  157 us
    ppermute x9, waiting for transfers between devices, reduce_all(): packed = packed + lax.ppermute(packed, a, perm)  68.2 us
    ppermute x9, starting transfers between devices, reduce_all(): packed = packed + lax.ppermute(packed, a, perm)  36.5 us
    reduce_scatter x1, waiting for transfers between devices, shards(): lax.psum_scatter(partial_value, REP_AXES, scatter_dimension=0, tiled=True)  22.7 us
  transfers between devices with their start and end apart: 11, of which 11 were waited for; matrix products, arithmetic and copies ran while one was open for 1% of the time, Pallas kernels for 0%

profile of v1, /device:TPU:1, one launch (start us, length us, event | category | flops | bytes accessed | tf_op | source)
XLA Modules:
  0.0 313.8 jit_solution(17097211827280277652)
XLA Ops:
  7.2 0.7 all-gather.2.cloned.1.call-update
  8.0 1.2 constant_dynamic-slice_fusion.1
  9.2 0.7 fusion.18
  9.9 0.7 compare_and_fusion
  10.6 0.6 iota_compare_fusion.1
  11.2 0.7 fusion.17
  11.9 157.0 %all-gather.2.cloned.1.call-done = bf16[16384,256]{1,0:T(8,128)(2,1)} async-done(((bf16[128,256]{1,0:T(8,128)(2,1)}), bf16[16384,256]{1,0:T(8,128)(2,1)}) %all-gather.2.cloned.1.call-update) | async-done | bytes 8388624 | tf_op jit(solution)/shard_map/all_gather | solution.py:110
  168.9 4.0 %gather_fusion = bf16[8,128,256]{2,1,0:T(8,128)(2,1)S(1)} fusion(bf16[128,128,256]{2,1,0:T(8,128)(2,1)} %bitcast.22, s32[1024]{0:T(1024)S(1)} %pad_clamp_fusion), kind=kCustom, calls=%fused_computation | custom fusion | bytes 1048608 | tf_op jit(solution)/shard_map/jit(_take)/gather | solution.py:111
  173.7 0.9 copy.11
  174.7 22.7 %reduce-scatter.2.cloned.1.call-done = f32[128,256]{1,0:T(8,128)} async-done(((f32[512,256]{1,0:T(8,128)}), f32[128,256]{1,0:T(8,128)}) %reduce-scatter.2.cloned.1.call-update) | async-done | bytes 131088 | tf_op jit(solution)/shard_map/reduce_scatter | solution.py:118
  197.4 1.8 convert_reduce_fusion
  199.2 1.1 fusion.8
  200.5 1.9 collective-permute-start
  202.4 1.5 collective-permute-done
  204.0 2.3 collective-permute-start.1
  206.4 7.5 %collective-permute-done.1 = f32[264,256]{1,0:T(8,128)S(1)} collective-permute-done((f32[264,256]{1,0:T(8,128)S(1)}, f32[264,256]{1,0:T(8,128)S(1)}, u32[]{:S(2)}, u32[]{:S(2)}) %collective-permute-start.1) | collective-permute-done | bytes 270368 | tf_op jit(solution)/shard_map/ppermute | solution.py:89
  213.8 7.7 %collective-permute-start.2 = (f32[264,256]{1,0:T(8,128)S(1)}, f32[264,256]{1,0:T(8,128)S(1)}, u32[]{:S(2)}, u32[]{:S(2)}) collective-permute-start(f32[264,256]{1,0:T(8,128)S(1)} %add.79), channel_id=1, source_target_pairs={{0,16},{4,20},{8,24},{12,28},{16,0},{20,4},{24,8},{28,12},{1,17},{... | collective-permute-start | bytes 811016 | tf_op jit(solution)/shard_map/ppermute | solution.py:89
  221.6 7.4 %collective-permute-done.2 = f32[264,256]{1,0:T(8,128)S(1)} collective-permute-done((f32[264,256]{1,0:T(8,128)S(1)}, f32[264,256]{1,0:T(8,128)S(1)}, u32[]{:S(2)}, u32[]{:S(2)}) %collective-permute-start.2) | collective-permute-done | bytes 270368 | tf_op jit(solution)/shard_map/ppermute | solution.py:89
  229.0 9.1 %collective-permute-start.3 = (f32[264,256]{1,0:T(8,128)S(1)}, f32[264,256]{1,0:T(8,128)S(1)}, u32[]{:S(2)}, u32[]{:S(2)}) collective-permute-start(f32[264,256]{1,0:T(8,128)S(1)} %add.80), channel_id=1, source_target_pairs={{0,8},{4,12},{8,0},{12,4},{16,24},{20,28},{24,16},{28,20},{1,9},{5... | collective-permute-start | bytes 811016 | tf_op jit(solution)/shard_map/ppermute | solution.py:89
  238.1 10.5 %collective-permute-done.3 = f32[264,256]{1,0:T(8,128)S(1)} collective-permute-done((f32[264,256]{1,0:T(8,128)S(1)}, f32[264,256]{1,0:T(8,128)S(1)}, u32[]{:S(2)}, u32[]{:S(2)}) %collective-permute-start.3) | collective-permute-done | bytes 270368 | tf_op jit(solution)/shard_map/ppermute | solution.py:89
  248.7 1.9 collective-permute-start.4
  250.6 7.5 %collective-permute-done.4 = f32[264,256]{1,0:T(8,128)S(1)} collective-permute-done((f32[264,256]{1,0:T(8,128)S(1)}, f32[264,256]{1,0:T(8,128)S(1)}, u32[]{:S(2)}, u32[]{:S(2)}) %collective-permute-start.4) | collective-permute-done | bytes 270368 | tf_op jit(solution)/shard_map/ppermute | solution.py:89
  258.1 2.4 collective-permute-start.5
  260.5 7.6 %collective-permute-done.5 = f32[264,256]{1,0:T(8,128)S(1)} collective-permute-done((f32[264,256]{1,0:T(8,128)S(1)}, f32[264,256]{1,0:T(8,128)S(1)}, u32[]{:S(2)}, u32[]{:S(2)}) %collective-permute-start.5) | collective-permute-done | bytes 270368 | tf_op jit(solution)/shard_map/ppermute | solution.py:89
  268.2 3.0 collective-permute-start.6
  271.2 4.6 %collective-permute-done.6 = f32[264,256]{1,0:T(8,128)S(1)} collective-permute-done((f32[264,256]{1,0:T(8,128)S(1)}, f32[264,256]{1,0:T(8,128)S(1)}, u32[]{:S(2)}, u32[]{:S(2)}) %collective-permute-start.6) | collective-permute-done | bytes 270368 | tf_op jit(solution)/shard_map/ppermute | solution.py:89
  275.9 6.2 %collective-permute-start.7 = (f32[264,256]{1,0:T(8,128)S(1)}, f32[264,256]{1,0:T(8,128)S(1)}, u32[]{:S(2)}, u32[]{:S(2)}) collective-permute-start(f32[264,256]{1,0:T(8,128)S(1)} %add.84), channel_id=1, source_target_pairs={{0,256},{128,384},{256,0},{384,128},{1,257},{129,385},{257,1},{385... | collective-permute-start | bytes 811016 | tf_op jit(solution)/shard_map/ppermute | solution.py:89
  282.1 8.3 %collective-permute-done.7 = f32[264,256]{1,0:T(8,128)S(1)} collective-permute-done((f32[264,256]{1,0:T(8,128)S(1)}, f32[264,256]{1,0:T(8,128)S(1)}, u32[]{:S(2)}, u32[]{:S(2)}) %collective-permute-start.7) | collective-permute-done | bytes 270368 | tf_op jit(solution)/shard_map/ppermute | solution.py:89
  290.4 1.9 collective-permute-start.8
  292.4 13.3 %collective-permute-done.8 = f32[264,256]{1,0:T(8,128)S(1)} collective-permute-done((f32[264,256]{1,0:T(8,128)S(1)}, f32[264,256]{1,0:T(8,128)S(1)}, u32[]{:S(2)}, u32[]{:S(2)}) %collective-permute-start.8) | collective-permute-done | bytes 270368 | tf_op jit(solution)/shard_map/ppermute | solution.py:89
  305.7 0.7 slice.10
  306.4 0.6 slice.11
  (20 shorter events, 1.4 us)
Async XLA Ops:
  7.2 165.7 %copy-start = (bf16[1,4,8,128,128]{4,3,2,1,0:T(8,128)(2,1)S(1)}, bf16[1,4,8,128,128]{4,3,2,1,0:T(8,128)(2,1)}, u32[]{:S(2)}) copy-start(bf16[1,4,8,128,128]{4,3,2,1,0:T(8,128)(2,1)} %param.11) | copy-start | bytes 3145732
  7.2 161.7 %all-gather.2.cloned.1.call-start = ((), (), s32[]{:S(2)}) async-start(), calls=%async_computation.1 | async-start | bytes 8454144 | tf_op jit(solution)/shard_map/all_gather | solution.py:110
  7.9 189.5 %reduce-scatter.2.cloned.1.call-start = ((), (), s32[]{:S(2)}) async-start(), calls=%async_computation.2 | async-start | bytes 655360 | tf_op jit(solution)/shard_map/reduce_scatter | solution.py:118
  200.5 3.4 %collective-permute-start = (f32[264,256]{1,0:T(8,128)S(1)}, f32[264,256]{1,0:T(8,128)S(1)}, u32[]{:S(2)}, u32[]{:S(2)}) collective-permute-start(f32[264,256]{1,0:T(8,128)S(1)} %maximum_maximum_fusion), channel_id=1, source_target_pairs={{0,1},{1,0},{2,3},{3,2},{4,5},{5,4},{6,7},{7,6},{8,9},{9,8},{10,11... | collective-permute-start | bytes 811016 | tf_op jit(solution)/shard_map/ppermute | solution.py:89
  204.0 9.8 %collective-permute-start.1 = (f32[264,256]{1,0:T(8,128)S(1)}, f32[264,256]{1,0:T(8,128)S(1)}, u32[]{:S(2)}, u32[]{:S(2)}) collective-permute-start(f32[264,256]{1,0:T(8,128)S(1)} %fusion.20), channel_id=1, source_target_pairs={{0,2},{2,0},{1,3},{3,1},{4,6},{6,4},{5,7},{7,5},{8,10},{10,8},{9,1... | collective-permute-start | bytes 811016 | tf_op jit(solution)/shard_map/ppermute | solution.py:89
  213.8 15.1 %collective-permute-start.2 = (f32[264,256]{1,0:T(8,128)S(1)}, f32[264,256]{1,0:T(8,128)S(1)}, u32[]{:S(2)}, u32[]{:S(2)}) collective-permute-start(f32[264,256]{1,0:T(8,128)S(1)} %add.79), channel_id=1, source_target_pairs={{0,16},{4,20},{8,24},{12,28},{16,0},{20,4},{24,8},{28,12},{1,17},{... | collective-permute-start | bytes 811016 | tf_op jit(solution)/shard_map/ppermute | solution.py:89
  229.0 19.7 %collective-permute-start.3 = (f32[264,256]{1,0:T(8,128)S(1)}, f32[264,256]{1,0:T(8,128)S(1)}, u32[]{:S(2)}, u32[]{:S(2)}) collective-permute-start(f32[264,256]{1,0:T(8,128)S(1)} %add.80), channel_id=1, source_target_pairs={{0,8},{4,12},{8,0},{12,4},{16,24},{20,28},{24,16},{28,20},{1,9},{5... | collective-permute-start | bytes 811016 | tf_op jit(solution)/shard_map/ppermute | solution.py:89
  248.7 9.4 %collective-permute-start.4 = (f32[264,256]{1,0:T(8,128)S(1)}, f32[264,256]{1,0:T(8,128)S(1)}, u32[]{:S(2)}, u32[]{:S(2)}) collective-permute-start(f32[264,256]{1,0:T(8,128)S(1)} %add.81), channel_id=1, source_target_pairs={{0,4},{4,0},{8,12},{12,8},{16,20},{20,16},{24,28},{28,24},{1,5},{5... | collective-permute-start | bytes 811016 | tf_op jit(solution)/shard_map/ppermute | solution.py:89
  258.1 10.0 %collective-permute-start.5 = (f32[264,256]{1,0:T(8,128)S(1)}, f32[264,256]{1,0:T(8,128)S(1)}, u32[]{:S(2)}, u32[]{:S(2)}) collective-permute-start(f32[264,256]{1,0:T(8,128)S(1)} %add.82), channel_id=1, source_target_pairs={{0,64},{32,96},{64,0},{96,32},{1,65},{33,97},{65,1},{97,33},{2,66}... | collective-permute-start | bytes 811016 | tf_op jit(solution)/shard_map/ppermute | solution.py:89
  268.2 7.7 %collective-permute-start.6 = (f32[264,256]{1,0:T(8,128)S(1)}, f32[264,256]{1,0:T(8,128)S(1)}, u32[]{:S(2)}, u32[]{:S(2)}) collective-permute-start(f32[264,256]{1,0:T(8,128)S(1)} %add.83), channel_id=1, source_target_pairs={{0,32},{32,0},{64,96},{96,64},{1,33},{33,1},{65,97},{97,65},{2,34}... | collective-permute-start | bytes 811016 | tf_op jit(solution)/shard_map/ppermute | solution.py:89
  275.9 14.5 %collective-permute-start.7 = (f32[264,256]{1,0:T(8,128)S(1)}, f32[264,256]{1,0:T(8,128)S(1)}, u32[]{:S(2)}, u32[]{:S(2)}) collective-permute-start(f32[264,256]{1,0:T(8,128)S(1)} %add.84), channel_id=1, source_target_pairs={{0,256},{128,384},{256,0},{384,128},{1,257},{129,385},{257,1},{385... | collective-permute-start | bytes 811016 | tf_op jit(solution)/shard_map/ppermute | solution.py:89
  290.4 15.2 %collective-permute-start.8 = (f32[264,256]{1,0:T(8,128)S(1)}, f32[264,256]{1,0:T(8,128)S(1)}, u32[]{:S(2)}, u32[]{:S(2)}) collective-permute-start(f32[264,256]{1,0:T(8,128)S(1)} %add.85), channel_id=1, source_target_pairs={{0,128},{128,0},{256,384},{384,256},{1,129},{129,1},{257,385},{385... | collective-permute-start | bytes 811016 | tf_op jit(solution)/shard_map/ppermute | solution.py:89
Sparse Core Ops, SparseCore 0:
  12.5 156.3 all-gather.1
  174.7 22.6 reduce-scatter.1

commit v2 on v1

--- a/solution.py
+++ b/solution.py
@@ -7,6 +7,7 @@
 ROW_AXES = ("y_hi", "x", "z")
 REP_AXES = ("y_lo", "core")
 ALL_AXES = ROW_AXES + REP_AXES
+SPLIT = 64
 
 
 def physical_mesh(mesh):
@@ -31,8 +32,7 @@
     return jnp.stack([pieces[d] for d in range(-(n // 2), n - n // 2)])
 
 
-def gather_blocks(features, cols):
-    order = ("y_hi", "x", "z")
+def ring_blocks(features, cols, order):
     stack = features
     for a in order:
         stack = ring_gather(stack, a)
@@ -107,8 +107,12 @@
     own_cols = lax.dynamic_index_in_dim(tile_col[0], rep_index, 0, keepdims=False)
     own_count = lax.dynamic_index_in_dim(tile_count[0], rep_index, 0, keepdims=False)
     capacity = own_rows.shape[0]
-    stripe_nodes = lax.all_gather(features, ROW_AXES, axis=0, tiled=True)
-    picked = jnp.take(stripe_nodes.reshape(-1, block_size, feature_width), own_cols, axis=0)
+    near = features[:SPLIT]
+    far = features[SPLIT:]
+    stripe_nodes = lax.all_gather(near, ROW_AXES, axis=0, tiled=True)
+    picked_near = jnp.take(stripe_nodes.reshape(-1, SPLIT, feature_width), own_cols, axis=0)
+    picked_far = ring_blocks(far, own_cols, ("y_hi", "z", "x"))
+    picked = jnp.concatenate([picked_near, picked_far], axis=1)
     product = jnp.einsum("tij,tjf->tif", own_tiles, picked, preferred_element_type=jnp.float32)
     live = jnp.arange(capacity, dtype=jnp.int32) < own_count
     local_ids = jnp.arange(row_count, dtype=jnp.int32)

time: 316 us -> 293 us (0.927)
  waiting for transfers between devices: 249 us -> 169 us
  starting transfers between devices: 36.6 us -> 88.3 us
    all_gather x1, waiting for transfers between devices: 157 us -> 33.8 us  [shards(): stripe_nodes = lax.all_gather(near, ROW_AXES, axis=0, tiled=True)]
    ppermute x0 -> x13, waiting for transfers between devices: none -> 49 us  [the longest x8 47.7 us: ring_gather(): left = lax.ppermute(left, axis, fwd)]
    ppermute x0 -> x13, starting transfers between devices: none -> 44.2 us  [the longest x8 23.3 us: ring_gather(): left = lax.ppermute(left, axis, fwd)]
    ppermute x9, starting transfers between devices: 36.5 us -> 44 us  [reduce_all(): packed = packed + lax.ppermute(packed, a, perm)]
    ppermute x9, waiting for transfers between devices: 68.2 us -> 62.6 us  [reduce_all(): packed = packed + lax.ppermute(packed, a, perm)]
    another operation x0 -> x2, other arithmetic: none -> 3.55 us  [ring_gather(): return jnp.stack([pieces[d] for d in range(-(n // 2), n - n // 2)])]
  transfers between devices with their start and end apart: 11 -> 24, of which waited for: 11 -> 19; matrix products, arithmetic and copies ran while one was open for 1% -> 3% of each run, Pallas kernels for 0% -> 0%
where the time goes in v2:
time: 293 us; the launch traced here: 292 us
  waiting for transfers between devices  169 us (58%)
  starting transfers between devices  88.3 us (30%)
  between operations  14.5 us (5%)
  local copies, waits for them, and re-layouts  11.3 us (4%)
  other arithmetic  5.54 us (2%)
  matrix products  3.56 us (1%)
    ppermute x9, waiting for transfers between devices, reduce_all(): packed = packed + lax.ppermute(packed, a, perm)  62.6 us
    ppermute x8, waiting for transfers between devices, ring_gather(): left = lax.ppermute(left, axis, fwd)  47.7 us
    ppermute x9, starting transfers between devices, reduce_all(): packed = packed + lax.ppermute(packed, a, perm)  44 us
    all_gather x1, waiting for transfers between devices, shards(): stripe_nodes = lax.all_gather(near, ROW_AXES, axis=0, tiled=True)  33.8 us
    reduce_scatter x1, waiting for transfers between devices, shards(): lax.psum_scatter(partial_value, REP_AXES, scatter_dimension=0, tiled=True)  23.4 us
    ppermute x8, starting transfers between devices, ring_gather(): left = lax.ppermute(left, axis, fwd)  23.3 us
    ppermute x5, starting transfers between devices, ring_gather(): right = lax.ppermute(right, axis, bwd)  21 us
  transfers between devices with their start and end apart: 24, of which 19 were waited for; matrix products, arithmetic and copies ran while one was open for 3% of the time, Pallas kernels for 0%

profile of v2, /device:TPU:1, one launch (start us, length us, event | category | flops | bytes accessed | tf_op | source)
XLA Modules:
  0.0 292.1 jit_solution(5295206120369320456)
XLA Ops:
  8.8 5.0 %collective-permute-start = (bf16[64,256]{1,0:T(8,128)(2,1)S(1)}, bf16[64,256]{1,0:T(8,128)(2,1)S(1)}, u32[]{:S(2)}, u32[]{:S(2)}) collective-permute-start(bf16[64,256]{1,0:T(8,128)(2,1)S(1)} %get-tuple-element.13), channel_id=1, source_target_pairs={{0,128},{128,256},{256,384},{384,0},{1,129},{129,257},{257,385},{3... | collective-permute-start | bytes 98312 | tf_op jit(solution)/shard_map/ppermute | solution.py:27
  13.8 3.6 %collective-permute-start.2 = (bf16[64,256]{1,0:T(8,128)(2,1)S(1)}, bf16[64,256]{1,0:T(8,128)(2,1)S(1)}, u32[]{:S(2)}, u32[]{:S(2)}) collective-permute-start(bf16[64,256]{1,0:T(8,128)(2,1)S(1)} %get-tuple-element.13), channel_id=1, source_target_pairs={{0,384},{128,0},{256,128},{384,256},{1,385},{129,1},{257,129},{385... | collective-permute-start | bytes 98312 | tf_op jit(solution)/shard_map/ppermute | solution.py:30
  17.4 3.8 %collective-permute-start.1 = (bf16[64,256]{1,0:T(8,128)(2,1)S(1)}, bf16[64,256]{1,0:T(8,128)(2,1)S(1)}, u32[]{:S(2)}, u32[]{:S(2)}) collective-permute-start(bf16[64,256]{1,0:T(8,128)(2,1)S(1)} %collective-permute-done), channel_id=1, source_target_pairs={{0,128},{128,256},{256,384},{384,0},{1,129},{129,257},{257,385},{3... | collective-permute-start | bytes 98312 | tf_op jit(solution)/shard_map/ppermute | solution.py:27
  21.2 3.0 %collective-permute-done.1 = bf16[64,256]{1,0:T(8,128)(2,1)S(1)} collective-permute-done((bf16[64,256]{1,0:T(8,128)(2,1)S(1)}, bf16[64,256]{1,0:T(8,128)(2,1)S(1)}, u32[]{:S(2)}, u32[]{:S(2)}) %collective-permute-start.1) | collective-permute-done | bytes 32800 | tf_op jit(solution)/shard_map/ppermute | solution.py:27
  24.3 4.0 %collective-permute-start.3 = (bf16[4,64,256]{2,1,0:T(8,128)(2,1)S(1)}, bf16[4,64,256]{2,1,0:T(8,128)(2,1)S(1)}, u32[]{:S(2)}, u32[]{:S(2)}) collective-permute-start(bf16[4,64,256]{2,1,0:T(8,128)(2,1)S(1)} %pad_maximum_fusion.1), channel_id=1, source_target_pairs={{0,4},{4,8},{8,12},{12,16},{16,20},{20,24},{24,28},{28,0},{1,5},{5... | collective-permute-start | bytes 393224 | tf_op jit(solution)/shard_map/ppermute | solution.py:27
  28.3 9.0 %collective-permute-done.3 = bf16[4,64,256]{2,1,0:T(8,128)(2,1)S(1)} collective-permute-done((bf16[4,64,256]{2,1,0:T(8,128)(2,1)S(1)}, bf16[4,64,256]{2,1,0:T(8,128)(2,1)S(1)}, u32[]{:S(2)}, u32[]{:S(2)}) %collective-permute-start.3) | collective-permute-done | bytes 131104 | tf_op jit(solution)/shard_map/ppermute | solution.py:27
  39.2 4.6 %collective-permute-start.7 = (bf16[4,64,256]{2,1,0:T(8,128)(2,1)S(1)}, bf16[4,64,256]{2,1,0:T(8,128)(2,1)S(1)}, u32[]{:S(2)}, u32[]{:S(2)}) collective-permute-start(bf16[4,64,256]{2,1,0:T(8,128)(2,1)S(1)} %pad_maximum_fusion.1), channel_id=1, source_target_pairs={{0,28},{4,0},{8,4},{12,8},{16,12},{20,16},{24,20},{28,24},{1,29},{... | collective-permute-start | bytes 393224 | tf_op jit(solution)/shard_map/ppermute | solution.py:30
  46.5 4.6 %collective-permute-start.8 = (bf16[4,64,256]{2,1,0:T(8,128)(2,1)S(1)}, bf16[4,64,256]{2,1,0:T(8,128)(2,1)S(1)}, u32[]{:S(2)}, u32[]{:S(2)}) collective-permute-start(bf16[4,64,256]{2,1,0:T(8,128)(2,1)S(1)} %collective-permute-done.7), channel_id=1, source_target_pairs={{0,28},{4,0},{8,4},{12,8},{16,12},{20,16},{24,20},{28,24},{1,29},{... | collective-permute-start | bytes 393224 | tf_op jit(solution)/shard_map/ppermute | solution.py:30
  53.5 4.6 %collective-permute-start.9 = (bf16[4,64,256]{2,1,0:T(8,128)(2,1)S(1)}, bf16[4,64,256]{2,1,0:T(8,128)(2,1)S(1)}, u32[]{:S(2)}, u32[]{:S(2)}) collective-permute-start(bf16[4,64,256]{2,1,0:T(8,128)(2,1)S(1)} %collective-permute-done.8), channel_id=1, source_target_pairs={{0,28},{4,0},{8,4},{12,8},{16,12},{20,16},{24,20},{28,24},{1,29},{... | collective-permute-start | bytes 393224 | tf_op jit(solution)/shard_map/ppermute | solution.py:30
  60.0 2.8 collective-permute-start.10
  62.9 3.6 %collective-permute-start.12 = (bf16[8,4,64,256]{3,2,1,0:T(8,128)(2,1)S(1)}, bf16[8,4,64,256]{3,2,1,0:T(8,128)(2,1)}, u32[]{:S(2)}, u32[]{:S(2)}) collective-permute-start(bf16[8,4,64,256]{3,2,1,0:T(8,128)(2,1)S(1)} %bitcast_dynamic-update-slice_fusion), channel_id=1, source_target_pairs={{0,96},{32,0},{64,32},{96,64},{1,97},{33,1},{65,33},{97,65},{2,98}... | collective-permute-start | bytes 3145736 | tf_op jit(solution)/shard_map/ppermute | solution.py:30
  66.5 16.2 %collective-permute-done.10 = bf16[8,4,64,256]{3,2,1,0:T(8,128)(2,1)S(1)} collective-permute-done((bf16[8,4,64,256]{3,2,1,0:T(8,128)(2,1)S(1)}, bf16[8,4,64,256]{3,2,1,0:T(8,128)(2,1)S(1)}, u32[]{:S(2)}, u32[]{:S(2)}) %collective-permute-start.10) | collective-permute-done | bytes 1048608 | tf_op jit(solution)/shard_map/ppermute | solution.py:27
  88.0 17.8 %collective-permute-done.11 = bf16[8,4,64,256]{3,2,1,0:T(8,128)(2,1)} collective-permute-done((bf16[8,4,64,256]{3,2,1,0:T(8,128)(2,1)S(1)}, bf16[8,4,64,256]{3,2,1,0:T(8,128)(2,1)}, u32[]{:S(2)}, u32[]{:S(2)}) %collective-permute-start.11) | collective-permute-done | bytes 1048608 | tf_op jit(solution)/shard_map/ppermute | solution.py:27
  105.7 3.5 %pad_maximum_fusion = bf16[4,8,4,64,256]{4,3,2,1,0:T(8,128)(2,1)} fusion(bf16[1,8,4,64,256]{4,3,2,1,0:T(8,128)(2,1)} %bitcast.21, bf16[1,8,4,64,256]{4,3,2,1,0:T(8,128)(2,1)S(1)} %bitcast.51, bf16[1,8,4,64,256]{4,3,2,1,0:T(8,128)(2,1)S(1)} %bitcast.52, bf16[1,8,4,64,256]{4,3,2,1,0:T(8,128)(2,1)} %bitcast.18), kind=kLoop, calls=%fused_computation.2 | loop fusion | flops 6291456 | bytes 8388608 | tf_op jit(solution)/shard_map/stack | solution.py:32
  109.3 2.8 gather_fusion.1
  112.1 33.8 %all-gather.2.cloned.1.call-done = bf16[8192,256]{1,0:T(8,128)(2,1)} async-done(((bf16[64,256]{1,0:T(8,128)(2,1)}), bf16[8192,256]{1,0:T(8,128)(2,1)}) %all-gather.2.cloned.1.call-update) | async-done | bytes 4194320 | tf_op jit(solution)/shard_map/all_gather | solution.py:112
  145.9 2.7 gather_fusion
  150.5 23.4 %reduce-scatter.2.cloned.1.call-done = f32[128,256]{1,0:T(8,128)} async-done(((f32[512,256]{1,0:T(8,128)}), f32[128,256]{1,0:T(8,128)}) %reduce-scatter.2.cloned.1.call-update) | async-done | bytes 131088 | tf_op jit(solution)/shard_map/reduce_scatter | solution.py:122
  180.4 2.4 collective-permute-start.14
  182.8 7.4 %collective-permute-done.14 = f32[264,256]{1,0:T(8,128)S(1)} collective-permute-done((f32[264,256]{1,0:T(8,128)S(1)}, f32[264,256]{1,0:T(8,128)S(1)}, u32[]{:S(2)}, u32[]{:S(2)}) %collective-permute-start.14) | collective-permute-done | bytes 270368 | tf_op jit(solution)/shard_map/ppermute | solution.py:89
  190.3 7.8 %collective-permute-start.15 = (f32[264,256]{1,0:T(8,128)S(1)}, f32[264,256]{1,0:T(8,128)S(1)}, u32[]{:S(2)}, u32[]{:S(2)}) collective-permute-start(f32[264,256]{1,0:T(8,128)S(1)} %add.119), channel_id=1, source_target_pairs={{0,16},{4,20},{8,24},{12,28},{16,0},{20,4},{24,8},{28,12},{1,17},{... | collective-permute-start | bytes 811016 | tf_op jit(solution)/shard_map/ppermute | solution.py:89
  198.0 7.4 %collective-permute-done.15 = f32[264,256]{1,0:T(8,128)S(1)} collective-permute-done((f32[264,256]{1,0:T(8,128)S(1)}, f32[264,256]{1,0:T(8,128)S(1)}, u32[]{:S(2)}, u32[]{:S(2)}) %collective-permute-start.15) | collective-permute-done | bytes 270368 | tf_op jit(solution)/shard_map/ppermute | solution.py:89
  205.4 9.2 %collective-permute-start.16 = (f32[264,256]{1,0:T(8,128)S(1)}, f32[264,256]{1,0:T(8,128)S(1)}, u32[]{:S(2)}, u32[]{:S(2)}) collective-permute-start(f32[264,256]{1,0:T(8,128)S(1)} %add.120), channel_id=1, source_target_pairs={{0,8},{4,12},{8,0},{12,4},{16,24},{20,28},{24,16},{28,20},{1,9},{5... | collective-permute-start | bytes 811016 | tf_op jit(solution)/shard_map/ppermute | solution.py:89
  214.6 9.0 %collective-permute-done.16 = f32[264,256]{1,0:T(8,128)S(1)} collective-permute-done((f32[264,256]{1,0:T(8,128)S(1)}, f32[264,256]{1,0:T(8,128)S(1)}, u32[]{:S(2)}, u32[]{:S(2)}) %collective-permute-start.16) | collective-permute-done | bytes 270368 | tf_op jit(solution)/shard_map/ppermute | solution.py:89
  225.6 6.7 %collective-permute-done.17 = f32[264,256]{1,0:T(8,128)S(1)} collective-permute-done((f32[264,256]{1,0:T(8,128)S(1)}, f32[264,256]{1,0:T(8,128)S(1)}, u32[]{:S(2)}, u32[]{:S(2)}) %collective-permute-start.17) | collective-permute-done | bytes 270368 | tf_op jit(solution)/shard_map/ppermute | solution.py:89
  232.3 7.0 %collective-permute-start.18 = (f32[264,256]{1,0:T(8,128)S(1)}, f32[264,256]{1,0:T(8,128)S(1)}, u32[]{:S(2)}, u32[]{:S(2)}) collective-permute-start(f32[264,256]{1,0:T(8,128)S(1)} %add.122), channel_id=1, source_target_pairs={{0,64},{32,96},{64,0},{96,32},{1,65},{33,97},{65,1},{97,33},{2,66}... | collective-permute-start | bytes 811016 | tf_op jit(solution)/shard_map/ppermute | solution.py:89
  239.3 5.4 %collective-permute-done.18 = f32[264,256]{1,0:T(8,128)S(1)} collective-permute-done((f32[264,256]{1,0:T(8,128)S(1)}, f32[264,256]{1,0:T(8,128)S(1)}, u32[]{:S(2)}, u32[]{:S(2)}) %collective-permute-start.18) | collective-permute-done | bytes 270368 | tf_op jit(solution)/shard_map/ppermute | solution.py:89
  246.7 6.0 %collective-permute-done.19 = f32[264,256]{1,0:T(8,128)S(1)} collective-permute-done((f32[264,256]{1,0:T(8,128)S(1)}, f32[264,256]{1,0:T(8,128)S(1)}, u32[]{:S(2)}, u32[]{:S(2)}) %collective-permute-start.19) | collective-permute-done | bytes 270368 | tf_op jit(solution)/shard_map/ppermute | solution.py:89
  252.7 6.0 %collective-permute-start.20 = (f32[264,256]{1,0:T(8,128)S(1)}, f32[264,256]{1,0:T(8,128)S(1)}, u32[]{:S(2)}, u32[]{:S(2)}) collective-permute-start(f32[264,256]{1,0:T(8,128)S(1)} %add.124), channel_id=1, source_target_pairs={{0,256},{128,384},{256,0},{384,128},{1,257},{129,385},{257,1},{385... | collective-permute-start | bytes 811016 | tf_op jit(solution)/shard_map/ppermute | solution.py:89
  258.7 8.8 %collective-permute-done.20 = f32[264,256]{1,0:T(8,128)S(1)} collective-permute-done((f32[264,256]{1,0:T(8,128)S(1)}, f32[264,256]{1,0:T(8,128)S(1)}, u32[]{:S(2)}, u32[]{:S(2)}) %collective-permute-start.20) | collective-permute-done | bytes 270368 | tf_op jit(solution)/shard_map/ppermute | solution.py:89
  267.6 5.9 %collective-permute-start.21 = (f32[264,256]{1,0:T(8,128)S(1)}, f32[264,256]{1,0:T(8,128)S(1)}, u32[]{:S(2)}, u32[]{:S(2)}) collective-permute-start(f32[264,256]{1,0:T(8,128)S(1)} %add.125), channel_id=1, source_target_pairs={{0,128},{128,0},{256,384},{384,256},{1,129},{129,1},{257,385},{385... | collective-permute-start | bytes 811016 | tf_op jit(solution)/shard_map/ppermute | solution.py:89
  273.5 10.5 %collective-permute-done.21 = f32[264,256]{1,0:T(8,128)S(1)} collective-permute-done((f32[264,256]{1,0:T(8,128)S(1)}, f32[264,256]{1,0:T(8,128)S(1)}, u32[]{:S(2)}, u32[]{:S(2)}) %collective-permute-start.21) | collective-permute-done | bytes 270368 | tf_op jit(solution)/shard_map/ppermute | solution.py:89
  (65 shorter events, 29.5 us)
Async XLA Ops:
  7.2 141.6 %copy-start = (bf16[1,4,8,128,128]{4,3,2,1,0:T(8,128)(2,1)S(1)}, bf16[1,4,8,128,128]{4,3,2,1,0:T(8,128)(2,1)}, u32[]{:S(2)}) copy-start(bf16[1,4,8,128,128]{4,3,2,1,0:T(8,128)(2,1)} %param.13) | copy-start | bytes 3145732
  7.2 138.7 %all-gather.2.cloned.1.call-start = ((), (), s32[]{:S(2)}) async-start(), calls=%async_computation.1 | async-start | bytes 4227072 | tf_op jit(solution)/shard_map/all_gather | solution.py:112
  8.7 165.2 %reduce-scatter.2.cloned.1.call-start = ((), (), s32[]{:S(2)}) async-start(), calls=%async_computation.2 | async-start | bytes 655360 | tf_op jit(solution)/shard_map/reduce_scatter | solution.py:122
  8.8 8.6 %collective-permute-start = (bf16[64,256]{1,0:T(8,128)(2,1)S(1)}, bf16[64,256]{1,0:T(8,128)(2,1)S(1)}, u32[]{:S(2)}, u32[]{:S(2)}) collective-permute-start(bf16[64,256]{1,0:T(8,128)(2,1)S(1)} %get-tuple-element.13), channel_id=1, source_target_pairs={{0,128},{128,256},{256,384},{384,0},{1,129},{129,257},{257,385},{3... | collective-permute-start | bytes 98312 | tf_op jit(solution)/shard_map/ppermute | solution.py:27
  13.8 7.4 %collective-permute-start.2 = (bf16[64,256]{1,0:T(8,128)(2,1)S(1)}, bf16[64,256]{1,0:T(8,128)(2,1)S(1)}, u32[]{:S(2)}, u32[]{:S(2)}) collective-permute-start(bf16[64,256]{1,0:T(8,128)(2,1)S(1)} %get-tuple-element.13), channel_id=1, source_target_pairs={{0,384},{128,0},{256,128},{384,256},{1,385},{129,1},{257,129},{385... | collective-permute-start | bytes 98312 | tf_op jit(solution)/shard_map/ppermute | solution.py:30
  17.4 6.8 %collective-permute-start.1 = (bf16[64,256]{1,0:T(8,128)(2,1)S(1)}, bf16[64,256]{1,0:T(8,128)(2,1)S(1)}, u32[]{:S(2)}, u32[]{:S(2)}) collective-permute-start(bf16[64,256]{1,0:T(8,128)(2,1)S(1)} %collective-permute-done), channel_id=1, source_target_pairs={{0,128},{128,256},{256,384},{384,0},{1,129},{129,257},{257,385},{3... | collective-permute-start | bytes 98312 | tf_op jit(solution)/shard_map/ppermute | solution.py:27
  24.3 13.0 %collective-permute-start.3 = (bf16[4,64,256]{2,1,0:T(8,128)(2,1)S(1)}, bf16[4,64,256]{2,1,0:T(8,128)(2,1)S(1)}, u32[]{:S(2)}, u32[]{:S(2)}) collective-permute-start(bf16[4,64,256]{2,1,0:T(8,128)(2,1)S(1)} %pad_maximum_fusion.1), channel_id=1, source_target_pairs={{0,4},{4,8},{8,12},{12,16},{16,20},{20,24},{24,28},{28,0},{1,5},{5... | collective-permute-start | bytes 393224 | tf_op jit(solution)/shard_map/ppermute | solution.py:27
  37.3 7.3 %collective-permute-start.4 = (bf16[4,64,256]{2,1,0:T(8,128)(2,1)S(1)}, bf16[4,64,256]{2,1,0:T(8,128)(2,1)S(1)}, u32[]{:S(2)}, u32[]{:S(2)}) collective-permute-start(bf16[4,64,256]{2,1,0:T(8,128)(2,1)S(1)} %collective-permute-done.3), channel_id=1, source_target_pairs={{0,4},{4,8},{8,12},{12,16},{16,20},{20,24},{24,28},{28,0},{1,5},{5... | collective-permute-start | bytes 393224 | tf_op jit(solution)/shard_map/ppermute | solution.py:27
  39.2 7.3 %collective-permute-start.7 = (bf16[4,64,256]{2,1,0:T(8,128)(2,1)S(1)}, bf16[4,64,256]{2,1,0:T(8,128)(2,1)S(1)}, u32[]{:S(2)}, u32[]{:S(2)}) collective-permute-start(bf16[4,64,256]{2,1,0:T(8,128)(2,1)S(1)} %pad_maximum_fusion.1), channel_id=1, source_target_pairs={{0,28},{4,0},{8,4},{12,8},{16,12},{20,16},{24,20},{28,24},{1,29},{... | collective-permute-start | bytes 393224 | tf_op jit(solution)/shard_map/ppermute | solution.py:30
  44.6 6.9 %collective-permute-start.5 = (bf16[4,64,256]{2,1,0:T(8,128)(2,1)S(1)}, bf16[4,64,256]{2,1,0:T(8,128)(2,1)S(1)}, u32[]{:S(2)}, u32[]{:S(2)}) collective-permute-start(bf16[4,64,256]{2,1,0:T(8,128)(2,1)S(1)} %collective-permute-done.4), channel_id=1, source_target_pairs={{0,4},{4,8},{8,12},{12,16},{16,20},{20,24},{24,28},{28,0},{1,5},{5... | collective-permute-start | bytes 393224 | tf_op jit(solution)/shard_map/ppermute | solution.py:27
  46.5 6.9 %collective-permute-start.8 = (bf16[4,64,256]{2,1,0:T(8,128)(2,1)S(1)}, bf16[4,64,256]{2,1,0:T(8,128)(2,1)S(1)}, u32[]{:S(2)}, u32[]{:S(2)}) collective-permute-start(bf16[4,64,256]{2,1,0:T(8,128)(2,1)S(1)} %collective-permute-done.7), channel_id=1, source_target_pairs={{0,28},{4,0},{8,4},{12,8},{16,12},{20,16},{24,20},{28,24},{1,29},{... | collective-permute-start | bytes 393224 | tf_op jit(solution)/shard_map/ppermute | solution.py:30
  51.6 7.0 %collective-permute-start.6 = (bf16[4,64,256]{2,1,0:T(8,128)(2,1)S(1)}, bf16[4,64,256]{2,1,0:T(8,128)(2,1)S(1)}, u32[]{:S(2)}, u32[]{:S(2)}) collective-permute-start(bf16[4,64,256]{2,1,0:T(8,128)(2,1)S(1)} %collective-permute-done.5), channel_id=1, source_target_pairs={{0,4},{4,8},{8,12},{12,16},{16,20},{20,24},{24,28},{28,0},{1,5},{5... | collective-permute-start | bytes 393224 | tf_op jit(solution)/shard_map/ppermute | solution.py:27
  53.5 6.5 %collective-permute-start.9 = (bf16[4,64,256]{2,1,0:T(8,128)(2,1)S(1)}, bf16[4,64,256]{2,1,0:T(8,128)(2,1)S(1)}, u32[]{:S(2)}, u32[]{:S(2)}) collective-permute-start(bf16[4,64,256]{2,1,0:T(8,128)(2,1)S(1)} %collective-permute-done.8), channel_id=1, source_target_pairs={{0,28},{4,0},{8,4},{12,8},{16,12},{20,16},{24,20},{28,24},{1,29},{... | collective-permute-start | bytes 393224 | tf_op jit(solution)/shard_map/ppermute | solution.py:30
  60.0 22.7 %collective-permute-start.10 = (bf16[8,4,64,256]{3,2,1,0:T(8,128)(2,1)S(1)}, bf16[8,4,64,256]{3,2,1,0:T(8,128)(2,1)S(1)}, u32[]{:S(2)}, u32[]{:S(2)}) collective-permute-start(bf16[8,4,64,256]{3,2,1,0:T(8,128)(2,1)S(1)} %bitcast_dynamic-update-slice_fusion), channel_id=1, source_target_pairs={{0,32},{32,64},{64,96},{96,0},{1,33},{33,65},{65,97},{97,1},{2,34}... | collective-permute-start | bytes 3145736 | tf_op jit(solution)/shard_map/ppermute | solution.py:27
  62.9 25.1 %collective-permute-start.12 = (bf16[8,4,64,256]{3,2,1,0:T(8,128)(2,1)S(1)}, bf16[8,4,64,256]{3,2,1,0:T(8,128)(2,1)}, u32[]{:S(2)}, u32[]{:S(2)}) collective-permute-start(bf16[8,4,64,256]{3,2,1,0:T(8,128)(2,1)S(1)} %bitcast_dynamic-update-slice_fusion), channel_id=1, source_target_pairs={{0,96},{32,0},{64,32},{96,64},{1,97},{33,1},{65,33},{97,65},{2,98}... | collective-permute-start | bytes 3145736 | tf_op jit(solution)/shard_map/ppermute | solution.py:30
  82.7 23.0 %collective-permute-start.11 = (bf16[8,4,64,256]{3,2,1,0:T(8,128)(2,1)S(1)}, bf16[8,4,64,256]{3,2,1,0:T(8,128)(2,1)}, u32[]{:S(2)}, u32[]{:S(2)}) collective-permute-start(bf16[8,4,64,256]{3,2,1,0:T(8,128)(2,1)S(1)} %collective-permute-done.10), channel_id=1, source_target_pairs={{0,32},{32,64},{64,96},{96,0},{1,33},{33,65},{65,97},{97,1},{2,34}... | collective-permute-start | bytes 3145736 | tf_op jit(solution)/shard_map/ppermute | solution.py:27
  109.2 64.6 %copy-start.1 = (bf16[256,256]{1,0:T(8,128)(2,1)S(1)}, bf16[256,256]{1,0:T(8,128)(2,1)}, u32[]{:S(2)}) copy-start(bf16[256,256]{1,0:T(8,128)(2,1)} %param.11) | copy-start | bytes 393220
  109.2 64.6 %copy-start.2 = (bf16[128,256]{1,0:T(8,128)(2,1)S(1)}, bf16[128,256]{1,0:T(8,128)(2,1)}, u32[]{:S(2)}) copy-start(bf16[128,256]{1,0:T(8,128)(2,1)} %param.17) | copy-start | bytes 196612
  109.2 64.6 %copy-start.3 = (f32[256]{0:T(256)S(1)}, f32[256]{0:T(256)}, u32[]{:S(2)}) copy-start(f32[256]{0:T(256)} %param.12) | copy-start | bytes 3076
  176.9 3.4 %collective-permute-start.13 = (f32[264,256]{1,0:T(8,128)S(1)}, f32[264,256]{1,0:T(8,128)S(1)}, u32[]{:S(2)}, u32[]{:S(2)}) collective-permute-start(f32[264,256]{1,0:T(8,128)S(1)} %maximum_maximum_fusion), channel_id=1, source_target_pairs={{0,1},{1,0},{2,3},{3,2},{4,5},{5,4},{6,7},{7,6},{8,9},{9,8},{10,11... | collective-permute-start | bytes 811016 | tf_op jit(solution)/shard_map/ppermute | solution.py:89
  180.4 9.8 %collective-permute-start.14 = (f32[264,256]{1,0:T(8,128)S(1)}, f32[264,256]{1,0:T(8,128)S(1)}, u32[]{:S(2)}, u32[]{:S(2)}) collective-permute-start(f32[264,256]{1,0:T(8,128)S(1)} %fusion.33), channel_id=1, source_target_pairs={{0,2},{2,0},{1,3},{3,1},{4,6},{6,4},{5,7},{7,5},{8,10},{10,8},{9,1... | collective-permute-start | bytes 811016 | tf_op jit(solution)/shard_map/ppermute | solution.py:89
  190.3 15.1 %collective-permute-start.15 = (f32[264,256]{1,0:T(8,128)S(1)}, f32[264,256]{1,0:T(8,128)S(1)}, u32[]{:S(2)}, u32[]{:S(2)}) collective-permute-start(f32[264,256]{1,0:T(8,128)S(1)} %add.119), channel_id=1, source_target_pairs={{0,16},{4,20},{8,24},{12,28},{16,0},{20,4},{24,8},{28,12},{1,17},{... | collective-permute-start | bytes 811016 | tf_op jit(solution)/shard_map/ppermute | solution.py:89
  205.4 18.2 %collective-permute-start.16 = (f32[264,256]{1,0:T(8,128)S(1)}, f32[264,256]{1,0:T(8,128)S(1)}, u32[]{:S(2)}, u32[]{:S(2)}) collective-permute-start(f32[264,256]{1,0:T(8,128)S(1)} %add.120), channel_id=1, source_target_pairs={{0,8},{4,12},{8,0},{12,4},{16,24},{20,28},{24,16},{28,20},{1,9},{5... | collective-permute-start | bytes 811016 | tf_op jit(solution)/shard_map/ppermute | solution.py:89
  223.6 8.6 %collective-permute-start.17 = (f32[264,256]{1,0:T(8,128)S(1)}, f32[264,256]{1,0:T(8,128)S(1)}, u32[]{:S(2)}, u32[]{:S(2)}) collective-permute-start(f32[264,256]{1,0:T(8,128)S(1)} %add.121), channel_id=1, source_target_pairs={{0,4},{4,0},{8,12},{12,8},{16,20},{20,16},{24,28},{28,24},{1,5},{5... | collective-permute-start | bytes 811016 | tf_op jit(solution)/shard_map/ppermute | solution.py:89
  232.3 12.4 %collective-permute-start.18 = (f32[264,256]{1,0:T(8,128)S(1)}, f32[264,256]{1,0:T(8,128)S(1)}, u32[]{:S(2)}, u32[]{:S(2)}) collective-permute-start(f32[264,256]{1,0:T(8,128)S(1)} %add.122), channel_id=1, source_target_pairs={{0,64},{32,96},{64,0},{96,32},{1,65},{33,97},{65,1},{97,33},{2,66}... | collective-permute-start | bytes 811016 | tf_op jit(solution)/shard_map/ppermute | solution.py:89
  244.7 8.0 %collective-permute-start.19 = (f32[264,256]{1,0:T(8,128)S(1)}, f32[264,256]{1,0:T(8,128)S(1)}, u32[]{:S(2)}, u32[]{:S(2)}) collective-permute-start(f32[264,256]{1,0:T(8,128)S(1)} %add.123), channel_id=1, source_target_pairs={{0,32},{32,0},{64,96},{96,64},{1,33},{33,1},{65,97},{97,65},{2,34}... | collective-permute-start | bytes 811016 | tf_op jit(solution)/shard_map/ppermute | solution.py:89
  252.7 14.8 %collective-permute-start.20 = (f32[264,256]{1,0:T(8,128)S(1)}, f32[264,256]{1,0:T(8,128)S(1)}, u32[]{:S(2)}, u32[]{:S(2)}) collective-permute-start(f32[264,256]{1,0:T(8,128)S(1)} %add.124), channel_id=1, source_target_pairs={{0,256},{128,384},{256,0},{384,128},{1,257},{129,385},{257,1},{385... | collective-permute-start | bytes 811016 | tf_op jit(solution)/shard_map/ppermute | solution.py:89
  267.6 16.4 %collective-permute-start.21 = (f32[264,256]{1,0:T(8,128)S(1)}, f32[264,256]{1,0:T(8,128)S(1)}, u32[]{:S(2)}, u32[]{:S(2)}) collective-permute-start(f32[264,256]{1,0:T(8,128)S(1)} %add.125), channel_id=1, source_target_pairs={{0,128},{128,0},{256,384},{384,256},{1,129},{129,1},{257,385},{385... | collective-permute-start | bytes 811016 | tf_op jit(solution)/shard_map/ppermute | solution.py:89
Sparse Core Ops, SparseCore 0:
  13.1 132.7 all-gather.1
  150.5 23.3 reduce-scatter.1

commit v3 on v2

--- a/solution.py
+++ b/solution.py
@@ -85,16 +85,26 @@
 
 
 def reduce_all(packed):
-    for a, b, perm in halving_steps(("core", "y_lo", "z", "x", "y_hi")):
-        packed = packed + lax.ppermute(packed, a, perm)
-    return packed
+    rep_steps = halving_steps(("core", "y_lo"))
+    flat = reduce_scatter_flat(packed.reshape(-1), rep_steps)
+    for a, b, perm in halving_steps(ROW_AXES[::-1]):
+        flat = flat + lax.ppermute(flat, a, perm)
+    flat = all_gather_flat(flat, rep_steps)
+    return flat.reshape(packed.shape)
 
 
 def reduce_over_rep(partial_value):
-    steps = halving_steps(("y_lo", "core"))
     rows, width = partial_value.shape
-    flat = reduce_scatter_flat(partial_value.reshape(-1), steps)
-    return flat.reshape(rows // lax.axis_size(REP_AXES), width)
+    blocks = partial_value.reshape(lax.axis_size("y_lo"), lax.axis_size("core"), -1)
+    core = lax.axis_index("core")
+    send = jnp.where(core == 1, blocks[:, 0], blocks[:, 1])
+    keep = jnp.where(core == 1, blocks[:, 1], blocks[:, 0])
+    pairs = keep + lax.ppermute(send, "core", [(0, 1), (1, 0)])
+    y_lo = lax.axis_index("y_lo")
+    send = jnp.where(y_lo == 1, pairs[0], pairs[1])
+    keep = jnp.where(y_lo == 1, pairs[1], pairs[0])
+    own = keep + lax.ppermute(send, "y_lo", [(0, 1), (1, 0)])
+    return own.reshape(rows // lax.axis_size(REP_AXES), width)
 
 
 def shards(features, weight, bias_terms, tile_data, tile_row, tile_col, tile_count, grad_out):
@@ -119,9 +129,7 @@
     select = ((own_rows[None, :] == local_ids[:, None]) & live[None, :]).astype(jnp.float32)
     partial_value = jnp.einsum("bt,tif->bif", select, product)
     partial_value = partial_value.reshape(row_count * block_size, feature_width)
-    propagated = lax.psum_scatter(partial_value, REP_AXES, scatter_dimension=0, tiled=True).astype(
-        jnp.bfloat16
-    )
+    propagated = reduce_over_rep(partial_value).astype(jnp.bfloat16)
     preact = jnp.dot(propagated, weight, preferred_element_type=jnp.float32) + bias_terms
     sigma = jax.nn.sigmoid(preact)
     layer_out = (preact * sigma).astype(jnp.bfloat16)

time: 293 us -> 251 us (0.86)
  waiting for transfers between devices: 169 us -> 118 us
  starting transfers between devices: 88.3 us -> 98 us
    ppermute x9 -> x13, waiting for transfers between devices: 62.6 us -> 35.5 us  [the longest x7 22.6 us: reduce_all(): flat = flat + lax.ppermute(flat, a, perm)]
    reduce_scatter x1 -> x0, waiting for transfers between devices: 23.4 us -> none  [shards(): lax.psum_scatter(partial_value, REP_AXES, scatter_dimension=0, tiled=True)]
    ppermute x9 -> x13, starting transfers between devices: 44 us -> 53.8 us  [the longest x7 27.6 us: reduce_all(): flat = flat + lax.ppermute(flat, a, perm)]
  transfers between devices with their start and end apart: 24 -> 27, of which waited for: 19 -> 22; matrix products, arithmetic and copies ran while one was open for 3% -> 4% of each run, Pallas kernels for 0% -> 0%
where the time goes in v3:
time: 251 us; the launch traced here: 250 us
  waiting for transfers between devices  118 us (47%)
  starting transfers between devices  98 us (39%)
  between operations  14.6 us (6%)
  local copies, waits for them, and re-layouts  9.87 us (4%)
  other arithmetic  7.64 us (3%)
    ppermute x8, waiting for transfers between devices, ring_gather(): left = lax.ppermute(left, axis, fwd)  47.7 us
    all_gather x1, waiting for transfers between devices, shards(): stripe_nodes = lax.all_gather(near, ROW_AXES, axis=0, tiled=True)  33.4 us
    ppermute x7, starting transfers between devices, reduce_all(): flat = flat + lax.ppermute(flat, a, perm)  27.6 us
    ppermute x8, starting transfers between devices, ring_gather(): left = lax.ppermute(left, axis, fwd)  23.3 us
    ppermute x7, waiting for transfers between devices, reduce_all(): flat = flat + lax.ppermute(flat, a, perm)  22.6 us
    ppermute x5, starting transfers between devices, ring_gather(): right = lax.ppermute(right, axis, bwd)  20.9 us
    ppermute x2, starting transfers between devices, all_gather_flat(): other = lax.ppermute(flat, a, perm)  12.7 us
    ppermute x1, starting transfers between devices, reduce_over_rep(): pairs = keep + lax.ppermute(send, 'core', [(0, 1), (1, 0)])  5.54 us
  transfers between devices with their start and end apart: 27, of which 22 were waited for; matrix products, arithmetic and copies ran while one was open for 4% of the time, Pallas kernels for 0%

profile of v3, /device:TPU:1, one launch (start us, length us, event | category | flops | bytes accessed | tf_op | source)
XLA Modules:
  0.0 249.8 jit_solution(15242185687770093398)
XLA Ops:
  8.7 5.0 %collective-permute-start = (bf16[64,256]{1,0:T(8,128)(2,1)S(1)}, bf16[64,256]{1,0:T(8,128)(2,1)S(1)}, u32[]{:S(2)}, u32[]{:S(2)}) collective-permute-start(bf16[64,256]{1,0:T(8,128)(2,1)S(1)} %get-tuple-element.20), channel_id=1, source_target_pairs={{0,128},{128,256},{256,384},{384,0},{1,129},{129,257},{257,385},{3... | collective-permute-start | bytes 98312 | tf_op jit(solution)/shard_map/ppermute | solution.py:27
  13.8 3.6 %collective-permute-start.2 = (bf16[64,256]{1,0:T(8,128)(2,1)S(1)}, bf16[64,256]{1,0:T(8,128)(2,1)S(1)}, u32[]{:S(2)}, u32[]{:S(2)}) collective-permute-start(bf16[64,256]{1,0:T(8,128)(2,1)S(1)} %get-tuple-element.20), channel_id=1, source_target_pairs={{0,384},{128,0},{256,128},{384,256},{1,385},{129,1},{257,129},{385... | collective-permute-start | bytes 98312 | tf_op jit(solution)/shard_map/ppermute | solution.py:30
  17.4 3.8 %collective-permute-start.1 = (bf16[64,256]{1,0:T(8,128)(2,1)S(1)}, bf16[64,256]{1,0:T(8,128)(2,1)S(1)}, u32[]{:S(2)}, u32[]{:S(2)}) collective-permute-start(bf16[64,256]{1,0:T(8,128)(2,1)S(1)} %collective-permute-done), channel_id=1, source_target_pairs={{0,128},{128,256},{256,384},{384,0},{1,129},{129,257},{257,385},{3... | collective-permute-start | bytes 98312 | tf_op jit(solution)/shard_map/ppermute | solution.py:27
  21.2 3.0 %collective-permute-done.1 = bf16[64,256]{1,0:T(8,128)(2,1)S(1)} collective-permute-done((bf16[64,256]{1,0:T(8,128)(2,1)S(1)}, bf16[64,256]{1,0:T(8,128)(2,1)S(1)}, u32[]{:S(2)}, u32[]{:S(2)}) %collective-permute-start.1) | collective-permute-done | bytes 32800 | tf_op jit(solution)/shard_map/ppermute | solution.py:27
  24.2 4.0 %collective-permute-start.3 = (bf16[4,64,256]{2,1,0:T(8,128)(2,1)S(1)}, bf16[4,64,256]{2,1,0:T(8,128)(2,1)S(1)}, u32[]{:S(2)}, u32[]{:S(2)}) collective-permute-start(bf16[4,64,256]{2,1,0:T(8,128)(2,1)S(1)} %pad_maximum_fusion.4), channel_id=1, source_target_pairs={{0,4},{4,8},{8,12},{12,16},{16,20},{20,24},{24,28},{28,0},{1,5},{5... | collective-permute-start | bytes 393224 | tf_op jit(solution)/shard_map/ppermute | solution.py:27
  28.2 9.0 %collective-permute-done.3 = bf16[4,64,256]{2,1,0:T(8,128)(2,1)S(1)} collective-permute-done((bf16[4,64,256]{2,1,0:T(8,128)(2,1)S(1)}, bf16[4,64,256]{2,1,0:T(8,128)(2,1)S(1)}, u32[]{:S(2)}, u32[]{:S(2)}) %collective-permute-start.3) | collective-permute-done | bytes 131104 | tf_op jit(solution)/shard_map/ppermute | solution.py:27
  39.2 4.6 %collective-permute-start.7 = (bf16[4,64,256]{2,1,0:T(8,128)(2,1)S(1)}, bf16[4,64,256]{2,1,0:T(8,128)(2,1)S(1)}, u32[]{:S(2)}, u32[]{:S(2)}) collective-permute-start(bf16[4,64,256]{2,1,0:T(8,128)(2,1)S(1)} %pad_maximum_fusion.4), channel_id=1, source_target_pairs={{0,28},{4,0},{8,4},{12,8},{16,12},{20,16},{24,20},{28,24},{1,29},{... | collective-permute-start | bytes 393224 | tf_op jit(solution)/shard_map/ppermute | solution.py:30
  46.5 4.6 %collective-permute-start.8 = (bf16[4,64,256]{2,1,0:T(8,128)(2,1)S(1)}, bf16[4,64,256]{2,1,0:T(8,128)(2,1)S(1)}, u32[]{:S(2)}, u32[]{:S(2)}) collective-permute-start(bf16[4,64,256]{2,1,0:T(8,128)(2,1)S(1)} %collective-permute-done.7), channel_id=1, source_target_pairs={{0,28},{4,0},{8,4},{12,8},{16,12},{20,16},{24,20},{28,24},{1,29},{... | collective-permute-start | bytes 393224 | tf_op jit(solution)/shard_map/ppermute | solution.py:30
  53.4 4.6 %collective-permute-start.9 = (bf16[4,64,256]{2,1,0:T(8,128)(2,1)S(1)}, bf16[4,64,256]{2,1,0:T(8,128)(2,1)S(1)}, u32[]{:S(2)}, u32[]{:S(2)}) collective-permute-start(bf16[4,64,256]{2,1,0:T(8,128)(2,1)S(1)} %collective-permute-done.8), channel_id=1, source_target_pairs={{0,28},{4,0},{8,4},{12,8},{16,12},{20,16},{24,20},{28,24},{1,29},{... | collective-permute-start | bytes 393224 | tf_op jit(solution)/shard_map/ppermute | solution.py:30
  59.9 2.9 %collective-permute-start.10 = (bf16[8,4,64,256]{3,2,1,0:T(8,128)(2,1)S(1)}, bf16[8,4,64,256]{3,2,1,0:T(8,128)(2,1)S(1)}, u32[]{:S(2)}, u32[]{:S(2)}) collective-permute-start(bf16[8,4,64,256]{3,2,1,0:T(8,128)(2,1)S(1)} %bitcast_dynamic-update-slice_fusion), channel_id=1, source_target_pairs={{0,32},{32,64},{64,96},{96,0},{1,33},{33,65},{65,97},{97,1},{2,34}... | collective-permute-start | bytes 3145736 | tf_op jit(solution)/shard_map/ppermute | solution.py:27
  62.9 3.6 %collective-permute-start.12 = (bf16[8,4,64,256]{3,2,1,0:T(8,128)(2,1)S(1)}, bf16[8,4,64,256]{3,2,1,0:T(8,128)(2,1)}, u32[]{:S(2)}, u32[]{:S(2)}) collective-permute-start(bf16[8,4,64,256]{3,2,1,0:T(8,128)(2,1)S(1)} %bitcast_dynamic-update-slice_fusion), channel_id=1, source_target_pairs={{0,96},{32,0},{64,32},{96,64},{1,97},{33,1},{65,33},{97,65},{2,98}... | collective-permute-start | bytes 3145736 | tf_op jit(solution)/shard_map/ppermute | solution.py:30
  66.5 16.2 %collective-permute-done.10 = bf16[8,4,64,256]{3,2,1,0:T(8,128)(2,1)S(1)} collective-permute-done((bf16[8,4,64,256]{3,2,1,0:T(8,128)(2,1)S(1)}, bf16[8,4,64,256]{3,2,1,0:T(8,128)(2,1)S(1)}, u32[]{:S(2)}, u32[]{:S(2)}) %collective-permute-start.10) | collective-permute-done | bytes 1048608 | tf_op jit(solution)/shard_map/ppermute | solution.py:27
  87.9 17.8 %collective-permute-done.11 = bf16[8,4,64,256]{3,2,1,0:T(8,128)(2,1)} collective-permute-done((bf16[8,4,64,256]{3,2,1,0:T(8,128)(2,1)S(1)}, bf16[8,4,64,256]{3,2,1,0:T(8,128)(2,1)}, u32[]{:S(2)}, u32[]{:S(2)}) %collective-permute-start.11) | collective-permute-done | bytes 1048608 | tf_op jit(solution)/shard_map/ppermute | solution.py:27
  105.7 3.5 %pad_maximum_fusion = bf16[4,8,4,64,256]{4,3,2,1,0:T(8,128)(2,1)} fusion(bf16[1,8,4,64,256]{4,3,2,1,0:T(8,128)(2,1)} %bitcast.21, bf16[1,8,4,64,256]{4,3,2,1,0:T(8,128)(2,1)S(1)} %bitcast.59, bf16[1,8,4,64,256]{4,3,2,1,0:T(8,128)(2,1)S(1)} %bitcast.60, bf16[1,8,4,64,256]{4,3,2,1,0:T(8,128)(2,1)} %bitcast.18), kind=kLoop, calls=%fused_computation.2 | loop fusion | flops 6291456 | bytes 8388608 | tf_op jit(solution)/shard_map/stack | solution.py:32
  109.1 2.7 %gather_fusion.1 = bf16[8,64,256]{2,1,0:T(8,128)(2,1)S(1)} fusion(bf16[128,64,256]{2,1,0:T(8,128)(2,1)} %bitcast.58, s32[1024]{0:T(1024)S(1)} %pad_clamp_fusion), kind=kCustom, calls=%fused_computation.1.clone | custom fusion | bytes 524320 | tf_op jit(solution)/shard_map/jit(_take)/gather | solution.py:40
  111.9 33.4 %all-gather.2.cloned.1.call-done = bf16[8192,256]{1,0:T(8,128)(2,1)} async-done(((bf16[64,256]{1,0:T(8,128)(2,1)}), bf16[8192,256]{1,0:T(8,128)(2,1)}) %all-gather.2.cloned.1.call-update) | async-done | bytes 4194320 | tf_op jit(solution)/shard_map/all_gather | solution.py:122
  145.3 2.7 %gather_fusion = bf16[8,64,256]{2,1,0:T(8,128)(2,1)S(1)} fusion(bf16[128,64,256]{2,1,0:T(8,128)(2,1)} %bitcast.70, s32[1024]{0:T(1024)S(1)} %pad_clamp_fusion.1), kind=kCustom, calls=%fused_computation.clone | custom fusion | bytes 524320 | tf_op jit(solution)/shard_map/jit(_take)/gather | solution.py:123
  150.1 5.5 %collective-permute-start.13 = (f32[2,32768]{1,0:T(2,128)S(1)}, f32[2,32768]{1,0:T(2,128)S(1)}, u32[]{:S(2)}, u32[]{:S(2)}) collective-permute-start(f32[2,32768]{1,0:T(2,128)S(1)} %bitcast.62), channel_id=1, source_target_pairs={{0,1},{1,0},{2,3},{3,2},{4,5},{5,4},{6,7},{7,6},{8,9},{9,8},{10,11... | collective-permute-start | bytes 786440 | tf_op jit(solution)/shard_map/ppermute | solution.py:102
  159.8 4.1 %collective-permute-done.14 = f32[32768]{0:T(1024)S(1)} collective-permute-done((f32[32768]{0:T(1024)S(1)}, f32[32768]{0:T(1024)S(1)}, u32[]{:S(2)}, u32[]{:S(2)}) %collective-permute-start.14) | collective-permute-done | bytes 131104 | tf_op jit(solution)/shard_map/ppermute | solution.py:106
  165.2 3.1 %collective-permute-start.15 = (f32[33792]{0:T(1024)S(1)}, f32[33792]{0:T(1024)S(1)}, u32[]{:S(2)}, u32[]{:S(2)}) collective-permute-start(f32[33792]{0:T(1024)S(1)} %select_n.166), channel_id=1, source_target_pairs={{0,1},{1,0},{2,3},{3,2},{4,5},{5,4},{6,7},{7,6},{8,9},{9,8},{10,11... | collective-permute-start | bytes 405512 | tf_op jit(solution)/shard_map/ppermute | solution.py:73
  174.4 5.3 %collective-permute-start.17 = (f32[16896]{0:T(1024)S(1)}, f32[16896]{0:T(1024)S(1)}, u32[]{:S(2)}, u32[]{:S(2)}) collective-permute-start(f32[16896]{0:T(1024)S(1)} %select_add_fusion), channel_id=1, source_target_pairs={{0,16},{4,20},{8,24},{12,28},{16,0},{20,4},{24,8},{28,12},{1,17},{... | collective-permute-start | bytes 202760 | tf_op jit(solution)/shard_map/ppermute | solution.py:91
  179.8 3.7 %collective-permute-done.17 = f32[16896]{0:T(1024)S(1)} collective-permute-done((f32[16896]{0:T(1024)S(1)}, f32[16896]{0:T(1024)S(1)}, u32[]{:S(2)}, u32[]{:S(2)}) %collective-permute-start.17) | collective-permute-done | bytes 67616 | tf_op jit(solution)/shard_map/ppermute | solution.py:91
  183.5 4.3 %collective-permute-start.18 = (f32[16896]{0:T(1024)S(1)}, f32[16896]{0:T(1024)S(1)}, u32[]{:S(2)}, u32[]{:S(2)}) collective-permute-start(f32[16896]{0:T(1024)S(1)} %add.126), channel_id=1, source_target_pairs={{0,8},{4,12},{8,0},{12,4},{16,24},{20,28},{24,16},{28,20},{1,9},{5... | collective-permute-start | bytes 202760 | tf_op jit(solution)/shard_map/ppermute | solution.py:91
  192.2 3.1 %collective-permute-done.19 = f32[16896]{0:T(1024)S(1)} collective-permute-done((f32[16896]{0:T(1024)S(1)}, f32[16896]{0:T(1024)S(1)}, u32[]{:S(2)}, u32[]{:S(2)}) %collective-permute-start.19) | collective-permute-done | bytes 67616 | tf_op jit(solution)/shard_map/ppermute | solution.py:91
  195.3 4.6 %collective-permute-start.20 = (f32[16896]{0:T(1024)S(1)}, f32[16896]{0:T(1024)S(1)}, u32[]{:S(2)}, u32[]{:S(2)}) collective-permute-start(f32[16896]{0:T(1024)S(1)} %add.128), channel_id=1, source_target_pairs={{0,64},{32,96},{64,0},{96,32},{1,65},{33,97},{65,1},{97,33},{2,66}... | collective-permute-start | bytes 202760 | tf_op jit(solution)/shard_map/ppermute | solution.py:91
  201.9 2.9 %collective-permute-start.21 = (f32[16896]{0:T(1024)S(1)}, f32[16896]{0:T(1024)S(1)}, u32[]{:S(2)}, u32[]{:S(2)}) collective-permute-start(f32[16896]{0:T(1024)S(1)} %add.129), channel_id=1, source_target_pairs={{0,32},{32,0},{64,96},{96,64},{1,33},{33,1},{65,97},{97,65},{2,34}... | collective-permute-start | bytes 202760 | tf_op jit(solution)/shard_map/ppermute | solution.py:91
  207.5 4.1 %collective-permute-start.22 = (f32[16896]{0:T(1024)S(1)}, f32[16896]{0:T(1024)S(1)}, u32[]{:S(2)}, u32[]{:S(2)}) collective-permute-start(f32[16896]{0:T(1024)S(1)} %add.130), channel_id=1, source_target_pairs={{0,256},{128,384},{256,0},{384,128},{1,257},{129,385},{257,1},{385... | collective-permute-start | bytes 202760 | tf_op jit(solution)/shard_map/ppermute | solution.py:91
  211.6 5.0 %collective-permute-done.22 = f32[16896]{0:T(1024)S(1)} collective-permute-done((f32[16896]{0:T(1024)S(1)}, f32[16896]{0:T(1024)S(1)}, u32[]{:S(2)}, u32[]{:S(2)}) %collective-permute-start.22) | collective-permute-done | bytes 67616 | tf_op jit(solution)/shard_map/ppermute | solution.py:91
  216.6 4.4 %collective-permute-start.23 = (f32[16896]{0:T(1024)S(1)}, f32[16896]{0:T(1024)S(1)}, u32[]{:S(2)}, u32[]{:S(2)}) collective-permute-start(f32[16896]{0:T(1024)S(1)} %add.131), channel_id=1, source_target_pairs={{0,128},{128,0},{256,384},{384,256},{1,129},{129,1},{257,385},{385... | collective-permute-start | bytes 202760 | tf_op jit(solution)/shard_map/ppermute | solution.py:91
  221.0 3.8 %collective-permute-done.23 = f32[16896]{0:T(1024)S(1)} collective-permute-done((f32[16896]{0:T(1024)S(1)}, f32[16896]{0:T(1024)S(1)}, u32[]{:S(2)}, u32[]{:S(2)}) %collective-permute-start.23) | collective-permute-done | bytes 67616 | tf_op jit(solution)/shard_map/ppermute | solution.py:91
  226.7 3.1 %collective-permute-done.24 = f32[16896]{0:T(1024)S(1)} collective-permute-done((f32[16896]{0:T(1024)S(1)}, f32[16896]{0:T(1024)S(1)}, u32[]{:S(2)}, u32[]{:S(2)}) %collective-permute-start.24) | collective-permute-done | bytes 67616 | tf_op jit(solution)/shard_map/ppermute | solution.py:80
  229.9 10.8 %collective-permute-start.25 = (f32[33792]{0:T(1024)S(1)}, f32[33792]{0:T(1024)S(1)}, u32[]{:S(2)}, u32[]{:S(2)}) collective-permute-start(f32[33792]{0:T(1024)S(1)} %maximum_select_fusion.1), channel_id=1, source_target_pairs={{0,1},{1,0},{2,3},{3,2},{4,5},{5,4},{6,7},{7,6},{8,9},{9,8},{10,11... | collective-permute-start | bytes 405512 | tf_op jit(solution)/shard_map/ppermute | solution.py:80
  (85 shorter events, 42.3 us)
Async XLA Ops:
  7.2 141.1 %copy-start = (bf16[1,4,8,128,128]{4,3,2,1,0:T(8,128)(2,1)S(1)}, bf16[1,4,8,128,128]{4,3,2,1,0:T(8,128)(2,1)}, u32[]{:S(2)}) copy-start(bf16[1,4,8,128,128]{4,3,2,1,0:T(8,128)(2,1)} %param.13) | copy-start | bytes 3145732
  7.2 138.1 %all-gather.2.cloned.1.call-start = ((), (), s32[]{:S(2)}) async-start(), calls=%async_computation | async-start | bytes 4227072 | tf_op jit(solution)/shard_map/all_gather | solution.py:122
  8.7 8.6 %collective-permute-start = (bf16[64,256]{1,0:T(8,128)(2,1)S(1)}, bf16[64,256]{1,0:T(8,128)(2,1)S(1)}, u32[]{:S(2)}, u32[]{:S(2)}) collective-permute-start(bf16[64,256]{1,0:T(8,128)(2,1)S(1)} %get-tuple-element.20), channel_id=1, source_target_pairs={{0,128},{128,256},{256,384},{384,0},{1,129},{129,257},{257,385},{3... | collective-permute-start | bytes 98312 | tf_op jit(solution)/shard_map/ppermute | solution.py:27
  13.8 7.4 %collective-permute-start.2 = (bf16[64,256]{1,0:T(8,128)(2,1)S(1)}, bf16[64,256]{1,0:T(8,128)(2,1)S(1)}, u32[]{:S(2)}, u32[]{:S(2)}) collective-permute-start(bf16[64,256]{1,0:T(8,128)(2,1)S(1)} %get-tuple-element.20), channel_id=1, source_target_pairs={{0,384},{128,0},{256,128},{384,256},{1,385},{129,1},{257,129},{385... | collective-permute-start | bytes 98312 | tf_op jit(solution)/shard_map/ppermute | solution.py:30
  17.4 6.8 %collective-permute-start.1 = (bf16[64,256]{1,0:T(8,128)(2,1)S(1)}, bf16[64,256]{1,0:T(8,128)(2,1)S(1)}, u32[]{:S(2)}, u32[]{:S(2)}) collective-permute-start(bf16[64,256]{1,0:T(8,128)(2,1)S(1)} %collective-permute-done), channel_id=1, source_target_pairs={{0,128},{128,256},{256,384},{384,0},{1,129},{129,257},{257,385},{3... | collective-permute-start | bytes 98312 | tf_op jit(solution)/shard_map/ppermute | solution.py:27
  24.2 13.0 %collective-permute-start.3 = (bf16[4,64,256]{2,1,0:T(8,128)(2,1)S(1)}, bf16[4,64,256]{2,1,0:T(8,128)(2,1)S(1)}, u32[]{:S(2)}, u32[]{:S(2)}) collective-permute-start(bf16[4,64,256]{2,1,0:T(8,128)(2,1)S(1)} %pad_maximum_fusion.4), channel_id=1, source_target_pairs={{0,4},{4,8},{8,12},{12,16},{16,20},{20,24},{24,28},{28,0},{1,5},{5... | collective-permute-start | bytes 393224 | tf_op jit(solution)/shard_map/ppermute | solution.py:27
  37.2 7.3 %collective-permute-start.4 = (bf16[4,64,256]{2,1,0:T(8,128)(2,1)S(1)}, bf16[4,64,256]{2,1,0:T(8,128)(2,1)S(1)}, u32[]{:S(2)}, u32[]{:S(2)}) collective-permute-start(bf16[4,64,256]{2,1,0:T(8,128)(2,1)S(1)} %collective-permute-done.3), channel_id=1, source_target_pairs={{0,4},{4,8},{8,12},{12,16},{16,20},{20,24},{24,28},{28,0},{1,5},{5... | collective-permute-start | bytes 393224 | tf_op jit(solution)/shard_map/ppermute | solution.py:27
  39.2 7.3 %collective-permute-start.7 = (bf16[4,64,256]{2,1,0:T(8,128)(2,1)S(1)}, bf16[4,64,256]{2,1,0:T(8,128)(2,1)S(1)}, u32[]{:S(2)}, u32[]{:S(2)}) collective-permute-start(bf16[4,64,256]{2,1,0:T(8,128)(2,1)S(1)} %pad_maximum_fusion.4), channel_id=1, source_target_pairs={{0,28},{4,0},{8,4},{12,8},{16,12},{20,16},{24,20},{28,24},{1,29},{... | collective-permute-start | bytes 393224 | tf_op jit(solution)/shard_map/ppermute | solution.py:30
  44.5 6.9 %collective-permute-start.5 = (bf16[4,64,256]{2,1,0:T(8,128)(2,1)S(1)}, bf16[4,64,256]{2,1,0:T(8,128)(2,1)S(1)}, u32[]{:S(2)}, u32[]{:S(2)}) collective-permute-start(bf16[4,64,256]{2,1,0:T(8,128)(2,1)S(1)} %collective-permute-done.4), channel_id=1, source_target_pairs={{0,4},{4,8},{8,12},{12,16},{16,20},{20,24},{24,28},{28,0},{1,5},{5... | collective-permute-start | bytes 393224 | tf_op jit(solution)/shard_map/ppermute | solution.py:27
  46.5 6.9 %collective-permute-start.8 = (bf16[4,64,256]{2,1,0:T(8,128)(2,1)S(1)}, bf16[4,64,256]{2,1,0:T(8,128)(2,1)S(1)}, u32[]{:S(2)}, u32[]{:S(2)}) collective-permute-start(bf16[4,64,256]{2,1,0:T(8,128)(2,1)S(1)} %collective-permute-done.7), channel_id=1, source_target_pairs={{0,28},{4,0},{8,4},{12,8},{16,12},{20,16},{24,20},{28,24},{1,29},{... | collective-permute-start | bytes 393224 | tf_op jit(solution)/shard_map/ppermute | solution.py:30
  51.5 7.0 %collective-permute-start.6 = (bf16[4,64,256]{2,1,0:T(8,128)(2,1)S(1)}, bf16[4,64,256]{2,1,0:T(8,128)(2,1)S(1)}, u32[]{:S(2)}, u32[]{:S(2)}) collective-permute-start(bf16[4,64,256]{2,1,0:T(8,128)(2,1)S(1)} %collective-permute-done.5), channel_id=1, source_target_pairs={{0,4},{4,8},{8,12},{12,16},{16,20},{20,24},{24,28},{28,0},{1,5},{5... | collective-permute-start | bytes 393224 | tf_op jit(solution)/shard_map/ppermute | solution.py:27
  53.4 6.5 %collective-permute-start.9 = (bf16[4,64,256]{2,1,0:T(8,128)(2,1)S(1)}, bf16[4,64,256]{2,1,0:T(8,128)(2,1)S(1)}, u32[]{:S(2)}, u32[]{:S(2)}) collective-permute-start(bf16[4,64,256]{2,1,0:T(8,128)(2,1)S(1)} %collective-permute-done.8), channel_id=1, source_target_pairs={{0,28},{4,0},{8,4},{12,8},{16,12},{20,16},{24,20},{28,24},{1,29},{... | collective-permute-start | bytes 393224 | tf_op jit(solution)/shard_map/ppermute | solution.py:30
  59.9 22.7 %collective-permute-start.10 = (bf16[8,4,64,256]{3,2,1,0:T(8,128)(2,1)S(1)}, bf16[8,4,64,256]{3,2,1,0:T(8,128)(2,1)S(1)}, u32[]{:S(2)}, u32[]{:S(2)}) collective-permute-start(bf16[8,4,64,256]{3,2,1,0:T(8,128)(2,1)S(1)} %bitcast_dynamic-update-slice_fusion), channel_id=1, source_target_pairs={{0,32},{32,64},{64,96},{96,0},{1,33},{33,65},{65,97},{97,1},{2,34}... | collective-permute-start | bytes 3145736 | tf_op jit(solution)/shard_map/ppermute | solution.py:27
  62.9 25.0 %collective-permute-start.12 = (bf16[8,4,64,256]{3,2,1,0:T(8,128)(2,1)S(1)}, bf16[8,4,64,256]{3,2,1,0:T(8,128)(2,1)}, u32[]{:S(2)}, u32[]{:S(2)}) collective-permute-start(bf16[8,4,64,256]{3,2,1,0:T(8,128)(2,1)S(1)} %bitcast_dynamic-update-slice_fusion), channel_id=1, source_target_pairs={{0,96},{32,0},{64,32},{96,64},{1,97},{33,1},{65,33},{97,65},{2,98}... | collective-permute-start | bytes 3145736 | tf_op jit(solution)/shard_map/ppermute | solution.py:30
  82.6 23.0 %collective-permute-start.11 = (bf16[8,4,64,256]{3,2,1,0:T(8,128)(2,1)S(1)}, bf16[8,4,64,256]{3,2,1,0:T(8,128)(2,1)}, u32[]{:S(2)}, u32[]{:S(2)}) collective-permute-start(bf16[8,4,64,256]{3,2,1,0:T(8,128)(2,1)S(1)} %collective-permute-done.10), channel_id=1, source_target_pairs={{0,32},{32,64},{64,96},{96,0},{1,33},{33,65},{65,97},{97,1},{2,34}... | collective-permute-start | bytes 3145736 | tf_op jit(solution)/shard_map/ppermute | solution.py:27
  148.2 15.8 %copy-start.1 = (bf16[256,256]{1,0:T(8,128)(2,1)S(1)}, bf16[256,256]{1,0:T(8,128)(2,1)}, u32[]{:S(2)}) copy-start(bf16[256,256]{1,0:T(8,128)(2,1)} %param.11) | copy-start | bytes 393220
  148.2 15.8 %copy-start.2 = (bf16[128,256]{1,0:T(8,128)(2,1)S(1)}, bf16[128,256]{1,0:T(8,128)(2,1)}, u32[]{:S(2)}) copy-start(bf16[128,256]{1,0:T(8,128)(2,1)} %param.17) | copy-start | bytes 196612
  148.2 15.8 %copy-start.3 = (f32[256]{0:T(256)S(1)}, f32[256]{0:T(256)}, u32[]{:S(2)}) copy-start(f32[256]{0:T(256)} %param.12) | copy-start | bytes 3076
  150.1 6.7 %collective-permute-start.13 = (f32[2,32768]{1,0:T(2,128)S(1)}, f32[2,32768]{1,0:T(2,128)S(1)}, u32[]{:S(2)}, u32[]{:S(2)}) collective-permute-start(f32[2,32768]{1,0:T(2,128)S(1)} %bitcast.62), channel_id=1, source_target_pairs={{0,1},{1,0},{2,3},{3,2},{4,5},{5,4},{6,7},{7,6},{8,9},{9,8},{10,11... | collective-permute-start | bytes 786440 | tf_op jit(solution)/shard_map/ppermute | solution.py:102
  157.4 6.6 %collective-permute-start.14 = (f32[32768]{0:T(1024)S(1)}, f32[32768]{0:T(1024)S(1)}, u32[]{:S(2)}, u32[]{:S(2)}) collective-permute-start(f32[32768]{0:T(1024)S(1)} %bitcast.63), channel_id=1, source_target_pairs={{0,2},{2,0},{1,3},{3,1},{4,6},{6,4},{5,7},{7,5},{8,10},{10,8},{9,1... | collective-permute-start | bytes 393224 | tf_op jit(solution)/shard_map/ppermute | solution.py:106
  165.2 4.1 %collective-permute-start.15 = (f32[33792]{0:T(1024)S(1)}, f32[33792]{0:T(1024)S(1)}, u32[]{:S(2)}, u32[]{:S(2)}) collective-permute-start(f32[33792]{0:T(1024)S(1)} %select_n.166), channel_id=1, source_target_pairs={{0,1},{1,0},{2,3},{3,2},{4,5},{5,4},{6,7},{7,6},{8,9},{9,8},{10,11... | collective-permute-start | bytes 405512 | tf_op jit(solution)/shard_map/ppermute | solution.py:73
  169.4 5.1 %collective-permute-start.16 = (f32[16896]{0:T(1024)S(1)}, f32[16896]{0:T(1024)S(1)}, u32[]{:S(2)}, u32[]{:S(2)}) collective-permute-start(f32[16896]{0:T(1024)S(1)} %slice_select_fusion.2), channel_id=1, source_target_pairs={{0,2},{2,0},{1,3},{3,1},{4,6},{6,4},{5,7},{7,5},{8,10},{10,8},{9,1... | collective-permute-start | bytes 202760 | tf_op jit(solution)/shard_map/ppermute | solution.py:73
  174.4 9.1 %collective-permute-start.17 = (f32[16896]{0:T(1024)S(1)}, f32[16896]{0:T(1024)S(1)}, u32[]{:S(2)}, u32[]{:S(2)}) collective-permute-start(f32[16896]{0:T(1024)S(1)} %select_add_fusion), channel_id=1, source_target_pairs={{0,16},{4,20},{8,24},{12,28},{16,0},{20,4},{24,8},{28,12},{1,17},{... | collective-permute-start | bytes 202760 | tf_op jit(solution)/shard_map/ppermute | solution.py:91
  183.5 6.7 %collective-permute-start.18 = (f32[16896]{0:T(1024)S(1)}, f32[16896]{0:T(1024)S(1)}, u32[]{:S(2)}, u32[]{:S(2)}) collective-permute-start(f32[16896]{0:T(1024)S(1)} %add.126), channel_id=1, source_target_pairs={{0,8},{4,12},{8,0},{12,4},{16,24},{20,28},{24,16},{28,20},{1,9},{5... | collective-permute-start | bytes 202760 | tf_op jit(solution)/shard_map/ppermute | solution.py:91
  190.2 5.1 %collective-permute-start.19 = (f32[16896]{0:T(1024)S(1)}, f32[16896]{0:T(1024)S(1)}, u32[]{:S(2)}, u32[]{:S(2)}) collective-permute-start(f32[16896]{0:T(1024)S(1)} %add.127), channel_id=1, source_target_pairs={{0,4},{4,0},{8,12},{12,8},{16,20},{20,16},{24,28},{28,24},{1,5},{5... | collective-permute-start | bytes 202760 | tf_op jit(solution)/shard_map/ppermute | solution.py:91
  195.3 6.6 %collective-permute-start.20 = (f32[16896]{0:T(1024)S(1)}, f32[16896]{0:T(1024)S(1)}, u32[]{:S(2)}, u32[]{:S(2)}) collective-permute-start(f32[16896]{0:T(1024)S(1)} %add.128), channel_id=1, source_target_pairs={{0,64},{32,96},{64,0},{96,32},{1,65},{33,97},{65,1},{97,33},{2,66}... | collective-permute-start | bytes 202760 | tf_op jit(solution)/shard_map/ppermute | solution.py:91
  201.9 5.6 %collective-permute-start.21 = (f32[16896]{0:T(1024)S(1)}, f32[16896]{0:T(1024)S(1)}, u32[]{:S(2)}, u32[]{:S(2)}) collective-permute-start(f32[16896]{0:T(1024)S(1)} %add.129), channel_id=1, source_target_pairs={{0,32},{32,0},{64,96},{96,64},{1,33},{33,1},{65,97},{97,65},{2,34}... | collective-permute-start | bytes 202760 | tf_op jit(solution)/shard_map/ppermute | solution.py:91
  207.5 9.1 %collective-permute-start.22 = (f32[16896]{0:T(1024)S(1)}, f32[16896]{0:T(1024)S(1)}, u32[]{:S(2)}, u32[]{:S(2)}) collective-permute-start(f32[16896]{0:T(1024)S(1)} %add.130), channel_id=1, source_target_pairs={{0,256},{128,384},{256,0},{384,128},{1,257},{129,385},{257,1},{385... | collective-permute-start | bytes 202760 | tf_op jit(solution)/shard_map/ppermute | solution.py:91
  216.6 8.2 %collective-permute-start.23 = (f32[16896]{0:T(1024)S(1)}, f32[16896]{0:T(1024)S(1)}, u32[]{:S(2)}, u32[]{:S(2)}) collective-permute-start(f32[16896]{0:T(1024)S(1)} %add.131), channel_id=1, source_target_pairs={{0,128},{128,0},{256,384},{384,256},{1,129},{129,1},{257,385},{385... | collective-permute-start | bytes 202760 | tf_op jit(solution)/shard_map/ppermute | solution.py:91
  224.8 5.1 %collective-permute-start.24 = (f32[16896]{0:T(1024)S(1)}, f32[16896]{0:T(1024)S(1)}, u32[]{:S(2)}, u32[]{:S(2)}) collective-permute-start(f32[16896]{0:T(1024)S(1)} %add.132), channel_id=1, source_target_pairs={{0,2},{2,0},{1,3},{3,1},{4,6},{6,4},{5,7},{7,5},{8,10},{10,8},{9,1... | collective-permute-start | bytes 202760 | tf_op jit(solution)/shard_map/ppermute | solution.py:80
  229.9 11.8 %collective-permute-start.25 = (f32[33792]{0:T(1024)S(1)}, f32[33792]{0:T(1024)S(1)}, u32[]{:S(2)}, u32[]{:S(2)}) collective-permute-start(f32[33792]{0:T(1024)S(1)} %maximum_select_fusion.1), channel_id=1, source_target_pairs={{0,1},{1,0},{2,3},{3,2},{4,5},{5,4},{6,7},{7,6},{8,9},{9,8},{10,11... | collective-permute-start | bytes 405512 | tf_op jit(solution)/shard_map/ppermute | solution.py:80
Sparse Core Ops, SparseCore 0:
  13.1 132.1 all-gather.1

commit v4 on v3

--- a/solution.py
+++ b/solution.py
@@ -117,11 +117,8 @@
     own_cols = lax.dynamic_index_in_dim(tile_col[0], rep_index, 0, keepdims=False)
     own_count = lax.dynamic_index_in_dim(tile_count[0], rep_index, 0, keepdims=False)
     capacity = own_rows.shape[0]
-    near = features[:SPLIT]
-    far = features[SPLIT:]
-    stripe_nodes = lax.all_gather(near, ROW_AXES, axis=0, tiled=True)
-    picked_near = jnp.take(stripe_nodes.reshape(-1, SPLIT, feature_width), own_cols, axis=0)
-    picked_far = ring_blocks(far, own_cols, ("y_hi", "z", "x"))
+    picked_near = ring_blocks(features[:SPLIT], own_cols, ("y_hi", "x", "z"))
+    picked_far = ring_blocks(features[SPLIT:], own_cols, ("y_hi", "z", "x"))
     picked = jnp.concatenate([picked_near, picked_far], axis=1)
     product = jnp.einsum("tij,tjf->tif", own_tiles, picked, preferred_element_type=jnp.float32)
     live = jnp.arange(capacity, dtype=jnp.int32) < own_count

time: 251 us -> 240 us (0.956)
  waiting for transfers between devices: 118 us -> 65 us
  starting transfers between devices: 98 us -> 145 us
  between operations: 14.6 us -> 1.57 us
  local copies, waits for them, and re-layouts: 9.87 us -> 16.2 us
    all_gather x1 -> x0, waiting for transfers between devices: 33.4 us -> none  [shards(): stripe_nodes = lax.all_gather(near, ROW_AXES, axis=0, tiled=True)]
    ppermute x5 -> x10, starting transfers between devices: 20.9 us -> 44 us  [ring_gather(): right = lax.ppermute(right, axis, bwd)]
    ppermute x8 -> x16, waiting for transfers between devices: 47.7 us -> 24.8 us  [ring_gather(): left = lax.ppermute(left, axis, fwd)]
    ppermute x8 -> x16, starting transfers between devices: 23.3 us -> 46.1 us  [ring_gather(): left = lax.ppermute(left, axis, fwd)]
    unnamed x15 -> x33, local copies, waits for them, and re-layouts: 0.3 us -> 6.69 us
    ppermute x1, starting transfers between devices: 5.54 us -> 11.2 us  [reduce_over_rep(): pairs = keep + lax.ppermute(send, 'core', [(0, 1), (1, 0)])]
    ppermute x7, waiting for transfers between devices: 22.6 us -> 26.4 us  [reduce_all(): flat = flat + lax.ppermute(flat, a, perm)]
    ppermute x7, starting transfers between devices: 27.6 us -> 23.9 us  [reduce_all(): flat = flat + lax.ppermute(flat, a, perm)]
  transfers between devices with their start and end apart: 27 -> 39, of which waited for: 22 -> 17; matrix products, arithmetic and copies ran while one was open for 4% -> 5% of each run, Pallas kernels for 0% -> 0%
where the time goes in v4:
time: 240 us; the launch traced here: 238 us
  starting transfers between devices  145 us (60%)
  waiting for transfers between devices  65 us (27%)
  local copies, waits for them, and re-layouts  16.2 us (7%)
  other arithmetic  9.1 us (4%)
    ppermute x16, starting transfers between devices, ring_gather(): left = lax.ppermute(left, axis, fwd)  46.1 us
    ppermute x10, starting transfers between devices, ring_gather(): right = lax.ppermute(right, axis, bwd)  44 us
    ppermute x7, waiting for transfers between devices, reduce_all(): flat = flat + lax.ppermute(flat, a, perm)  26.4 us
    ppermute x16, waiting for transfers between devices, ring_gather(): left = lax.ppermute(left, axis, fwd)  24.8 us
    ppermute x7, starting transfers between devices, reduce_all(): flat = flat + lax.ppermute(flat, a, perm)  23.9 us
    ppermute x2, starting transfers between devices, all_gather_flat(): other = lax.ppermute(flat, a, perm)  12.4 us
    ppermute x1, starting transfers between devices, reduce_over_rep(): pairs = keep + lax.ppermute(send, 'core', [(0, 1), (1, 0)])  11.2 us
    unnamed x33, local copies, waits for them, and re-layouts  6.69 us
  transfers between devices with their start and end apart: 39, of which 17 were waited for; matrix products, arithmetic and copies ran while one was open for 5% of the time, Pallas kernels for 0%

profile of v4, /device:TPU:1, one launch (start us, length us, event | category | flops | bytes accessed | tf_op | source)
XLA Modules:
  0.0 238.3 jit_solution(7227669024155074950)
XLA Ops:
  1.5 5.0 %collective-permute-start.13 = (bf16[64,256]{1,0:T(8,128)(2,1)S(1)}, bf16[64,256]{1,0:T(8,128)(2,1)S(1)}, u32[]{:S(2)}, u32[]{:S(2)}) collective-permute-start(bf16[64,256]{1,0:T(8,128)(2,1)S(1)} %get-tuple-element.27), channel_id=1, source_target_pairs={{0,128},{128,256},{256,384},{384,0},{1,129},{129,257},{257,385},{3... | collective-permute-start | bytes 98312 | tf_op jit(solution)/shard_map/ppermute | solution.py:27
  6.6 3.6 %collective-permute-start.15 = (bf16[64,256]{1,0:T(8,128)(2,1)S(1)}, bf16[64,256]{1,0:T(8,128)(2,1)S(1)}, u32[]{:S(2)}, u32[]{:S(2)}) collective-permute-start(bf16[64,256]{1,0:T(8,128)(2,1)S(1)} %get-tuple-element.27), channel_id=1, source_target_pairs={{0,384},{128,0},{256,128},{384,256},{1,385},{129,1},{257,129},{385... | collective-permute-start | bytes 98312 | tf_op jit(solution)/shard_map/ppermute | solution.py:30
  10.2 3.8 %collective-permute-start.14 = (bf16[64,256]{1,0:T(8,128)(2,1)S(1)}, bf16[64,256]{1,0:T(8,128)(2,1)S(1)}, u32[]{:S(2)}, u32[]{:S(2)}) collective-permute-start(bf16[64,256]{1,0:T(8,128)(2,1)S(1)} %collective-permute-done.13), channel_id=1, source_target_pairs={{0,128},{128,256},{256,384},{384,0},{1,129},{129,257},{257,385},{3... | collective-permute-start | bytes 98312 | tf_op jit(solution)/shard_map/ppermute | solution.py:27
  17.0 4.0 %collective-permute-start.16 = (bf16[4,64,256]{2,1,0:T(8,128)(2,1)S(1)}, bf16[4,64,256]{2,1,0:T(8,128)(2,1)S(1)}, u32[]{:S(2)}, u32[]{:S(2)}) collective-permute-start(bf16[4,64,256]{2,1,0:T(8,128)(2,1)S(1)} %pad_maximum_fusion.6), channel_id=1, source_target_pairs={{0,4},{4,8},{8,12},{12,16},{16,20},{20,24},{24,28},{28,0},{1,5},{5... | collective-permute-start | bytes 393224 | tf_op jit(solution)/shard_map/ppermute | solution.py:27
  21.0 3.4 %collective-permute-start = (bf16[64,256]{1,0:T(8,128)(2,1)S(1)}, bf16[64,256]{1,0:T(8,128)(2,1)S(1)}, u32[]{:S(2)}, u32[]{:S(2)}) collective-permute-start(bf16[64,256]{1,0:T(8,128)(2,1)S(1)} %get-tuple-element.28), channel_id=1, source_target_pairs={{0,128},{128,256},{256,384},{384,0},{1,129},{129,257},{257,385},{3... | collective-permute-start | bytes 98312 | tf_op jit(solution)/shard_map/ppermute | solution.py:27
  24.5 4.0 %collective-permute-start.2 = (bf16[64,256]{1,0:T(8,128)(2,1)S(1)}, bf16[64,256]{1,0:T(8,128)(2,1)S(1)}, u32[]{:S(2)}, u32[]{:S(2)}) collective-permute-start(bf16[64,256]{1,0:T(8,128)(2,1)S(1)} %get-tuple-element.28), channel_id=1, source_target_pairs={{0,384},{128,0},{256,128},{384,256},{1,385},{129,1},{257,129},{385... | collective-permute-start | bytes 98312 | tf_op jit(solution)/shard_map/ppermute | solution.py:30
  28.4 3.7 %collective-permute-start.1 = (bf16[64,256]{1,0:T(8,128)(2,1)S(1)}, bf16[64,256]{1,0:T(8,128)(2,1)S(1)}, u32[]{:S(2)}, u32[]{:S(2)}) collective-permute-start(bf16[64,256]{1,0:T(8,128)(2,1)S(1)} %collective-permute-done), channel_id=1, source_target_pairs={{0,128},{128,256},{256,384},{384,0},{1,129},{129,257},{257,385},{3... | collective-permute-start | bytes 98312 | tf_op jit(solution)/shard_map/ppermute | solution.py:27
  32.2 4.0 %collective-permute-start.17 = (bf16[4,64,256]{2,1,0:T(8,128)(2,1)S(1)}, bf16[4,64,256]{2,1,0:T(8,128)(2,1)S(1)}, u32[]{:S(2)}, u32[]{:S(2)}) collective-permute-start(bf16[4,64,256]{2,1,0:T(8,128)(2,1)S(1)} %collective-permute-done.16), channel_id=1, source_target_pairs={{0,4},{4,8},{8,12},{12,16},{16,20},{20,24},{24,28},{28,0},{1,5},{5... | collective-permute-start | bytes 393224 | tf_op jit(solution)/shard_map/ppermute | solution.py:27
  39.4 7.6 %collective-permute-start.20 = (bf16[4,64,256]{2,1,0:T(8,128)(2,1)S(1)}, bf16[4,64,256]{2,1,0:T(8,128)(2,1)S(1)}, u32[]{:S(2)}, u32[]{:S(2)}) collective-permute-start(bf16[4,64,256]{2,1,0:T(8,128)(2,1)S(1)} %pad_maximum_fusion.6), channel_id=1, source_target_pairs={{0,28},{4,0},{8,4},{12,8},{16,12},{20,16},{24,20},{28,24},{1,29},{... | collective-permute-start | bytes 393224 | tf_op jit(solution)/shard_map/ppermute | solution.py:30
  48.9 3.4 %collective-permute-start.5 = (bf16[4,64,256]{2,1,0:T(8,128)(2,1)S(1)}, bf16[4,64,256]{2,1,0:T(8,128)(2,1)S(1)}, u32[]{:S(2)}, u32[]{:S(2)}) collective-permute-start(bf16[4,64,256]{2,1,0:T(8,128)(2,1)S(1)} %get-tuple-element.24), channel_id=1, source_target_pairs={{0,96},{32,0},{64,32},{96,64},{1,97},{33,1},{65,33},{97,65},{2,98}... | collective-permute-start | bytes 393224 | tf_op jit(solution)/shard_map/ppermute | solution.py:30
  54.2 4.6 %collective-permute-start.21 = (bf16[4,64,256]{2,1,0:T(8,128)(2,1)S(1)}, bf16[4,64,256]{2,1,0:T(8,128)(2,1)S(1)}, u32[]{:S(2)}, u32[]{:S(2)}) collective-permute-start(bf16[4,64,256]{2,1,0:T(8,128)(2,1)S(1)} %collective-permute-done.20), channel_id=1, source_target_pairs={{0,28},{4,0},{8,4},{12,8},{16,12},{20,16},{24,20},{28,24},{1,29},{... | collective-permute-start | bytes 393224 | tf_op jit(solution)/shard_map/ppermute | solution.py:30
  63.6 4.6 %collective-permute-start.10 = (bf16[4,4,64,256]{3,2,1,0:T(8,128)(2,1)}, bf16[4,4,64,256]{3,2,1,0:T(8,128)(2,1)}, u32[]{:S(2)}, u32[]{:S(2)}) collective-permute-start(bf16[4,4,64,256]{3,2,1,0:T(8,128)(2,1)} %pad_maximum_fusion.1), channel_id=1, source_target_pairs={{0,28},{4,0},{8,4},{12,8},{16,12},{20,16},{24,20},{28,24},{1,29},{... | collective-permute-start | bytes 1572872 | tf_op jit(solution)/shard_map/ppermute | solution.py:30
  68.2 3.4 %collective-permute-start.22 = (bf16[4,64,256]{2,1,0:T(8,128)(2,1)S(1)}, bf16[4,64,256]{2,1,0:T(8,128)(2,1)S(1)}, u32[]{:S(2)}, u32[]{:S(2)}) collective-permute-start(bf16[4,64,256]{2,1,0:T(8,128)(2,1)S(1)} %collective-permute-done.21), channel_id=1, source_target_pairs={{0,28},{4,0},{8,4},{12,8},{16,12},{20,16},{24,20},{28,24},{1,29},{... | collective-permute-start | bytes 393224 | tf_op jit(solution)/shard_map/ppermute | solution.py:30
  71.6 4.2 %collective-permute-done.6 = bf16[4,4,64,256]{3,2,1,0:T(8,128)(2,1)S(1)} collective-permute-done((bf16[4,4,64,256]{3,2,1,0:T(8,128)(2,1)}, bf16[4,4,64,256]{3,2,1,0:T(8,128)(2,1)S(1)}, u32[]{:S(2)}, u32[]{:S(2)}) %collective-permute-start.6) | collective-permute-done | bytes 524320 | tf_op jit(solution)/shard_map/ppermute | solution.py:27
  77.8 9.8 %collective-permute-done.7 = bf16[4,4,64,256]{3,2,1,0:T(8,128)(2,1)} collective-permute-done((bf16[4,4,64,256]{3,2,1,0:T(8,128)(2,1)S(1)}, bf16[4,4,64,256]{3,2,1,0:T(8,128)(2,1)}, u32[]{:S(2)}, u32[]{:S(2)}) %collective-permute-start.7) | collective-permute-done | bytes 524320 | tf_op jit(solution)/shard_map/ppermute | solution.py:27
  95.9 4.6 %collective-permute-start.11 = (bf16[4,4,64,256]{3,2,1,0:T(8,128)(2,1)}, bf16[4,4,64,256]{3,2,1,0:T(8,128)(2,1)S(1)}, u32[]{:S(2)}, u32[]{:S(2)}) collective-permute-start(bf16[4,4,64,256]{3,2,1,0:T(8,128)(2,1)} %collective-permute-done.10), channel_id=1, source_target_pairs={{0,28},{4,0},{8,4},{12,8},{16,12},{20,16},{24,20},{28,24},{1,29},{... | collective-permute-start | bytes 1572872 | tf_op jit(solution)/shard_map/ppermute | solution.py:30
  103.6 3.4 %collective-permute-start.25 = (bf16[8,4,64,256]{3,2,1,0:T(8,128)(2,1)S(1)}, bf16[8,4,64,256]{3,2,1,0:T(8,128)(2,1)}, u32[]{:S(2)}, u32[]{:S(2)}) collective-permute-start(bf16[8,4,64,256]{3,2,1,0:T(8,128)(2,1)S(1)} %bitcast_dynamic-update-slice_fusion.8), channel_id=1, source_target_pairs={{0,96},{32,0},{64,32},{96,64},{1,97},{33,1},{65,33},{97,65},{2,98}... | collective-permute-start | bytes 3145736 | tf_op jit(solution)/shard_map/ppermute | solution.py:30
  107.1 5.0 %collective-permute-start.12 = (bf16[4,4,64,256]{3,2,1,0:T(8,128)(2,1)S(1)}, bf16[4,4,64,256]{3,2,1,0:T(8,128)(2,1)S(1)}, u32[]{:S(2)}, u32[]{:S(2)}) collective-permute-start(bf16[4,4,64,256]{3,2,1,0:T(8,128)(2,1)S(1)} %collective-permute-done.11), channel_id=1, source_target_pairs={{0,28},{4,0},{8,4},{12,8},{16,12},{20,16},{24,20},{28,24},{1,29},{... | collective-permute-start | bytes 1572872 | tf_op jit(solution)/shard_map/ppermute | solution.py:30
  124.0 7.7 %collective-permute-done.24 = bf16[8,4,64,256]{3,2,1,0:T(8,128)(2,1)} collective-permute-done((bf16[8,4,64,256]{3,2,1,0:T(8,128)(2,1)S(1)}, bf16[8,4,64,256]{3,2,1,0:T(8,128)(2,1)}, u32[]{:S(2)}, u32[]{:S(2)}) %collective-permute-start.24) | collective-permute-done | bytes 1048608 | tf_op jit(solution)/shard_map/ppermute | solution.py:27
  131.6 3.5 %pad_maximum_fusion = bf16[4,8,4,64,256]{4,3,2,1,0:T(8,128)(2,1)} fusion(bf16[1,8,4,64,256]{4,3,2,1,0:T(8,128)(2,1)} %bitcast.37, bf16[1,8,4,64,256]{4,3,2,1,0:T(8,128)(2,1)S(1)} %bitcast.84, bf16[1,8,4,64,256]{4,3,2,1,0:T(8,128)(2,1)S(1)} %bitcast.85, bf16[1,8,4,64,256]{4,3,2,1,0:T(8,128)(2,1)} %bitcast.34), kind=kLoop, calls=%fused_computation.2 | loop fusion | flops 6291456 | bytes 8388608 | tf_op jit(solution)/shard_map/stack | solution.py:32
  139.9 11.2 %collective-permute-start.26 = (f32[2,32768]{1,0:T(2,128)S(1)}, f32[2,32768]{1,0:T(2,128)S(1)}, u32[]{:S(2)}, u32[]{:S(2)}) collective-permute-start(f32[2,32768]{1,0:T(2,128)S(1)} %bitcast.93), channel_id=1, source_target_pairs={{0,1},{1,0},{2,3},{3,2},{4,5},{5,4},{6,7},{7,6},{8,9},{9,8},{10,11... | collective-permute-start | bytes 786440 | tf_op jit(solution)/shard_map/ppermute | solution.py:102
  154.8 4.6 %collective-permute-done.27 = f32[32768]{0:T(1024)S(1)} collective-permute-done((f32[32768]{0:T(1024)S(1)}, f32[32768]{0:T(1024)S(1)}, u32[]{:S(2)}, u32[]{:S(2)}) %collective-permute-start.27) | collective-permute-done | bytes 131104 | tf_op jit(solution)/shard_map/ppermute | solution.py:106
  160.7 3.1 %collective-permute-start.28 = (f32[33792]{0:T(1024)S(1)}, f32[33792]{0:T(1024)S(1)}, u32[]{:S(2)}, u32[]{:S(2)}) collective-permute-start(f32[33792]{0:T(1024)S(1)} %select_n.180), channel_id=1, source_target_pairs={{0,1},{1,0},{2,3},{3,2},{4,5},{5,4},{6,7},{7,6},{8,9},{9,8},{10,11... | collective-permute-start | bytes 405512 | tf_op jit(solution)/shard_map/ppermute | solution.py:73
  166.8 3.1 %collective-permute-done.29 = f32[16896]{0:T(1024)S(1)} collective-permute-done((f32[16896]{0:T(1024)S(1)}, f32[16896]{0:T(1024)S(1)}, u32[]{:S(2)}, u32[]{:S(2)}) %collective-permute-start.29) | collective-permute-done | bytes 67616 | tf_op jit(solution)/shard_map/ppermute | solution.py:73
  169.9 4.8 %collective-permute-start.30 = (f32[16896]{0:T(1024)S(1)}, f32[16896]{0:T(1024)S(1)}, u32[]{:S(2)}, u32[]{:S(2)}) collective-permute-start(f32[16896]{0:T(1024)S(1)} %select_add_fusion), channel_id=1, source_target_pairs={{0,16},{4,20},{8,24},{12,28},{16,0},{20,4},{24,8},{28,12},{1,17},{... | collective-permute-start | bytes 202760 | tf_op jit(solution)/shard_map/ppermute | solution.py:91
  174.7 5.0 %collective-permute-done.30 = f32[16896]{0:T(1024)S(1)} collective-permute-done((f32[16896]{0:T(1024)S(1)}, f32[16896]{0:T(1024)S(1)}, u32[]{:S(2)}, u32[]{:S(2)}) %collective-permute-start.30) | collective-permute-done | bytes 67616 | tf_op jit(solution)/shard_map/ppermute | solution.py:91
  181.7 4.7 %collective-permute-done.31 = f32[16896]{0:T(1024)S(1)} collective-permute-done((f32[16896]{0:T(1024)S(1)}, f32[16896]{0:T(1024)S(1)}, u32[]{:S(2)}, u32[]{:S(2)}) %collective-permute-start.31) | collective-permute-done | bytes 67616 | tf_op jit(solution)/shard_map/ppermute | solution.py:91
  193.7 4.3 %collective-permute-done.33 = f32[16896]{0:T(1024)S(1)} collective-permute-done((f32[16896]{0:T(1024)S(1)}, f32[16896]{0:T(1024)S(1)}, u32[]{:S(2)}, u32[]{:S(2)}) %collective-permute-start.33) | collective-permute-done | bytes 67616 | tf_op jit(solution)/shard_map/ppermute | solution.py:91
  203.1 5.6 %collective-permute-start.35 = (f32[16896]{0:T(1024)S(1)}, f32[16896]{0:T(1024)S(1)}, u32[]{:S(2)}, u32[]{:S(2)}) collective-permute-start(f32[16896]{0:T(1024)S(1)} %add.153), channel_id=1, source_target_pairs={{0,256},{128,384},{256,0},{384,128},{1,257},{129,385},{257,1},{385... | collective-permute-start | bytes 202760 | tf_op jit(solution)/shard_map/ppermute | solution.py:91
  208.8 3.3 %collective-permute-done.35 = f32[16896]{0:T(1024)S(1)} collective-permute-done((f32[16896]{0:T(1024)S(1)}, f32[16896]{0:T(1024)S(1)}, u32[]{:S(2)}, u32[]{:S(2)}) %collective-permute-start.35) | collective-permute-done | bytes 67616 | tf_op jit(solution)/shard_map/ppermute | solution.py:91
  212.1 5.4 %collective-permute-start.36 = (f32[16896]{0:T(1024)S(1)}, f32[16896]{0:T(1024)S(1)}, u32[]{:S(2)}, u32[]{:S(2)}) collective-permute-start(f32[16896]{0:T(1024)S(1)} %add.154), channel_id=1, source_target_pairs={{0,128},{128,0},{256,384},{384,256},{1,129},{129,1},{257,385},{385... | collective-permute-start | bytes 202760 | tf_op jit(solution)/shard_map/ppermute | solution.py:91
  225.5 10.5 %collective-permute-start.38 = (f32[33792]{0:T(1024)S(1)}, f32[33792]{0:T(1024)S(1)}, u32[]{:S(2)}, u32[]{:S(2)}) collective-permute-start(f32[33792]{0:T(1024)S(1)} %maximum_select_fusion.1), channel_id=1, source_target_pairs={{0,1},{1,0},{2,3},{3,2},{4,5},{5,4},{6,7},{7,6},{8,9},{9,8},{10,11... | collective-permute-start | bytes 405512 | tf_op jit(solution)/shard_map/ppermute | solution.py:80
  (132 shorter events, 77.9 us)
Async XLA Ops:
  1.5 8.6 %collective-permute-start.13 = (bf16[64,256]{1,0:T(8,128)(2,1)S(1)}, bf16[64,256]{1,0:T(8,128)(2,1)S(1)}, u32[]{:S(2)}, u32[]{:S(2)}) collective-permute-start(bf16[64,256]{1,0:T(8,128)(2,1)S(1)} %get-tuple-element.27), channel_id=1, source_target_pairs={{0,128},{128,256},{256,384},{384,0},{1,129},{129,257},{257,385},{3... | collective-permute-start | bytes 98312 | tf_op jit(solution)/shard_map/ppermute | solution.py:27
  6.6 7.4 %collective-permute-start.15 = (bf16[64,256]{1,0:T(8,128)(2,1)S(1)}, bf16[64,256]{1,0:T(8,128)(2,1)S(1)}, u32[]{:S(2)}, u32[]{:S(2)}) collective-permute-start(bf16[64,256]{1,0:T(8,128)(2,1)S(1)} %get-tuple-element.27), channel_id=1, source_target_pairs={{0,384},{128,0},{256,128},{384,256},{1,385},{129,1},{257,129},{385... | collective-permute-start | bytes 98312 | tf_op jit(solution)/shard_map/ppermute | solution.py:30
  10.2 6.8 %collective-permute-start.14 = (bf16[64,256]{1,0:T(8,128)(2,1)S(1)}, bf16[64,256]{1,0:T(8,128)(2,1)S(1)}, u32[]{:S(2)}, u32[]{:S(2)}) collective-permute-start(bf16[64,256]{1,0:T(8,128)(2,1)S(1)} %collective-permute-done.13), channel_id=1, source_target_pairs={{0,128},{128,256},{256,384},{384,0},{1,129},{129,257},{257,385},{3... | collective-permute-start | bytes 98312 | tf_op jit(solution)/shard_map/ppermute | solution.py:27
  17.0 15.1 %collective-permute-start.16 = (bf16[4,64,256]{2,1,0:T(8,128)(2,1)S(1)}, bf16[4,64,256]{2,1,0:T(8,128)(2,1)S(1)}, u32[]{:S(2)}, u32[]{:S(2)}) collective-permute-start(bf16[4,64,256]{2,1,0:T(8,128)(2,1)S(1)} %pad_maximum_fusion.6), channel_id=1, source_target_pairs={{0,4},{4,8},{8,12},{12,16},{16,20},{20,24},{24,28},{28,0},{1,5},{5... | collective-permute-start | bytes 393224 | tf_op jit(solution)/shard_map/ppermute | solution.py:27
  21.0 7.4 %collective-permute-start = (bf16[64,256]{1,0:T(8,128)(2,1)S(1)}, bf16[64,256]{1,0:T(8,128)(2,1)S(1)}, u32[]{:S(2)}, u32[]{:S(2)}) collective-permute-start(bf16[64,256]{1,0:T(8,128)(2,1)S(1)} %get-tuple-element.28), channel_id=1, source_target_pairs={{0,128},{128,256},{256,384},{384,0},{1,129},{129,257},{257,385},{3... | collective-permute-start | bytes 98312 | tf_op jit(solution)/shard_map/ppermute | solution.py:27
  24.5 11.7 %collective-permute-start.2 = (bf16[64,256]{1,0:T(8,128)(2,1)S(1)}, bf16[64,256]{1,0:T(8,128)(2,1)S(1)}, u32[]{:S(2)}, u32[]{:S(2)}) collective-permute-start(bf16[64,256]{1,0:T(8,128)(2,1)S(1)} %get-tuple-element.28), channel_id=1, source_target_pairs={{0,384},{128,0},{256,128},{384,256},{1,385},{129,1},{257,129},{385... | collective-permute-start | bytes 98312 | tf_op jit(solution)/shard_map/ppermute | solution.py:30
  28.4 7.7 %collective-permute-start.1 = (bf16[64,256]{1,0:T(8,128)(2,1)S(1)}, bf16[64,256]{1,0:T(8,128)(2,1)S(1)}, u32[]{:S(2)}, u32[]{:S(2)}) collective-permute-start(bf16[64,256]{1,0:T(8,128)(2,1)S(1)} %collective-permute-done), channel_id=1, source_target_pairs={{0,128},{128,256},{256,384},{384,0},{1,129},{129,257},{257,385},{3... | collective-permute-start | bytes 98312 | tf_op jit(solution)/shard_map/ppermute | solution.py:27
  32.2 14.8 %collective-permute-start.17 = (bf16[4,64,256]{2,1,0:T(8,128)(2,1)S(1)}, bf16[4,64,256]{2,1,0:T(8,128)(2,1)S(1)}, u32[]{:S(2)}, u32[]{:S(2)}) collective-permute-start(bf16[4,64,256]{2,1,0:T(8,128)(2,1)S(1)} %collective-permute-done.16), channel_id=1, source_target_pairs={{0,4},{4,8},{8,12},{12,16},{16,20},{20,24},{24,28},{28,0},{1,5},{5... | collective-permute-start | bytes 393224 | tf_op jit(solution)/shard_map/ppermute | solution.py:27
  36.2 16.1 %collective-permute-start.3 = (bf16[4,64,256]{2,1,0:T(8,128)(2,1)S(1)}, bf16[4,64,256]{2,1,0:T(8,128)(2,1)S(1)}, u32[]{:S(2)}, u32[]{:S(2)}) collective-permute-start(bf16[4,64,256]{2,1,0:T(8,128)(2,1)S(1)} %get-tuple-element.24), channel_id=1, source_target_pairs={{0,32},{32,64},{64,96},{96,0},{1,33},{33,65},{65,97},{97,1},{2,34}... | collective-permute-start | bytes 393224 | tf_op jit(solution)/shard_map/ppermute | solution.py:27
  39.4 14.9 %collective-permute-start.20 = (bf16[4,64,256]{2,1,0:T(8,128)(2,1)S(1)}, bf16[4,64,256]{2,1,0:T(8,128)(2,1)S(1)}, u32[]{:S(2)}, u32[]{:S(2)}) collective-permute-start(bf16[4,64,256]{2,1,0:T(8,128)(2,1)S(1)} %pad_maximum_fusion.6), channel_id=1, source_target_pairs={{0,28},{4,0},{8,4},{12,8},{16,12},{20,16},{24,20},{28,24},{1,29},{... | collective-permute-start | bytes 393224 | tf_op jit(solution)/shard_map/ppermute | solution.py:30
  47.0 11.8 %collective-permute-start.18 = (bf16[4,64,256]{2,1,0:T(8,128)(2,1)S(1)}, bf16[4,64,256]{2,1,0:T(8,128)(2,1)S(1)}, u32[]{:S(2)}, u32[]{:S(2)}) collective-permute-start(bf16[4,64,256]{2,1,0:T(8,128)(2,1)S(1)} %collective-permute-done.17), channel_id=1, source_target_pairs={{0,4},{4,8},{8,12},{12,16},{16,20},{20,24},{24,28},{28,0},{1,5},{5... | collective-permute-start | bytes 393224 | tf_op jit(solution)/shard_map/ppermute | solution.py:27
  48.9 11.9 %collective-permute-start.5 = (bf16[4,64,256]{2,1,0:T(8,128)(2,1)S(1)}, bf16[4,64,256]{2,1,0:T(8,128)(2,1)S(1)}, u32[]{:S(2)}, u32[]{:S(2)}) collective-permute-start(bf16[4,64,256]{2,1,0:T(8,128)(2,1)S(1)} %get-tuple-element.24), channel_id=1, source_target_pairs={{0,96},{32,0},{64,32},{96,64},{1,97},{33,1},{65,33},{97,65},{2,98}... | collective-permute-start | bytes 393224 | tf_op jit(solution)/shard_map/ppermute | solution.py:30
  52.3 8.5 %collective-permute-start.4 = (bf16[4,64,256]{2,1,0:T(8,128)(2,1)S(1)}, bf16[4,64,256]{2,1,0:T(8,128)(2,1)S(1)}, u32[]{:S(2)}, u32[]{:S(2)}) collective-permute-start(bf16[4,64,256]{2,1,0:T(8,128)(2,1)S(1)} %collective-permute-done.3), channel_id=1, source_target_pairs={{0,32},{32,64},{64,96},{96,0},{1,33},{33,65},{65,97},{97,1},{2,34}... | collective-permute-start | bytes 393224 | tf_op jit(solution)/shard_map/ppermute | solution.py:27
  54.2 13.9 %collective-permute-start.21 = (bf16[4,64,256]{2,1,0:T(8,128)(2,1)S(1)}, bf16[4,64,256]{2,1,0:T(8,128)(2,1)S(1)}, u32[]{:S(2)}, u32[]{:S(2)}) collective-permute-start(bf16[4,64,256]{2,1,0:T(8,128)(2,1)S(1)} %collective-permute-done.20), channel_id=1, source_target_pairs={{0,28},{4,0},{8,4},{12,8},{16,12},{20,16},{24,20},{28,24},{1,29},{... | collective-permute-start | bytes 393224 | tf_op jit(solution)/shard_map/ppermute | solution.py:30
  58.8 12.7 %collective-permute-start.19 = (bf16[4,64,256]{2,1,0:T(8,128)(2,1)S(1)}, bf16[4,64,256]{2,1,0:T(8,128)(2,1)S(1)}, u32[]{:S(2)}, u32[]{:S(2)}) collective-permute-start(bf16[4,64,256]{2,1,0:T(8,128)(2,1)S(1)} %collective-permute-done.18), channel_id=1, source_target_pairs={{0,4},{4,8},{8,12},{12,16},{16,20},{20,24},{24,28},{28,0},{1,5},{5... | collective-permute-start | bytes 393224 | tf_op jit(solution)/shard_map/ppermute | solution.py:27
  61.7 14.2 %collective-permute-start.6 = (bf16[4,4,64,256]{3,2,1,0:T(8,128)(2,1)}, bf16[4,4,64,256]{3,2,1,0:T(8,128)(2,1)S(1)}, u32[]{:S(2)}, u32[]{:S(2)}) collective-permute-start(bf16[4,4,64,256]{3,2,1,0:T(8,128)(2,1)} %pad_maximum_fusion.1), channel_id=1, source_target_pairs={{0,4},{4,8},{8,12},{12,16},{16,20},{20,24},{24,28},{28,0},{1,5},{5... | collective-permute-start | bytes 1572872 | tf_op jit(solution)/shard_map/ppermute | solution.py:27
  63.6 32.3 %collective-permute-start.10 = (bf16[4,4,64,256]{3,2,1,0:T(8,128)(2,1)}, bf16[4,4,64,256]{3,2,1,0:T(8,128)(2,1)}, u32[]{:S(2)}, u32[]{:S(2)}) collective-permute-start(bf16[4,4,64,256]{3,2,1,0:T(8,128)(2,1)} %pad_maximum_fusion.1), channel_id=1, source_target_pairs={{0,28},{4,0},{8,4},{12,8},{16,12},{20,16},{24,20},{28,24},{1,29},{... | collective-permute-start | bytes 1572872 | tf_op jit(solution)/shard_map/ppermute | solution.py:30
  68.2 21.4 %collective-permute-start.22 = (bf16[4,64,256]{2,1,0:T(8,128)(2,1)S(1)}, bf16[4,64,256]{2,1,0:T(8,128)(2,1)S(1)}, u32[]{:S(2)}, u32[]{:S(2)}) collective-permute-start(bf16[4,64,256]{2,1,0:T(8,128)(2,1)S(1)} %collective-permute-done.21), channel_id=1, source_target_pairs={{0,28},{4,0},{8,4},{12,8},{16,12},{20,16},{24,20},{28,24},{1,29},{... | collective-permute-start | bytes 393224 | tf_op jit(solution)/shard_map/ppermute | solution.py:30
  75.8 11.8 %collective-permute-start.7 = (bf16[4,4,64,256]{3,2,1,0:T(8,128)(2,1)S(1)}, bf16[4,4,64,256]{3,2,1,0:T(8,128)(2,1)}, u32[]{:S(2)}, u32[]{:S(2)}) collective-permute-start(bf16[4,4,64,256]{3,2,1,0:T(8,128)(2,1)S(1)} %collective-permute-done.6), channel_id=1, source_target_pairs={{0,4},{4,8},{8,12},{12,16},{16,20},{20,24},{24,28},{28,0},{1,5},{5... | collective-permute-start | bytes 1572872 | tf_op jit(solution)/shard_map/ppermute | solution.py:27
  87.6 12.8 %collective-permute-start.8 = (bf16[4,4,64,256]{3,2,1,0:T(8,128)(2,1)}, bf16[4,4,64,256]{3,2,1,0:T(8,128)(2,1)}, u32[]{:S(2)}, u32[]{:S(2)}) collective-permute-start(bf16[4,4,64,256]{3,2,1,0:T(8,128)(2,1)} %collective-permute-done.7), channel_id=1, source_target_pairs={{0,4},{4,8},{8,12},{12,16},{16,20},{20,24},{24,28},{28,0},{1,5},{5... | collective-permute-start | bytes 1572872 | tf_op jit(solution)/shard_map/ppermute | solution.py:27
  89.6 22.5 %collective-permute-start.23 = (bf16[8,4,64,256]{3,2,1,0:T(8,128)(2,1)S(1)}, bf16[8,4,64,256]{3,2,1,0:T(8,128)(2,1)S(1)}, u32[]{:S(2)}, u32[]{:S(2)}) collective-permute-start(bf16[8,4,64,256]{3,2,1,0:T(8,128)(2,1)S(1)} %bitcast_dynamic-update-slice_fusion.8), channel_id=1, source_target_pairs={{0,32},{32,64},{64,96},{96,0},{1,33},{33,65},{65,97},{97,1},{2,34}... | collective-permute-start | bytes 3145736 | tf_op jit(solution)/shard_map/ppermute | solution.py:27
  95.9 11.2 %collective-permute-start.11 = (bf16[4,4,64,256]{3,2,1,0:T(8,128)(2,1)}, bf16[4,4,64,256]{3,2,1,0:T(8,128)(2,1)S(1)}, u32[]{:S(2)}, u32[]{:S(2)}) collective-permute-start(bf16[4,4,64,256]{3,2,1,0:T(8,128)(2,1)} %collective-permute-done.10), channel_id=1, source_target_pairs={{0,28},{4,0},{8,4},{12,8},{16,12},{20,16},{24,20},{28,24},{1,29},{... | collective-permute-start | bytes 1572872 | tf_op jit(solution)/shard_map/ppermute | solution.py:30
  100.5 14.2 %collective-permute-start.9 = (bf16[4,4,64,256]{3,2,1,0:T(8,128)(2,1)}, bf16[4,4,64,256]{3,2,1,0:T(8,128)(2,1)S(1)}, u32[]{:S(2)}, u32[]{:S(2)}) collective-permute-start(bf16[4,4,64,256]{3,2,1,0:T(8,128)(2,1)} %collective-permute-done.8), channel_id=1, source_target_pairs={{0,4},{4,8},{8,12},{12,16},{16,20},{20,24},{24,28},{28,0},{1,5},{5... | collective-permute-start | bytes 1572872 | tf_op jit(solution)/shard_map/ppermute | solution.py:27
  103.6 20.3 %collective-permute-start.25 = (bf16[8,4,64,256]{3,2,1,0:T(8,128)(2,1)S(1)}, bf16[8,4,64,256]{3,2,1,0:T(8,128)(2,1)}, u32[]{:S(2)}, u32[]{:S(2)}) collective-permute-start(bf16[8,4,64,256]{3,2,1,0:T(8,128)(2,1)S(1)} %bitcast_dynamic-update-slice_fusion.8), channel_id=1, source_target_pairs={{0,96},{32,0},{64,32},{96,64},{1,97},{33,1},{65,33},{97,65},{2,98}... | collective-permute-start | bytes 3145736 | tf_op jit(solution)/shard_map/ppermute | solution.py:30
  107.1 12.1 %collective-permute-start.12 = (bf16[4,4,64,256]{3,2,1,0:T(8,128)(2,1)S(1)}, bf16[4,4,64,256]{3,2,1,0:T(8,128)(2,1)S(1)}, u32[]{:S(2)}, u32[]{:S(2)}) collective-permute-start(bf16[4,4,64,256]{3,2,1,0:T(8,128)(2,1)S(1)} %collective-permute-done.11), channel_id=1, source_target_pairs={{0,28},{4,0},{8,4},{12,8},{16,12},{20,16},{24,20},{28,24},{1,29},{... | collective-permute-start | bytes 1572872 | tf_op jit(solution)/shard_map/ppermute | solution.py:30
  112.1 19.5 %collective-permute-start.24 = (bf16[8,4,64,256]{3,2,1,0:T(8,128)(2,1)S(1)}, bf16[8,4,64,256]{3,2,1,0:T(8,128)(2,1)}, u32[]{:S(2)}, u32[]{:S(2)}) collective-permute-start(bf16[8,4,64,256]{3,2,1,0:T(8,128)(2,1)S(1)} %collective-permute-done.23), channel_id=1, source_target_pairs={{0,32},{32,64},{64,96},{96,0},{1,33},{33,65},{65,97},{97,1},{2,34}... | collective-permute-start | bytes 3145736 | tf_op jit(solution)/shard_map/ppermute | solution.py:27
  139.9 12.3 %collective-permute-start.26 = (f32[2,32768]{1,0:T(2,128)S(1)}, f32[2,32768]{1,0:T(2,128)S(1)}, u32[]{:S(2)}, u32[]{:S(2)}) collective-permute-start(f32[2,32768]{1,0:T(2,128)S(1)} %bitcast.93), channel_id=1, source_target_pairs={{0,1},{1,0},{2,3},{3,2},{4,5},{5,4},{6,7},{7,6},{8,9},{9,8},{10,11... | collective-permute-start | bytes 786440 | tf_op jit(solution)/shard_map/ppermute | solution.py:102
  169.9 9.8 %collective-permute-start.30 = (f32[16896]{0:T(1024)S(1)}, f32[16896]{0:T(1024)S(1)}, u32[]{:S(2)}, u32[]{:S(2)}) collective-permute-start(f32[16896]{0:T(1024)S(1)} %select_add_fusion), channel_id=1, source_target_pairs={{0,16},{4,20},{8,24},{12,28},{16,0},{20,4},{24,8},{28,12},{1,17},{... | collective-permute-start | bytes 202760 | tf_op jit(solution)/shard_map/ppermute | solution.py:91
  179.7 6.7 %collective-permute-start.31 = (f32[16896]{0:T(1024)S(1)}, f32[16896]{0:T(1024)S(1)}, u32[]{:S(2)}, u32[]{:S(2)}) collective-permute-start(f32[16896]{0:T(1024)S(1)} %add.149), channel_id=1, source_target_pairs={{0,8},{4,12},{8,0},{12,4},{16,24},{20,28},{24,16},{28,20},{1,9},{5... | collective-permute-start | bytes 202760 | tf_op jit(solution)/shard_map/ppermute | solution.py:91
  203.1 9.0 %collective-permute-start.35 = (f32[16896]{0:T(1024)S(1)}, f32[16896]{0:T(1024)S(1)}, u32[]{:S(2)}, u32[]{:S(2)}) collective-permute-start(f32[16896]{0:T(1024)S(1)} %add.153), channel_id=1, source_target_pairs={{0,256},{128,384},{256,0},{384,128},{1,257},{129,385},{257,1},{385... | collective-permute-start | bytes 202760 | tf_op jit(solution)/shard_map/ppermute | solution.py:91
  212.1 8.3 %collective-permute-start.36 = (f32[16896]{0:T(1024)S(1)}, f32[16896]{0:T(1024)S(1)}, u32[]{:S(2)}, u32[]{:S(2)}) collective-permute-start(f32[16896]{0:T(1024)S(1)} %add.154), channel_id=1, source_target_pairs={{0,128},{128,0},{256,384},{384,256},{1,129},{129,1},{257,385},{385... | collective-permute-start | bytes 202760 | tf_op jit(solution)/shard_map/ppermute | solution.py:91
  225.5 11.5 %collective-permute-start.38 = (f32[33792]{0:T(1024)S(1)}, f32[33792]{0:T(1024)S(1)}, u32[]{:S(2)}, u32[]{:S(2)}) collective-permute-start(f32[33792]{0:T(1024)S(1)} %maximum_select_fusion.1), channel_id=1, source_target_pairs={{0,1},{1,0},{2,3},{3,2},{4,5},{5,4},{6,7},{7,6},{8,9},{9,8},{10,11... | collective-permute-start | bytes 405512 | tf_op jit(solution)/shard_map/ppermute | solution.py:80
  (17 other events, 304.4 us)

commit v5 on v4

--- a/solution.py
+++ b/solution.py
@@ -7,7 +7,6 @@
 ROW_AXES = ("y_hi", "x", "z")
 REP_AXES = ("y_lo", "core")
 ALL_AXES = ROW_AXES + REP_AXES
-SPLIT = 64
 
 
 def physical_mesh(mesh):
@@ -32,26 +31,32 @@
     return jnp.stack([pieces[d] for d in range(-(n // 2), n - n // 2)])
 
 
-def ring_blocks(features, cols, order):
+def plane_blocks(features, cols):
+    sizes = {a: lax.axis_size(a) for a in ROW_AXES}
+    n_plane = sizes["y_hi"]
+    peer_cols = {
+        s: lax.ppermute(cols, "y_hi", [(i, (i - s) % n_plane) for i in range(n_plane)])
+        for s in range(1, n_plane)
+    }
     stack = features
-    for a in order:
+    for a in ("z", "x"):
         stack = ring_gather(stack, a)
-    blocks = stack.reshape(-1, features.shape[0], features.shape[1])
-    return jnp.take(blocks, nested_slot(cols, order), axis=0)
+    plane = stack.reshape(-1, features.shape[0], features.shape[1])
 
+    def in_plane(c):
+        z = c % sizes["z"]
+        x = (c // sizes["z"]) % sizes["x"]
+        kz = (z - lax.axis_index("z") + sizes["z"] // 2) % sizes["z"]
+        kx = (x - lax.axis_index("x") + sizes["x"] // 2) % sizes["x"]
+        return kx * sizes["z"] + kz
 
-def nested_slot(cols, order):
-    sizes = {a: lax.axis_size(a) for a in ROW_AXES}
-    coords = {}
-    rest = cols
-    for a in reversed(ROW_AXES):
-        coords[a] = rest % sizes[a]
-        rest = rest // sizes[a]
-    flat = jnp.zeros_like(cols)
-    for a in reversed(order):
-        k = (coords[a] - lax.axis_index(a) + sizes[a] // 2) % sizes[a]
-        flat = flat * sizes[a] + k
-    return flat
+    picked = jnp.take(plane, in_plane(cols), axis=0)
+    source = (lax.axis_index("y_hi") - cols // (sizes["z"] * sizes["x"])) % n_plane
+    for s in range(1, n_plane):
+        sent = jnp.take(plane, in_plane(peer_cols[s]), axis=0)
+        got = lax.ppermute(sent, "y_hi", [(i, (i + s) % n_plane) for i in range(n_plane)])
+        picked = jnp.where((source == s)[:, None, None], got, picked)
+    return picked
 
 
 def halving_steps(axes):
@@ -117,9 +122,7 @@
     own_cols = lax.dynamic_index_in_dim(tile_col[0], rep_index, 0, keepdims=False)
     own_count = lax.dynamic_index_in_dim(tile_count[0], rep_index, 0, keepdims=False)
     capacity = own_rows.shape[0]
-    picked_near = ring_blocks(features[:SPLIT], own_cols, ("y_hi", "x", "z"))
-    picked_far = ring_blocks(features[SPLIT:], own_cols, ("y_hi", "z", "x"))
-    picked = jnp.concatenate([picked_near, picked_far], axis=1)
+    picked = plane_blocks(features, own_cols)
     product = jnp.einsum("tij,tjf->tif", own_tiles, picked, preferred_element_type=jnp.float32)
     live = jnp.arange(capacity, dtype=jnp.int32) < own_count
     local_ids = jnp.arange(row_count, dtype=jnp.int32)

time: 240 us -> 227 us (0.946)
  starting transfers between devices: 145 us -> 116 us
  waiting for transfers between devices: 65 us -> 84 us
  local copies, waits for them, and re-layouts: 16.2 us -> 9.24 us
  other arithmetic: 9.1 us -> 11.5 us
    ppermute x16 -> x6, starting transfers between devices: 46.1 us -> 15.7 us  [ring_gather(): left = lax.ppermute(left, axis, fwd)]
    ppermute x10 -> x4, starting transfers between devices: 44 us -> 17.1 us  [ring_gather(): right = lax.ppermute(right, axis, bwd)]
    ppermute x0 -> x6, waiting for transfers between devices: none -> 25.6 us  [the longest x3 25.6 us: plane_blocks(): lax.ppermute(sent, 'y_hi', [(i, (i + s) % n_plane) for i in range(n_plane)])]
    ppermute x0 -> x6, starting transfers between devices: none -> 23.1 us  [the longest x3 14.8 us: plane_blocks(): lax.ppermute(cols, 'y_hi', [(i, (i - s) % n_plane) for i in range(n_plane)])]
    ppermute x1, starting transfers between devices: 1.92 us -> 13.8 us  [reduce_over_rep(): own = keep + lax.ppermute(send, 'y_lo', [(0, 1), (1, 0)])]
    ppermute x16 -> x6, waiting for transfers between devices: 24.8 us -> 13.1 us  [ring_gather(): left = lax.ppermute(left, axis, fwd)]
    unnamed x33 -> x20, local copies, waits for them, and re-layouts: 6.69 us -> 1.13 us
    select_n x2 -> x3, other arithmetic: 0.81 us -> 5.86 us  [plane_blocks(): sent = jnp.take(plane, in_plane(peer_cols[s]), axis=0)]
  transfers between devices with their start and end apart: 39 -> 29, of which waited for: 17 -> 20; matrix products, arithmetic and copies ran while one was open for 5% -> 6% of each run, Pallas kernels for 0% -> 0%
where the time goes in v5:
time: 227 us; the launch traced here: 226 us
  starting transfers between devices  116 us (51%)
  waiting for transfers between devices  84 us (37%)
  other arithmetic  11.5 us (5%)
  local copies, waits for them, and re-layouts  9.24 us (4%)
  matrix products  3.4 us (1%)
    ppermute x7, waiting for transfers between devices, reduce_all(): flat = flat + lax.ppermute(flat, a, perm)  29.2 us
    ppermute x3, waiting for transfers between devices, plane_blocks(): lax.ppermute(sent, 'y_hi', [(i, (i + s) % n_plane) for i in range(n_plane)])  25.6 us
    ppermute x7, starting transfers between devices, reduce_all(): flat = flat + lax.ppermute(flat, a, perm)  19.8 us
    ppermute x4, starting transfers between devices, ring_gather(): right = lax.ppermute(right, axis, bwd)  17.1 us
    ppermute x6, starting transfers between devices, ring_gather(): left = lax.ppermute(left, axis, fwd)  15.7 us
    ppermute x3, starting transfers between devices, plane_blocks(): lax.ppermute(cols, 'y_hi', [(i, (i - s) % n_plane) for i in range(n_plane)])  14.8 us
    ppermute x1, starting transfers between devices, reduce_over_rep(): own = keep + lax.ppermute(send, 'y_lo', [(0, 1), (1, 0)])  13.8 us
    ppermute x6, waiting for transfers between devices, ring_gather(): left = lax.ppermute(left, axis, fwd)  13.1 us
  transfers between devices with their start and end apart: 29, of which 20 were waited for; matrix products, arithmetic and copies ran while one was open for 6% of the time, Pallas kernels for 0%

profile of v5, /device:TPU:1, one launch (start us, length us, event | category | flops | bytes accessed | tf_op | source)
XLA Modules:
  0.0 225.5 jit_solution(16652843084569507206)
XLA Ops:
  0.6 5.0 %collective-permute-start = (bf16[128,256]{1,0:T(8,128)(2,1)}, bf16[128,256]{1,0:T(8,128)(2,1)S(1)}, u32[]{:S(2)}, u32[]{:S(2)}) collective-permute-start(bf16[128,256]{1,0:T(8,128)(2,1)} %param.10), channel_id=1, source_target_pairs={{0,4},{4,8},{8,12},{12,16},{16,20},{20,24},{24,28},{28,0},{1,5},{5... | collective-permute-start | bytes 196616 | tf_op jit(solution)/shard_map/ppermute | solution.py:26
  5.6 8.5 %collective-permute-done = bf16[128,256]{1,0:T(8,128)(2,1)S(1)} collective-permute-done((bf16[128,256]{1,0:T(8,128)(2,1)}, bf16[128,256]{1,0:T(8,128)(2,1)S(1)}, u32[]{:S(2)}, u32[]{:S(2)}) %collective-permute-start) | collective-permute-done | bytes 65568 | tf_op jit(solution)/shard_map/ppermute | solution.py:26
  16.0 4.6 %collective-permute-start.4 = (bf16[128,256]{1,0:T(8,128)(2,1)}, bf16[128,256]{1,0:T(8,128)(2,1)S(1)}, u32[]{:S(2)}, u32[]{:S(2)}) collective-permute-start(bf16[128,256]{1,0:T(8,128)(2,1)} %param.10), channel_id=1, source_target_pairs={{0,28},{4,0},{8,4},{12,8},{16,12},{20,16},{24,20},{28,24},{1,29},{... | collective-permute-start | bytes 196616 | tf_op jit(solution)/shard_map/ppermute | solution.py:29
  22.6 4.6 %collective-permute-start.5 = (bf16[128,256]{1,0:T(8,128)(2,1)S(1)}, bf16[128,256]{1,0:T(8,128)(2,1)S(1)}, u32[]{:S(2)}, u32[]{:S(2)}) collective-permute-start(bf16[128,256]{1,0:T(8,128)(2,1)S(1)} %collective-permute-done.4), channel_id=1, source_target_pairs={{0,28},{4,0},{8,4},{12,8},{16,12},{20,16},{24,20},{28,24},{1,29},{... | collective-permute-start | bytes 196616 | tf_op jit(solution)/shard_map/ppermute | solution.py:29
  29.1 4.6 %collective-permute-start.6 = (bf16[128,256]{1,0:T(8,128)(2,1)S(1)}, bf16[128,256]{1,0:T(8,128)(2,1)S(1)}, u32[]{:S(2)}, u32[]{:S(2)}) collective-permute-start(bf16[128,256]{1,0:T(8,128)(2,1)S(1)} %collective-permute-done.5), channel_id=1, source_target_pairs={{0,28},{4,0},{8,4},{12,8},{16,12},{20,16},{24,20},{28,24},{1,29},{... | collective-permute-start | bytes 196616 | tf_op jit(solution)/shard_map/ppermute | solution.py:29
  35.0 3.1 %collective-permute-start.7 = (bf16[8,128,256]{2,1,0:T(8,128)(2,1)S(1)}, bf16[8,128,256]{2,1,0:T(8,128)(2,1)S(1)}, u32[]{:S(2)}, u32[]{:S(2)}) collective-permute-start(bf16[8,128,256]{2,1,0:T(8,128)(2,1)S(1)} %bitcast_dynamic-update-slice_fusion), channel_id=1, source_target_pairs={{0,32},{32,64},{64,96},{96,0},{1,33},{33,65},{65,97},{97,1},{2,34}... | collective-permute-start | bytes 1572872 | tf_op jit(solution)/shard_map/ppermute | solution.py:26
  38.8 4.2 %collective-permute-start.10 = (s32[8]{0:T(128)S(1)}, s32[8]{0:T(128)S(1)}, u32[]{:S(2)}, u32[]{:S(2)}) collective-permute-start(s32[8]{0:T(128)S(1)} %get-tuple-element.8), channel_id=1, source_target_pairs={{0,128},{128,256},{256,384},{384,0},{1,129},{129,257},{257,385},{3... | collective-permute-start | bytes 104 | tf_op jit(solution)/shard_map/ppermute | solution.py:38
  43.1 3.6 %collective-permute-start.14 = (s32[8]{0:T(128)S(1)}, s32[8]{0:T(128)S(1)}, u32[]{:S(2)}, u32[]{:S(2)}) collective-permute-start(s32[8]{0:T(128)S(1)} %get-tuple-element.8), channel_id=1, source_target_pairs={{0,384},{128,0},{256,128},{384,256},{1,385},{129,1},{257,129},{385... | collective-permute-start | bytes 104 | tf_op jit(solution)/shard_map/ppermute | solution.py:38
  46.7 7.0 %collective-permute-start.12 = (s32[8]{0:T(128)S(1)}, s32[8]{0:T(128)S(1)}, u32[]{:S(2)}, u32[]{:S(2)}) collective-permute-start(s32[8]{0:T(128)S(1)} %get-tuple-element.8), channel_id=1, source_target_pairs={{0,256},{128,384},{256,0},{384,128},{1,257},{129,385},{257,1},{385... | collective-permute-start | bytes 104 | tf_op jit(solution)/shard_map/ppermute | solution.py:38
  55.0 3.4 %collective-permute-start.9 = (bf16[8,128,256]{2,1,0:T(8,128)(2,1)S(1)}, bf16[8,128,256]{2,1,0:T(8,128)(2,1)S(1)}, u32[]{:S(2)}, u32[]{:S(2)}) collective-permute-start(bf16[8,128,256]{2,1,0:T(8,128)(2,1)S(1)} %bitcast_dynamic-update-slice_fusion), channel_id=1, source_target_pairs={{0,96},{32,0},{64,32},{96,64},{1,97},{33,1},{65,33},{97,65},{2,98}... | collective-permute-start | bytes 1572872 | tf_op jit(solution)/shard_map/ppermute | solution.py:29
  60.4 4.5 %collective-permute-done.9 = bf16[8,128,256]{2,1,0:T(8,128)(2,1)S(1)} collective-permute-done((bf16[8,128,256]{2,1,0:T(8,128)(2,1)S(1)}, bf16[8,128,256]{2,1,0:T(8,128)(2,1)S(1)}, u32[]{:S(2)}, u32[]{:S(2)}) %collective-permute-start.9) | collective-permute-done | bytes 524320 | tf_op jit(solution)/shard_map/ppermute | solution.py:29
  64.9 4.6 %collective-permute-done.8 = bf16[8,128,256]{2,1,0:T(8,128)(2,1)S(1)} collective-permute-done((bf16[8,128,256]{2,1,0:T(8,128)(2,1)S(1)}, bf16[8,128,256]{2,1,0:T(8,128)(2,1)S(1)}, u32[]{:S(2)}, u32[]{:S(2)}) %collective-permute-start.8) | collective-permute-done | bytes 524320 | tf_op jit(solution)/shard_map/ppermute | solution.py:26
  79.6 4.5 %collective-permute-start.13 = (bf16[8,128,256]{2,1,0:T(8,128)(2,1)}, bf16[8,128,256]{2,1,0:T(8,128)(2,1)}, u32[]{:S(2)}, u32[]{:S(2)}) collective-permute-start(bf16[8,128,256]{2,1,0:T(8,128)(2,1)} %broadcast_select_fusion.1), channel_id=1, source_target_pairs={{0,256},{128,384},{256,0},{384,128},{1,257},{129,385},{257,1},{385... | collective-permute-start | bytes 1572872 | tf_op jit(solution)/shard_map/ppermute | solution.py:57
  92.1 10.8 %collective-permute-done.11 = bf16[8,128,256]{2,1,0:T(8,128)(2,1)} collective-permute-done((bf16[8,128,256]{2,1,0:T(8,128)(2,1)}, bf16[8,128,256]{2,1,0:T(8,128)(2,1)}, u32[]{:S(2)}, u32[]{:S(2)}) %collective-permute-start.11) | collective-permute-done | bytes 524320 | tf_op jit(solution)/shard_map/ppermute | solution.py:57
  103.9 13.8 %collective-permute-done.15 = bf16[8,128,256]{2,1,0:T(8,128)(2,1)} collective-permute-done((bf16[8,128,256]{2,1,0:T(8,128)(2,1)}, bf16[8,128,256]{2,1,0:T(8,128)(2,1)}, u32[]{:S(2)}, u32[]{:S(2)}) %collective-permute-start.15) | collective-permute-done | bytes 524320 | tf_op jit(solution)/shard_map/ppermute | solution.py:57
  121.3 7.4 %collective-permute-start.16 = (f32[2,32768]{1,0:T(2,128)S(1)}, f32[2,32768]{1,0:T(2,128)S(1)}, u32[]{:S(2)}, u32[]{:S(2)}) collective-permute-start(f32[2,32768]{1,0:T(2,128)S(1)} %bitcast.56), channel_id=1, source_target_pairs={{0,1},{1,0},{2,3},{3,2},{4,5},{5,4},{6,7},{7,6},{8,9},{9,8},{10,11... | collective-permute-start | bytes 786440 | tf_op jit(solution)/shard_map/ppermute | solution.py:107
  130.4 13.8 %collective-permute-start.17 = (f32[32768]{0:T(1024)S(1)}, f32[32768]{0:T(1024)S(1)}, u32[]{:S(2)}, u32[]{:S(2)}) collective-permute-start(f32[32768]{0:T(1024)S(1)} %bitcast.57), channel_id=1, source_target_pairs={{0,2},{2,0},{1,3},{3,1},{4,6},{6,4},{5,7},{7,5},{8,10},{10,8},{9,1... | collective-permute-start | bytes 393224 | tf_op jit(solution)/shard_map/ppermute | solution.py:111
  144.2 3.4 %collective-permute-done.17 = f32[32768]{0:T(1024)S(1)} collective-permute-done((f32[32768]{0:T(1024)S(1)}, f32[32768]{0:T(1024)S(1)}, u32[]{:S(2)}, u32[]{:S(2)}) %collective-permute-start.17) | collective-permute-done | bytes 131104 | tf_op jit(solution)/shard_map/ppermute | solution.py:111
  148.9 2.9 %collective-permute-start.18 = (f32[33792]{0:T(1024)S(1)}, f32[33792]{0:T(1024)S(1)}, u32[]{:S(2)}, u32[]{:S(2)}) collective-permute-start(f32[33792]{0:T(1024)S(1)} %select_n.266), channel_id=1, source_target_pairs={{0,1},{1,0},{2,3},{3,2},{4,5},{5,4},{6,7},{7,6},{8,9},{9,8},{10,11... | collective-permute-start | bytes 405512 | tf_op jit(solution)/shard_map/ppermute | solution.py:78
  152.8 3.4 %collective-permute-start.19 = (f32[16896]{0:T(1024)S(1)}, f32[16896]{0:T(1024)S(1)}, u32[]{:S(2)}, u32[]{:S(2)}) collective-permute-start(f32[16896]{0:T(1024)S(1)} %slice_select_fusion.2), channel_id=1, source_target_pairs={{0,2},{2,0},{1,3},{3,1},{4,6},{6,4},{5,7},{7,5},{8,10},{10,8},{9,1... | collective-permute-start | bytes 202760 | tf_op jit(solution)/shard_map/ppermute | solution.py:78
  157.9 4.5 %collective-permute-start.20 = (f32[16896]{0:T(1024)S(1)}, f32[16896]{0:T(1024)S(1)}, u32[]{:S(2)}, u32[]{:S(2)}) collective-permute-start(f32[16896]{0:T(1024)S(1)} %select_add_fusion), channel_id=1, source_target_pairs={{0,16},{4,20},{8,24},{12,28},{16,0},{20,4},{24,8},{28,12},{1,17},{... | collective-permute-start | bytes 202760 | tf_op jit(solution)/shard_map/ppermute | solution.py:96
  162.4 4.4 %collective-permute-done.20 = f32[16896]{0:T(1024)S(1)} collective-permute-done((f32[16896]{0:T(1024)S(1)}, f32[16896]{0:T(1024)S(1)}, u32[]{:S(2)}, u32[]{:S(2)}) %collective-permute-start.20) | collective-permute-done | bytes 67616 | tf_op jit(solution)/shard_map/ppermute | solution.py:96
  166.8 2.8 %collective-permute-start.21 = (f32[16896]{0:T(1024)S(1)}, f32[16896]{0:T(1024)S(1)}, u32[]{:S(2)}, u32[]{:S(2)}) collective-permute-start(f32[16896]{0:T(1024)S(1)} %add.232), channel_id=1, source_target_pairs={{0,8},{4,12},{8,0},{12,4},{16,24},{20,28},{24,16},{28,20},{1,9},{5... | collective-permute-start | bytes 202760 | tf_op jit(solution)/shard_map/ppermute | solution.py:96
  169.6 3.2 %collective-permute-done.21 = f32[16896]{0:T(1024)S(1)} collective-permute-done((f32[16896]{0:T(1024)S(1)}, f32[16896]{0:T(1024)S(1)}, u32[]{:S(2)}, u32[]{:S(2)}) %collective-permute-start.21) | collective-permute-done | bytes 67616 | tf_op jit(solution)/shard_map/ppermute | solution.py:96
  172.8 3.7 %collective-permute-start.22 = (f32[16896]{0:T(1024)S(1)}, f32[16896]{0:T(1024)S(1)}, u32[]{:S(2)}, u32[]{:S(2)}) collective-permute-start(f32[16896]{0:T(1024)S(1)} %add.233), channel_id=1, source_target_pairs={{0,4},{4,0},{8,12},{12,8},{16,20},{20,16},{24,28},{28,24},{1,5},{5... | collective-permute-start | bytes 202760 | tf_op jit(solution)/shard_map/ppermute | solution.py:96
  178.3 2.5 %collective-permute-start.23 = (f32[16896]{0:T(1024)S(1)}, f32[16896]{0:T(1024)S(1)}, u32[]{:S(2)}, u32[]{:S(2)}) collective-permute-start(f32[16896]{0:T(1024)S(1)} %add.234), channel_id=1, source_target_pairs={{0,64},{32,96},{64,0},{96,32},{1,65},{33,97},{65,1},{97,33},{2,66}... | collective-permute-start | bytes 202760 | tf_op jit(solution)/shard_map/ppermute | solution.py:96
  180.8 4.0 %collective-permute-done.23 = f32[16896]{0:T(1024)S(1)} collective-permute-done((f32[16896]{0:T(1024)S(1)}, f32[16896]{0:T(1024)S(1)}, u32[]{:S(2)}, u32[]{:S(2)}) %collective-permute-start.23) | collective-permute-done | bytes 67616 | tf_op jit(solution)/shard_map/ppermute | solution.py:96
  186.8 3.4 %collective-permute-done.24 = f32[16896]{0:T(1024)S(1)} collective-permute-done((f32[16896]{0:T(1024)S(1)}, f32[16896]{0:T(1024)S(1)}, u32[]{:S(2)}, u32[]{:S(2)}) %collective-permute-start.24) | collective-permute-done | bytes 67616 | tf_op jit(solution)/shard_map/ppermute | solution.py:96
  192.5 6.9 %collective-permute-done.25 = f32[16896]{0:T(1024)S(1)} collective-permute-done((f32[16896]{0:T(1024)S(1)}, f32[16896]{0:T(1024)S(1)}, u32[]{:S(2)}, u32[]{:S(2)}) %collective-permute-start.25) | collective-permute-done | bytes 67616 | tf_op jit(solution)/shard_map/ppermute | solution.py:96
  201.3 5.6 %collective-permute-done.26 = f32[16896]{0:T(1024)S(1)} collective-permute-done((f32[16896]{0:T(1024)S(1)}, f32[16896]{0:T(1024)S(1)}, u32[]{:S(2)}, u32[]{:S(2)}) %collective-permute-start.26) | collective-permute-done | bytes 67616 | tf_op jit(solution)/shard_map/ppermute | solution.py:96
  208.9 3.1 %collective-permute-done.27 = f32[16896]{0:T(1024)S(1)} collective-permute-done((f32[16896]{0:T(1024)S(1)}, f32[16896]{0:T(1024)S(1)}, u32[]{:S(2)}, u32[]{:S(2)}) %collective-permute-start.27) | collective-permute-done | bytes 67616 | tf_op jit(solution)/shard_map/ppermute | solution.py:85
  212.0 11.2 %collective-permute-start.28 = (f32[33792]{0:T(1024)S(1)}, f32[33792]{0:T(1024)S(1)}, u32[]{:S(2)}, u32[]{:S(2)}) collective-permute-start(f32[33792]{0:T(1024)S(1)} %maximum_select_fusion.1), channel_id=1, source_target_pairs={{0,1},{1,0},{2,3},{3,2},{4,5},{5,4},{6,7},{7,6},{8,9},{9,8},{10,11... | collective-permute-start | bytes 405512 | tf_op jit(solution)/shard_map/ppermute | solution.py:85
  (99 shorter events, 51.5 us)
Async XLA Ops:
  0.6 117.1 %copy-start = (bf16[1,4,8,128,128]{4,3,2,1,0:T(8,128)(2,1)S(1)}, bf16[1,4,8,128,128]{4,3,2,1,0:T(8,128)(2,1)}, u32[]{:S(2)}) copy-start(bf16[1,4,8,128,128]{4,3,2,1,0:T(8,128)(2,1)} %param.13) | copy-start | bytes 3145732
  0.6 13.5 %collective-permute-start = (bf16[128,256]{1,0:T(8,128)(2,1)}, bf16[128,256]{1,0:T(8,128)(2,1)S(1)}, u32[]{:S(2)}, u32[]{:S(2)}) collective-permute-start(bf16[128,256]{1,0:T(8,128)(2,1)} %param.10), channel_id=1, source_target_pairs={{0,4},{4,8},{8,12},{12,16},{16,20},{20,24},{24,28},{28,0},{1,5},{5... | collective-permute-start | bytes 196616 | tf_op jit(solution)/shard_map/ppermute | solution.py:26
  14.1 6.5 %collective-permute-start.1 = (bf16[128,256]{1,0:T(8,128)(2,1)S(1)}, bf16[128,256]{1,0:T(8,128)(2,1)S(1)}, u32[]{:S(2)}, u32[]{:S(2)}) collective-permute-start(bf16[128,256]{1,0:T(8,128)(2,1)S(1)} %collective-permute-done), channel_id=1, source_target_pairs={{0,4},{4,8},{8,12},{12,16},{16,20},{20,24},{24,28},{28,0},{1,5},{5... | collective-permute-start | bytes 196616 | tf_op jit(solution)/shard_map/ppermute | solution.py:26
  16.0 6.5 %collective-permute-start.4 = (bf16[128,256]{1,0:T(8,128)(2,1)}, bf16[128,256]{1,0:T(8,128)(2,1)S(1)}, u32[]{:S(2)}, u32[]{:S(2)}) collective-permute-start(bf16[128,256]{1,0:T(8,128)(2,1)} %param.10), channel_id=1, source_target_pairs={{0,28},{4,0},{8,4},{12,8},{16,12},{20,16},{24,20},{28,24},{1,29},{... | collective-permute-start | bytes 196616 | tf_op jit(solution)/shard_map/ppermute | solution.py:29
  20.6 6.5 %collective-permute-start.2 = (bf16[128,256]{1,0:T(8,128)(2,1)S(1)}, bf16[128,256]{1,0:T(8,128)(2,1)S(1)}, u32[]{:S(2)}, u32[]{:S(2)}) collective-permute-start(bf16[128,256]{1,0:T(8,128)(2,1)S(1)} %collective-permute-done.1), channel_id=1, source_target_pairs={{0,4},{4,8},{8,12},{12,16},{16,20},{20,24},{24,28},{28,0},{1,5},{5... | collective-permute-start | bytes 196616 | tf_op jit(solution)/shard_map/ppermute | solution.py:26
  22.6 6.5 %collective-permute-start.5 = (bf16[128,256]{1,0:T(8,128)(2,1)S(1)}, bf16[128,256]{1,0:T(8,128)(2,1)S(1)}, u32[]{:S(2)}, u32[]{:S(2)}) collective-permute-start(bf16[128,256]{1,0:T(8,128)(2,1)S(1)} %collective-permute-done.4), channel_id=1, source_target_pairs={{0,28},{4,0},{8,4},{12,8},{16,12},{20,16},{24,20},{28,24},{1,29},{... | collective-permute-start | bytes 196616 | tf_op jit(solution)/shard_map/ppermute | solution.py:29
  27.2 6.5 %collective-permute-start.3 = (bf16[128,256]{1,0:T(8,128)(2,1)S(1)}, bf16[128,256]{1,0:T(8,128)(2,1)S(1)}, u32[]{:S(2)}, u32[]{:S(2)}) collective-permute-start(bf16[128,256]{1,0:T(8,128)(2,1)S(1)} %collective-permute-done.2), channel_id=1, source_target_pairs={{0,4},{4,8},{8,12},{12,16},{16,20},{20,24},{24,28},{28,0},{1,5},{5... | collective-permute-start | bytes 196616 | tf_op jit(solution)/shard_map/ppermute | solution.py:26
  29.1 5.9 %collective-permute-start.6 = (bf16[128,256]{1,0:T(8,128)(2,1)S(1)}, bf16[128,256]{1,0:T(8,128)(2,1)S(1)}, u32[]{:S(2)}, u32[]{:S(2)}) collective-permute-start(bf16[128,256]{1,0:T(8,128)(2,1)S(1)} %collective-permute-done.5), channel_id=1, source_target_pairs={{0,28},{4,0},{8,4},{12,8},{16,12},{20,16},{24,20},{28,24},{1,29},{... | collective-permute-start | bytes 196616 | tf_op jit(solution)/shard_map/ppermute | solution.py:29
  35.0 34.5 %copy-start.1 = (bf16[8,128,256]{2,1,0:T(8,128)(2,1)}, bf16[8,128,256]{2,1,0:T(8,128)(2,1)S(1)}, u32[]{:S(2)}) copy-start(bf16[8,128,256]{2,1,0:T(8,128)(2,1)S(1)} %bitcast_dynamic-update-slice_fusion) | copy-start | bytes 1572868
  35.0 23.4 %collective-permute-start.7 = (bf16[8,128,256]{2,1,0:T(8,128)(2,1)S(1)}, bf16[8,128,256]{2,1,0:T(8,128)(2,1)S(1)}, u32[]{:S(2)}, u32[]{:S(2)}) collective-permute-start(bf16[8,128,256]{2,1,0:T(8,128)(2,1)S(1)} %bitcast_dynamic-update-slice_fusion), channel_id=1, source_target_pairs={{0,32},{32,64},{64,96},{96,0},{1,33},{33,65},{65,97},{97,1},{2,34}... | collective-permute-start | bytes 1572872 | tf_op jit(solution)/shard_map/ppermute | solution.py:26
  38.8 16.1 %collective-permute-start.10 = (s32[8]{0:T(128)S(1)}, s32[8]{0:T(128)S(1)}, u32[]{:S(2)}, u32[]{:S(2)}) collective-permute-start(s32[8]{0:T(128)S(1)} %get-tuple-element.8), channel_id=1, source_target_pairs={{0,128},{128,256},{256,384},{384,0},{1,129},{129,257},{257,385},{3... | collective-permute-start | bytes 104 | tf_op jit(solution)/shard_map/ppermute | solution.py:38
  43.1 17.3 %collective-permute-start.14 = (s32[8]{0:T(128)S(1)}, s32[8]{0:T(128)S(1)}, u32[]{:S(2)}, u32[]{:S(2)}) collective-permute-start(s32[8]{0:T(128)S(1)} %get-tuple-element.8), channel_id=1, source_target_pairs={{0,384},{128,0},{256,128},{384,256},{1,385},{129,1},{257,129},{385... | collective-permute-start | bytes 104 | tf_op jit(solution)/shard_map/ppermute | solution.py:38
  46.7 13.7 %collective-permute-start.12 = (s32[8]{0:T(128)S(1)}, s32[8]{0:T(128)S(1)}, u32[]{:S(2)}, u32[]{:S(2)}) collective-permute-start(s32[8]{0:T(128)S(1)} %get-tuple-element.8), channel_id=1, source_target_pairs={{0,256},{128,384},{256,0},{384,128},{1,257},{129,385},{257,1},{385... | collective-permute-start | bytes 104 | tf_op jit(solution)/shard_map/ppermute | solution.py:38
  55.0 9.9 %collective-permute-start.9 = (bf16[8,128,256]{2,1,0:T(8,128)(2,1)S(1)}, bf16[8,128,256]{2,1,0:T(8,128)(2,1)S(1)}, u32[]{:S(2)}, u32[]{:S(2)}) collective-permute-start(bf16[8,128,256]{2,1,0:T(8,128)(2,1)S(1)} %bitcast_dynamic-update-slice_fusion), channel_id=1, source_target_pairs={{0,96},{32,0},{64,32},{96,64},{1,97},{33,1},{65,33},{97,65},{2,98}... | collective-permute-start | bytes 1572872 | tf_op jit(solution)/shard_map/ppermute | solution.py:29
  58.4 11.1 %collective-permute-start.8 = (bf16[8,128,256]{2,1,0:T(8,128)(2,1)S(1)}, bf16[8,128,256]{2,1,0:T(8,128)(2,1)S(1)}, u32[]{:S(2)}, u32[]{:S(2)}) collective-permute-start(bf16[8,128,256]{2,1,0:T(8,128)(2,1)S(1)} %collective-permute-done.7), channel_id=1, source_target_pairs={{0,32},{32,64},{64,96},{96,0},{1,33},{33,65},{65,97},{97,1},{2,34}... | collective-permute-start | bytes 1572872 | tf_op jit(solution)/shard_map/ppermute | solution.py:26
  74.3 28.6 %collective-permute-start.11 = (bf16[8,128,256]{2,1,0:T(8,128)(2,1)}, bf16[8,128,256]{2,1,0:T(8,128)(2,1)}, u32[]{:S(2)}, u32[]{:S(2)}) collective-permute-start(bf16[8,128,256]{2,1,0:T(8,128)(2,1)} %broadcast_select_fusion.2), channel_id=1, source_target_pairs={{0,384},{128,0},{256,128},{384,256},{1,385},{129,1},{257,129},{385... | collective-permute-start | bytes 1572872 | tf_op jit(solution)/shard_map/ppermute | solution.py:57
  79.6 24.3 %collective-permute-start.13 = (bf16[8,128,256]{2,1,0:T(8,128)(2,1)}, bf16[8,128,256]{2,1,0:T(8,128)(2,1)}, u32[]{:S(2)}, u32[]{:S(2)}) collective-permute-start(bf16[8,128,256]{2,1,0:T(8,128)(2,1)} %broadcast_select_fusion.1), channel_id=1, source_target_pairs={{0,256},{128,384},{256,0},{384,128},{1,257},{129,385},{257,1},{385... | collective-permute-start | bytes 1572872 | tf_op jit(solution)/shard_map/ppermute | solution.py:57
  87.4 30.3 %collective-permute-start.15 = (bf16[8,128,256]{2,1,0:T(8,128)(2,1)}, bf16[8,128,256]{2,1,0:T(8,128)(2,1)}, u32[]{:S(2)}, u32[]{:S(2)}) collective-permute-start(bf16[8,128,256]{2,1,0:T(8,128)(2,1)} %broadcast_select_fusion), channel_id=1, source_target_pairs={{0,128},{128,256},{256,384},{384,0},{1,129},{129,257},{257,385},{3... | collective-permute-start | bytes 1572872 | tf_op jit(solution)/shard_map/ppermute | solution.py:57
  120.6 27.1 %copy-start.3 = (bf16[256,256]{1,0:T(8,128)(2,1)S(1)}, bf16[256,256]{1,0:T(8,128)(2,1)}, u32[]{:S(2)}) copy-start(bf16[256,256]{1,0:T(8,128)(2,1)} %param.11) | copy-start | bytes 393220
  121.3 8.5 %collective-permute-start.16 = (f32[2,32768]{1,0:T(2,128)S(1)}, f32[2,32768]{1,0:T(2,128)S(1)}, u32[]{:S(2)}, u32[]{:S(2)}) collective-permute-start(f32[2,32768]{1,0:T(2,128)S(1)} %bitcast.56), channel_id=1, source_target_pairs={{0,1},{1,0},{2,3},{3,2},{4,5},{5,4},{6,7},{7,6},{8,9},{9,8},{10,11... | collective-permute-start | bytes 786440 | tf_op jit(solution)/shard_map/ppermute | solution.py:107
  130.4 17.2 %collective-permute-start.17 = (f32[32768]{0:T(1024)S(1)}, f32[32768]{0:T(1024)S(1)}, u32[]{:S(2)}, u32[]{:S(2)}) collective-permute-start(f32[32768]{0:T(1024)S(1)} %bitcast.57), channel_id=1, source_target_pairs={{0,2},{2,0},{1,3},{3,1},{4,6},{6,4},{5,7},{7,5},{8,10},{10,8},{9,1... | collective-permute-start | bytes 393224 | tf_op jit(solution)/shard_map/ppermute | solution.py:111
  148.9 3.8 %collective-permute-start.18 = (f32[33792]{0:T(1024)S(1)}, f32[33792]{0:T(1024)S(1)}, u32[]{:S(2)}, u32[]{:S(2)}) collective-permute-start(f32[33792]{0:T(1024)S(1)} %select_n.266), channel_id=1, source_target_pairs={{0,1},{1,0},{2,3},{3,2},{4,5},{5,4},{6,7},{7,6},{8,9},{9,8},{10,11... | collective-permute-start | bytes 405512 | tf_op jit(solution)/shard_map/ppermute | solution.py:78
  152.8 5.1 %collective-permute-start.19 = (f32[16896]{0:T(1024)S(1)}, f32[16896]{0:T(1024)S(1)}, u32[]{:S(2)}, u32[]{:S(2)}) collective-permute-start(f32[16896]{0:T(1024)S(1)} %slice_select_fusion.2), channel_id=1, source_target_pairs={{0,2},{2,0},{1,3},{3,1},{4,6},{6,4},{5,7},{7,5},{8,10},{10,8},{9,1... | collective-permute-start | bytes 202760 | tf_op jit(solution)/shard_map/ppermute | solution.py:78
  157.9 9.0 %collective-permute-start.20 = (f32[16896]{0:T(1024)S(1)}, f32[16896]{0:T(1024)S(1)}, u32[]{:S(2)}, u32[]{:S(2)}) collective-permute-start(f32[16896]{0:T(1024)S(1)} %select_add_fusion), channel_id=1, source_target_pairs={{0,16},{4,20},{8,24},{12,28},{16,0},{20,4},{24,8},{28,12},{1,17},{... | collective-permute-start | bytes 202760 | tf_op jit(solution)/shard_map/ppermute | solution.py:96
  166.8 6.0 %collective-permute-start.21 = (f32[16896]{0:T(1024)S(1)}, f32[16896]{0:T(1024)S(1)}, u32[]{:S(2)}, u32[]{:S(2)}) collective-permute-start(f32[16896]{0:T(1024)S(1)} %add.232), channel_id=1, source_target_pairs={{0,8},{4,12},{8,0},{12,4},{16,24},{20,28},{24,16},{28,20},{1,9},{5... | collective-permute-start | bytes 202760 | tf_op jit(solution)/shard_map/ppermute | solution.py:96
  172.8 5.4 %collective-permute-start.22 = (f32[16896]{0:T(1024)S(1)}, f32[16896]{0:T(1024)S(1)}, u32[]{:S(2)}, u32[]{:S(2)}) collective-permute-start(f32[16896]{0:T(1024)S(1)} %add.233), channel_id=1, source_target_pairs={{0,4},{4,0},{8,12},{12,8},{16,20},{20,16},{24,28},{28,24},{1,5},{5... | collective-permute-start | bytes 202760 | tf_op jit(solution)/shard_map/ppermute | solution.py:96
  178.3 6.6 %collective-permute-start.23 = (f32[16896]{0:T(1024)S(1)}, f32[16896]{0:T(1024)S(1)}, u32[]{:S(2)}, u32[]{:S(2)}) collective-permute-start(f32[16896]{0:T(1024)S(1)} %add.234), channel_id=1, source_target_pairs={{0,64},{32,96},{64,0},{96,32},{1,65},{33,97},{65,1},{97,33},{2,66}... | collective-permute-start | bytes 202760 | tf_op jit(solution)/shard_map/ppermute | solution.py:96
  184.8 5.3 %collective-permute-start.24 = (f32[16896]{0:T(1024)S(1)}, f32[16896]{0:T(1024)S(1)}, u32[]{:S(2)}, u32[]{:S(2)}) collective-permute-start(f32[16896]{0:T(1024)S(1)} %add.235), channel_id=1, source_target_pairs={{0,32},{32,0},{64,96},{96,64},{1,33},{33,1},{65,97},{97,65},{2,34}... | collective-permute-start | bytes 202760 | tf_op jit(solution)/shard_map/ppermute | solution.py:96
  190.2 9.2 %collective-permute-start.25 = (f32[16896]{0:T(1024)S(1)}, f32[16896]{0:T(1024)S(1)}, u32[]{:S(2)}, u32[]{:S(2)}) collective-permute-start(f32[16896]{0:T(1024)S(1)} %add.236), channel_id=1, source_target_pairs={{0,256},{128,384},{256,0},{384,128},{1,257},{129,385},{257,1},{385... | collective-permute-start | bytes 202760 | tf_op jit(solution)/shard_map/ppermute | solution.py:96
  199.4 7.5 %collective-permute-start.26 = (f32[16896]{0:T(1024)S(1)}, f32[16896]{0:T(1024)S(1)}, u32[]{:S(2)}, u32[]{:S(2)}) collective-permute-start(f32[16896]{0:T(1024)S(1)} %add.237), channel_id=1, source_target_pairs={{0,128},{128,0},{256,384},{384,256},{1,129},{129,1},{257,385},{385... | collective-permute-start | bytes 202760 | tf_op jit(solution)/shard_map/ppermute | solution.py:96
  207.0 5.1 %collective-permute-start.27 = (f32[16896]{0:T(1024)S(1)}, f32[16896]{0:T(1024)S(1)}, u32[]{:S(2)}, u32[]{:S(2)}) collective-permute-start(f32[16896]{0:T(1024)S(1)} %add.238), channel_id=1, source_target_pairs={{0,2},{2,0},{1,3},{3,1},{4,6},{6,4},{5,7},{7,5},{8,10},{10,8},{9,1... | collective-permute-start | bytes 202760 | tf_op jit(solution)/shard_map/ppermute | solution.py:85
  212.0 12.2 %collective-permute-start.28 = (f32[33792]{0:T(1024)S(1)}, f32[33792]{0:T(1024)S(1)}, u32[]{:S(2)}, u32[]{:S(2)}) collective-permute-start(f32[33792]{0:T(1024)S(1)} %maximum_select_fusion.1), channel_id=1, source_target_pairs={{0,1},{1,0},{2,3},{3,2},{4,5},{5,4},{6,7},{7,6},{8,9},{9,8},{10,11... | collective-permute-start | bytes 405512 | tf_op jit(solution)/shard_map/ppermute | solution.py:85
  (3 other events, 65.4 us)

commit v6 on v5

--- a/solution.py
+++ b/solution.py
@@ -31,30 +31,39 @@
     return jnp.stack([pieces[d] for d in range(-(n // 2), n - n // 2)])
 
 
-def plane_blocks(features, cols):
-    sizes = {a: lax.axis_size(a) for a in ROW_AXES}
-    n_plane = sizes["y_hi"]
+def row_coords(c):
+    coords = {}
+    for a in reversed(ROW_AXES):
+        size = lax.axis_size(a)
+        coords[a] = c % size
+        c = c // size
+    return coords
+
+
+def plane_blocks(features, cols, across="x", within=("y_hi", "z")):
+    n_across = lax.axis_size(across)
     peer_cols = {
-        s: lax.ppermute(cols, "y_hi", [(i, (i - s) % n_plane) for i in range(n_plane)])
-        for s in range(1, n_plane)
+        s: lax.ppermute(cols, across, [(i, (i - s) % n_across) for i in range(n_across)])
+        for s in range(1, n_across)
     }
     stack = features
-    for a in ("z", "x"):
+    for a in within:
         stack = ring_gather(stack, a)
     plane = stack.reshape(-1, features.shape[0], features.shape[1])
 
     def in_plane(c):
-        z = c % sizes["z"]
-        x = (c // sizes["z"]) % sizes["x"]
-        kz = (z - lax.axis_index("z") + sizes["z"] // 2) % sizes["z"]
-        kx = (x - lax.axis_index("x") + sizes["x"] // 2) % sizes["x"]
-        return kx * sizes["z"] + kz
+        coords = row_coords(c)
+        flat = jnp.zeros_like(c)
+        for a in reversed(within):
+            size = lax.axis_size(a)
+            flat = flat * size + (coords[a] - lax.axis_index(a) + size // 2) % size
+        return flat
 
     picked = jnp.take(plane, in_plane(cols), axis=0)
-    source = (lax.axis_index("y_hi") - cols // (sizes["z"] * sizes["x"])) % n_plane
-    for s in range(1, n_plane):
+    source = (lax.axis_index(across) - row_coords(cols)[across]) % n_across
+    for s in range(1, n_across):
         sent = jnp.take(plane, in_plane(peer_cols[s]), axis=0)
-        got = lax.ppermute(sent, "y_hi", [(i, (i + s) % n_plane) for i in range(n_plane)])
+        got = lax.ppermute(sent, across, [(i, (i + s) % n_across) for i in range(n_across)])
         picked = jnp.where((source == s)[:, None, None], got, picked)
     return picked
 

time: 227 us -> 206 us (0.907)
  waiting for transfers between devices: 84 us -> 64 us
  starting transfers between devices: 116 us -> 113 us
    ppermute x6, waiting for transfers between devices: 25.6 us -> 9.41 us  [the longest x3 9.4 us: plane_blocks(): lax.ppermute(sent, across, [(i, (i + s) % n_across) for i in range(n_acro...]
    ppermute x1, starting transfers between devices: 13.8 us -> 3.22 us  [reduce_over_rep(): own = keep + lax.ppermute(send, 'y_lo', [(0, 1), (1, 0)])]
    ppermute x7, starting transfers between devices: 19.8 us -> 27.3 us  [reduce_all(): flat = flat + lax.ppermute(flat, a, perm)]
    ppermute x6, starting transfers between devices: 23.1 us -> 17.9 us  [the longest x3 9.92 us: plane_blocks(): lax.ppermute(cols, across, [(i, (i - s) % n_across) for i in range(n_acro...]
    ppermute x7, waiting for transfers between devices: 29.2 us -> 24.6 us  [reduce_all(): flat = flat + lax.ppermute(flat, a, perm)]
    ppermute x1, starting transfers between devices: 7.37 us -> 11.2 us  [reduce_over_rep(): pairs = keep + lax.ppermute(send, 'core', [(0, 1), (1, 0)])]
    ppermute x6, starting transfers between devices: 15.7 us -> 19.1 us  [ring_gather(): left = lax.ppermute(left, axis, fwd)]
    ppermute x2, starting transfers between devices: 13.1 us -> 10 us  [all_gather_flat(): other = lax.ppermute(flat, a, perm)]
  transfers between devices with their start and end apart: 29 -> 29, of which waited for: 20 -> 22; matrix products, arithmetic and copies ran while one was open for 6% -> 7% of each run, Pallas kernels for 0% -> 0%
where the time goes in v6:
time: 206 us; the launch traced here: 204 us
  starting transfers between devices  113 us (55%)
  waiting for transfers between devices  64 us (31%)
  other arithmetic  12.6 us (6%)
  local copies, waits for them, and re-layouts  9.53 us (5%)
  matrix products  3.4 us (2%)
    ppermute x7, starting transfers between devices, reduce_all(): flat = flat + lax.ppermute(flat, a, perm)  27.3 us
    ppermute x7, waiting for transfers between devices, reduce_all(): flat = flat + lax.ppermute(flat, a, perm)  24.6 us
    ppermute x6, starting transfers between devices, ring_gather(): left = lax.ppermute(left, axis, fwd)  19.1 us
    ppermute x4, starting transfers between devices, ring_gather(): right = lax.ppermute(right, axis, bwd)  18.2 us
    ppermute x6, waiting for transfers between devices, ring_gather(): left = lax.ppermute(left, axis, fwd)  12.8 us
    ppermute x1, starting transfers between devices, reduce_over_rep(): pairs = keep + lax.ppermute(send, 'core', [(0, 1), (1, 0)])  11.2 us
    ppermute x2, starting transfers between devices, all_gather_flat(): other = lax.ppermute(flat, a, perm)  10 us
    ppermute x3, starting transfers between devices, plane_blocks(): lax.ppermute(cols, across, [(i, (i - s) % n_across) for i in range(n_acro...  9.92 us
  transfers between devices with their start and end apart: 29, of which 22 were waited for; matrix products, arithmetic and copies ran while one was open for 7% of the time, Pallas kernels for 0%

profile of v6, /device:TPU:1, one launch (start us, length us, event | category | flops | bytes accessed | tf_op | source)
XLA Modules:
  0.0 204.2 jit_solution(215417384943430378)
XLA Ops:
  0.7 5.2 %collective-permute-start = (bf16[128,256]{1,0:T(8,128)(2,1)}, bf16[128,256]{1,0:T(8,128)(2,1)S(1)}, u32[]{:S(2)}, u32[]{:S(2)}) collective-permute-start(bf16[128,256]{1,0:T(8,128)(2,1)} %param.10), channel_id=1, source_target_pairs={{0,128},{128,256},{256,384},{384,0},{1,129},{129,257},{257,385},{3... | collective-permute-start | bytes 196616 | tf_op jit(solution)/shard_map/ppermute | solution.py:26
  5.8 3.6 %collective-permute-start.2 = (bf16[128,256]{1,0:T(8,128)(2,1)}, bf16[128,256]{1,0:T(8,128)(2,1)S(1)}, u32[]{:S(2)}, u32[]{:S(2)}) collective-permute-start(bf16[128,256]{1,0:T(8,128)(2,1)} %param.10), channel_id=1, source_target_pairs={{0,384},{128,0},{256,128},{384,256},{1,385},{129,1},{257,129},{385... | collective-permute-start | bytes 196616 | tf_op jit(solution)/shard_map/ppermute | solution.py:29
  9.4 4.2 %collective-permute-start.1 = (bf16[128,256]{1,0:T(8,128)(2,1)S(1)}, bf16[128,256]{1,0:T(8,128)(2,1)S(1)}, u32[]{:S(2)}, u32[]{:S(2)}) collective-permute-start(bf16[128,256]{1,0:T(8,128)(2,1)S(1)} %collective-permute-done), channel_id=1, source_target_pairs={{0,128},{128,256},{256,384},{384,0},{1,129},{129,257},{257,385},{3... | collective-permute-start | bytes 196616 | tf_op jit(solution)/shard_map/ppermute | solution.py:26
  17.5 4.0 %collective-permute-start.3 = (bf16[4,128,256]{2,1,0:T(8,128)(2,1)S(1)}, bf16[4,128,256]{2,1,0:T(8,128)(2,1)S(1)}, u32[]{:S(2)}, u32[]{:S(2)}) collective-permute-start(bf16[4,128,256]{2,1,0:T(8,128)(2,1)S(1)} %pad_maximum_fusion.2), channel_id=1, source_target_pairs={{0,4},{4,8},{8,12},{12,16},{16,20},{20,24},{24,28},{28,0},{1,5},{5... | collective-permute-start | bytes 786440 | tf_op jit(solution)/shard_map/ppermute | solution.py:26
  21.5 10.4 %collective-permute-done.3 = bf16[4,128,256]{2,1,0:T(8,128)(2,1)S(1)} collective-permute-done((bf16[4,128,256]{2,1,0:T(8,128)(2,1)S(1)}, bf16[4,128,256]{2,1,0:T(8,128)(2,1)S(1)}, u32[]{:S(2)}, u32[]{:S(2)}) %collective-permute-start.3) | collective-permute-done | bytes 262176 | tf_op jit(solution)/shard_map/ppermute | solution.py:26
  35.1 3.1 %collective-permute-start.10 = (s32[8]{0:T(128)S(1)}, s32[8]{0:T(128)S(1)}, u32[]{:S(2)}, u32[]{:S(2)}) collective-permute-start(s32[8]{0:T(128)S(1)} %get-tuple-element.9), channel_id=1, source_target_pairs={{0,32},{32,64},{64,96},{96,0},{1,33},{33,65},{65,97},{97,1},{2,34}... | collective-permute-start | bytes 104 | tf_op jit(solution)/shard_map/ppermute | solution.py:46
  38.2 3.4 %collective-permute-start.14 = (s32[8]{0:T(128)S(1)}, s32[8]{0:T(128)S(1)}, u32[]{:S(2)}, u32[]{:S(2)}) collective-permute-start(s32[8]{0:T(128)S(1)} %get-tuple-element.9), channel_id=1, source_target_pairs={{0,96},{32,0},{64,32},{96,64},{1,97},{33,1},{65,33},{97,65},{2,98}... | collective-permute-start | bytes 104 | tf_op jit(solution)/shard_map/ppermute | solution.py:46
  41.6 3.4 %collective-permute-start.12 = (s32[8]{0:T(128)S(1)}, s32[8]{0:T(128)S(1)}, u32[]{:S(2)}, u32[]{:S(2)}) collective-permute-start(s32[8]{0:T(128)S(1)} %get-tuple-element.9), channel_id=1, source_target_pairs={{0,64},{32,96},{64,0},{96,32},{1,65},{33,97},{65,1},{97,33},{2,66}... | collective-permute-start | bytes 104 | tf_op jit(solution)/shard_map/ppermute | solution.py:46
  46.3 4.6 %collective-permute-start.7 = (bf16[4,128,256]{2,1,0:T(8,128)(2,1)S(1)}, bf16[4,128,256]{2,1,0:T(8,128)(2,1)S(1)}, u32[]{:S(2)}, u32[]{:S(2)}) collective-permute-start(bf16[4,128,256]{2,1,0:T(8,128)(2,1)S(1)} %pad_maximum_fusion.2), channel_id=1, source_target_pairs={{0,28},{4,0},{8,4},{12,8},{16,12},{20,16},{24,20},{28,24},{1,29},{... | collective-permute-start | bytes 786440 | tf_op jit(solution)/shard_map/ppermute | solution.py:29
  54.2 5.0 %collective-permute-start.8 = (bf16[4,128,256]{2,1,0:T(8,128)(2,1)S(1)}, bf16[4,128,256]{2,1,0:T(8,128)(2,1)S(1)}, u32[]{:S(2)}, u32[]{:S(2)}) collective-permute-start(bf16[4,128,256]{2,1,0:T(8,128)(2,1)S(1)} %collective-permute-done.7), channel_id=1, source_target_pairs={{0,28},{4,0},{8,4},{12,8},{16,12},{20,16},{24,20},{28,24},{1,29},{... | collective-permute-start | bytes 786440 | tf_op jit(solution)/shard_map/ppermute | solution.py:29
  62.8 5.0 %collective-permute-start.9 = (bf16[4,128,256]{2,1,0:T(8,128)(2,1)S(1)}, bf16[4,128,256]{2,1,0:T(8,128)(2,1)S(1)}, u32[]{:S(2)}, u32[]{:S(2)}) collective-permute-start(bf16[4,128,256]{2,1,0:T(8,128)(2,1)S(1)} %collective-permute-done.8), channel_id=1, source_target_pairs={{0,28},{4,0},{8,4},{12,8},{16,12},{20,16},{24,20},{28,24},{1,29},{... | collective-permute-start | bytes 786440 | tf_op jit(solution)/shard_map/ppermute | solution.py:29
  69.3 3.2 %collective-permute-done.9 = bf16[4,128,256]{2,1,0:T(8,128)(2,1)S(1)} collective-permute-done((bf16[4,128,256]{2,1,0:T(8,128)(2,1)S(1)}, bf16[4,128,256]{2,1,0:T(8,128)(2,1)S(1)}, u32[]{:S(2)}, u32[]{:S(2)}) %collective-permute-start.9) | collective-permute-done | bytes 262176 | tf_op jit(solution)/shard_map/ppermute | solution.py:29
  75.9 2.8 %collective-permute-start.11 = (bf16[8,128,256]{2,1,0:T(8,128)(2,1)}, bf16[8,128,256]{2,1,0:T(8,128)(2,1)}, u32[]{:S(2)}, u32[]{:S(2)}) collective-permute-start(bf16[8,128,256]{2,1,0:T(8,128)(2,1)} %broadcast_select_fusion.2), channel_id=1, source_target_pairs={{0,96},{32,0},{64,32},{96,64},{1,97},{33,1},{65,33},{97,65},{2,98}... | collective-permute-start | bytes 1572872 | tf_op jit(solution)/shard_map/ppermute | solution.py:66
  82.0 3.1 %collective-permute-start.13 = (bf16[8,128,256]{2,1,0:T(8,128)(2,1)}, bf16[8,128,256]{2,1,0:T(8,128)(2,1)}, u32[]{:S(2)}, u32[]{:S(2)}) collective-permute-start(bf16[8,128,256]{2,1,0:T(8,128)(2,1)} %broadcast_select_fusion.1), channel_id=1, source_target_pairs={{0,64},{32,96},{64,0},{96,32},{1,65},{33,97},{65,1},{97,33},{2,66}... | collective-permute-start | bytes 1572872 | tf_op jit(solution)/shard_map/ppermute | solution.py:66
  93.8 9.0 %collective-permute-done.15 = bf16[8,128,256]{2,1,0:T(8,128)(2,1)} collective-permute-done((bf16[8,128,256]{2,1,0:T(8,128)(2,1)}, bf16[8,128,256]{2,1,0:T(8,128)(2,1)}, u32[]{:S(2)}, u32[]{:S(2)}) %collective-permute-start.15) | collective-permute-done | bytes 524320 | tf_op jit(solution)/shard_map/ppermute | solution.py:66
  106.3 11.2 %collective-permute-start.16 = (f32[2,32768]{1,0:T(2,128)S(1)}, f32[2,32768]{1,0:T(2,128)S(1)}, u32[]{:S(2)}, u32[]{:S(2)}) collective-permute-start(f32[2,32768]{1,0:T(2,128)S(1)} %bitcast.52), channel_id=1, source_target_pairs={{0,1},{1,0},{2,3},{3,2},{4,5},{5,4},{6,7},{7,6},{8,9},{9,8},{10,11... | collective-permute-start | bytes 786440 | tf_op jit(solution)/shard_map/ppermute | solution.py:116
  119.3 3.2 %collective-permute-start.17 = (f32[32768]{0:T(1024)S(1)}, f32[32768]{0:T(1024)S(1)}, u32[]{:S(2)}, u32[]{:S(2)}) collective-permute-start(f32[32768]{0:T(1024)S(1)} %bitcast.61), channel_id=1, source_target_pairs={{0,2},{2,0},{1,3},{3,1},{4,6},{6,4},{5,7},{7,5},{8,10},{10,8},{9,1... | collective-permute-start | bytes 393224 | tf_op jit(solution)/shard_map/ppermute | solution.py:120
  122.6 3.3 %collective-permute-done.17 = f32[32768]{0:T(1024)S(1)} collective-permute-done((f32[32768]{0:T(1024)S(1)}, f32[32768]{0:T(1024)S(1)}, u32[]{:S(2)}, u32[]{:S(2)}) %collective-permute-start.17) | collective-permute-done | bytes 131104 | tf_op jit(solution)/shard_map/ppermute | solution.py:120
  127.2 3.1 %collective-permute-start.18 = (f32[33792]{0:T(1024)S(1)}, f32[33792]{0:T(1024)S(1)}, u32[]{:S(2)}, u32[]{:S(2)}) collective-permute-start(f32[33792]{0:T(1024)S(1)} %select_n.294), channel_id=1, source_target_pairs={{0,1},{1,0},{2,3},{3,2},{4,5},{5,4},{6,7},{7,6},{8,9},{9,8},{10,11... | collective-permute-start | bytes 405512 | tf_op jit(solution)/shard_map/ppermute | solution.py:87
  131.3 3.2 %collective-permute-start.19 = (f32[16896]{0:T(1024)S(1)}, f32[16896]{0:T(1024)S(1)}, u32[]{:S(2)}, u32[]{:S(2)}) collective-permute-start(f32[16896]{0:T(1024)S(1)} %slice_select_fusion.2), channel_id=1, source_target_pairs={{0,2},{2,0},{1,3},{3,1},{4,6},{6,4},{5,7},{7,5},{8,10},{10,8},{9,1... | collective-permute-start | bytes 202760 | tf_op jit(solution)/shard_map/ppermute | solution.py:87
  136.4 5.1 %collective-permute-start.20 = (f32[16896]{0:T(1024)S(1)}, f32[16896]{0:T(1024)S(1)}, u32[]{:S(2)}, u32[]{:S(2)}) collective-permute-start(f32[16896]{0:T(1024)S(1)} %select_add_fusion), channel_id=1, source_target_pairs={{0,16},{4,20},{8,24},{12,28},{16,0},{20,4},{24,8},{28,12},{1,17},{... | collective-permute-start | bytes 202760 | tf_op jit(solution)/shard_map/ppermute | solution.py:105
  141.5 3.9 %collective-permute-done.20 = f32[16896]{0:T(1024)S(1)} collective-permute-done((f32[16896]{0:T(1024)S(1)}, f32[16896]{0:T(1024)S(1)}, u32[]{:S(2)}, u32[]{:S(2)}) %collective-permute-start.20) | collective-permute-done | bytes 67616 | tf_op jit(solution)/shard_map/ppermute | solution.py:105
  145.4 3.2 %collective-permute-start.21 = (f32[16896]{0:T(1024)S(1)}, f32[16896]{0:T(1024)S(1)}, u32[]{:S(2)}, u32[]{:S(2)}) collective-permute-start(f32[16896]{0:T(1024)S(1)} %add.250), channel_id=1, source_target_pairs={{0,8},{4,12},{8,0},{12,4},{16,24},{20,28},{24,16},{28,20},{1,9},{5... | collective-permute-start | bytes 202760 | tf_op jit(solution)/shard_map/ppermute | solution.py:105
  148.5 2.8 %collective-permute-done.21 = f32[16896]{0:T(1024)S(1)} collective-permute-done((f32[16896]{0:T(1024)S(1)}, f32[16896]{0:T(1024)S(1)}, u32[]{:S(2)}, u32[]{:S(2)}) %collective-permute-start.21) | collective-permute-done | bytes 67616 | tf_op jit(solution)/shard_map/ppermute | solution.py:105
  151.3 4.1 %collective-permute-start.22 = (f32[16896]{0:T(1024)S(1)}, f32[16896]{0:T(1024)S(1)}, u32[]{:S(2)}, u32[]{:S(2)}) collective-permute-start(f32[16896]{0:T(1024)S(1)} %add.251), channel_id=1, source_target_pairs={{0,4},{4,0},{8,12},{12,8},{16,20},{20,16},{24,28},{28,24},{1,5},{5... | collective-permute-start | bytes 202760 | tf_op jit(solution)/shard_map/ppermute | solution.py:105
  159.6 4.2 %collective-permute-done.23 = f32[16896]{0:T(1024)S(1)} collective-permute-done((f32[16896]{0:T(1024)S(1)}, f32[16896]{0:T(1024)S(1)}, u32[]{:S(2)}, u32[]{:S(2)}) %collective-permute-start.23) | collective-permute-done | bytes 67616 | tf_op jit(solution)/shard_map/ppermute | solution.py:105
  165.7 3.4 %collective-permute-done.24 = f32[16896]{0:T(1024)S(1)} collective-permute-done((f32[16896]{0:T(1024)S(1)}, f32[16896]{0:T(1024)S(1)}, u32[]{:S(2)}, u32[]{:S(2)}) %collective-permute-start.24) | collective-permute-done | bytes 67616 | tf_op jit(solution)/shard_map/ppermute | solution.py:105
  169.1 8.6 %collective-permute-start.25 = (f32[16896]{0:T(1024)S(1)}, f32[16896]{0:T(1024)S(1)}, u32[]{:S(2)}, u32[]{:S(2)}) collective-permute-start(f32[16896]{0:T(1024)S(1)} %add.254), channel_id=1, source_target_pairs={{0,256},{128,384},{256,0},{384,128},{1,257},{129,385},{257,1},{385... | collective-permute-start | bytes 202760 | tf_op jit(solution)/shard_map/ppermute | solution.py:105
  177.8 2.4 %collective-permute-done.25 = f32[16896]{0:T(1024)S(1)} collective-permute-done((f32[16896]{0:T(1024)S(1)}, f32[16896]{0:T(1024)S(1)}, u32[]{:S(2)}, u32[]{:S(2)}) %collective-permute-start.25) | collective-permute-done | bytes 67616 | tf_op jit(solution)/shard_map/ppermute | solution.py:105
  182.2 6.3 %collective-permute-done.26 = f32[16896]{0:T(1024)S(1)} collective-permute-done((f32[16896]{0:T(1024)S(1)}, f32[16896]{0:T(1024)S(1)}, u32[]{:S(2)}, u32[]{:S(2)}) %collective-permute-start.26) | collective-permute-done | bytes 67616 | tf_op jit(solution)/shard_map/ppermute | solution.py:105
  190.4 3.4 %collective-permute-done.27 = f32[16896]{0:T(1024)S(1)} collective-permute-done((f32[16896]{0:T(1024)S(1)}, f32[16896]{0:T(1024)S(1)}, u32[]{:S(2)}, u32[]{:S(2)}) %collective-permute-start.27) | collective-permute-done | bytes 67616 | tf_op jit(solution)/shard_map/ppermute | solution.py:94
  193.8 8.1 %collective-permute-start.28 = (f32[33792]{0:T(1024)S(1)}, f32[33792]{0:T(1024)S(1)}, u32[]{:S(2)}, u32[]{:S(2)}) collective-permute-start(f32[33792]{0:T(1024)S(1)} %maximum_select_fusion.1), channel_id=1, source_target_pairs={{0,1},{1,0},{2,3},{3,2},{4,5},{5,4},{6,7},{7,6},{8,9},{9,8},{10,11... | collective-permute-start | bytes 405512 | tf_op jit(solution)/shard_map/ppermute | solution.py:94
  (119 shorter events, 53.3 us)
Async XLA Ops:
  0.6 102.2 %copy-start = (bf16[1,4,8,128,128]{4,3,2,1,0:T(8,128)(2,1)S(1)}, bf16[1,4,8,128,128]{4,3,2,1,0:T(8,128)(2,1)}, u32[]{:S(2)}) copy-start(bf16[1,4,8,128,128]{4,3,2,1,0:T(8,128)(2,1)} %param.13) | copy-start | bytes 3145732
  0.6 68.6 %copy-start.2 = (bf16[128,256]{1,0:T(8,128)(2,1)S(1)}, bf16[128,256]{1,0:T(8,128)(2,1)}, u32[]{:S(2)}) copy-start(bf16[128,256]{1,0:T(8,128)(2,1)} %param.10) | copy-start | bytes 196612
  0.7 8.8 %collective-permute-start = (bf16[128,256]{1,0:T(8,128)(2,1)}, bf16[128,256]{1,0:T(8,128)(2,1)S(1)}, u32[]{:S(2)}, u32[]{:S(2)}) collective-permute-start(bf16[128,256]{1,0:T(8,128)(2,1)} %param.10), channel_id=1, source_target_pairs={{0,128},{128,256},{256,384},{384,0},{1,129},{129,257},{257,385},{3... | collective-permute-start | bytes 196616 | tf_op jit(solution)/shard_map/ppermute | solution.py:26
  5.8 8.7 %collective-permute-start.2 = (bf16[128,256]{1,0:T(8,128)(2,1)}, bf16[128,256]{1,0:T(8,128)(2,1)S(1)}, u32[]{:S(2)}, u32[]{:S(2)}) collective-permute-start(bf16[128,256]{1,0:T(8,128)(2,1)} %param.10), channel_id=1, source_target_pairs={{0,384},{128,0},{256,128},{384,256},{1,385},{129,1},{257,129},{385... | collective-permute-start | bytes 196616 | tf_op jit(solution)/shard_map/ppermute | solution.py:29
  9.4 7.1 %collective-permute-start.1 = (bf16[128,256]{1,0:T(8,128)(2,1)S(1)}, bf16[128,256]{1,0:T(8,128)(2,1)S(1)}, u32[]{:S(2)}, u32[]{:S(2)}) collective-permute-start(bf16[128,256]{1,0:T(8,128)(2,1)S(1)} %collective-permute-done), channel_id=1, source_target_pairs={{0,128},{128,256},{256,384},{384,0},{1,129},{129,257},{257,385},{3... | collective-permute-start | bytes 196616 | tf_op jit(solution)/shard_map/ppermute | solution.py:26
  14.5 53.3 %copy-start.3 = (bf16[128,256]{1,0:T(8,128)(2,1)}, bf16[128,256]{1,0:T(8,128)(2,1)S(1)}, u32[]{:S(2)}) copy-start(bf16[128,256]{1,0:T(8,128)(2,1)S(1)} %collective-permute-done.2) | copy-start | bytes 196612
  17.5 14.4 %collective-permute-start.3 = (bf16[4,128,256]{2,1,0:T(8,128)(2,1)S(1)}, bf16[4,128,256]{2,1,0:T(8,128)(2,1)S(1)}, u32[]{:S(2)}, u32[]{:S(2)}) collective-permute-start(bf16[4,128,256]{2,1,0:T(8,128)(2,1)S(1)} %pad_maximum_fusion.2), channel_id=1, source_target_pairs={{0,4},{4,8},{8,12},{12,16},{16,20},{20,24},{24,28},{28,0},{1,5},{5... | collective-permute-start | bytes 786440 | tf_op jit(solution)/shard_map/ppermute | solution.py:26
  31.9 19.0 %collective-permute-start.4 = (bf16[4,128,256]{2,1,0:T(8,128)(2,1)S(1)}, bf16[4,128,256]{2,1,0:T(8,128)(2,1)S(1)}, u32[]{:S(2)}, u32[]{:S(2)}) collective-permute-start(bf16[4,128,256]{2,1,0:T(8,128)(2,1)S(1)} %collective-permute-done.3), channel_id=1, source_target_pairs={{0,4},{4,8},{8,12},{12,16},{16,20},{20,24},{24,28},{28,0},{1,5},{5... | collective-permute-start | bytes 786440 | tf_op jit(solution)/shard_map/ppermute | solution.py:26
  35.1 17.8 %collective-permute-start.10 = (s32[8]{0:T(128)S(1)}, s32[8]{0:T(128)S(1)}, u32[]{:S(2)}, u32[]{:S(2)}) collective-permute-start(s32[8]{0:T(128)S(1)} %get-tuple-element.9), channel_id=1, source_target_pairs={{0,32},{32,64},{64,96},{96,0},{1,33},{33,65},{65,97},{97,1},{2,34}... | collective-permute-start | bytes 104 | tf_op jit(solution)/shard_map/ppermute | solution.py:46
  38.2 15.2 %collective-permute-start.14 = (s32[8]{0:T(128)S(1)}, s32[8]{0:T(128)S(1)}, u32[]{:S(2)}, u32[]{:S(2)}) collective-permute-start(s32[8]{0:T(128)S(1)} %get-tuple-element.9), channel_id=1, source_target_pairs={{0,96},{32,0},{64,32},{96,64},{1,97},{33,1},{65,33},{97,65},{2,98}... | collective-permute-start | bytes 104 | tf_op jit(solution)/shard_map/ppermute | solution.py:46
  41.6 19.6 %collective-permute-start.12 = (s32[8]{0:T(128)S(1)}, s32[8]{0:T(128)S(1)}, u32[]{:S(2)}, u32[]{:S(2)}) collective-permute-start(s32[8]{0:T(128)S(1)} %get-tuple-element.9), channel_id=1, source_target_pairs={{0,64},{32,96},{64,0},{96,32},{1,65},{33,97},{65,1},{97,33},{2,66}... | collective-permute-start | bytes 104 | tf_op jit(solution)/shard_map/ppermute | solution.py:46
  46.3 7.9 %collective-permute-start.7 = (bf16[4,128,256]{2,1,0:T(8,128)(2,1)S(1)}, bf16[4,128,256]{2,1,0:T(8,128)(2,1)S(1)}, u32[]{:S(2)}, u32[]{:S(2)}) collective-permute-start(bf16[4,128,256]{2,1,0:T(8,128)(2,1)S(1)} %pad_maximum_fusion.2), channel_id=1, source_target_pairs={{0,28},{4,0},{8,4},{12,8},{16,12},{20,16},{24,20},{28,24},{1,29},{... | collective-permute-start | bytes 786440 | tf_op jit(solution)/shard_map/ppermute | solution.py:29
  50.9 8.3 %collective-permute-start.5 = (bf16[4,128,256]{2,1,0:T(8,128)(2,1)S(1)}, bf16[4,128,256]{2,1,0:T(8,128)(2,1)S(1)}, u32[]{:S(2)}, u32[]{:S(2)}) collective-permute-start(bf16[4,128,256]{2,1,0:T(8,128)(2,1)S(1)} %collective-permute-done.4), channel_id=1, source_target_pairs={{0,4},{4,8},{8,12},{12,16},{16,20},{20,24},{24,28},{28,0},{1,5},{5... | collective-permute-start | bytes 786440 | tf_op jit(solution)/shard_map/ppermute | solution.py:26
  54.2 8.6 %collective-permute-start.8 = (bf16[4,128,256]{2,1,0:T(8,128)(2,1)S(1)}, bf16[4,128,256]{2,1,0:T(8,128)(2,1)S(1)}, u32[]{:S(2)}, u32[]{:S(2)}) collective-permute-start(bf16[4,128,256]{2,1,0:T(8,128)(2,1)S(1)} %collective-permute-done.7), channel_id=1, source_target_pairs={{0,28},{4,0},{8,4},{12,8},{16,12},{20,16},{24,20},{28,24},{1,29},{... | collective-permute-start | bytes 786440 | tf_op jit(solution)/shard_map/ppermute | solution.py:29
  59.3 8.9 %collective-permute-start.6 = (bf16[4,128,256]{2,1,0:T(8,128)(2,1)S(1)}, bf16[4,128,256]{2,1,0:T(8,128)(2,1)S(1)}, u32[]{:S(2)}, u32[]{:S(2)}) collective-permute-start(bf16[4,128,256]{2,1,0:T(8,128)(2,1)S(1)} %collective-permute-done.5), channel_id=1, source_target_pairs={{0,4},{4,8},{8,12},{12,16},{16,20},{20,24},{24,28},{28,0},{1,5},{5... | collective-permute-start | bytes 786440 | tf_op jit(solution)/shard_map/ppermute | solution.py:26
  62.8 9.8 %collective-permute-start.9 = (bf16[4,128,256]{2,1,0:T(8,128)(2,1)S(1)}, bf16[4,128,256]{2,1,0:T(8,128)(2,1)S(1)}, u32[]{:S(2)}, u32[]{:S(2)}) collective-permute-start(bf16[4,128,256]{2,1,0:T(8,128)(2,1)S(1)} %collective-permute-done.8), channel_id=1, source_target_pairs={{0,28},{4,0},{8,4},{12,8},{16,12},{20,16},{24,20},{28,24},{1,29},{... | collective-permute-start | bytes 786440 | tf_op jit(solution)/shard_map/ppermute | solution.py:29
  75.9 17.5 %collective-permute-start.11 = (bf16[8,128,256]{2,1,0:T(8,128)(2,1)}, bf16[8,128,256]{2,1,0:T(8,128)(2,1)}, u32[]{:S(2)}, u32[]{:S(2)}) collective-permute-start(bf16[8,128,256]{2,1,0:T(8,128)(2,1)} %broadcast_select_fusion.2), channel_id=1, source_target_pairs={{0,96},{32,0},{64,32},{96,64},{1,97},{33,1},{65,33},{97,65},{2,98}... | collective-permute-start | bytes 1572872 | tf_op jit(solution)/shard_map/ppermute | solution.py:66
  82.0 11.7 %collective-permute-start.13 = (bf16[8,128,256]{2,1,0:T(8,128)(2,1)}, bf16[8,128,256]{2,1,0:T(8,128)(2,1)}, u32[]{:S(2)}, u32[]{:S(2)}) collective-permute-start(bf16[8,128,256]{2,1,0:T(8,128)(2,1)} %broadcast_select_fusion.1), channel_id=1, source_target_pairs={{0,64},{32,96},{64,0},{96,32},{1,65},{33,97},{65,1},{97,33},{2,66}... | collective-permute-start | bytes 1572872 | tf_op jit(solution)/shard_map/ppermute | solution.py:66
  88.5 14.3 %collective-permute-start.15 = (bf16[8,128,256]{2,1,0:T(8,128)(2,1)}, bf16[8,128,256]{2,1,0:T(8,128)(2,1)}, u32[]{:S(2)}, u32[]{:S(2)}) collective-permute-start(bf16[8,128,256]{2,1,0:T(8,128)(2,1)} %broadcast_select_fusion), channel_id=1, source_target_pairs={{0,32},{32,64},{64,96},{96,0},{1,33},{33,65},{65,97},{97,1},{2,34}... | collective-permute-start | bytes 1572872 | tf_op jit(solution)/shard_map/ppermute | solution.py:66
  106.3 12.4 %collective-permute-start.16 = (f32[2,32768]{1,0:T(2,128)S(1)}, f32[2,32768]{1,0:T(2,128)S(1)}, u32[]{:S(2)}, u32[]{:S(2)}) collective-permute-start(f32[2,32768]{1,0:T(2,128)S(1)} %bitcast.52), channel_id=1, source_target_pairs={{0,1},{1,0},{2,3},{3,2},{4,5},{5,4},{6,7},{7,6},{8,9},{9,8},{10,11... | collective-permute-start | bytes 786440 | tf_op jit(solution)/shard_map/ppermute | solution.py:116
  119.3 6.6 %collective-permute-start.17 = (f32[32768]{0:T(1024)S(1)}, f32[32768]{0:T(1024)S(1)}, u32[]{:S(2)}, u32[]{:S(2)}) collective-permute-start(f32[32768]{0:T(1024)S(1)} %bitcast.61), channel_id=1, source_target_pairs={{0,2},{2,0},{1,3},{3,1},{4,6},{6,4},{5,7},{7,5},{8,10},{10,8},{9,1... | collective-permute-start | bytes 393224 | tf_op jit(solution)/shard_map/ppermute | solution.py:120
  127.2 4.1 %collective-permute-start.18 = (f32[33792]{0:T(1024)S(1)}, f32[33792]{0:T(1024)S(1)}, u32[]{:S(2)}, u32[]{:S(2)}) collective-permute-start(f32[33792]{0:T(1024)S(1)} %select_n.294), channel_id=1, source_target_pairs={{0,1},{1,0},{2,3},{3,2},{4,5},{5,4},{6,7},{7,6},{8,9},{9,8},{10,11... | collective-permute-start | bytes 405512 | tf_op jit(solution)/shard_map/ppermute | solution.py:87
  131.3 5.1 %collective-permute-start.19 = (f32[16896]{0:T(1024)S(1)}, f32[16896]{0:T(1024)S(1)}, u32[]{:S(2)}, u32[]{:S(2)}) collective-permute-start(f32[16896]{0:T(1024)S(1)} %slice_select_fusion.2), channel_id=1, source_target_pairs={{0,2},{2,0},{1,3},{3,1},{4,6},{6,4},{5,7},{7,5},{8,10},{10,8},{9,1... | collective-permute-start | bytes 202760 | tf_op jit(solution)/shard_map/ppermute | solution.py:87
  136.4 9.0 %collective-permute-start.20 = (f32[16896]{0:T(1024)S(1)}, f32[16896]{0:T(1024)S(1)}, u32[]{:S(2)}, u32[]{:S(2)}) collective-permute-start(f32[16896]{0:T(1024)S(1)} %select_add_fusion), channel_id=1, source_target_pairs={{0,16},{4,20},{8,24},{12,28},{16,0},{20,4},{24,8},{28,12},{1,17},{... | collective-permute-start | bytes 202760 | tf_op jit(solution)/shard_map/ppermute | solution.py:105
  145.4 6.0 %collective-permute-start.21 = (f32[16896]{0:T(1024)S(1)}, f32[16896]{0:T(1024)S(1)}, u32[]{:S(2)}, u32[]{:S(2)}) collective-permute-start(f32[16896]{0:T(1024)S(1)} %add.250), channel_id=1, source_target_pairs={{0,8},{4,12},{8,0},{12,4},{16,24},{20,28},{24,16},{28,20},{1,9},{5... | collective-permute-start | bytes 202760 | tf_op jit(solution)/shard_map/ppermute | solution.py:105
  151.3 5.8 %collective-permute-start.22 = (f32[16896]{0:T(1024)S(1)}, f32[16896]{0:T(1024)S(1)}, u32[]{:S(2)}, u32[]{:S(2)}) collective-permute-start(f32[16896]{0:T(1024)S(1)} %add.251), channel_id=1, source_target_pairs={{0,4},{4,0},{8,12},{12,8},{16,20},{20,16},{24,28},{28,24},{1,5},{5... | collective-permute-start | bytes 202760 | tf_op jit(solution)/shard_map/ppermute | solution.py:105
  157.2 6.6 %collective-permute-start.23 = (f32[16896]{0:T(1024)S(1)}, f32[16896]{0:T(1024)S(1)}, u32[]{:S(2)}, u32[]{:S(2)}) collective-permute-start(f32[16896]{0:T(1024)S(1)} %add.252), channel_id=1, source_target_pairs={{0,64},{32,96},{64,0},{96,32},{1,65},{33,97},{65,1},{97,33},{2,66}... | collective-permute-start | bytes 202760 | tf_op jit(solution)/shard_map/ppermute | solution.py:105
  163.8 5.3 %collective-permute-start.24 = (f32[16896]{0:T(1024)S(1)}, f32[16896]{0:T(1024)S(1)}, u32[]{:S(2)}, u32[]{:S(2)}) collective-permute-start(f32[16896]{0:T(1024)S(1)} %add.253), channel_id=1, source_target_pairs={{0,32},{32,0},{64,96},{96,64},{1,33},{33,1},{65,97},{97,65},{2,34}... | collective-permute-start | bytes 202760 | tf_op jit(solution)/shard_map/ppermute | solution.py:105
  169.1 11.1 %collective-permute-start.25 = (f32[16896]{0:T(1024)S(1)}, f32[16896]{0:T(1024)S(1)}, u32[]{:S(2)}, u32[]{:S(2)}) collective-permute-start(f32[16896]{0:T(1024)S(1)} %add.254), channel_id=1, source_target_pairs={{0,256},{128,384},{256,0},{384,128},{1,257},{129,385},{257,1},{385... | collective-permute-start | bytes 202760 | tf_op jit(solution)/shard_map/ppermute | solution.py:105
  180.2 8.2 %collective-permute-start.26 = (f32[16896]{0:T(1024)S(1)}, f32[16896]{0:T(1024)S(1)}, u32[]{:S(2)}, u32[]{:S(2)}) collective-permute-start(f32[16896]{0:T(1024)S(1)} %add.255), channel_id=1, source_target_pairs={{0,128},{128,0},{256,384},{384,256},{1,129},{129,1},{257,385},{385... | collective-permute-start | bytes 202760 | tf_op jit(solution)/shard_map/ppermute | solution.py:105
  188.4 5.3 %collective-permute-start.27 = (f32[16896]{0:T(1024)S(1)}, f32[16896]{0:T(1024)S(1)}, u32[]{:S(2)}, u32[]{:S(2)}) collective-permute-start(f32[16896]{0:T(1024)S(1)} %add.256), channel_id=1, source_target_pairs={{0,2},{2,0},{1,3},{3,1},{4,6},{6,4},{5,7},{7,5},{8,10},{10,8},{9,1... | collective-permute-start | bytes 202760 | tf_op jit(solution)/shard_map/ppermute | solution.py:94
  193.8 9.1 %collective-permute-start.28 = (f32[33792]{0:T(1024)S(1)}, f32[33792]{0:T(1024)S(1)}, u32[]{:S(2)}, u32[]{:S(2)}) collective-permute-start(f32[33792]{0:T(1024)S(1)} %maximum_select_fusion.1), channel_id=1, source_target_pairs={{0,1},{1,0},{2,3},{3,2},{4,5},{5,4},{6,7},{7,6},{8,9},{9,8},{10,11... | collective-permute-start | bytes 405512 | tf_op jit(solution)/shard_map/ppermute | solution.py:94
  (13 other events, 231.5 us)

commit v7 on v6

--- a/solution.py
+++ b/solution.py
@@ -59,12 +59,14 @@
             flat = flat * size + (coords[a] - lax.axis_index(a) + size // 2) % size
         return flat
 
-    picked = jnp.take(plane, in_plane(cols), axis=0)
-    source = (lax.axis_index(across) - row_coords(cols)[across]) % n_across
+    copies = [jnp.take(plane, in_plane(cols), axis=0)]
     for s in range(1, n_across):
         sent = jnp.take(plane, in_plane(peer_cols[s]), axis=0)
-        got = lax.ppermute(sent, across, [(i, (i + s) % n_across) for i in range(n_across)])
-        picked = jnp.where((source == s)[:, None, None], got, picked)
+        copies.append(lax.ppermute(sent, across, [(i, (i + s) % n_across) for i in range(n_across)]))
+    source = (lax.axis_index(across) - row_coords(cols)[across]) % n_across
+    picked = copies[0]
+    for s in range(1, n_across):
+        picked = jnp.where((source == s)[:, None, None], copies[s], picked)
     return picked
 
 
@@ -152,7 +154,8 @@
     packed = jnp.concatenate(
         [weight_term, bias_term[None, :], jnp.zeros((pad_rows, feature_width), jnp.float32)], axis=0
     )
-    packed = reduce_all(packed)
+    half = feature_width // 2
+    packed = jnp.concatenate([reduce_all(packed[:, :half]), reduce_all(packed[:, half:])], axis=1)
     weight_grad = packed[:feature_width]
     bias_grad = packed[feature_width]
     return (layer_out, weight_grad, bias_grad)

time: 206 us -> 216 us (1.049)
  starting transfers between devices: 113 us -> 146 us
  waiting for transfers between devices: 64 us -> 40.6 us
    ppermute x7 -> x14, starting transfers between devices: 27.3 us -> 48.1 us  [reduce_all(): flat = flat + lax.ppermute(flat, a, perm)]
    ppermute x7 -> x14, waiting for transfers between devices: 24.6 us -> 6.09 us  [reduce_all(): flat = flat + lax.ppermute(flat, a, perm)]
    ppermute x2 -> x4, starting transfers between devices: 10 us -> 18.1 us  [all_gather_flat(): other = lax.ppermute(flat, a, perm)]
    ppermute x2 -> x4, starting transfers between devices: 6.35 us -> 10.3 us  [reduce_scatter_flat(): flat = keep + lax.ppermute(send, a, perm)]
    ppermute x2 -> x4, waiting for transfers between devices: 4.29 us -> 1.05 us  [all_gather_flat(): other = lax.ppermute(flat, a, perm)]
  transfers between devices with their start and end apart: 29 -> 40, of which waited for: 22 -> 18; matrix products, arithmetic and copies ran while one was open for 7% -> 7% of each run, Pallas kernels for 0% -> 0%
where the time goes in v7:
time: 216 us; the launch traced here: 214 us
  starting transfers between devices  146 us (68%)
  waiting for transfers between devices  40.6 us (19%)
  other arithmetic  12.9 us (6%)
  local copies, waits for them, and re-layouts  9.48 us (4%)
  matrix products  3.4 us (2%)
    ppermute x14, starting transfers between devices, reduce_all(): flat = flat + lax.ppermute(flat, a, perm)  48.1 us
    ppermute x6, starting transfers between devices, ring_gather(): left = lax.ppermute(left, axis, fwd)  19.1 us
    ppermute x4, starting transfers between devices, ring_gather(): right = lax.ppermute(right, axis, bwd)  18.2 us
    ppermute x4, starting transfers between devices, all_gather_flat(): other = lax.ppermute(flat, a, perm)  18.1 us
    ppermute x6, waiting for transfers between devices, ring_gather(): left = lax.ppermute(left, axis, fwd)  12.8 us
    ppermute x1, starting transfers between devices, reduce_over_rep(): pairs = keep + lax.ppermute(send, 'core', [(0, 1), (1, 0)])  11.2 us
    ppermute x4, starting transfers between devices, reduce_scatter_flat(): flat = keep + lax.ppermute(send, a, perm)  10.3 us
    ppermute x3, starting transfers between devices, plane_blocks(): lax.ppermute(cols, across, [(i, (i - s) % n_across) for i in range(n_acro...  9.92 us
  transfers between devices with their start and end apart: 40, of which 18 were waited for; matrix products, arithmetic and copies ran while one was open for 7% of the time, Pallas kernels for 0%

profile of v7, /device:TPU:1, one launch (start us, length us, event | category | flops | bytes accessed | tf_op | source)
XLA Modules:
  0.0 214.1 jit_solution(129225331225643181)
XLA Ops:
  0.7 5.2 %collective-permute-start = (bf16[128,256]{1,0:T(8,128)(2,1)}, bf16[128,256]{1,0:T(8,128)(2,1)S(1)}, u32[]{:S(2)}, u32[]{:S(2)}) collective-permute-start(bf16[128,256]{1,0:T(8,128)(2,1)} %param.10), channel_id=1, source_target_pairs={{0,128},{128,256},{256,384},{384,0},{1,129},{129,257},{257,385},{3... | collective-permute-start | bytes 196616 | tf_op jit(solution)/shard_map/ppermute | solution.py:26
  5.8 3.6 %collective-permute-start.2 = (bf16[128,256]{1,0:T(8,128)(2,1)}, bf16[128,256]{1,0:T(8,128)(2,1)S(1)}, u32[]{:S(2)}, u32[]{:S(2)}) collective-permute-start(bf16[128,256]{1,0:T(8,128)(2,1)} %param.10), channel_id=1, source_target_pairs={{0,384},{128,0},{256,128},{384,256},{1,385},{129,1},{257,129},{385... | collective-permute-start | bytes 196616 | tf_op jit(solution)/shard_map/ppermute | solution.py:29
  9.4 4.2 %collective-permute-start.1 = (bf16[128,256]{1,0:T(8,128)(2,1)S(1)}, bf16[128,256]{1,0:T(8,128)(2,1)S(1)}, u32[]{:S(2)}, u32[]{:S(2)}) collective-permute-start(bf16[128,256]{1,0:T(8,128)(2,1)S(1)} %collective-permute-done), channel_id=1, source_target_pairs={{0,128},{128,256},{256,384},{384,0},{1,129},{129,257},{257,385},{3... | collective-permute-start | bytes 196616 | tf_op jit(solution)/shard_map/ppermute | solution.py:26
  17.5 4.0 %collective-permute-start.3 = (bf16[4,128,256]{2,1,0:T(8,128)(2,1)S(1)}, bf16[4,128,256]{2,1,0:T(8,128)(2,1)S(1)}, u32[]{:S(2)}, u32[]{:S(2)}) collective-permute-start(bf16[4,128,256]{2,1,0:T(8,128)(2,1)S(1)} %pad_maximum_fusion), channel_id=1, source_target_pairs={{0,4},{4,8},{8,12},{12,16},{16,20},{20,24},{24,28},{28,0},{1,5},{5... | collective-permute-start | bytes 786440 | tf_op jit(solution)/shard_map/ppermute | solution.py:26
  21.5 10.4 %collective-permute-done.3 = bf16[4,128,256]{2,1,0:T(8,128)(2,1)S(1)} collective-permute-done((bf16[4,128,256]{2,1,0:T(8,128)(2,1)S(1)}, bf16[4,128,256]{2,1,0:T(8,128)(2,1)S(1)}, u32[]{:S(2)}, u32[]{:S(2)}) %collective-permute-start.3) | collective-permute-done | bytes 262176 | tf_op jit(solution)/shard_map/ppermute | solution.py:26
  35.1 3.1 %collective-permute-start.10 = (s32[8]{0:T(128)S(1)}, s32[8]{0:T(128)S(1)}, u32[]{:S(2)}, u32[]{:S(2)}) collective-permute-start(s32[8]{0:T(128)S(1)} %get-tuple-element.9), channel_id=1, source_target_pairs={{0,32},{32,64},{64,96},{96,0},{1,33},{33,65},{65,97},{97,1},{2,34}... | collective-permute-start | bytes 104 | tf_op jit(solution)/shard_map/ppermute | solution.py:46
  38.2 3.4 %collective-permute-start.14 = (s32[8]{0:T(128)S(1)}, s32[8]{0:T(128)S(1)}, u32[]{:S(2)}, u32[]{:S(2)}) collective-permute-start(s32[8]{0:T(128)S(1)} %get-tuple-element.9), channel_id=1, source_target_pairs={{0,96},{32,0},{64,32},{96,64},{1,97},{33,1},{65,33},{97,65},{2,98}... | collective-permute-start | bytes 104 | tf_op jit(solution)/shard_map/ppermute | solution.py:46
  41.6 3.4 %collective-permute-start.12 = (s32[8]{0:T(128)S(1)}, s32[8]{0:T(128)S(1)}, u32[]{:S(2)}, u32[]{:S(2)}) collective-permute-start(s32[8]{0:T(128)S(1)} %get-tuple-element.9), channel_id=1, source_target_pairs={{0,64},{32,96},{64,0},{96,32},{1,65},{33,97},{65,1},{97,33},{2,66}... | collective-permute-start | bytes 104 | tf_op jit(solution)/shard_map/ppermute | solution.py:46
  46.4 4.6 %collective-permute-start.7 = (bf16[4,128,256]{2,1,0:T(8,128)(2,1)S(1)}, bf16[4,128,256]{2,1,0:T(8,128)(2,1)S(1)}, u32[]{:S(2)}, u32[]{:S(2)}) collective-permute-start(bf16[4,128,256]{2,1,0:T(8,128)(2,1)S(1)} %pad_maximum_fusion), channel_id=1, source_target_pairs={{0,28},{4,0},{8,4},{12,8},{16,12},{20,16},{24,20},{28,24},{1,29},{... | collective-permute-start | bytes 786440 | tf_op jit(solution)/shard_map/ppermute | solution.py:29
  54.2 5.0 %collective-permute-start.8 = (bf16[4,128,256]{2,1,0:T(8,128)(2,1)S(1)}, bf16[4,128,256]{2,1,0:T(8,128)(2,1)S(1)}, u32[]{:S(2)}, u32[]{:S(2)}) collective-permute-start(bf16[4,128,256]{2,1,0:T(8,128)(2,1)S(1)} %collective-permute-done.7), channel_id=1, source_target_pairs={{0,28},{4,0},{8,4},{12,8},{16,12},{20,16},{24,20},{28,24},{1,29},{... | collective-permute-start | bytes 786440 | tf_op jit(solution)/shard_map/ppermute | solution.py:29
  62.8 5.0 %collective-permute-start.9 = (bf16[4,128,256]{2,1,0:T(8,128)(2,1)S(1)}, bf16[4,128,256]{2,1,0:T(8,128)(2,1)S(1)}, u32[]{:S(2)}, u32[]{:S(2)}) collective-permute-start(bf16[4,128,256]{2,1,0:T(8,128)(2,1)S(1)} %collective-permute-done.8), channel_id=1, source_target_pairs={{0,28},{4,0},{8,4},{12,8},{16,12},{20,16},{24,20},{28,24},{1,29},{... | collective-permute-start | bytes 786440 | tf_op jit(solution)/shard_map/ppermute | solution.py:29
  69.4 3.2 %collective-permute-done.9 = bf16[4,128,256]{2,1,0:T(8,128)(2,1)S(1)} collective-permute-done((bf16[4,128,256]{2,1,0:T(8,128)(2,1)S(1)}, bf16[4,128,256]{2,1,0:T(8,128)(2,1)S(1)}, u32[]{:S(2)}, u32[]{:S(2)}) %collective-permute-start.9) | collective-permute-done | bytes 262176 | tf_op jit(solution)/shard_map/ppermute | solution.py:29
  76.0 2.8 %collective-permute-start.11 = (bf16[8,128,256]{2,1,0:T(8,128)(2,1)}, bf16[8,128,256]{2,1,0:T(8,128)(2,1)}, u32[]{:S(2)}, u32[]{:S(2)}) collective-permute-start(bf16[8,128,256]{2,1,0:T(8,128)(2,1)} %broadcast_select_fusion.2), channel_id=1, source_target_pairs={{0,96},{32,0},{64,32},{96,64},{1,97},{33,1},{65,33},{97,65},{2,98}... | collective-permute-start | bytes 1572872 | tf_op jit(solution)/shard_map/ppermute | solution.py:65
  82.1 3.1 %collective-permute-start.13 = (bf16[8,128,256]{2,1,0:T(8,128)(2,1)}, bf16[8,128,256]{2,1,0:T(8,128)(2,1)}, u32[]{:S(2)}, u32[]{:S(2)}) collective-permute-start(bf16[8,128,256]{2,1,0:T(8,128)(2,1)} %broadcast_select_fusion.1), channel_id=1, source_target_pairs={{0,64},{32,96},{64,0},{96,32},{1,65},{33,97},{65,1},{97,33},{2,66}... | collective-permute-start | bytes 1572872 | tf_op jit(solution)/shard_map/ppermute | solution.py:65
  93.8 9.0 %collective-permute-done.15 = bf16[8,128,256]{2,1,0:T(8,128)(2,1)} collective-permute-done((bf16[8,128,256]{2,1,0:T(8,128)(2,1)}, bf16[8,128,256]{2,1,0:T(8,128)(2,1)}, u32[]{:S(2)}, u32[]{:S(2)}) %collective-permute-start.15) | collective-permute-done | bytes 524320 | tf_op jit(solution)/shard_map/ppermute | solution.py:65
  106.4 11.2 %collective-permute-start.16 = (f32[2,32768]{1,0:T(2,128)S(1)}, f32[2,32768]{1,0:T(2,128)S(1)}, u32[]{:S(2)}, u32[]{:S(2)}) collective-permute-start(f32[2,32768]{1,0:T(2,128)S(1)} %bitcast.69), channel_id=1, source_target_pairs={{0,1},{1,0},{2,3},{3,2},{4,5},{5,4},{6,7},{7,6},{8,9},{9,8},{10,11... | collective-permute-start | bytes 786440 | tf_op jit(solution)/shard_map/ppermute | solution.py:118
  119.4 3.2 %collective-permute-start.17 = (f32[32768]{0:T(1024)S(1)}, f32[32768]{0:T(1024)S(1)}, u32[]{:S(2)}, u32[]{:S(2)}) collective-permute-start(f32[32768]{0:T(1024)S(1)} %bitcast.80), channel_id=1, source_target_pairs={{0,2},{2,0},{1,3},{3,1},{4,6},{6,4},{5,7},{7,5},{8,10},{10,8},{9,1... | collective-permute-start | bytes 393224 | tf_op jit(solution)/shard_map/ppermute | solution.py:122
  122.7 3.3 %collective-permute-done.17 = f32[32768]{0:T(1024)S(1)} collective-permute-done((f32[32768]{0:T(1024)S(1)}, f32[32768]{0:T(1024)S(1)}, u32[]{:S(2)}, u32[]{:S(2)}) %collective-permute-start.17) | collective-permute-done | bytes 131104 | tf_op jit(solution)/shard_map/ppermute | solution.py:122
  127.3 3.1 %collective-permute-start.29 = (f32[16896]{0:T(1024)S(1)}, f32[16896]{0:T(1024)S(1)}, u32[]{:S(2)}, u32[]{:S(2)}) collective-permute-start(f32[16896]{0:T(1024)S(1)} %get-tuple-element.20), channel_id=1, source_target_pairs={{0,1},{1,0},{2,3},{3,2},{4,5},{5,4},{6,7},{7,6},{8,9},{9,8},{10,11... | collective-permute-start | bytes 202760 | tf_op jit(solution)/shard_map/ppermute | solution.py:89
  133.6 3.2 %collective-permute-start.19 = (f32[8448]{0:T(1024)S(1)}, f32[8448]{0:T(1024)S(1)}, u32[]{:S(2)}, u32[]{:S(2)}) collective-permute-start(f32[8448]{0:T(1024)S(1)} %slice_select_fusion.1), channel_id=1, source_target_pairs={{0,2},{2,0},{1,3},{3,1},{4,6},{6,4},{5,7},{7,5},{8,10},{10,8},{9,1... | collective-permute-start | bytes 101384 | tf_op jit(solution)/shard_map/ppermute | solution.py:89
  139.0 5.1 %collective-permute-start.20 = (f32[8448]{0:T(1024)S(1)}, f32[8448]{0:T(1024)S(1)}, u32[]{:S(2)}, u32[]{:S(2)}) collective-permute-start(f32[8448]{0:T(1024)S(1)} %select_add_fusion.1), channel_id=1, source_target_pairs={{0,16},{4,20},{8,24},{12,28},{16,0},{20,4},{24,8},{28,12},{1,17},{... | collective-permute-start | bytes 101384 | tf_op jit(solution)/shard_map/ppermute | solution.py:107
  144.1 4.1 %collective-permute-start.31 = (f32[8448]{0:T(1024)S(1)}, f32[8448]{0:T(1024)S(1)}, u32[]{:S(2)}, u32[]{:S(2)}) collective-permute-start(f32[8448]{0:T(1024)S(1)} %select_add_fusion), channel_id=1, source_target_pairs={{0,16},{4,20},{8,24},{12,28},{16,0},{20,4},{24,8},{28,12},{1,17},{... | collective-permute-start | bytes 101384 | tf_op jit(solution)/shard_map/ppermute | solution.py:107
  148.2 3.2 %collective-permute-start.21 = (f32[8448]{0:T(1024)S(1)}, f32[8448]{0:T(1024)S(1)}, u32[]{:S(2)}, u32[]{:S(2)}) collective-permute-start(f32[8448]{0:T(1024)S(1)} %add.277), channel_id=1, source_target_pairs={{0,8},{4,12},{8,0},{12,4},{16,24},{20,28},{24,16},{28,20},{1,9},{5... | collective-permute-start | bytes 101384 | tf_op jit(solution)/shard_map/ppermute | solution.py:107
  155.3 4.6 %collective-permute-start.22 = (f32[8448]{0:T(1024)S(1)}, f32[8448]{0:T(1024)S(1)}, u32[]{:S(2)}, u32[]{:S(2)}) collective-permute-start(f32[8448]{0:T(1024)S(1)} %add.278), channel_id=1, source_target_pairs={{0,4},{4,0},{8,12},{12,8},{16,20},{20,16},{24,28},{28,24},{1,5},{5... | collective-permute-start | bytes 101384 | tf_op jit(solution)/shard_map/ppermute | solution.py:107
  161.9 2.6 %collective-permute-start.23 = (f32[8448]{0:T(1024)S(1)}, f32[8448]{0:T(1024)S(1)}, u32[]{:S(2)}, u32[]{:S(2)}) collective-permute-start(f32[8448]{0:T(1024)S(1)} %add.279), channel_id=1, source_target_pairs={{0,64},{32,96},{64,0},{96,32},{1,65},{33,97},{65,1},{97,33},{2,66}... | collective-permute-start | bytes 101384 | tf_op jit(solution)/shard_map/ppermute | solution.py:107
  164.6 4.1 %collective-permute-start.34 = (f32[8448]{0:T(1024)S(1)}, f32[8448]{0:T(1024)S(1)}, u32[]{:S(2)}, u32[]{:S(2)}) collective-permute-start(f32[8448]{0:T(1024)S(1)} %add.288), channel_id=1, source_target_pairs={{0,64},{32,96},{64,0},{96,32},{1,65},{33,97},{65,1},{97,33},{2,66}... | collective-permute-start | bytes 101384 | tf_op jit(solution)/shard_map/ppermute | solution.py:107
  170.8 3.2 %collective-permute-start.35 = (f32[8448]{0:T(1024)S(1)}, f32[8448]{0:T(1024)S(1)}, u32[]{:S(2)}, u32[]{:S(2)}) collective-permute-start(f32[8448]{0:T(1024)S(1)} %add.289), channel_id=1, source_target_pairs={{0,32},{32,0},{64,96},{96,64},{1,33},{33,1},{65,97},{97,65},{2,34}... | collective-permute-start | bytes 101384 | tf_op jit(solution)/shard_map/ppermute | solution.py:107
  174.1 8.6 %collective-permute-start.25 = (f32[8448]{0:T(1024)S(1)}, f32[8448]{0:T(1024)S(1)}, u32[]{:S(2)}, u32[]{:S(2)}) collective-permute-start(f32[8448]{0:T(1024)S(1)} %add.281), channel_id=1, source_target_pairs={{0,256},{128,384},{256,0},{384,128},{1,257},{129,385},{257,1},{385... | collective-permute-start | bytes 101384 | tf_op jit(solution)/shard_map/ppermute | solution.py:107
  187.1 4.2 %collective-permute-done.36 = f32[8448]{0:T(1024)S(1)} collective-permute-done((f32[8448]{0:T(1024)S(1)}, f32[8448]{0:T(1024)S(1)}, u32[]{:S(2)}, u32[]{:S(2)}) %collective-permute-start.36) | collective-permute-done | bytes 33824 | tf_op jit(solution)/shard_map/ppermute | solution.py:107
  193.3 3.4 %collective-permute-start.27 = (f32[8448]{0:T(1024)S(1)}, f32[8448]{0:T(1024)S(1)}, u32[]{:S(2)}, u32[]{:S(2)}) collective-permute-start(f32[8448]{0:T(1024)S(1)} %add.283), channel_id=1, source_target_pairs={{0,2},{2,0},{1,3},{3,1},{4,6},{6,4},{5,7},{7,5},{8,10},{10,8},{9,1... | collective-permute-start | bytes 101384 | tf_op jit(solution)/shard_map/ppermute | solution.py:96
  196.9 3.9 %collective-permute-start.38 = (f32[8448]{0:T(1024)S(1)}, f32[8448]{0:T(1024)S(1)}, u32[]{:S(2)}, u32[]{:S(2)}) collective-permute-start(f32[8448]{0:T(1024)S(1)} %add.292), channel_id=1, source_target_pairs={{0,2},{2,0},{1,3},{3,1},{4,6},{6,4},{5,7},{7,5},{8,10},{10,8},{9,1... | collective-permute-start | bytes 101384 | tf_op jit(solution)/shard_map/ppermute | solution.py:96
  200.9 8.8 %collective-permute-start.28 = (f32[16896]{0:T(1024)S(1)}, f32[16896]{0:T(1024)S(1)}, u32[]{:S(2)}, u32[]{:S(2)}) collective-permute-start(f32[16896]{0:T(1024)S(1)} %maximum_select_fusion.2), channel_id=1, source_target_pairs={{0,1},{1,0},{2,3},{3,2},{4,5},{5,4},{6,7},{7,6},{8,9},{9,8},{10,11... | collective-permute-start | bytes 202760 | tf_op jit(solution)/shard_map/ppermute | solution.py:96
  (150 shorter events, 62.8 us)
Async XLA Ops:
  0.7 8.8 %collective-permute-start = (bf16[128,256]{1,0:T(8,128)(2,1)}, bf16[128,256]{1,0:T(8,128)(2,1)S(1)}, u32[]{:S(2)}, u32[]{:S(2)}) collective-permute-start(bf16[128,256]{1,0:T(8,128)(2,1)} %param.10), channel_id=1, source_target_pairs={{0,128},{128,256},{256,384},{384,0},{1,129},{129,257},{257,385},{3... | collective-permute-start | bytes 196616 | tf_op jit(solution)/shard_map/ppermute | solution.py:26
  5.8 8.7 %collective-permute-start.2 = (bf16[128,256]{1,0:T(8,128)(2,1)}, bf16[128,256]{1,0:T(8,128)(2,1)S(1)}, u32[]{:S(2)}, u32[]{:S(2)}) collective-permute-start(bf16[128,256]{1,0:T(8,128)(2,1)} %param.10), channel_id=1, source_target_pairs={{0,384},{128,0},{256,128},{384,256},{1,385},{129,1},{257,129},{385... | collective-permute-start | bytes 196616 | tf_op jit(solution)/shard_map/ppermute | solution.py:29
  9.4 7.1 %collective-permute-start.1 = (bf16[128,256]{1,0:T(8,128)(2,1)S(1)}, bf16[128,256]{1,0:T(8,128)(2,1)S(1)}, u32[]{:S(2)}, u32[]{:S(2)}) collective-permute-start(bf16[128,256]{1,0:T(8,128)(2,1)S(1)} %collective-permute-done), channel_id=1, source_target_pairs={{0,128},{128,256},{256,384},{384,0},{1,129},{129,257},{257,385},{3... | collective-permute-start | bytes 196616 | tf_op jit(solution)/shard_map/ppermute | solution.py:26
  17.5 14.4 %collective-permute-start.3 = (bf16[4,128,256]{2,1,0:T(8,128)(2,1)S(1)}, bf16[4,128,256]{2,1,0:T(8,128)(2,1)S(1)}, u32[]{:S(2)}, u32[]{:S(2)}) collective-permute-start(bf16[4,128,256]{2,1,0:T(8,128)(2,1)S(1)} %pad_maximum_fusion), channel_id=1, source_target_pairs={{0,4},{4,8},{8,12},{12,16},{16,20},{20,24},{24,28},{28,0},{1,5},{5... | collective-permute-start | bytes 786440 | tf_op jit(solution)/shard_map/ppermute | solution.py:26
  31.9 19.1 %collective-permute-start.4 = (bf16[4,128,256]{2,1,0:T(8,128)(2,1)S(1)}, bf16[4,128,256]{2,1,0:T(8,128)(2,1)S(1)}, u32[]{:S(2)}, u32[]{:S(2)}) collective-permute-start(bf16[4,128,256]{2,1,0:T(8,128)(2,1)S(1)} %collective-permute-done.3), channel_id=1, source_target_pairs={{0,4},{4,8},{8,12},{12,16},{16,20},{20,24},{24,28},{28,0},{1,5},{5... | collective-permute-start | bytes 786440 | tf_op jit(solution)/shard_map/ppermute | solution.py:26
  35.1 17.8 %collective-permute-start.10 = (s32[8]{0:T(128)S(1)}, s32[8]{0:T(128)S(1)}, u32[]{:S(2)}, u32[]{:S(2)}) collective-permute-start(s32[8]{0:T(128)S(1)} %get-tuple-element.9), channel_id=1, source_target_pairs={{0,32},{32,64},{64,96},{96,0},{1,33},{33,65},{65,97},{97,1},{2,34}... | collective-permute-start | bytes 104 | tf_op jit(solution)/shard_map/ppermute | solution.py:46
  38.2 15.3 %collective-permute-start.14 = (s32[8]{0:T(128)S(1)}, s32[8]{0:T(128)S(1)}, u32[]{:S(2)}, u32[]{:S(2)}) collective-permute-start(s32[8]{0:T(128)S(1)} %get-tuple-element.9), channel_id=1, source_target_pairs={{0,96},{32,0},{64,32},{96,64},{1,97},{33,1},{65,33},{97,65},{2,98}... | collective-permute-start | bytes 104 | tf_op jit(solution)/shard_map/ppermute | solution.py:46
  41.6 19.6 %collective-permute-start.12 = (s32[8]{0:T(128)S(1)}, s32[8]{0:T(128)S(1)}, u32[]{:S(2)}, u32[]{:S(2)}) collective-permute-start(s32[8]{0:T(128)S(1)} %get-tuple-element.9), channel_id=1, source_target_pairs={{0,64},{32,96},{64,0},{96,32},{1,65},{33,97},{65,1},{97,33},{2,66}... | collective-permute-start | bytes 104 | tf_op jit(solution)/shard_map/ppermute | solution.py:46
  46.4 7.9 %collective-permute-start.7 = (bf16[4,128,256]{2,1,0:T(8,128)(2,1)S(1)}, bf16[4,128,256]{2,1,0:T(8,128)(2,1)S(1)}, u32[]{:S(2)}, u32[]{:S(2)}) collective-permute-start(bf16[4,128,256]{2,1,0:T(8,128)(2,1)S(1)} %pad_maximum_fusion), channel_id=1, source_target_pairs={{0,28},{4,0},{8,4},{12,8},{16,12},{20,16},{24,20},{28,24},{1,29},{... | collective-permute-start | bytes 786440 | tf_op jit(solution)/shard_map/ppermute | solution.py:29
  51.0 8.3 %collective-permute-start.5 = (bf16[4,128,256]{2,1,0:T(8,128)(2,1)S(1)}, bf16[4,128,256]{2,1,0:T(8,128)(2,1)S(1)}, u32[]{:S(2)}, u32[]{:S(2)}) collective-permute-start(bf16[4,128,256]{2,1,0:T(8,128)(2,1)S(1)} %collective-permute-done.4), channel_id=1, source_target_pairs={{0,4},{4,8},{8,12},{12,16},{16,20},{20,24},{24,28},{28,0},{1,5},{5... | collective-permute-start | bytes 786440 | tf_op jit(solution)/shard_map/ppermute | solution.py:26
  54.2 8.6 %collective-permute-start.8 = (bf16[4,128,256]{2,1,0:T(8,128)(2,1)S(1)}, bf16[4,128,256]{2,1,0:T(8,128)(2,1)S(1)}, u32[]{:S(2)}, u32[]{:S(2)}) collective-permute-start(bf16[4,128,256]{2,1,0:T(8,128)(2,1)S(1)} %collective-permute-done.7), channel_id=1, source_target_pairs={{0,28},{4,0},{8,4},{12,8},{16,12},{20,16},{24,20},{28,24},{1,29},{... | collective-permute-start | bytes 786440 | tf_op jit(solution)/shard_map/ppermute | solution.py:29
  59.3 8.9 %collective-permute-start.6 = (bf16[4,128,256]{2,1,0:T(8,128)(2,1)S(1)}, bf16[4,128,256]{2,1,0:T(8,128)(2,1)S(1)}, u32[]{:S(2)}, u32[]{:S(2)}) collective-permute-start(bf16[4,128,256]{2,1,0:T(8,128)(2,1)S(1)} %collective-permute-done.5), channel_id=1, source_target_pairs={{0,4},{4,8},{8,12},{12,16},{16,20},{20,24},{24,28},{28,0},{1,5},{5... | collective-permute-start | bytes 786440 | tf_op jit(solution)/shard_map/ppermute | solution.py:26
  62.8 9.8 %collective-permute-start.9 = (bf16[4,128,256]{2,1,0:T(8,128)(2,1)S(1)}, bf16[4,128,256]{2,1,0:T(8,128)(2,1)S(1)}, u32[]{:S(2)}, u32[]{:S(2)}) collective-permute-start(bf16[4,128,256]{2,1,0:T(8,128)(2,1)S(1)} %collective-permute-done.8), channel_id=1, source_target_pairs={{0,28},{4,0},{8,4},{12,8},{16,12},{20,16},{24,20},{28,24},{1,29},{... | collective-permute-start | bytes 786440 | tf_op jit(solution)/shard_map/ppermute | solution.py:29
  76.0 17.6 %collective-permute-start.11 = (bf16[8,128,256]{2,1,0:T(8,128)(2,1)}, bf16[8,128,256]{2,1,0:T(8,128)(2,1)}, u32[]{:S(2)}, u32[]{:S(2)}) collective-permute-start(bf16[8,128,256]{2,1,0:T(8,128)(2,1)} %broadcast_select_fusion.2), channel_id=1, source_target_pairs={{0,96},{32,0},{64,32},{96,64},{1,97},{33,1},{65,33},{97,65},{2,98}... | collective-permute-start | bytes 1572872 | tf_op jit(solution)/shard_map/ppermute | solution.py:65
  82.1 11.7 %collective-permute-start.13 = (bf16[8,128,256]{2,1,0:T(8,128)(2,1)}, bf16[8,128,256]{2,1,0:T(8,128)(2,1)}, u32[]{:S(2)}, u32[]{:S(2)}) collective-permute-start(bf16[8,128,256]{2,1,0:T(8,128)(2,1)} %broadcast_select_fusion.1), channel_id=1, source_target_pairs={{0,64},{32,96},{64,0},{96,32},{1,65},{33,97},{65,1},{97,33},{2,66}... | collective-permute-start | bytes 1572872 | tf_op jit(solution)/shard_map/ppermute | solution.py:65
  88.6 14.3 %collective-permute-start.15 = (bf16[8,128,256]{2,1,0:T(8,128)(2,1)}, bf16[8,128,256]{2,1,0:T(8,128)(2,1)}, u32[]{:S(2)}, u32[]{:S(2)}) collective-permute-start(bf16[8,128,256]{2,1,0:T(8,128)(2,1)} %broadcast_select_fusion), channel_id=1, source_target_pairs={{0,32},{32,64},{64,96},{96,0},{1,33},{33,65},{65,97},{97,1},{2,34}... | collective-permute-start | bytes 1572872 | tf_op jit(solution)/shard_map/ppermute | solution.py:65
  106.4 12.4 %collective-permute-start.16 = (f32[2,32768]{1,0:T(2,128)S(1)}, f32[2,32768]{1,0:T(2,128)S(1)}, u32[]{:S(2)}, u32[]{:S(2)}) collective-permute-start(f32[2,32768]{1,0:T(2,128)S(1)} %bitcast.69), channel_id=1, source_target_pairs={{0,1},{1,0},{2,3},{3,2},{4,5},{5,4},{6,7},{7,6},{8,9},{9,8},{10,11... | collective-permute-start | bytes 786440 | tf_op jit(solution)/shard_map/ppermute | solution.py:118
  119.4 6.6 %collective-permute-start.17 = (f32[32768]{0:T(1024)S(1)}, f32[32768]{0:T(1024)S(1)}, u32[]{:S(2)}, u32[]{:S(2)}) collective-permute-start(f32[32768]{0:T(1024)S(1)} %bitcast.80), channel_id=1, source_target_pairs={{0,2},{2,0},{1,3},{3,1},{4,6},{6,4},{5,7},{7,5},{8,10},{10,8},{9,1... | collective-permute-start | bytes 393224 | tf_op jit(solution)/shard_map/ppermute | solution.py:122
  136.8 7.2 %collective-permute-start.30 = (f32[8448]{0:T(1024)S(1)}, f32[8448]{0:T(1024)S(1)}, u32[]{:S(2)}, u32[]{:S(2)}) collective-permute-start(f32[8448]{0:T(1024)S(1)} %slice_select_fusion), channel_id=1, source_target_pairs={{0,2},{2,0},{1,3},{3,1},{4,6},{6,4},{5,7},{7,5},{8,10},{10,8},{9,1... | collective-permute-start | bytes 101384 | tf_op jit(solution)/shard_map/ppermute | solution.py:89
  139.0 9.2 %collective-permute-start.20 = (f32[8448]{0:T(1024)S(1)}, f32[8448]{0:T(1024)S(1)}, u32[]{:S(2)}, u32[]{:S(2)}) collective-permute-start(f32[8448]{0:T(1024)S(1)} %select_add_fusion.1), channel_id=1, source_target_pairs={{0,16},{4,20},{8,24},{12,28},{16,0},{20,4},{24,8},{28,12},{1,17},{... | collective-permute-start | bytes 101384 | tf_op jit(solution)/shard_map/ppermute | solution.py:107
  144.1 8.6 %collective-permute-start.31 = (f32[8448]{0:T(1024)S(1)}, f32[8448]{0:T(1024)S(1)}, u32[]{:S(2)}, u32[]{:S(2)}) collective-permute-start(f32[8448]{0:T(1024)S(1)} %select_add_fusion), channel_id=1, source_target_pairs={{0,16},{4,20},{8,24},{12,28},{16,0},{20,4},{24,8},{28,12},{1,17},{... | collective-permute-start | bytes 101384 | tf_op jit(solution)/shard_map/ppermute | solution.py:107
  148.2 7.1 %collective-permute-start.21 = (f32[8448]{0:T(1024)S(1)}, f32[8448]{0:T(1024)S(1)}, u32[]{:S(2)}, u32[]{:S(2)}) collective-permute-start(f32[8448]{0:T(1024)S(1)} %add.277), channel_id=1, source_target_pairs={{0,8},{4,12},{8,0},{12,4},{16,24},{20,28},{24,16},{28,20},{1,9},{5... | collective-permute-start | bytes 101384 | tf_op jit(solution)/shard_map/ppermute | solution.py:107
  152.7 7.1 %collective-permute-start.32 = (f32[8448]{0:T(1024)S(1)}, f32[8448]{0:T(1024)S(1)}, u32[]{:S(2)}, u32[]{:S(2)}) collective-permute-start(f32[8448]{0:T(1024)S(1)} %add.286), channel_id=1, source_target_pairs={{0,8},{4,12},{8,0},{12,4},{16,24},{20,28},{24,16},{28,20},{1,9},{5... | collective-permute-start | bytes 101384 | tf_op jit(solution)/shard_map/ppermute | solution.py:107
  155.3 6.6 %collective-permute-start.22 = (f32[8448]{0:T(1024)S(1)}, f32[8448]{0:T(1024)S(1)}, u32[]{:S(2)}, u32[]{:S(2)}) collective-permute-start(f32[8448]{0:T(1024)S(1)} %add.278), channel_id=1, source_target_pairs={{0,4},{4,0},{8,12},{12,8},{16,20},{20,16},{24,28},{28,24},{1,5},{5... | collective-permute-start | bytes 101384 | tf_op jit(solution)/shard_map/ppermute | solution.py:107
  161.9 6.8 %collective-permute-start.23 = (f32[8448]{0:T(1024)S(1)}, f32[8448]{0:T(1024)S(1)}, u32[]{:S(2)}, u32[]{:S(2)}) collective-permute-start(f32[8448]{0:T(1024)S(1)} %add.279), channel_id=1, source_target_pairs={{0,64},{32,96},{64,0},{96,32},{1,65},{33,97},{65,1},{97,33},{2,66}... | collective-permute-start | bytes 101384 | tf_op jit(solution)/shard_map/ppermute | solution.py:107
  170.8 11.9 %collective-permute-start.35 = (f32[8448]{0:T(1024)S(1)}, f32[8448]{0:T(1024)S(1)}, u32[]{:S(2)}, u32[]{:S(2)}) collective-permute-start(f32[8448]{0:T(1024)S(1)} %add.289), channel_id=1, source_target_pairs={{0,32},{32,0},{64,96},{96,64},{1,33},{33,1},{65,97},{97,65},{2,34}... | collective-permute-start | bytes 101384 | tf_op jit(solution)/shard_map/ppermute | solution.py:107
  174.1 10.5 %collective-permute-start.25 = (f32[8448]{0:T(1024)S(1)}, f32[8448]{0:T(1024)S(1)}, u32[]{:S(2)}, u32[]{:S(2)}) collective-permute-start(f32[8448]{0:T(1024)S(1)} %add.281), channel_id=1, source_target_pairs={{0,256},{128,384},{256,0},{384,128},{1,257},{129,385},{257,1},{385... | collective-permute-start | bytes 101384 | tf_op jit(solution)/shard_map/ppermute | solution.py:107
  182.7 8.6 %collective-permute-start.36 = (f32[8448]{0:T(1024)S(1)}, f32[8448]{0:T(1024)S(1)}, u32[]{:S(2)}, u32[]{:S(2)}) collective-permute-start(f32[8448]{0:T(1024)S(1)} %add.290), channel_id=1, source_target_pairs={{0,256},{128,384},{256,0},{384,128},{1,257},{129,385},{257,1},{385... | collective-permute-start | bytes 101384 | tf_op jit(solution)/shard_map/ppermute | solution.py:107
  184.6 8.6 %collective-permute-start.26 = (f32[8448]{0:T(1024)S(1)}, f32[8448]{0:T(1024)S(1)}, u32[]{:S(2)}, u32[]{:S(2)}) collective-permute-start(f32[8448]{0:T(1024)S(1)} %add.282), channel_id=1, source_target_pairs={{0,128},{128,0},{256,384},{384,256},{1,129},{129,1},{257,385},{385... | collective-permute-start | bytes 101384 | tf_op jit(solution)/shard_map/ppermute | solution.py:107
  193.3 7.6 %collective-permute-start.27 = (f32[8448]{0:T(1024)S(1)}, f32[8448]{0:T(1024)S(1)}, u32[]{:S(2)}, u32[]{:S(2)}) collective-permute-start(f32[8448]{0:T(1024)S(1)} %add.283), channel_id=1, source_target_pairs={{0,2},{2,0},{1,3},{3,1},{4,6},{6,4},{5,7},{7,5},{8,10},{10,8},{9,1... | collective-permute-start | bytes 101384 | tf_op jit(solution)/shard_map/ppermute | solution.py:96
  196.9 12.7 %collective-permute-start.38 = (f32[8448]{0:T(1024)S(1)}, f32[8448]{0:T(1024)S(1)}, u32[]{:S(2)}, u32[]{:S(2)}) collective-permute-start(f32[8448]{0:T(1024)S(1)} %add.292), channel_id=1, source_target_pairs={{0,2},{2,0},{1,3},{3,1},{4,6},{6,4},{5,7},{7,5},{8,10},{10,8},{9,1... | collective-permute-start | bytes 101384 | tf_op jit(solution)/shard_map/ppermute | solution.py:96
  200.9 10.9 %collective-permute-start.28 = (f32[16896]{0:T(1024)S(1)}, f32[16896]{0:T(1024)S(1)}, u32[]{:S(2)}, u32[]{:S(2)}) collective-permute-start(f32[16896]{0:T(1024)S(1)} %maximum_select_fusion.2), channel_id=1, source_target_pairs={{0,1},{1,0},{2,3},{3,2},{4,5},{5,4},{6,7},{7,6},{8,9},{9,8},{10,11... | collective-permute-start | bytes 202760 | tf_op jit(solution)/shard_map/ppermute | solution.py:96
  (24 other events, 494.5 us)

commit v8 on v7

--- a/solution.py
+++ b/solution.py
@@ -59,9 +59,9 @@
             flat = flat * size + (coords[a] - lax.axis_index(a) + size // 2) % size
         return flat
 
-    copies = [jnp.take(plane, in_plane(cols), axis=0)]
+    copies = [jnp.take(plane, in_plane(cols), axis=0, mode="clip")]
     for s in range(1, n_across):
-        sent = jnp.take(plane, in_plane(peer_cols[s]), axis=0)
+        sent = jnp.take(plane, in_plane(peer_cols[s]), axis=0, mode="clip")
         copies.append(lax.ppermute(sent, across, [(i, (i + s) % n_across) for i in range(n_across)]))
     source = (lax.axis_index(across) - row_coords(cols)[across]) % n_across
     picked = copies[0]
@@ -154,8 +154,7 @@
     packed = jnp.concatenate(
         [weight_term, bias_term[None, :], jnp.zeros((pad_rows, feature_width), jnp.float32)], axis=0
     )
-    half = feature_width // 2
-    packed = jnp.concatenate([reduce_all(packed[:, :half]), reduce_all(packed[:, half:])], axis=1)
+    packed = reduce_all(packed)
     weight_grad = packed[:feature_width]
     bias_grad = packed[feature_width]
     return (layer_out, weight_grad, bias_grad)

time: 216 us -> 194 us (0.90)
  starting transfers between devices: 146 us -> 124 us
  other arithmetic: 12.9 us -> 6.25 us
  waiting for transfers between devices: 40.6 us -> 47.2 us
    ppermute x14 -> x7, starting transfers between devices: 48.1 us -> 32 us  [reduce_all(): flat = flat + lax.ppermute(flat, a, perm)]
    ppermute x14 -> x7, waiting for transfers between devices: 6.09 us -> 18.3 us  [reduce_all(): flat = flat + lax.ppermute(flat, a, perm)]
    ppermute x6, waiting for transfers between devices: 12.8 us -> 2.12 us  [ring_gather(): left = lax.ppermute(left, axis, fwd)]
    select_n x3 -> x0, other arithmetic: 5.87 us -> none  [plane_blocks(): sent = jnp.take(plane, in_plane(peer_cols[s]), axis=0)]
    ppermute x4 -> x2, starting transfers between devices: 18.1 us -> 14 us  [all_gather_flat(): other = lax.ppermute(flat, a, perm)]
    ppermute x4 -> x2, starting transfers between devices: 10.3 us -> 6.41 us  [reduce_scatter_flat(): flat = keep + lax.ppermute(send, a, perm)]
    ppermute x1, starting transfers between devices: 11.2 us -> 7.66 us  [reduce_over_rep(): pairs = keep + lax.ppermute(send, 'core', [(0, 1), (1, 0)])]
  transfers between devices with their start and end apart: 40 -> 29, of which waited for: 18 -> 20; matrix products, arithmetic and copies ran while one was open for 7% -> 5% of each run, Pallas kernels for 0% -> 0%
where the time goes in v8:
time: 194 us; the launch traced here: 191 us
  starting transfers between devices  124 us (64%)
  waiting for transfers between devices  47.2 us (24%)
  local copies, waits for them, and re-layouts  9.55 us (5%)
  other arithmetic  6.25 us (3%)
  matrix products  3.41 us (2%)
    ppermute x7, starting transfers between devices, reduce_all(): flat = flat + lax.ppermute(flat, a, perm)  32 us
    ppermute x6, starting transfers between devices, ring_gather(): left = lax.ppermute(left, axis, fwd)  21.2 us
    ppermute x4, starting transfers between devices, ring_gather(): right = lax.ppermute(right, axis, bwd)  20.2 us
    ppermute x7, waiting for transfers between devices, reduce_all(): flat = flat + lax.ppermute(flat, a, perm)  18.3 us
    ppermute x2, starting transfers between devices, all_gather_flat(): other = lax.ppermute(flat, a, perm)  14 us
    ppermute x3, waiting for transfers between devices, plane_blocks(): lax.ppermute(sent, across, [(i, (i + s) % n_across) for i in range(n_acro...  11.1 us
    ppermute x3, starting transfers between devices, plane_blocks(): lax.ppermute(cols, across, [(i, (i - s) % n_across) for i in range(n_acro...  9.92 us
    ppermute x3, starting transfers between devices, plane_blocks(): lax.ppermute(sent, across, [(i, (i + s) % n_across) for i in range(n_acro...  8.73 us
  transfers between devices with their start and end apart: 29, of which 20 were waited for; matrix products, arithmetic and copies ran while one was open for 5% of the time, Pallas kernels for 0%

profile of v8, /device:TPU:1, one launch (start us, length us, event | category | flops | bytes accessed | tf_op | source)
XLA Modules:
  0.0 191.3 jit_solution(12881038120398617270)
XLA Ops:
  0.7 5.2 %collective-permute-start = (bf16[128,256]{1,0:T(8,128)(2,1)}, bf16[128,256]{1,0:T(8,128)(2,1)S(1)}, u32[]{:S(2)}, u32[]{:S(2)}) collective-permute-start(bf16[128,256]{1,0:T(8,128)(2,1)} %param.8), channel_id=1, source_target_pairs={{0,128},{128,256},{256,384},{384,0},{1,129},{129,257},{257,385},{3... | collective-permute-start | bytes 196616 | tf_op jit(solution)/shard_map/ppermute | solution.py:26
  5.8 3.6 %collective-permute-start.2 = (bf16[128,256]{1,0:T(8,128)(2,1)}, bf16[128,256]{1,0:T(8,128)(2,1)S(1)}, u32[]{:S(2)}, u32[]{:S(2)}) collective-permute-start(bf16[128,256]{1,0:T(8,128)(2,1)} %param.8), channel_id=1, source_target_pairs={{0,384},{128,0},{256,128},{384,256},{1,385},{129,1},{257,129},{385... | collective-permute-start | bytes 196616 | tf_op jit(solution)/shard_map/ppermute | solution.py:29
  9.4 4.2 %collective-permute-start.1 = (bf16[128,256]{1,0:T(8,128)(2,1)S(1)}, bf16[128,256]{1,0:T(8,128)(2,1)S(1)}, u32[]{:S(2)}, u32[]{:S(2)}) collective-permute-start(bf16[128,256]{1,0:T(8,128)(2,1)S(1)} %collective-permute-done), channel_id=1, source_target_pairs={{0,128},{128,256},{256,384},{384,0},{1,129},{129,257},{257,385},{3... | collective-permute-start | bytes 196616 | tf_op jit(solution)/shard_map/ppermute | solution.py:26
  17.5 4.0 %collective-permute-start.3 = (bf16[4,128,256]{2,1,0:T(8,128)(2,1)S(1)}, bf16[4,128,256]{2,1,0:T(8,128)(2,1)S(1)}, u32[]{:S(2)}, u32[]{:S(2)}) collective-permute-start(bf16[4,128,256]{2,1,0:T(8,128)(2,1)S(1)} %pad_maximum_fusion.2), channel_id=1, source_target_pairs={{0,4},{4,8},{8,12},{12,16},{16,20},{20,24},{24,28},{28,0},{1,5},{5... | collective-permute-start | bytes 786440 | tf_op jit(solution)/shard_map/ppermute | solution.py:26
  22.7 4.6 %collective-permute-start.12 = (s32[8]{0:T(128)S(1)}, s32[8]{0:T(128)S(1)}, u32[]{:S(2)}, u32[]{:S(2)}) collective-permute-start(s32[8]{0:T(128)S(1)} %get-tuple-element.7), channel_id=1, source_target_pairs={{0,64},{32,96},{64,0},{96,32},{1,65},{33,97},{65,1},{97,33},{2,66}... | collective-permute-start | bytes 104 | tf_op jit(solution)/shard_map/ppermute | solution.py:46
  27.4 2.8 %collective-permute-start.14 = (s32[8]{0:T(128)S(1)}, s32[8]{0:T(128)S(1)}, u32[]{:S(2)}, u32[]{:S(2)}) collective-permute-start(s32[8]{0:T(128)S(1)} %get-tuple-element.7), channel_id=1, source_target_pairs={{0,96},{32,0},{64,32},{96,64},{1,97},{33,1},{65,33},{97,65},{2,98}... | collective-permute-start | bytes 104 | tf_op jit(solution)/shard_map/ppermute | solution.py:46
  30.1 2.5 %collective-permute-start.10 = (s32[8]{0:T(128)S(1)}, s32[8]{0:T(128)S(1)}, u32[]{:S(2)}, u32[]{:S(2)}) collective-permute-start(s32[8]{0:T(128)S(1)} %get-tuple-element.7), channel_id=1, source_target_pairs={{0,32},{32,64},{64,96},{96,0},{1,33},{33,65},{65,97},{97,1},{2,34}... | collective-permute-start | bytes 104 | tf_op jit(solution)/shard_map/ppermute | solution.py:46
  32.7 4.0 %collective-permute-start.4 = (bf16[4,128,256]{2,1,0:T(8,128)(2,1)S(1)}, bf16[4,128,256]{2,1,0:T(8,128)(2,1)S(1)}, u32[]{:S(2)}, u32[]{:S(2)}) collective-permute-start(bf16[4,128,256]{2,1,0:T(8,128)(2,1)S(1)} %collective-permute-done.3), channel_id=1, source_target_pairs={{0,4},{4,8},{8,12},{12,16},{16,20},{20,24},{24,28},{28,0},{1,5},{5... | collective-permute-start | bytes 786440 | tf_op jit(solution)/shard_map/ppermute | solution.py:26
  38.8 6.6 %collective-permute-start.7 = (bf16[4,128,256]{2,1,0:T(8,128)(2,1)S(1)}, bf16[4,128,256]{2,1,0:T(8,128)(2,1)S(1)}, u32[]{:S(2)}, u32[]{:S(2)}) collective-permute-start(bf16[4,128,256]{2,1,0:T(8,128)(2,1)S(1)} %pad_maximum_fusion.2), channel_id=1, source_target_pairs={{0,28},{4,0},{8,4},{12,8},{16,12},{20,16},{24,20},{28,24},{1,29},{... | collective-permute-start | bytes 786440 | tf_op jit(solution)/shard_map/ppermute | solution.py:29
  48.7 5.0 %collective-permute-start.8 = (bf16[4,128,256]{2,1,0:T(8,128)(2,1)S(1)}, bf16[4,128,256]{2,1,0:T(8,128)(2,1)S(1)}, u32[]{:S(2)}, u32[]{:S(2)}) collective-permute-start(bf16[4,128,256]{2,1,0:T(8,128)(2,1)S(1)} %collective-permute-done.7), channel_id=1, source_target_pairs={{0,28},{4,0},{8,4},{12,8},{16,12},{20,16},{24,20},{28,24},{1,29},{... | collective-permute-start | bytes 786440 | tf_op jit(solution)/shard_map/ppermute | solution.py:29
  57.0 5.0 %collective-permute-start.9 = (bf16[4,128,256]{2,1,0:T(8,128)(2,1)S(1)}, bf16[4,128,256]{2,1,0:T(8,128)(2,1)S(1)}, u32[]{:S(2)}, u32[]{:S(2)}) collective-permute-start(bf16[4,128,256]{2,1,0:T(8,128)(2,1)S(1)} %collective-permute-done.8), channel_id=1, source_target_pairs={{0,28},{4,0},{8,4},{12,8},{16,12},{20,16},{24,20},{28,24},{1,29},{... | collective-permute-start | bytes 786440 | tf_op jit(solution)/shard_map/ppermute | solution.py:29
  63.2 2.4 %collective-permute-done.9 = bf16[4,128,256]{2,1,0:T(8,128)(2,1)S(1)} collective-permute-done((bf16[4,128,256]{2,1,0:T(8,128)(2,1)S(1)}, bf16[4,128,256]{2,1,0:T(8,128)(2,1)S(1)}, u32[]{:S(2)}, u32[]{:S(2)}) %collective-permute-start.9) | collective-permute-done | bytes 262176 | tf_op jit(solution)/shard_map/ppermute | solution.py:29
  70.7 4.2 %collective-permute-start.15 = (bf16[8,128,256]{2,1,0:T(8,128)(2,1)}, bf16[8,128,256]{2,1,0:T(8,128)(2,1)}, u32[]{:S(2)}, u32[]{:S(2)}) collective-permute-start(bf16[8,128,256]{2,1,0:T(8,128)(2,1)} %gather_fusion.2), channel_id=1, source_target_pairs={{0,32},{32,64},{64,96},{96,0},{1,33},{33,65},{65,97},{97,1},{2,34}... | collective-permute-start | bytes 1572872 | tf_op jit(solution)/shard_map/ppermute | solution.py:65
  76.3 2.3 %collective-permute-start.11 = (bf16[8,128,256]{2,1,0:T(8,128)(2,1)}, bf16[8,128,256]{2,1,0:T(8,128)(2,1)}, u32[]{:S(2)}, u32[]{:S(2)}) collective-permute-start(bf16[8,128,256]{2,1,0:T(8,128)(2,1)} %gather_fusion), channel_id=1, source_target_pairs={{0,96},{32,0},{64,32},{96,64},{1,97},{33,1},{65,33},{97,65},{2,98}... | collective-permute-start | bytes 1572872 | tf_op jit(solution)/shard_map/ppermute | solution.py:65
  81.3 10.7 %collective-permute-done.15 = bf16[8,128,256]{2,1,0:T(8,128)(2,1)} collective-permute-done((bf16[8,128,256]{2,1,0:T(8,128)(2,1)}, bf16[8,128,256]{2,1,0:T(8,128)(2,1)}, u32[]{:S(2)}, u32[]{:S(2)}) %collective-permute-start.15) | collective-permute-done | bytes 524320 | tf_op jit(solution)/shard_map/ppermute | solution.py:65
  96.0 7.7 %collective-permute-start.16 = (f32[2,32768]{1,0:T(2,128)S(1)}, f32[2,32768]{1,0:T(2,128)S(1)}, u32[]{:S(2)}, u32[]{:S(2)}) collective-permute-start(f32[2,32768]{1,0:T(2,128)S(1)} %bitcast.69), channel_id=1, source_target_pairs={{0,1},{1,0},{2,3},{3,2},{4,5},{5,4},{6,7},{7,6},{8,9},{9,8},{10,11... | collective-permute-start | bytes 786440 | tf_op jit(solution)/shard_map/ppermute | solution.py:118
  105.4 3.5 %collective-permute-start.17 = (f32[32768]{0:T(1024)S(1)}, f32[32768]{0:T(1024)S(1)}, u32[]{:S(2)}, u32[]{:S(2)}) collective-permute-start(f32[32768]{0:T(1024)S(1)} %bitcast.78), channel_id=1, source_target_pairs={{0,2},{2,0},{1,3},{3,1},{4,6},{6,4},{5,7},{7,5},{8,10},{10,8},{9,1... | collective-permute-start | bytes 393224 | tf_op jit(solution)/shard_map/ppermute | solution.py:122
  108.9 3.2 %collective-permute-done.17 = f32[32768]{0:T(1024)S(1)} collective-permute-done((f32[32768]{0:T(1024)S(1)}, f32[32768]{0:T(1024)S(1)}, u32[]{:S(2)}, u32[]{:S(2)}) %collective-permute-start.17) | collective-permute-done | bytes 131104 | tf_op jit(solution)/shard_map/ppermute | solution.py:122
  113.4 3.0 %collective-permute-start.18 = (f32[33792]{0:T(1024)S(1)}, f32[33792]{0:T(1024)S(1)}, u32[]{:S(2)}, u32[]{:S(2)}) collective-permute-start(f32[33792]{0:T(1024)S(1)} %select_n.333), channel_id=1, source_target_pairs={{0,1},{1,0},{2,3},{3,2},{4,5},{5,4},{6,7},{7,6},{8,9},{9,8},{10,11... | collective-permute-start | bytes 405512 | tf_op jit(solution)/shard_map/ppermute | solution.py:89
  117.5 3.4 %collective-permute-start.19 = (f32[16896]{0:T(1024)S(1)}, f32[16896]{0:T(1024)S(1)}, u32[]{:S(2)}, u32[]{:S(2)}) collective-permute-start(f32[16896]{0:T(1024)S(1)} %slice_select_fusion.2), channel_id=1, source_target_pairs={{0,2},{2,0},{1,3},{3,1},{4,6},{6,4},{5,7},{7,5},{8,10},{10,8},{9,1... | collective-permute-start | bytes 202760 | tf_op jit(solution)/shard_map/ppermute | solution.py:89
  122.6 6.5 %collective-permute-start.20 = (f32[16896]{0:T(1024)S(1)}, f32[16896]{0:T(1024)S(1)}, u32[]{:S(2)}, u32[]{:S(2)}) collective-permute-start(f32[16896]{0:T(1024)S(1)} %select_add_fusion), channel_id=1, source_target_pairs={{0,16},{4,20},{8,24},{12,28},{16,0},{20,4},{24,8},{28,12},{1,17},{... | collective-permute-start | bytes 202760 | tf_op jit(solution)/shard_map/ppermute | solution.py:107
  129.0 2.5 %collective-permute-done.20 = f32[16896]{0:T(1024)S(1)} collective-permute-done((f32[16896]{0:T(1024)S(1)}, f32[16896]{0:T(1024)S(1)}, u32[]{:S(2)}, u32[]{:S(2)}) %collective-permute-start.20) | collective-permute-done | bytes 67616 | tf_op jit(solution)/shard_map/ppermute | solution.py:107
  131.5 4.7 %collective-permute-start.21 = (f32[16896]{0:T(1024)S(1)}, f32[16896]{0:T(1024)S(1)}, u32[]{:S(2)}, u32[]{:S(2)}) collective-permute-start(f32[16896]{0:T(1024)S(1)} %add.310), channel_id=1, source_target_pairs={{0,8},{4,12},{8,0},{12,4},{16,24},{20,28},{24,16},{28,20},{1,9},{5... | collective-permute-start | bytes 202760 | tf_op jit(solution)/shard_map/ppermute | solution.py:107
  138.0 5.7 %collective-permute-start.22 = (f32[16896]{0:T(1024)S(1)}, f32[16896]{0:T(1024)S(1)}, u32[]{:S(2)}, u32[]{:S(2)}) collective-permute-start(f32[16896]{0:T(1024)S(1)} %add.311), channel_id=1, source_target_pairs={{0,4},{4,0},{8,12},{12,8},{16,20},{20,16},{24,28},{28,24},{1,5},{5... | collective-permute-start | bytes 202760 | tf_op jit(solution)/shard_map/ppermute | solution.py:107
  145.4 3.1 %collective-permute-start.23 = (f32[16896]{0:T(1024)S(1)}, f32[16896]{0:T(1024)S(1)}, u32[]{:S(2)}, u32[]{:S(2)}) collective-permute-start(f32[16896]{0:T(1024)S(1)} %add.312), channel_id=1, source_target_pairs={{0,64},{32,96},{64,0},{96,32},{1,65},{33,97},{65,1},{97,33},{2,66}... | collective-permute-start | bytes 202760 | tf_op jit(solution)/shard_map/ppermute | solution.py:107
  148.5 3.4 %collective-permute-done.23 = f32[16896]{0:T(1024)S(1)} collective-permute-done((f32[16896]{0:T(1024)S(1)}, f32[16896]{0:T(1024)S(1)}, u32[]{:S(2)}, u32[]{:S(2)}) %collective-permute-start.23) | collective-permute-done | bytes 67616 | tf_op jit(solution)/shard_map/ppermute | solution.py:107
  154.0 3.0 %collective-permute-done.24 = f32[16896]{0:T(1024)S(1)} collective-permute-done((f32[16896]{0:T(1024)S(1)}, f32[16896]{0:T(1024)S(1)}, u32[]{:S(2)}, u32[]{:S(2)}) %collective-permute-start.24) | collective-permute-done | bytes 67616 | tf_op jit(solution)/shard_map/ppermute | solution.py:107
  157.0 7.7 %collective-permute-start.25 = (f32[16896]{0:T(1024)S(1)}, f32[16896]{0:T(1024)S(1)}, u32[]{:S(2)}, u32[]{:S(2)}) collective-permute-start(f32[16896]{0:T(1024)S(1)} %add.314), channel_id=1, source_target_pairs={{0,256},{128,384},{256,0},{384,128},{1,257},{129,385},{257,1},{385... | collective-permute-start | bytes 202760 | tf_op jit(solution)/shard_map/ppermute | solution.py:107
  166.4 2.3 %collective-permute-start.26 = (f32[16896]{0:T(1024)S(1)}, f32[16896]{0:T(1024)S(1)}, u32[]{:S(2)}, u32[]{:S(2)}) collective-permute-start(f32[16896]{0:T(1024)S(1)} %add.315), channel_id=1, source_target_pairs={{0,128},{128,0},{256,384},{384,256},{1,129},{129,1},{257,385},{385... | collective-permute-start | bytes 202760 | tf_op jit(solution)/shard_map/ppermute | solution.py:107
  168.7 4.3 %collective-permute-done.26 = f32[16896]{0:T(1024)S(1)} collective-permute-done((f32[16896]{0:T(1024)S(1)}, f32[16896]{0:T(1024)S(1)}, u32[]{:S(2)}, u32[]{:S(2)}) %collective-permute-start.26) | collective-permute-done | bytes 67616 | tf_op jit(solution)/shard_map/ppermute | solution.py:107
  173.0 3.8 %collective-permute-start.27 = (f32[16896]{0:T(1024)S(1)}, f32[16896]{0:T(1024)S(1)}, u32[]{:S(2)}, u32[]{:S(2)}) collective-permute-start(f32[16896]{0:T(1024)S(1)} %add.316), channel_id=1, source_target_pairs={{0,2},{2,0},{1,3},{3,1},{4,6},{6,4},{5,7},{7,5},{8,10},{10,8},{9,1... | collective-permute-start | bytes 202760 | tf_op jit(solution)/shard_map/ppermute | solution.py:96
  178.8 10.2 %collective-permute-start.28 = (f32[33792]{0:T(1024)S(1)}, f32[33792]{0:T(1024)S(1)}, u32[]{:S(2)}, u32[]{:S(2)}) collective-permute-start(f32[33792]{0:T(1024)S(1)} %maximum_select_fusion.1), channel_id=1, source_target_pairs={{0,1},{1,0},{2,3},{3,2},{4,5},{5,4},{6,7},{7,6},{8,9},{9,8},{10,11... | collective-permute-start | bytes 405512 | tf_op jit(solution)/shard_map/ppermute | solution.py:96
  (110 shorter events, 44.9 us)
Async XLA Ops:
  0.6 91.8 %copy-start = (bf16[1,4,8,128,128]{4,3,2,1,0:T(8,128)(2,1)S(1)}, bf16[1,4,8,128,128]{4,3,2,1,0:T(8,128)(2,1)}, u32[]{:S(2)}) copy-start(bf16[1,4,8,128,128]{4,3,2,1,0:T(8,128)(2,1)} %param.11) | copy-start | bytes 3145732
  0.6 62.5 %copy-start.2 = (bf16[128,256]{1,0:T(8,128)(2,1)S(1)}, bf16[128,256]{1,0:T(8,128)(2,1)}, u32[]{:S(2)}) copy-start(bf16[128,256]{1,0:T(8,128)(2,1)} %param.8) | copy-start | bytes 196612
  0.7 8.8 %collective-permute-start = (bf16[128,256]{1,0:T(8,128)(2,1)}, bf16[128,256]{1,0:T(8,128)(2,1)S(1)}, u32[]{:S(2)}, u32[]{:S(2)}) collective-permute-start(bf16[128,256]{1,0:T(8,128)(2,1)} %param.8), channel_id=1, source_target_pairs={{0,128},{128,256},{256,384},{384,0},{1,129},{129,257},{257,385},{3... | collective-permute-start | bytes 196616 | tf_op jit(solution)/shard_map/ppermute | solution.py:26
  5.8 8.7 %collective-permute-start.2 = (bf16[128,256]{1,0:T(8,128)(2,1)}, bf16[128,256]{1,0:T(8,128)(2,1)S(1)}, u32[]{:S(2)}, u32[]{:S(2)}) collective-permute-start(bf16[128,256]{1,0:T(8,128)(2,1)} %param.8), channel_id=1, source_target_pairs={{0,384},{128,0},{256,128},{384,256},{1,385},{129,1},{257,129},{385... | collective-permute-start | bytes 196616 | tf_op jit(solution)/shard_map/ppermute | solution.py:29
  9.4 7.1 %collective-permute-start.1 = (bf16[128,256]{1,0:T(8,128)(2,1)S(1)}, bf16[128,256]{1,0:T(8,128)(2,1)S(1)}, u32[]{:S(2)}, u32[]{:S(2)}) collective-permute-start(bf16[128,256]{1,0:T(8,128)(2,1)S(1)} %collective-permute-done), channel_id=1, source_target_pairs={{0,128},{128,256},{256,384},{384,0},{1,129},{129,257},{257,385},{3... | collective-permute-start | bytes 196616 | tf_op jit(solution)/shard_map/ppermute | solution.py:26
  17.5 15.2 %collective-permute-start.3 = (bf16[4,128,256]{2,1,0:T(8,128)(2,1)S(1)}, bf16[4,128,256]{2,1,0:T(8,128)(2,1)S(1)}, u32[]{:S(2)}, u32[]{:S(2)}) collective-permute-start(bf16[4,128,256]{2,1,0:T(8,128)(2,1)S(1)} %pad_maximum_fusion.2), channel_id=1, source_target_pairs={{0,4},{4,8},{8,12},{12,16},{16,20},{20,24},{24,28},{28,0},{1,5},{5... | collective-permute-start | bytes 786440 | tf_op jit(solution)/shard_map/ppermute | solution.py:26
  22.7 16.0 %collective-permute-start.12 = (s32[8]{0:T(128)S(1)}, s32[8]{0:T(128)S(1)}, u32[]{:S(2)}, u32[]{:S(2)}) collective-permute-start(s32[8]{0:T(128)S(1)} %get-tuple-element.7), channel_id=1, source_target_pairs={{0,64},{32,96},{64,0},{96,32},{1,65},{33,97},{65,1},{97,33},{2,66}... | collective-permute-start | bytes 104 | tf_op jit(solution)/shard_map/ppermute | solution.py:46
  27.4 20.0 %collective-permute-start.14 = (s32[8]{0:T(128)S(1)}, s32[8]{0:T(128)S(1)}, u32[]{:S(2)}, u32[]{:S(2)}) collective-permute-start(s32[8]{0:T(128)S(1)} %get-tuple-element.7), channel_id=1, source_target_pairs={{0,96},{32,0},{64,32},{96,64},{1,97},{33,1},{65,33},{97,65},{2,98}... | collective-permute-start | bytes 104 | tf_op jit(solution)/shard_map/ppermute | solution.py:46
  30.1 17.3 %collective-permute-start.10 = (s32[8]{0:T(128)S(1)}, s32[8]{0:T(128)S(1)}, u32[]{:S(2)}, u32[]{:S(2)}) collective-permute-start(s32[8]{0:T(128)S(1)} %get-tuple-element.7), channel_id=1, source_target_pairs={{0,32},{32,64},{64,96},{96,0},{1,33},{33,65},{65,97},{97,1},{2,34}... | collective-permute-start | bytes 104 | tf_op jit(solution)/shard_map/ppermute | solution.py:46
  32.7 12.7 %collective-permute-start.4 = (bf16[4,128,256]{2,1,0:T(8,128)(2,1)S(1)}, bf16[4,128,256]{2,1,0:T(8,128)(2,1)S(1)}, u32[]{:S(2)}, u32[]{:S(2)}) collective-permute-start(bf16[4,128,256]{2,1,0:T(8,128)(2,1)S(1)} %collective-permute-done.3), channel_id=1, source_target_pairs={{0,4},{4,8},{8,12},{12,16},{16,20},{20,24},{24,28},{28,0},{1,5},{5... | collective-permute-start | bytes 786440 | tf_op jit(solution)/shard_map/ppermute | solution.py:26
  38.8 9.9 %collective-permute-start.7 = (bf16[4,128,256]{2,1,0:T(8,128)(2,1)S(1)}, bf16[4,128,256]{2,1,0:T(8,128)(2,1)S(1)}, u32[]{:S(2)}, u32[]{:S(2)}) collective-permute-start(bf16[4,128,256]{2,1,0:T(8,128)(2,1)S(1)} %pad_maximum_fusion.2), channel_id=1, source_target_pairs={{0,28},{4,0},{8,4},{12,8},{16,12},{20,16},{24,20},{28,24},{1,29},{... | collective-permute-start | bytes 786440 | tf_op jit(solution)/shard_map/ppermute | solution.py:29
  45.4 8.3 %collective-permute-start.5 = (bf16[4,128,256]{2,1,0:T(8,128)(2,1)S(1)}, bf16[4,128,256]{2,1,0:T(8,128)(2,1)S(1)}, u32[]{:S(2)}, u32[]{:S(2)}) collective-permute-start(bf16[4,128,256]{2,1,0:T(8,128)(2,1)S(1)} %collective-permute-done.4), channel_id=1, source_target_pairs={{0,4},{4,8},{8,12},{12,16},{16,20},{20,24},{24,28},{28,0},{1,5},{5... | collective-permute-start | bytes 786440 | tf_op jit(solution)/shard_map/ppermute | solution.py:26
  48.7 8.3 %collective-permute-start.8 = (bf16[4,128,256]{2,1,0:T(8,128)(2,1)S(1)}, bf16[4,128,256]{2,1,0:T(8,128)(2,1)S(1)}, u32[]{:S(2)}, u32[]{:S(2)}) collective-permute-start(bf16[4,128,256]{2,1,0:T(8,128)(2,1)S(1)} %collective-permute-done.7), channel_id=1, source_target_pairs={{0,28},{4,0},{8,4},{12,8},{16,12},{20,16},{24,20},{28,24},{1,29},{... | collective-permute-start | bytes 786440 | tf_op jit(solution)/shard_map/ppermute | solution.py:29
  53.8 8.3 %collective-permute-start.6 = (bf16[4,128,256]{2,1,0:T(8,128)(2,1)S(1)}, bf16[4,128,256]{2,1,0:T(8,128)(2,1)S(1)}, u32[]{:S(2)}, u32[]{:S(2)}) collective-permute-start(bf16[4,128,256]{2,1,0:T(8,128)(2,1)S(1)} %collective-permute-done.5), channel_id=1, source_target_pairs={{0,4},{4,8},{8,12},{12,16},{16,20},{20,24},{24,28},{28,0},{1,5},{5... | collective-permute-start | bytes 786440 | tf_op jit(solution)/shard_map/ppermute | solution.py:26
  57.0 8.6 %collective-permute-start.9 = (bf16[4,128,256]{2,1,0:T(8,128)(2,1)S(1)}, bf16[4,128,256]{2,1,0:T(8,128)(2,1)S(1)}, u32[]{:S(2)}, u32[]{:S(2)}) collective-permute-start(bf16[4,128,256]{2,1,0:T(8,128)(2,1)S(1)} %collective-permute-done.8), channel_id=1, source_target_pairs={{0,28},{4,0},{8,4},{12,8},{16,12},{20,16},{24,20},{28,24},{1,29},{... | collective-permute-start | bytes 786440 | tf_op jit(solution)/shard_map/ppermute | solution.py:29
  65.6 26.8 %copy-start.7 = (pred[8]{0:T(512)(128)(4,1)S(1)}, pred[8]{0:T(512)(128)(4,1)}, u32[]{:S(2)}) copy-start(pred[8]{0:T(512)(128)(4,1)} %get-tuple-element.5) | copy-start | bytes 28
  67.1 14.3 %collective-permute-start.13 = (bf16[8,128,256]{2,1,0:T(8,128)(2,1)}, bf16[8,128,256]{2,1,0:T(8,128)(2,1)}, u32[]{:S(2)}, u32[]{:S(2)}) collective-permute-start(bf16[8,128,256]{2,1,0:T(8,128)(2,1)} %gather_fusion.1), channel_id=1, source_target_pairs={{0,64},{32,96},{64,0},{96,32},{1,65},{33,97},{65,1},{97,33},{2,66}... | collective-permute-start | bytes 1572872 | tf_op jit(solution)/shard_map/ppermute | solution.py:65
  70.7 21.4 %collective-permute-start.15 = (bf16[8,128,256]{2,1,0:T(8,128)(2,1)}, bf16[8,128,256]{2,1,0:T(8,128)(2,1)}, u32[]{:S(2)}, u32[]{:S(2)}) collective-permute-start(bf16[8,128,256]{2,1,0:T(8,128)(2,1)} %gather_fusion.2), channel_id=1, source_target_pairs={{0,32},{32,64},{64,96},{96,0},{1,33},{33,65},{65,97},{97,1},{2,34}... | collective-permute-start | bytes 1572872 | tf_op jit(solution)/shard_map/ppermute | solution.py:65
  76.3 16.1 %collective-permute-start.11 = (bf16[8,128,256]{2,1,0:T(8,128)(2,1)}, bf16[8,128,256]{2,1,0:T(8,128)(2,1)}, u32[]{:S(2)}, u32[]{:S(2)}) collective-permute-start(bf16[8,128,256]{2,1,0:T(8,128)(2,1)} %gather_fusion), channel_id=1, source_target_pairs={{0,96},{32,0},{64,32},{96,64},{1,97},{33,1},{65,33},{97,65},{2,98}... | collective-permute-start | bytes 1572872 | tf_op jit(solution)/shard_map/ppermute | solution.py:65
  96.0 8.8 %collective-permute-start.16 = (f32[2,32768]{1,0:T(2,128)S(1)}, f32[2,32768]{1,0:T(2,128)S(1)}, u32[]{:S(2)}, u32[]{:S(2)}) collective-permute-start(f32[2,32768]{1,0:T(2,128)S(1)} %bitcast.69), channel_id=1, source_target_pairs={{0,1},{1,0},{2,3},{3,2},{4,5},{5,4},{6,7},{7,6},{8,9},{9,8},{10,11... | collective-permute-start | bytes 786440 | tf_op jit(solution)/shard_map/ppermute | solution.py:118
  105.4 6.8 %collective-permute-start.17 = (f32[32768]{0:T(1024)S(1)}, f32[32768]{0:T(1024)S(1)}, u32[]{:S(2)}, u32[]{:S(2)}) collective-permute-start(f32[32768]{0:T(1024)S(1)} %bitcast.78), channel_id=1, source_target_pairs={{0,2},{2,0},{1,3},{3,1},{4,6},{6,4},{5,7},{7,5},{8,10},{10,8},{9,1... | collective-permute-start | bytes 393224 | tf_op jit(solution)/shard_map/ppermute | solution.py:122
  113.4 4.0 %collective-permute-start.18 = (f32[33792]{0:T(1024)S(1)}, f32[33792]{0:T(1024)S(1)}, u32[]{:S(2)}, u32[]{:S(2)}) collective-permute-start(f32[33792]{0:T(1024)S(1)} %select_n.333), channel_id=1, source_target_pairs={{0,1},{1,0},{2,3},{3,2},{4,5},{5,4},{6,7},{7,6},{8,9},{9,8},{10,11... | collective-permute-start | bytes 405512 | tf_op jit(solution)/shard_map/ppermute | solution.py:89
  117.5 5.1 %collective-permute-start.19 = (f32[16896]{0:T(1024)S(1)}, f32[16896]{0:T(1024)S(1)}, u32[]{:S(2)}, u32[]{:S(2)}) collective-permute-start(f32[16896]{0:T(1024)S(1)} %slice_select_fusion.2), channel_id=1, source_target_pairs={{0,2},{2,0},{1,3},{3,1},{4,6},{6,4},{5,7},{7,5},{8,10},{10,8},{9,1... | collective-permute-start | bytes 202760 | tf_op jit(solution)/shard_map/ppermute | solution.py:89
  122.6 9.0 %collective-permute-start.20 = (f32[16896]{0:T(1024)S(1)}, f32[16896]{0:T(1024)S(1)}, u32[]{:S(2)}, u32[]{:S(2)}) collective-permute-start(f32[16896]{0:T(1024)S(1)} %select_add_fusion), channel_id=1, source_target_pairs={{0,16},{4,20},{8,24},{12,28},{16,0},{20,4},{24,8},{28,12},{1,17},{... | collective-permute-start | bytes 202760 | tf_op jit(solution)/shard_map/ppermute | solution.py:107
  131.5 6.4 %collective-permute-start.21 = (f32[16896]{0:T(1024)S(1)}, f32[16896]{0:T(1024)S(1)}, u32[]{:S(2)}, u32[]{:S(2)}) collective-permute-start(f32[16896]{0:T(1024)S(1)} %add.310), channel_id=1, source_target_pairs={{0,8},{4,12},{8,0},{12,4},{16,24},{20,28},{24,16},{28,20},{1,9},{5... | collective-permute-start | bytes 202760 | tf_op jit(solution)/shard_map/ppermute | solution.py:107
  138.0 7.4 %collective-permute-start.22 = (f32[16896]{0:T(1024)S(1)}, f32[16896]{0:T(1024)S(1)}, u32[]{:S(2)}, u32[]{:S(2)}) collective-permute-start(f32[16896]{0:T(1024)S(1)} %add.311), channel_id=1, source_target_pairs={{0,4},{4,0},{8,12},{12,8},{16,20},{20,16},{24,28},{28,24},{1,5},{5... | collective-permute-start | bytes 202760 | tf_op jit(solution)/shard_map/ppermute | solution.py:107
  145.4 6.6 %collective-permute-start.23 = (f32[16896]{0:T(1024)S(1)}, f32[16896]{0:T(1024)S(1)}, u32[]{:S(2)}, u32[]{:S(2)}) collective-permute-start(f32[16896]{0:T(1024)S(1)} %add.312), channel_id=1, source_target_pairs={{0,64},{32,96},{64,0},{96,32},{1,65},{33,97},{65,1},{97,33},{2,66}... | collective-permute-start | bytes 202760 | tf_op jit(solution)/shard_map/ppermute | solution.py:107
  151.9 5.1 %collective-permute-start.24 = (f32[16896]{0:T(1024)S(1)}, f32[16896]{0:T(1024)S(1)}, u32[]{:S(2)}, u32[]{:S(2)}) collective-permute-start(f32[16896]{0:T(1024)S(1)} %add.313), channel_id=1, source_target_pairs={{0,32},{32,0},{64,96},{96,64},{1,33},{33,1},{65,97},{97,65},{2,34}... | collective-permute-start | bytes 202760 | tf_op jit(solution)/shard_map/ppermute | solution.py:107
  157.0 9.4 %collective-permute-start.25 = (f32[16896]{0:T(1024)S(1)}, f32[16896]{0:T(1024)S(1)}, u32[]{:S(2)}, u32[]{:S(2)}) collective-permute-start(f32[16896]{0:T(1024)S(1)} %add.314), channel_id=1, source_target_pairs={{0,256},{128,384},{256,0},{384,128},{1,257},{129,385},{257,1},{385... | collective-permute-start | bytes 202760 | tf_op jit(solution)/shard_map/ppermute | solution.py:107
  166.4 6.6 %collective-permute-start.26 = (f32[16896]{0:T(1024)S(1)}, f32[16896]{0:T(1024)S(1)}, u32[]{:S(2)}, u32[]{:S(2)}) collective-permute-start(f32[16896]{0:T(1024)S(1)} %add.315), channel_id=1, source_target_pairs={{0,128},{128,0},{256,384},{384,256},{1,129},{129,1},{257,385},{385... | collective-permute-start | bytes 202760 | tf_op jit(solution)/shard_map/ppermute | solution.py:107
  173.0 5.8 %collective-permute-start.27 = (f32[16896]{0:T(1024)S(1)}, f32[16896]{0:T(1024)S(1)}, u32[]{:S(2)}, u32[]{:S(2)}) collective-permute-start(f32[16896]{0:T(1024)S(1)} %add.316), channel_id=1, source_target_pairs={{0,2},{2,0},{1,3},{3,1},{4,6},{6,4},{5,7},{7,5},{8,10},{10,8},{9,1... | collective-permute-start | bytes 202760 | tf_op jit(solution)/shard_map/ppermute | solution.py:96
  178.8 11.1 %collective-permute-start.28 = (f32[33792]{0:T(1024)S(1)}, f32[33792]{0:T(1024)S(1)}, u32[]{:S(2)}, u32[]{:S(2)}) collective-permute-start(f32[33792]{0:T(1024)S(1)} %maximum_select_fusion.1), channel_id=1, source_target_pairs={{0,1},{1,0},{2,3},{3,2},{4,5},{5,4},{6,7},{7,6},{8,9},{9,8},{10,11... | collective-permute-start | bytes 405512 | tf_op jit(solution)/shard_map/ppermute | solution.py:96
  (9 other events, 167.3 us)

commit v9 on v8

--- a/solution.py
+++ b/solution.py
@@ -121,6 +121,27 @@
     keep = jnp.where(y_lo == 1, pairs[1], pairs[0])
     own = keep + lax.ppermute(send, "y_lo", [(0, 1), (1, 0)])
     return own.reshape(rows // lax.axis_size(REP_AXES), width)
+
+
+def swap(x, axis):
+    return lax.ppermute(x, axis, [(0, 1), (1, 0)])
+
+
+def gather_over_rep(block):
+    other = swap(block, "core")
+    pair = jnp.where(
+        lax.axis_index("core") == 1, jnp.stack([other, block]), jnp.stack([block, other])
+    )
+    other = swap(pair, "y_lo")
+    quad = jnp.where(
+        lax.axis_index("y_lo") == 1, jnp.concatenate([other, pair]), jnp.concatenate([pair, other])
+    )
+    return quad.reshape(-1, *block.shape[1:])
+
+
+def sum_over_rep(value):
+    value = value + swap(value, "core")
+    return value + swap(value, "y_lo")
 
 
 def shards(features, weight, bias_terms, tile_data, tile_row, tile_col, tile_count, grad_out):
@@ -140,12 +161,14 @@
     select = ((own_rows[None, :] == local_ids[:, None]) & live[None, :]).astype(jnp.float32)
     partial_value = jnp.einsum("bt,tif->bif", select, product)
     partial_value = partial_value.reshape(row_count * block_size, feature_width)
-    propagated = reduce_over_rep(partial_value).astype(jnp.bfloat16)
+    propagated = sum_over_rep(partial_value).astype(jnp.bfloat16)
+    group_grad_out = gather_over_rep(grad_out)
     preact = jnp.dot(propagated, weight, preferred_element_type=jnp.float32) + bias_terms
     sigma = jax.nn.sigmoid(preact)
     layer_out = (preact * sigma).astype(jnp.bfloat16)
+    layer_out = lax.dynamic_slice_in_dim(layer_out, rep_index * block_size, block_size, 0)
     slope = sigma * (1.0 + preact * (1.0 - sigma))
-    grad_pre = (grad_out.astype(jnp.float32) * slope).astype(jnp.bfloat16)
+    grad_pre = (group_grad_out.astype(jnp.float32) * slope).astype(jnp.bfloat16)
     weight_term = lax.dot_general(
         propagated, grad_pre, (((0,), (0,)), ((), ())), preferred_element_type=jnp.float32
     )
@@ -154,7 +177,12 @@
     packed = jnp.concatenate(
         [weight_term, bias_term[None, :], jnp.zeros((pad_rows, feature_width), jnp.float32)], axis=0
     )
-    packed = reduce_all(packed)
+    rep_steps = halving_steps(("core", "y_lo"))
+    quarter = lax.axis_index("core") * lax.axis_size("y_lo") + lax.axis_index("y_lo")
+    flat = lax.dynamic_index_in_dim(packed.reshape(row_count, -1), quarter, 0, keepdims=False)
+    for a, b, perm in halving_steps(ROW_AXES[::-1]):
+        flat = flat + lax.ppermute(flat, a, perm)
+    packed = all_gather_flat(flat, rep_steps).reshape(packed.shape)
     weight_grad = packed[:feature_width]
     bias_grad = packed[feature_width]
     return (layer_out, weight_grad, bias_grad)

time: 194 us -> 194 us (level)
  waiting for transfers between devices: 47.2 us -> 55 us
  starting transfers between devices: 124 us -> 118 us
    ppermute x11, waiting for transfers between devices: 25.3 us -> 31.7 us  [the longest x7 20.2 us: shards(): flat = flat + lax.ppermute(flat, a, perm)]
    ppermute x2, starting transfers between devices: 14 us -> 10.1 us  [all_gather_flat(): other = lax.ppermute(flat, a, perm)]
    ppermute x11, starting transfers between devices: 49.5 us -> 47.6 us  [the longest x7 31.8 us: shards(): flat = flat + lax.ppermute(flat, a, perm)]
  transfers between devices with their start and end apart: 29 -> 29, of which waited for: 20 -> 19; matrix products, arithmetic and copies ran while one was open for 5% -> 5% of each run, Pallas kernels for 0% -> 0%
where the time goes in v9:
time: 194 us; the launch traced here: 192 us
  starting transfers between devices  118 us (61%)
  waiting for transfers between devices  55 us (28%)
  local copies, waits for them, and re-layouts  8.95 us (5%)
  other arithmetic  5.93 us (3%)
  matrix products  3.02 us (2%)
    ppermute x7, starting transfers between devices, shards(): flat = flat + lax.ppermute(flat, a, perm)  31.8 us
    ppermute x6, starting transfers between devices, ring_gather(): left = lax.ppermute(left, axis, fwd)  21.2 us
    ppermute x7, waiting for transfers between devices, shards(): flat = flat + lax.ppermute(flat, a, perm)  20.2 us
    ppermute x4, starting transfers between devices, ring_gather(): right = lax.ppermute(right, axis, bwd)  20.1 us
    ppermute x4, starting transfers between devices, swap(): return lax.ppermute(x, axis, [(0, 1), (1, 0)])  15.8 us
    ppermute x4, waiting for transfers between devices, swap(): return lax.ppermute(x, axis, [(0, 1), (1, 0)])  11.4 us
    ppermute x3, waiting for transfers between devices, plane_blocks(): lax.ppermute(sent, across, [(i, (i + s) % n_across) for i in range(n_acro...  11.2 us
    ppermute x2, starting transfers between devices, all_gather_flat(): other = lax.ppermute(flat, a, perm)  10.1 us
  transfers between devices with their start and end apart: 29, of which 19 were waited for; matrix products, arithmetic and copies ran while one was open for 5% of the time, Pallas kernels for 0%

profile of v9, /device:TPU:1, one launch (start us, length us, event | category | flops | bytes accessed | tf_op | source)
XLA Modules:
  0.0 191.8 jit_solution(742582103538856812)
XLA Ops:
  0.7 5.2 %collective-permute-start = (bf16[128,256]{1,0:T(8,128)(2,1)}, bf16[128,256]{1,0:T(8,128)(2,1)S(1)}, u32[]{:S(2)}, u32[]{:S(2)}) collective-permute-start(bf16[128,256]{1,0:T(8,128)(2,1)} %param.8), channel_id=1, source_target_pairs={{0,128},{128,256},{256,384},{384,0},{1,129},{129,257},{257,385},{3... | collective-permute-start | bytes 196616 | tf_op jit(solution)/shard_map/ppermute | solution.py:26
  5.8 3.6 %collective-permute-start.2 = (bf16[128,256]{1,0:T(8,128)(2,1)}, bf16[128,256]{1,0:T(8,128)(2,1)S(1)}, u32[]{:S(2)}, u32[]{:S(2)}) collective-permute-start(bf16[128,256]{1,0:T(8,128)(2,1)} %param.8), channel_id=1, source_target_pairs={{0,384},{128,0},{256,128},{384,256},{1,385},{129,1},{257,129},{385... | collective-permute-start | bytes 196616 | tf_op jit(solution)/shard_map/ppermute | solution.py:29
  9.4 4.2 %collective-permute-start.1 = (bf16[128,256]{1,0:T(8,128)(2,1)S(1)}, bf16[128,256]{1,0:T(8,128)(2,1)S(1)}, u32[]{:S(2)}, u32[]{:S(2)}) collective-permute-start(bf16[128,256]{1,0:T(8,128)(2,1)S(1)} %collective-permute-done), channel_id=1, source_target_pairs={{0,128},{128,256},{256,384},{384,0},{1,129},{129,257},{257,385},{3... | collective-permute-start | bytes 196616 | tf_op jit(solution)/shard_map/ppermute | solution.py:26
  17.5 4.0 %collective-permute-start.3 = (bf16[4,128,256]{2,1,0:T(8,128)(2,1)S(1)}, bf16[4,128,256]{2,1,0:T(8,128)(2,1)S(1)}, u32[]{:S(2)}, u32[]{:S(2)}) collective-permute-start(bf16[4,128,256]{2,1,0:T(8,128)(2,1)S(1)} %pad_maximum_fusion.2), channel_id=1, source_target_pairs={{0,4},{4,8},{8,12},{12,16},{16,20},{20,24},{24,28},{28,0},{1,5},{5... | collective-permute-start | bytes 786440 | tf_op jit(solution)/shard_map/ppermute | solution.py:26
  22.7 4.6 %collective-permute-start.12 = (s32[8]{0:T(128)S(1)}, s32[8]{0:T(128)S(1)}, u32[]{:S(2)}, u32[]{:S(2)}) collective-permute-start(s32[8]{0:T(128)S(1)} %get-tuple-element.7), channel_id=1, source_target_pairs={{0,64},{32,96},{64,0},{96,32},{1,65},{33,97},{65,1},{97,33},{2,66}... | collective-permute-start | bytes 104 | tf_op jit(solution)/shard_map/ppermute | solution.py:46
  27.4 2.8 %collective-permute-start.14 = (s32[8]{0:T(128)S(1)}, s32[8]{0:T(128)S(1)}, u32[]{:S(2)}, u32[]{:S(2)}) collective-permute-start(s32[8]{0:T(128)S(1)} %get-tuple-element.7), channel_id=1, source_target_pairs={{0,96},{32,0},{64,32},{96,64},{1,97},{33,1},{65,33},{97,65},{2,98}... | collective-permute-start | bytes 104 | tf_op jit(solution)/shard_map/ppermute | solution.py:46
  30.1 2.5 %collective-permute-start.10 = (s32[8]{0:T(128)S(1)}, s32[8]{0:T(128)S(1)}, u32[]{:S(2)}, u32[]{:S(2)}) collective-permute-start(s32[8]{0:T(128)S(1)} %get-tuple-element.7), channel_id=1, source_target_pairs={{0,32},{32,64},{64,96},{96,0},{1,33},{33,65},{65,97},{97,1},{2,34}... | collective-permute-start | bytes 104 | tf_op jit(solution)/shard_map/ppermute | solution.py:46
  32.7 4.0 %collective-permute-start.4 = (bf16[4,128,256]{2,1,0:T(8,128)(2,1)S(1)}, bf16[4,128,256]{2,1,0:T(8,128)(2,1)S(1)}, u32[]{:S(2)}, u32[]{:S(2)}) collective-permute-start(bf16[4,128,256]{2,1,0:T(8,128)(2,1)S(1)} %collective-permute-done.3), channel_id=1, source_target_pairs={{0,4},{4,8},{8,12},{12,16},{16,20},{20,24},{24,28},{28,0},{1,5},{5... | collective-permute-start | bytes 786440 | tf_op jit(solution)/shard_map/ppermute | solution.py:26
  38.7 6.5 %collective-permute-start.7 = (bf16[4,128,256]{2,1,0:T(8,128)(2,1)S(1)}, bf16[4,128,256]{2,1,0:T(8,128)(2,1)S(1)}, u32[]{:S(2)}, u32[]{:S(2)}) collective-permute-start(bf16[4,128,256]{2,1,0:T(8,128)(2,1)S(1)} %pad_maximum_fusion.2), channel_id=1, source_target_pairs={{0,28},{4,0},{8,4},{12,8},{16,12},{20,16},{24,20},{28,24},{1,29},{... | collective-permute-start | bytes 786440 | tf_op jit(solution)/shard_map/ppermute | solution.py:29
  48.5 5.0 %collective-permute-start.8 = (bf16[4,128,256]{2,1,0:T(8,128)(2,1)S(1)}, bf16[4,128,256]{2,1,0:T(8,128)(2,1)S(1)}, u32[]{:S(2)}, u32[]{:S(2)}) collective-permute-start(bf16[4,128,256]{2,1,0:T(8,128)(2,1)S(1)} %collective-permute-done.7), channel_id=1, source_target_pairs={{0,28},{4,0},{8,4},{12,8},{16,12},{20,16},{24,20},{28,24},{1,29},{... | collective-permute-start | bytes 786440 | tf_op jit(solution)/shard_map/ppermute | solution.py:29
  56.8 5.0 %collective-permute-start.9 = (bf16[4,128,256]{2,1,0:T(8,128)(2,1)S(1)}, bf16[4,128,256]{2,1,0:T(8,128)(2,1)S(1)}, u32[]{:S(2)}, u32[]{:S(2)}) collective-permute-start(bf16[4,128,256]{2,1,0:T(8,128)(2,1)S(1)} %collective-permute-done.8), channel_id=1, source_target_pairs={{0,28},{4,0},{8,4},{12,8},{16,12},{20,16},{24,20},{28,24},{1,29},{... | collective-permute-start | bytes 786440 | tf_op jit(solution)/shard_map/ppermute | solution.py:29
  62.8 2.6 %collective-permute-done.9 = bf16[4,128,256]{2,1,0:T(8,128)(2,1)S(1)} collective-permute-done((bf16[4,128,256]{2,1,0:T(8,128)(2,1)S(1)}, bf16[4,128,256]{2,1,0:T(8,128)(2,1)S(1)}, u32[]{:S(2)}, u32[]{:S(2)}) %collective-permute-start.9) | collective-permute-done | bytes 262176 | tf_op jit(solution)/shard_map/ppermute | solution.py:29
  66.8 2.3 %collective-permute-start.13 = (bf16[8,128,256]{2,1,0:T(8,128)(2,1)}, bf16[8,128,256]{2,1,0:T(8,128)(2,1)}, u32[]{:S(2)}, u32[]{:S(2)}) collective-permute-start(bf16[8,128,256]{2,1,0:T(8,128)(2,1)} %gather_fusion.1), channel_id=1, source_target_pairs={{0,64},{32,96},{64,0},{96,32},{1,65},{33,97},{65,1},{97,33},{2,66}... | collective-permute-start | bytes 1572872 | tf_op jit(solution)/shard_map/ppermute | solution.py:65
  70.5 4.2 %collective-permute-start.15 = (bf16[8,128,256]{2,1,0:T(8,128)(2,1)}, bf16[8,128,256]{2,1,0:T(8,128)(2,1)}, u32[]{:S(2)}, u32[]{:S(2)}) collective-permute-start(bf16[8,128,256]{2,1,0:T(8,128)(2,1)} %gather_fusion.2), channel_id=1, source_target_pairs={{0,32},{32,64},{64,96},{96,0},{1,33},{33,65},{65,97},{97,1},{2,34}... | collective-permute-start | bytes 1572872 | tf_op jit(solution)/shard_map/ppermute | solution.py:65
  76.0 2.3 %collective-permute-start.11 = (bf16[8,128,256]{2,1,0:T(8,128)(2,1)}, bf16[8,128,256]{2,1,0:T(8,128)(2,1)}, u32[]{:S(2)}, u32[]{:S(2)}) collective-permute-start(bf16[8,128,256]{2,1,0:T(8,128)(2,1)} %gather_fusion), channel_id=1, source_target_pairs={{0,96},{32,0},{64,32},{96,64},{1,97},{33,1},{65,33},{97,65},{2,98}... | collective-permute-start | bytes 1572872 | tf_op jit(solution)/shard_map/ppermute | solution.py:65
  81.0 10.8 %collective-permute-done.15 = bf16[8,128,256]{2,1,0:T(8,128)(2,1)} collective-permute-done((bf16[8,128,256]{2,1,0:T(8,128)(2,1)}, bf16[8,128,256]{2,1,0:T(8,128)(2,1)}, u32[]{:S(2)}, u32[]{:S(2)}) %collective-permute-start.15) | collective-permute-done | bytes 524320 | tf_op jit(solution)/shard_map/ppermute | solution.py:65
  94.7 7.8 %collective-permute-start.16 = (f32[512,256]{1,0:T(8,128)S(1)}, f32[512,256]{1,0:T(8,128)S(1)}, u32[]{:S(2)}, u32[]{:S(2)}) collective-permute-start(f32[512,256]{1,0:T(8,128)S(1)} %bitcast.67), channel_id=1, source_target_pairs={{0,1},{1,0},{2,3},{3,2},{4,5},{5,4},{6,7},{7,6},{8,9},{9,8},{10,11... | collective-permute-start | bytes 1572872 | tf_op jit(solution)/shard_map/ppermute | solution.py:127
  104.1 3.5 %collective-permute-start.17 = (f32[512,256]{1,0:T(8,128)S(1)}, f32[512,256]{1,0:T(8,128)S(1)}, u32[]{:S(2)}, u32[]{:S(2)}) collective-permute-start(f32[512,256]{1,0:T(8,128)S(1)} %bitcast_add_fusion), channel_id=1, source_target_pairs={{0,2},{2,0},{1,3},{3,1},{4,6},{6,4},{5,7},{7,5},{8,10},{10,8},{9,1... | collective-permute-start | bytes 1572872 | tf_op jit(solution)/shard_map/ppermute | solution.py:127
  107.6 2.6 %collective-permute-start.18 = (bf16[128,256]{1,0:T(8,128)(2,1)S(1)}, bf16[128,256]{1,0:T(8,128)(2,1)S(1)}, u32[]{:S(2)}, u32[]{:S(2)}) collective-permute-start(bf16[128,256]{1,0:T(8,128)(2,1)S(1)} %copy-done.6), channel_id=1, source_target_pairs={{0,1},{1,0},{2,3},{3,2},{4,5},{5,4},{6,7},{7,6},{8,9},{9,8},{10,11... | collective-permute-start | bytes 196616 | tf_op jit(solution)/shard_map/ppermute | solution.py:127
  113.1 9.0 %collective-permute-done.19 = bf16[2,128,256]{2,1,0:T(8,128)(2,1)S(1)} collective-permute-done((bf16[2,128,256]{2,1,0:T(8,128)(2,1)S(1)}, bf16[2,128,256]{2,1,0:T(8,128)(2,1)S(1)}, u32[]{:S(2)}, u32[]{:S(2)}) %collective-permute-start.19) | collective-permute-done | bytes 131104 | tf_op jit(solution)/shard_map/ppermute | solution.py:127
  123.4 6.3 %collective-permute-start.20 = (f32[16896]{0:T(1024)S(1)}, f32[16896]{0:T(1024)S(1)}, u32[]{:S(2)}, u32[]{:S(2)}) collective-permute-start(f32[16896]{0:T(1024)S(1)} %dynamic-slice_reduce_fusion), channel_id=1, source_target_pairs={{0,16},{4,20},{8,24},{12,28},{16,0},{20,4},{24,8},{28,12},{1,17},{... | collective-permute-start | bytes 202760 | tf_op jit(solution)/shard_map/ppermute | solution.py:184
  129.7 2.6 %collective-permute-done.20 = f32[16896]{0:T(1024)S(1)} collective-permute-done((f32[16896]{0:T(1024)S(1)}, f32[16896]{0:T(1024)S(1)}, u32[]{:S(2)}, u32[]{:S(2)}) %collective-permute-start.20) | collective-permute-done | bytes 67616 | tf_op jit(solution)/shard_map/ppermute | solution.py:184
  132.3 4.8 %collective-permute-start.21 = (f32[16896]{0:T(1024)S(1)}, f32[16896]{0:T(1024)S(1)}, u32[]{:S(2)}, u32[]{:S(2)}) collective-permute-start(f32[16896]{0:T(1024)S(1)} %add.315), channel_id=1, source_target_pairs={{0,8},{4,12},{8,0},{12,4},{16,24},{20,28},{24,16},{28,20},{1,9},{5... | collective-permute-start | bytes 202760 | tf_op jit(solution)/shard_map/ppermute | solution.py:184
  138.8 5.3 %collective-permute-start.22 = (f32[16896]{0:T(1024)S(1)}, f32[16896]{0:T(1024)S(1)}, u32[]{:S(2)}, u32[]{:S(2)}) collective-permute-start(f32[16896]{0:T(1024)S(1)} %add.316), channel_id=1, source_target_pairs={{0,4},{4,0},{8,12},{12,8},{16,20},{20,16},{24,28},{28,24},{1,5},{5... | collective-permute-start | bytes 202760 | tf_op jit(solution)/shard_map/ppermute | solution.py:184
  145.9 3.1 %collective-permute-start.23 = (f32[16896]{0:T(1024)S(1)}, f32[16896]{0:T(1024)S(1)}, u32[]{:S(2)}, u32[]{:S(2)}) collective-permute-start(f32[16896]{0:T(1024)S(1)} %add.317), channel_id=1, source_target_pairs={{0,64},{32,96},{64,0},{96,32},{1,65},{33,97},{65,1},{97,33},{2,66}... | collective-permute-start | bytes 202760 | tf_op jit(solution)/shard_map/ppermute | solution.py:184
  149.0 3.4 %collective-permute-done.23 = f32[16896]{0:T(1024)S(1)} collective-permute-done((f32[16896]{0:T(1024)S(1)}, f32[16896]{0:T(1024)S(1)}, u32[]{:S(2)}, u32[]{:S(2)}) %collective-permute-start.23) | collective-permute-done | bytes 67616 | tf_op jit(solution)/shard_map/ppermute | solution.py:184
  154.6 2.9 %collective-permute-done.24 = f32[16896]{0:T(1024)S(1)} collective-permute-done((f32[16896]{0:T(1024)S(1)}, f32[16896]{0:T(1024)S(1)}, u32[]{:S(2)}, u32[]{:S(2)}) %collective-permute-start.24) | collective-permute-done | bytes 67616 | tf_op jit(solution)/shard_map/ppermute | solution.py:184
  157.5 8.1 %collective-permute-start.25 = (f32[16896]{0:T(1024)S(1)}, f32[16896]{0:T(1024)S(1)}, u32[]{:S(2)}, u32[]{:S(2)}) collective-permute-start(f32[16896]{0:T(1024)S(1)} %add.319), channel_id=1, source_target_pairs={{0,256},{128,384},{256,0},{384,128},{1,257},{129,385},{257,1},{385... | collective-permute-start | bytes 202760 | tf_op jit(solution)/shard_map/ppermute | solution.py:184
  165.6 2.4 %collective-permute-done.25 = f32[16896]{0:T(1024)S(1)} collective-permute-done((f32[16896]{0:T(1024)S(1)}, f32[16896]{0:T(1024)S(1)}, u32[]{:S(2)}, u32[]{:S(2)}) %collective-permute-start.25) | collective-permute-done | bytes 67616 | tf_op jit(solution)/shard_map/ppermute | solution.py:184
  170.0 5.5 %collective-permute-done.26 = f32[16896]{0:T(1024)S(1)} collective-permute-done((f32[16896]{0:T(1024)S(1)}, f32[16896]{0:T(1024)S(1)}, u32[]{:S(2)}, u32[]{:S(2)}) %collective-permute-start.26) | collective-permute-done | bytes 67616 | tf_op jit(solution)/shard_map/ppermute | solution.py:184
  177.5 3.9 %collective-permute-done.27 = f32[16896]{0:T(1024)S(1)} collective-permute-done((f32[16896]{0:T(1024)S(1)}, f32[16896]{0:T(1024)S(1)}, u32[]{:S(2)}, u32[]{:S(2)}) %collective-permute-start.27) | collective-permute-done | bytes 67616 | tf_op jit(solution)/shard_map/ppermute | solution.py:96
  181.4 8.1 %collective-permute-start.28 = (f32[33792]{0:T(1024)S(1)}, f32[33792]{0:T(1024)S(1)}, u32[]{:S(2)}, u32[]{:S(2)}) collective-permute-start(f32[33792]{0:T(1024)S(1)} %maximum_select_fusion.2), channel_id=1, source_target_pairs={{0,1},{1,0},{2,3},{3,2},{4,5},{5,4},{6,7},{7,6},{8,9},{9,8},{10,11... | collective-permute-start | bytes 405512 | tf_op jit(solution)/shard_map/ppermute | solution.py:96
  (103 shorter events, 41.5 us)
Async XLA Ops:
  0.6 91.5 %copy-start = (bf16[1,4,8,128,128]{4,3,2,1,0:T(8,128)(2,1)S(1)}, bf16[1,4,8,128,128]{4,3,2,1,0:T(8,128)(2,1)}, u32[]{:S(2)}) copy-start(bf16[1,4,8,128,128]{4,3,2,1,0:T(8,128)(2,1)} %param.11) | copy-start | bytes 3145732
  0.6 61.4 %copy-start.1 = (bf16[128,256]{1,0:T(8,128)(2,1)S(1)}, bf16[128,256]{1,0:T(8,128)(2,1)}, u32[]{:S(2)}) copy-start(bf16[128,256]{1,0:T(8,128)(2,1)} %param.8) | copy-start | bytes 196612
  0.7 8.8 %collective-permute-start = (bf16[128,256]{1,0:T(8,128)(2,1)}, bf16[128,256]{1,0:T(8,128)(2,1)S(1)}, u32[]{:S(2)}, u32[]{:S(2)}) collective-permute-start(bf16[128,256]{1,0:T(8,128)(2,1)} %param.8), channel_id=1, source_target_pairs={{0,128},{128,256},{256,384},{384,0},{1,129},{129,257},{257,385},{3... | collective-permute-start | bytes 196616 | tf_op jit(solution)/shard_map/ppermute | solution.py:26
  5.8 8.7 %collective-permute-start.2 = (bf16[128,256]{1,0:T(8,128)(2,1)}, bf16[128,256]{1,0:T(8,128)(2,1)S(1)}, u32[]{:S(2)}, u32[]{:S(2)}) collective-permute-start(bf16[128,256]{1,0:T(8,128)(2,1)} %param.8), channel_id=1, source_target_pairs={{0,384},{128,0},{256,128},{384,256},{1,385},{129,1},{257,129},{385... | collective-permute-start | bytes 196616 | tf_op jit(solution)/shard_map/ppermute | solution.py:29
  9.4 7.1 %collective-permute-start.1 = (bf16[128,256]{1,0:T(8,128)(2,1)S(1)}, bf16[128,256]{1,0:T(8,128)(2,1)S(1)}, u32[]{:S(2)}, u32[]{:S(2)}) collective-permute-start(bf16[128,256]{1,0:T(8,128)(2,1)S(1)} %collective-permute-done), channel_id=1, source_target_pairs={{0,128},{128,256},{256,384},{384,0},{1,129},{129,257},{257,385},{3... | collective-permute-start | bytes 196616 | tf_op jit(solution)/shard_map/ppermute | solution.py:26
  14.5 47.3 %copy-start.2 = (bf16[128,256]{1,0:T(8,128)(2,1)}, bf16[128,256]{1,0:T(8,128)(2,1)S(1)}, u32[]{:S(2)}) copy-start(bf16[128,256]{1,0:T(8,128)(2,1)S(1)} %collective-permute-done.2) | copy-start | bytes 196612
  17.5 15.2 %collective-permute-start.3 = (bf16[4,128,256]{2,1,0:T(8,128)(2,1)S(1)}, bf16[4,128,256]{2,1,0:T(8,128)(2,1)S(1)}, u32[]{:S(2)}, u32[]{:S(2)}) collective-permute-start(bf16[4,128,256]{2,1,0:T(8,128)(2,1)S(1)} %pad_maximum_fusion.2), channel_id=1, source_target_pairs={{0,4},{4,8},{8,12},{12,16},{16,20},{20,24},{24,28},{28,0},{1,5},{5... | collective-permute-start | bytes 786440 | tf_op jit(solution)/shard_map/ppermute | solution.py:26
  22.7 15.9 %collective-permute-start.12 = (s32[8]{0:T(128)S(1)}, s32[8]{0:T(128)S(1)}, u32[]{:S(2)}, u32[]{:S(2)}) collective-permute-start(s32[8]{0:T(128)S(1)} %get-tuple-element.7), channel_id=1, source_target_pairs={{0,64},{32,96},{64,0},{96,32},{1,65},{33,97},{65,1},{97,33},{2,66}... | collective-permute-start | bytes 104 | tf_op jit(solution)/shard_map/ppermute | solution.py:46
  27.4 19.8 %collective-permute-start.14 = (s32[8]{0:T(128)S(1)}, s32[8]{0:T(128)S(1)}, u32[]{:S(2)}, u32[]{:S(2)}) collective-permute-start(s32[8]{0:T(128)S(1)} %get-tuple-element.7), channel_id=1, source_target_pairs={{0,96},{32,0},{64,32},{96,64},{1,97},{33,1},{65,33},{97,65},{2,98}... | collective-permute-start | bytes 104 | tf_op jit(solution)/shard_map/ppermute | solution.py:46
  30.1 17.1 %collective-permute-start.10 = (s32[8]{0:T(128)S(1)}, s32[8]{0:T(128)S(1)}, u32[]{:S(2)}, u32[]{:S(2)}) collective-permute-start(s32[8]{0:T(128)S(1)} %get-tuple-element.7), channel_id=1, source_target_pairs={{0,32},{32,64},{64,96},{96,0},{1,33},{33,65},{65,97},{97,1},{2,34}... | collective-permute-start | bytes 104 | tf_op jit(solution)/shard_map/ppermute | solution.py:46
  32.7 12.5 %collective-permute-start.4 = (bf16[4,128,256]{2,1,0:T(8,128)(2,1)S(1)}, bf16[4,128,256]{2,1,0:T(8,128)(2,1)S(1)}, u32[]{:S(2)}, u32[]{:S(2)}) collective-permute-start(bf16[4,128,256]{2,1,0:T(8,128)(2,1)S(1)} %collective-permute-done.3), channel_id=1, source_target_pairs={{0,4},{4,8},{8,12},{12,16},{16,20},{20,24},{24,28},{28,0},{1,5},{5... | collective-permute-start | bytes 786440 | tf_op jit(solution)/shard_map/ppermute | solution.py:26
  38.7 9.8 %collective-permute-start.7 = (bf16[4,128,256]{2,1,0:T(8,128)(2,1)S(1)}, bf16[4,128,256]{2,1,0:T(8,128)(2,1)S(1)}, u32[]{:S(2)}, u32[]{:S(2)}) collective-permute-start(bf16[4,128,256]{2,1,0:T(8,128)(2,1)S(1)} %pad_maximum_fusion.2), channel_id=1, source_target_pairs={{0,28},{4,0},{8,4},{12,8},{16,12},{20,16},{24,20},{28,24},{1,29},{... | collective-permute-start | bytes 786440 | tf_op jit(solution)/shard_map/ppermute | solution.py:29
  45.2 8.3 %collective-permute-start.5 = (bf16[4,128,256]{2,1,0:T(8,128)(2,1)S(1)}, bf16[4,128,256]{2,1,0:T(8,128)(2,1)S(1)}, u32[]{:S(2)}, u32[]{:S(2)}) collective-permute-start(bf16[4,128,256]{2,1,0:T(8,128)(2,1)S(1)} %collective-permute-done.4), channel_id=1, source_target_pairs={{0,4},{4,8},{8,12},{12,16},{16,20},{20,24},{24,28},{28,0},{1,5},{5... | collective-permute-start | bytes 786440 | tf_op jit(solution)/shard_map/ppermute | solution.py:26
  48.5 8.3 %collective-permute-start.8 = (bf16[4,128,256]{2,1,0:T(8,128)(2,1)S(1)}, bf16[4,128,256]{2,1,0:T(8,128)(2,1)S(1)}, u32[]{:S(2)}, u32[]{:S(2)}) collective-permute-start(bf16[4,128,256]{2,1,0:T(8,128)(2,1)S(1)} %collective-permute-done.7), channel_id=1, source_target_pairs={{0,28},{4,0},{8,4},{12,8},{16,12},{20,16},{24,20},{28,24},{1,29},{... | collective-permute-start | bytes 786440 | tf_op jit(solution)/shard_map/ppermute | solution.py:29
  53.5 8.3 %collective-permute-start.6 = (bf16[4,128,256]{2,1,0:T(8,128)(2,1)S(1)}, bf16[4,128,256]{2,1,0:T(8,128)(2,1)S(1)}, u32[]{:S(2)}, u32[]{:S(2)}) collective-permute-start(bf16[4,128,256]{2,1,0:T(8,128)(2,1)S(1)} %collective-permute-done.5), channel_id=1, source_target_pairs={{0,4},{4,8},{8,12},{12,16},{16,20},{20,24},{24,28},{28,0},{1,5},{5... | collective-permute-start | bytes 786440 | tf_op jit(solution)/shard_map/ppermute | solution.py:26
  56.8 8.6 %collective-permute-start.9 = (bf16[4,128,256]{2,1,0:T(8,128)(2,1)S(1)}, bf16[4,128,256]{2,1,0:T(8,128)(2,1)S(1)}, u32[]{:S(2)}, u32[]{:S(2)}) collective-permute-start(bf16[4,128,256]{2,1,0:T(8,128)(2,1)S(1)} %collective-permute-done.8), channel_id=1, source_target_pairs={{0,28},{4,0},{8,4},{12,8},{16,12},{20,16},{24,20},{28,24},{1,29},{... | collective-permute-start | bytes 786440 | tf_op jit(solution)/shard_map/ppermute | solution.py:29
  66.8 14.2 %collective-permute-start.13 = (bf16[8,128,256]{2,1,0:T(8,128)(2,1)}, bf16[8,128,256]{2,1,0:T(8,128)(2,1)}, u32[]{:S(2)}, u32[]{:S(2)}) collective-permute-start(bf16[8,128,256]{2,1,0:T(8,128)(2,1)} %gather_fusion.1), channel_id=1, source_target_pairs={{0,64},{32,96},{64,0},{96,32},{1,65},{33,97},{65,1},{97,33},{2,66}... | collective-permute-start | bytes 1572872 | tf_op jit(solution)/shard_map/ppermute | solution.py:65
  70.5 21.4 %collective-permute-start.15 = (bf16[8,128,256]{2,1,0:T(8,128)(2,1)}, bf16[8,128,256]{2,1,0:T(8,128)(2,1)}, u32[]{:S(2)}, u32[]{:S(2)}) collective-permute-start(bf16[8,128,256]{2,1,0:T(8,128)(2,1)} %gather_fusion.2), channel_id=1, source_target_pairs={{0,32},{32,64},{64,96},{96,0},{1,33},{33,65},{65,97},{97,1},{2,34}... | collective-permute-start | bytes 1572872 | tf_op jit(solution)/shard_map/ppermute | solution.py:65
  76.0 16.1 %collective-permute-start.11 = (bf16[8,128,256]{2,1,0:T(8,128)(2,1)}, bf16[8,128,256]{2,1,0:T(8,128)(2,1)}, u32[]{:S(2)}, u32[]{:S(2)}) collective-permute-start(bf16[8,128,256]{2,1,0:T(8,128)(2,1)} %gather_fusion), channel_id=1, source_target_pairs={{0,96},{32,0},{64,32},{96,64},{1,97},{33,1},{65,33},{97,65},{2,98}... | collective-permute-start | bytes 1572872 | tf_op jit(solution)/shard_map/ppermute | solution.py:65
  94.7 9.3 %collective-permute-start.16 = (f32[512,256]{1,0:T(8,128)S(1)}, f32[512,256]{1,0:T(8,128)S(1)}, u32[]{:S(2)}, u32[]{:S(2)}) collective-permute-start(f32[512,256]{1,0:T(8,128)S(1)} %bitcast.67), channel_id=1, source_target_pairs={{0,1},{1,0},{2,3},{3,2},{4,5},{5,4},{6,7},{7,6},{8,9},{9,8},{10,11... | collective-permute-start | bytes 1572872 | tf_op jit(solution)/shard_map/ppermute | solution.py:127
  104.1 18.0 %collective-permute-start.17 = (f32[512,256]{1,0:T(8,128)S(1)}, f32[512,256]{1,0:T(8,128)S(1)}, u32[]{:S(2)}, u32[]{:S(2)}) collective-permute-start(f32[512,256]{1,0:T(8,128)S(1)} %bitcast_add_fusion), channel_id=1, source_target_pairs={{0,2},{2,0},{1,3},{3,1},{4,6},{6,4},{5,7},{7,5},{8,10},{10,8},{9,1... | collective-permute-start | bytes 1572872 | tf_op jit(solution)/shard_map/ppermute | solution.py:127
  107.6 3.5 %collective-permute-start.18 = (bf16[128,256]{1,0:T(8,128)(2,1)S(1)}, bf16[128,256]{1,0:T(8,128)(2,1)S(1)}, u32[]{:S(2)}, u32[]{:S(2)}) collective-permute-start(bf16[128,256]{1,0:T(8,128)(2,1)S(1)} %copy-done.6), channel_id=1, source_target_pairs={{0,1},{1,0},{2,3},{3,2},{4,5},{5,4},{6,7},{7,6},{8,9},{9,8},{10,11... | collective-permute-start | bytes 196616 | tf_op jit(solution)/shard_map/ppermute | solution.py:127
  111.0 11.1 %collective-permute-start.19 = (bf16[2,128,256]{2,1,0:T(8,128)(2,1)S(1)}, bf16[2,128,256]{2,1,0:T(8,128)(2,1)S(1)}, u32[]{:S(2)}, u32[]{:S(2)}) collective-permute-start(bf16[2,128,256]{2,1,0:T(8,128)(2,1)S(1)} %maximum_select_fusion.3), channel_id=1, source_target_pairs={{0,2},{2,0},{1,3},{3,1},{4,6},{6,4},{5,7},{7,5},{8,10},{10,8},{9,1... | collective-permute-start | bytes 393224 | tf_op jit(solution)/shard_map/ppermute | solution.py:127
  123.4 9.0 %collective-permute-start.20 = (f32[16896]{0:T(1024)S(1)}, f32[16896]{0:T(1024)S(1)}, u32[]{:S(2)}, u32[]{:S(2)}) collective-permute-start(f32[16896]{0:T(1024)S(1)} %dynamic-slice_reduce_fusion), channel_id=1, source_target_pairs={{0,16},{4,20},{8,24},{12,28},{16,0},{20,4},{24,8},{28,12},{1,17},{... | collective-permute-start | bytes 202760 | tf_op jit(solution)/shard_map/ppermute | solution.py:184
  132.3 6.5 %collective-permute-start.21 = (f32[16896]{0:T(1024)S(1)}, f32[16896]{0:T(1024)S(1)}, u32[]{:S(2)}, u32[]{:S(2)}) collective-permute-start(f32[16896]{0:T(1024)S(1)} %add.315), channel_id=1, source_target_pairs={{0,8},{4,12},{8,0},{12,4},{16,24},{20,28},{24,16},{28,20},{1,9},{5... | collective-permute-start | bytes 202760 | tf_op jit(solution)/shard_map/ppermute | solution.py:184
  138.8 7.0 %collective-permute-start.22 = (f32[16896]{0:T(1024)S(1)}, f32[16896]{0:T(1024)S(1)}, u32[]{:S(2)}, u32[]{:S(2)}) collective-permute-start(f32[16896]{0:T(1024)S(1)} %add.316), channel_id=1, source_target_pairs={{0,4},{4,0},{8,12},{12,8},{16,20},{20,16},{24,28},{28,24},{1,5},{5... | collective-permute-start | bytes 202760 | tf_op jit(solution)/shard_map/ppermute | solution.py:184
  145.9 6.6 %collective-permute-start.23 = (f32[16896]{0:T(1024)S(1)}, f32[16896]{0:T(1024)S(1)}, u32[]{:S(2)}, u32[]{:S(2)}) collective-permute-start(f32[16896]{0:T(1024)S(1)} %add.317), channel_id=1, source_target_pairs={{0,64},{32,96},{64,0},{96,32},{1,65},{33,97},{65,1},{97,33},{2,66}... | collective-permute-start | bytes 202760 | tf_op jit(solution)/shard_map/ppermute | solution.py:184
  152.4 5.1 %collective-permute-start.24 = (f32[16896]{0:T(1024)S(1)}, f32[16896]{0:T(1024)S(1)}, u32[]{:S(2)}, u32[]{:S(2)}) collective-permute-start(f32[16896]{0:T(1024)S(1)} %add.318), channel_id=1, source_target_pairs={{0,32},{32,0},{64,96},{96,64},{1,33},{33,1},{65,97},{97,65},{2,34}... | collective-permute-start | bytes 202760 | tf_op jit(solution)/shard_map/ppermute | solution.py:184
  157.5 10.6 %collective-permute-start.25 = (f32[16896]{0:T(1024)S(1)}, f32[16896]{0:T(1024)S(1)}, u32[]{:S(2)}, u32[]{:S(2)}) collective-permute-start(f32[16896]{0:T(1024)S(1)} %add.319), channel_id=1, source_target_pairs={{0,256},{128,384},{256,0},{384,128},{1,257},{129,385},{257,1},{385... | collective-permute-start | bytes 202760 | tf_op jit(solution)/shard_map/ppermute | solution.py:184
  168.1 7.4 %collective-permute-start.26 = (f32[16896]{0:T(1024)S(1)}, f32[16896]{0:T(1024)S(1)}, u32[]{:S(2)}, u32[]{:S(2)}) collective-permute-start(f32[16896]{0:T(1024)S(1)} %add.320), channel_id=1, source_target_pairs={{0,128},{128,0},{256,384},{384,256},{1,129},{129,1},{257,385},{385... | collective-permute-start | bytes 202760 | tf_op jit(solution)/shard_map/ppermute | solution.py:184
  175.5 5.8 %collective-permute-start.27 = (f32[16896]{0:T(1024)S(1)}, f32[16896]{0:T(1024)S(1)}, u32[]{:S(2)}, u32[]{:S(2)}) collective-permute-start(f32[16896]{0:T(1024)S(1)} %add.321), channel_id=1, source_target_pairs={{0,2},{2,0},{1,3},{3,1},{4,6},{6,4},{5,7},{7,5},{8,10},{10,8},{9,1... | collective-permute-start | bytes 202760 | tf_op jit(solution)/shard_map/ppermute | solution.py:96
  181.4 9.1 %collective-permute-start.28 = (f32[33792]{0:T(1024)S(1)}, f32[33792]{0:T(1024)S(1)}, u32[]{:S(2)}, u32[]{:S(2)}) collective-permute-start(f32[33792]{0:T(1024)S(1)} %maximum_select_fusion.2), channel_id=1, source_target_pairs={{0,1},{1,0},{2,3},{3,2},{4,5},{5,4},{6,7},{7,6},{8,9},{9,8},{10,11... | collective-permute-start | bytes 405512 | tf_op jit(solution)/shard_map/ppermute | solution.py:96
  (8 other events, 159.1 us)

commit v10 on v9

--- a/solution.py
+++ b/solution.py
@@ -76,6 +76,16 @@
         n = lax.axis_size(a)
         for b in reversed(range(n.bit_length() - 1)):
             steps.append((a, b, [(i, i ^ (1 << b)) for i in range(n)]))
+    return steps
+
+
+def doubling_steps(axes):
+    steps = []
+    for a in axes:
+        n = lax.axis_size(a)
+        for b in range(n.bit_length() - 2):
+            steps.append((a, [(i, i ^ (1 << b)) for i in range(n)]))
+        steps.append((a, [(i, n - 1 - i) for i in range(n)]))
     return steps
 
 
@@ -180,7 +190,7 @@
     rep_steps = halving_steps(("core", "y_lo"))
     quarter = lax.axis_index("core") * lax.axis_size("y_lo") + lax.axis_index("y_lo")
     flat = lax.dynamic_index_in_dim(packed.reshape(row_count, -1), quarter, 0, keepdims=False)
-    for a, b, perm in halving_steps(ROW_AXES[::-1]):
+    for a, perm in doubling_steps(ROW_AXES[::-1]):
         flat = flat + lax.ppermute(flat, a, perm)
     packed = all_gather_flat(flat, rep_steps).reshape(packed.shape)
     weight_grad = packed[:feature_width]

time: 194 us -> 190 us (0.979)
  waiting for transfers between devices: 55 us -> 49.2 us
    ppermute x2, starting transfers between devices: 10.1 us -> 14.5 us  [all_gather_flat(): other = lax.ppermute(flat, a, perm)]
    ppermute x7, starting transfers between devices: 31.8 us -> 27.8 us  [shards(): flat = flat + lax.ppermute(flat, a, perm)]
    ppermute x7, waiting for transfers between devices: 20.2 us -> 16.5 us  [shards(): flat = flat + lax.ppermute(flat, a, perm)]
    ppermute x2, waiting for transfers between devices: 4.09 us -> 1.92 us  [all_gather_flat(): other = lax.ppermute(flat, a, perm)]
where the time goes in v10:
time: 190 us; the launch traced here: 186 us
  starting transfers between devices  118 us (62%)
  waiting for transfers between devices  49.2 us (26%)
  local copies, waits for them, and re-layouts  8.95 us (5%)
  other arithmetic  5.93 us (3%)
  matrix products  3.02 us (2%)
    ppermute x7, starting transfers between devices, shards(): flat = flat + lax.ppermute(flat, a, perm)  27.8 us
    ppermute x6, starting transfers between devices, ring_gather(): left = lax.ppermute(left, axis, fwd)  21.2 us
    ppermute x4, starting transfers between devices, ring_gather(): right = lax.ppermute(right, axis, bwd)  20.1 us
    ppermute x7, waiting for transfers between devices, shards(): flat = flat + lax.ppermute(flat, a, perm)  16.5 us
    ppermute x4, starting transfers between devices, swap(): return lax.ppermute(x, axis, [(0, 1), (1, 0)])  15.8 us
    ppermute x2, starting transfers between devices, all_gather_flat(): other = lax.ppermute(flat, a, perm)  14.5 us
    ppermute x4, waiting for transfers between devices, swap(): return lax.ppermute(x, axis, [(0, 1), (1, 0)])  11.4 us
    ppermute x3, waiting for transfers between devices, plane_blocks(): lax.ppermute(sent, across, [(i, (i + s) % n_across) for i in range(n_acro...  11.2 us
  transfers between devices with their start and end apart: 29, of which 19 were waited for; matrix products, arithmetic and copies ran while one was open for 5% of the time, Pallas kernels for 0%

profile of v10, /device:TPU:1, one launch (start us, length us, event | category | flops | bytes accessed | tf_op | source)
XLA Modules:
  0.0 186.4 jit_solution(895619652850788954)
XLA Ops:
  0.7 5.2 %collective-permute-start = (bf16[128,256]{1,0:T(8,128)(2,1)}, bf16[128,256]{1,0:T(8,128)(2,1)S(1)}, u32[]{:S(2)}, u32[]{:S(2)}) collective-permute-start(bf16[128,256]{1,0:T(8,128)(2,1)} %param.8), channel_id=1, source_target_pairs={{0,128},{128,256},{256,384},{384,0},{1,129},{129,257},{257,385},{3... | collective-permute-start | bytes 196616 | tf_op jit(solution)/shard_map/ppermute | solution.py:26
  5.8 3.6 %collective-permute-start.2 = (bf16[128,256]{1,0:T(8,128)(2,1)}, bf16[128,256]{1,0:T(8,128)(2,1)S(1)}, u32[]{:S(2)}, u32[]{:S(2)}) collective-permute-start(bf16[128,256]{1,0:T(8,128)(2,1)} %param.8), channel_id=1, source_target_pairs={{0,384},{128,0},{256,128},{384,256},{1,385},{129,1},{257,129},{385... | collective-permute-start | bytes 196616 | tf_op jit(solution)/shard_map/ppermute | solution.py:29
  9.4 4.2 %collective-permute-start.1 = (bf16[128,256]{1,0:T(8,128)(2,1)S(1)}, bf16[128,256]{1,0:T(8,128)(2,1)S(1)}, u32[]{:S(2)}, u32[]{:S(2)}) collective-permute-start(bf16[128,256]{1,0:T(8,128)(2,1)S(1)} %collective-permute-done), channel_id=1, source_target_pairs={{0,128},{128,256},{256,384},{384,0},{1,129},{129,257},{257,385},{3... | collective-permute-start | bytes 196616 | tf_op jit(solution)/shard_map/ppermute | solution.py:26
  17.5 4.0 %collective-permute-start.3 = (bf16[4,128,256]{2,1,0:T(8,128)(2,1)S(1)}, bf16[4,128,256]{2,1,0:T(8,128)(2,1)S(1)}, u32[]{:S(2)}, u32[]{:S(2)}) collective-permute-start(bf16[4,128,256]{2,1,0:T(8,128)(2,1)S(1)} %pad_maximum_fusion.2), channel_id=1, source_target_pairs={{0,4},{4,8},{8,12},{12,16},{16,20},{20,24},{24,28},{28,0},{1,5},{5... | collective-permute-start | bytes 786440 | tf_op jit(solution)/shard_map/ppermute | solution.py:26
  22.7 4.6 %collective-permute-start.12 = (s32[8]{0:T(128)S(1)}, s32[8]{0:T(128)S(1)}, u32[]{:S(2)}, u32[]{:S(2)}) collective-permute-start(s32[8]{0:T(128)S(1)} %get-tuple-element.7), channel_id=1, source_target_pairs={{0,64},{32,96},{64,0},{96,32},{1,65},{33,97},{65,1},{97,33},{2,66}... | collective-permute-start | bytes 104 | tf_op jit(solution)/shard_map/ppermute | solution.py:46
  27.4 2.8 %collective-permute-start.14 = (s32[8]{0:T(128)S(1)}, s32[8]{0:T(128)S(1)}, u32[]{:S(2)}, u32[]{:S(2)}) collective-permute-start(s32[8]{0:T(128)S(1)} %get-tuple-element.7), channel_id=1, source_target_pairs={{0,96},{32,0},{64,32},{96,64},{1,97},{33,1},{65,33},{97,65},{2,98}... | collective-permute-start | bytes 104 | tf_op jit(solution)/shard_map/ppermute | solution.py:46
  30.1 2.5 %collective-permute-start.10 = (s32[8]{0:T(128)S(1)}, s32[8]{0:T(128)S(1)}, u32[]{:S(2)}, u32[]{:S(2)}) collective-permute-start(s32[8]{0:T(128)S(1)} %get-tuple-element.7), channel_id=1, source_target_pairs={{0,32},{32,64},{64,96},{96,0},{1,33},{33,65},{65,97},{97,1},{2,34}... | collective-permute-start | bytes 104 | tf_op jit(solution)/shard_map/ppermute | solution.py:46
  32.7 4.0 %collective-permute-start.4 = (bf16[4,128,256]{2,1,0:T(8,128)(2,1)S(1)}, bf16[4,128,256]{2,1,0:T(8,128)(2,1)S(1)}, u32[]{:S(2)}, u32[]{:S(2)}) collective-permute-start(bf16[4,128,256]{2,1,0:T(8,128)(2,1)S(1)} %collective-permute-done.3), channel_id=1, source_target_pairs={{0,4},{4,8},{8,12},{12,16},{16,20},{20,24},{24,28},{28,0},{1,5},{5... | collective-permute-start | bytes 786440 | tf_op jit(solution)/shard_map/ppermute | solution.py:26
  38.7 6.5 %collective-permute-start.7 = (bf16[4,128,256]{2,1,0:T(8,128)(2,1)S(1)}, bf16[4,128,256]{2,1,0:T(8,128)(2,1)S(1)}, u32[]{:S(2)}, u32[]{:S(2)}) collective-permute-start(bf16[4,128,256]{2,1,0:T(8,128)(2,1)S(1)} %pad_maximum_fusion.2), channel_id=1, source_target_pairs={{0,28},{4,0},{8,4},{12,8},{16,12},{20,16},{24,20},{28,24},{1,29},{... | collective-permute-start | bytes 786440 | tf_op jit(solution)/shard_map/ppermute | solution.py:29
  48.5 5.0 %collective-permute-start.8 = (bf16[4,128,256]{2,1,0:T(8,128)(2,1)S(1)}, bf16[4,128,256]{2,1,0:T(8,128)(2,1)S(1)}, u32[]{:S(2)}, u32[]{:S(2)}) collective-permute-start(bf16[4,128,256]{2,1,0:T(8,128)(2,1)S(1)} %collective-permute-done.7), channel_id=1, source_target_pairs={{0,28},{4,0},{8,4},{12,8},{16,12},{20,16},{24,20},{28,24},{1,29},{... | collective-permute-start | bytes 786440 | tf_op jit(solution)/shard_map/ppermute | solution.py:29
  56.8 5.0 %collective-permute-start.9 = (bf16[4,128,256]{2,1,0:T(8,128)(2,1)S(1)}, bf16[4,128,256]{2,1,0:T(8,128)(2,1)S(1)}, u32[]{:S(2)}, u32[]{:S(2)}) collective-permute-start(bf16[4,128,256]{2,1,0:T(8,128)(2,1)S(1)} %collective-permute-done.8), channel_id=1, source_target_pairs={{0,28},{4,0},{8,4},{12,8},{16,12},{20,16},{24,20},{28,24},{1,29},{... | collective-permute-start | bytes 786440 | tf_op jit(solution)/shard_map/ppermute | solution.py:29
  62.8 2.6 %collective-permute-done.9 = bf16[4,128,256]{2,1,0:T(8,128)(2,1)S(1)} collective-permute-done((bf16[4,128,256]{2,1,0:T(8,128)(2,1)S(1)}, bf16[4,128,256]{2,1,0:T(8,128)(2,1)S(1)}, u32[]{:S(2)}, u32[]{:S(2)}) %collective-permute-start.9) | collective-permute-done | bytes 262176 | tf_op jit(solution)/shard_map/ppermute | solution.py:29
  70.5 4.2 %collective-permute-start.15 = (bf16[8,128,256]{2,1,0:T(8,128)(2,1)}, bf16[8,128,256]{2,1,0:T(8,128)(2,1)}, u32[]{:S(2)}, u32[]{:S(2)}) collective-permute-start(bf16[8,128,256]{2,1,0:T(8,128)(2,1)} %gather_fusion.2), channel_id=1, source_target_pairs={{0,32},{32,64},{64,96},{96,0},{1,33},{33,65},{65,97},{97,1},{2,34}... | collective-permute-start | bytes 1572872 | tf_op jit(solution)/shard_map/ppermute | solution.py:65
  76.0 2.3 %collective-permute-start.11 = (bf16[8,128,256]{2,1,0:T(8,128)(2,1)}, bf16[8,128,256]{2,1,0:T(8,128)(2,1)}, u32[]{:S(2)}, u32[]{:S(2)}) collective-permute-start(bf16[8,128,256]{2,1,0:T(8,128)(2,1)} %gather_fusion), channel_id=1, source_target_pairs={{0,96},{32,0},{64,32},{96,64},{1,97},{33,1},{65,33},{97,65},{2,98}... | collective-permute-start | bytes 1572872 | tf_op jit(solution)/shard_map/ppermute | solution.py:65
  81.0 10.8 %collective-permute-done.15 = bf16[8,128,256]{2,1,0:T(8,128)(2,1)} collective-permute-done((bf16[8,128,256]{2,1,0:T(8,128)(2,1)}, bf16[8,128,256]{2,1,0:T(8,128)(2,1)}, u32[]{:S(2)}, u32[]{:S(2)}) %collective-permute-start.15) | collective-permute-done | bytes 524320 | tf_op jit(solution)/shard_map/ppermute | solution.py:65
  94.7 7.8 %collective-permute-start.16 = (f32[512,256]{1,0:T(8,128)S(1)}, f32[512,256]{1,0:T(8,128)S(1)}, u32[]{:S(2)}, u32[]{:S(2)}) collective-permute-start(f32[512,256]{1,0:T(8,128)S(1)} %bitcast.67), channel_id=1, source_target_pairs={{0,1},{1,0},{2,3},{3,2},{4,5},{5,4},{6,7},{7,6},{8,9},{9,8},{10,11... | collective-permute-start | bytes 1572872 | tf_op jit(solution)/shard_map/ppermute | solution.py:137
  104.1 3.5 %collective-permute-start.17 = (f32[512,256]{1,0:T(8,128)S(1)}, f32[512,256]{1,0:T(8,128)S(1)}, u32[]{:S(2)}, u32[]{:S(2)}) collective-permute-start(f32[512,256]{1,0:T(8,128)S(1)} %bitcast_add_fusion), channel_id=1, source_target_pairs={{0,2},{2,0},{1,3},{3,1},{4,6},{6,4},{5,7},{7,5},{8,10},{10,8},{9,1... | collective-permute-start | bytes 1572872 | tf_op jit(solution)/shard_map/ppermute | solution.py:137
  107.6 2.6 %collective-permute-start.18 = (bf16[128,256]{1,0:T(8,128)(2,1)S(1)}, bf16[128,256]{1,0:T(8,128)(2,1)S(1)}, u32[]{:S(2)}, u32[]{:S(2)}) collective-permute-start(bf16[128,256]{1,0:T(8,128)(2,1)S(1)} %copy-done.6), channel_id=1, source_target_pairs={{0,1},{1,0},{2,3},{3,2},{4,5},{5,4},{6,7},{7,6},{8,9},{9,8},{10,11... | collective-permute-start | bytes 196616 | tf_op jit(solution)/shard_map/ppermute | solution.py:137
  113.1 9.0 %collective-permute-done.19 = bf16[2,128,256]{2,1,0:T(8,128)(2,1)S(1)} collective-permute-done((bf16[2,128,256]{2,1,0:T(8,128)(2,1)S(1)}, bf16[2,128,256]{2,1,0:T(8,128)(2,1)S(1)}, u32[]{:S(2)}, u32[]{:S(2)}) %collective-permute-start.19) | collective-permute-done | bytes 131104 | tf_op jit(solution)/shard_map/ppermute | solution.py:137
  123.4 2.6 %collective-permute-start.20 = (f32[16896]{0:T(1024)S(1)}, f32[16896]{0:T(1024)S(1)}, u32[]{:S(2)}, u32[]{:S(2)}) collective-permute-start(f32[16896]{0:T(1024)S(1)} %dynamic-slice_reduce_fusion), channel_id=1, source_target_pairs={{0,4},{4,0},{8,12},{12,8},{16,20},{20,16},{24,28},{28,24},{1,5},{5... | collective-permute-start | bytes 202760 | tf_op jit(solution)/shard_map/ppermute | solution.py:194
  126.0 2.4 %collective-permute-done.20 = f32[16896]{0:T(1024)S(1)} collective-permute-done((f32[16896]{0:T(1024)S(1)}, f32[16896]{0:T(1024)S(1)}, u32[]{:S(2)}, u32[]{:S(2)}) %collective-permute-start.20) | collective-permute-done | bytes 67616 | tf_op jit(solution)/shard_map/ppermute | solution.py:194
  128.4 6.4 %collective-permute-start.21 = (f32[16896]{0:T(1024)S(1)}, f32[16896]{0:T(1024)S(1)}, u32[]{:S(2)}, u32[]{:S(2)}) collective-permute-start(f32[16896]{0:T(1024)S(1)} %add.315), channel_id=1, source_target_pairs={{0,8},{4,12},{8,0},{12,4},{16,24},{20,28},{24,16},{28,20},{1,9},{5... | collective-permute-start | bytes 202760 | tf_op jit(solution)/shard_map/ppermute | solution.py:194
  136.5 3.7 %collective-permute-start.22 = (f32[16896]{0:T(1024)S(1)}, f32[16896]{0:T(1024)S(1)}, u32[]{:S(2)}, u32[]{:S(2)}) collective-permute-start(f32[16896]{0:T(1024)S(1)} %add.316), channel_id=1, source_target_pairs={{0,28},{4,24},{8,20},{12,16},{16,12},{20,8},{24,4},{28,0},{1,29},{... | collective-permute-start | bytes 202760 | tf_op jit(solution)/shard_map/ppermute | solution.py:194
  140.3 2.5 %collective-permute-done.22 = f32[16896]{0:T(1024)S(1)} collective-permute-done((f32[16896]{0:T(1024)S(1)}, f32[16896]{0:T(1024)S(1)}, u32[]{:S(2)}, u32[]{:S(2)}) %collective-permute-start.22) | collective-permute-done | bytes 67616 | tf_op jit(solution)/shard_map/ppermute | solution.py:194
  144.9 2.9 %collective-permute-done.23 = f32[16896]{0:T(1024)S(1)} collective-permute-done((f32[16896]{0:T(1024)S(1)}, f32[16896]{0:T(1024)S(1)}, u32[]{:S(2)}, u32[]{:S(2)}) %collective-permute-start.23) | collective-permute-done | bytes 67616 | tf_op jit(solution)/shard_map/ppermute | solution.py:194
  147.9 3.9 %collective-permute-start.24 = (f32[16896]{0:T(1024)S(1)}, f32[16896]{0:T(1024)S(1)}, u32[]{:S(2)}, u32[]{:S(2)}) collective-permute-start(f32[16896]{0:T(1024)S(1)} %add.318), channel_id=1, source_target_pairs={{0,96},{32,64},{64,32},{96,0},{1,97},{33,65},{65,33},{97,1},{2,98}... | collective-permute-start | bytes 202760 | tf_op jit(solution)/shard_map/ppermute | solution.py:194
  151.8 2.4 %collective-permute-done.24 = f32[16896]{0:T(1024)S(1)} collective-permute-done((f32[16896]{0:T(1024)S(1)}, f32[16896]{0:T(1024)S(1)}, u32[]{:S(2)}, u32[]{:S(2)}) %collective-permute-start.24) | collective-permute-done | bytes 67616 | tf_op jit(solution)/shard_map/ppermute | solution.py:194
  154.2 3.0 %collective-permute-start.25 = (f32[16896]{0:T(1024)S(1)}, f32[16896]{0:T(1024)S(1)}, u32[]{:S(2)}, u32[]{:S(2)}) collective-permute-start(f32[16896]{0:T(1024)S(1)} %add.319), channel_id=1, source_target_pairs={{0,128},{128,0},{256,384},{384,256},{1,129},{129,1},{257,385},{385... | collective-permute-start | bytes 202760 | tf_op jit(solution)/shard_map/ppermute | solution.py:194
  157.2 2.9 %collective-permute-done.25 = f32[16896]{0:T(1024)S(1)} collective-permute-done((f32[16896]{0:T(1024)S(1)}, f32[16896]{0:T(1024)S(1)}, u32[]{:S(2)}, u32[]{:S(2)}) %collective-permute-start.25) | collective-permute-done | bytes 67616 | tf_op jit(solution)/shard_map/ppermute | solution.py:194
  160.1 6.0 %collective-permute-start.26 = (f32[16896]{0:T(1024)S(1)}, f32[16896]{0:T(1024)S(1)}, u32[]{:S(2)}, u32[]{:S(2)}) collective-permute-start(f32[16896]{0:T(1024)S(1)} %add.320), channel_id=1, source_target_pairs={{0,384},{128,256},{256,128},{384,0},{1,385},{129,257},{257,129},{3... | collective-permute-start | bytes 202760 | tf_op jit(solution)/shard_map/ppermute | solution.py:194
  167.8 3.8 %collective-permute-start.27 = (f32[16896]{0:T(1024)S(1)}, f32[16896]{0:T(1024)S(1)}, u32[]{:S(2)}, u32[]{:S(2)}) collective-permute-start(f32[16896]{0:T(1024)S(1)} %add.321), channel_id=1, source_target_pairs={{0,2},{2,0},{1,3},{3,1},{4,6},{6,4},{5,7},{7,5},{8,10},{10,8},{9,1... | collective-permute-start | bytes 202760 | tf_op jit(solution)/shard_map/ppermute | solution.py:106
  173.4 10.7 %collective-permute-start.28 = (f32[33792]{0:T(1024)S(1)}, f32[33792]{0:T(1024)S(1)}, u32[]{:S(2)}, u32[]{:S(2)}) collective-permute-start(f32[33792]{0:T(1024)S(1)} %maximum_select_fusion.2), channel_id=1, source_target_pairs={{0,1},{1,0},{2,3},{3,2},{4,5},{5,4},{6,7},{7,6},{8,9},{9,8},{10,11... | collective-permute-start | bytes 405512 | tf_op jit(solution)/shard_map/ppermute | solution.py:106
  (103 shorter events, 41.6 us)
Async XLA Ops:
  0.6 91.5 %copy-start = (bf16[1,4,8,128,128]{4,3,2,1,0:T(8,128)(2,1)S(1)}, bf16[1,4,8,128,128]{4,3,2,1,0:T(8,128)(2,1)}, u32[]{:S(2)}) copy-start(bf16[1,4,8,128,128]{4,3,2,1,0:T(8,128)(2,1)} %param.11) | copy-start | bytes 3145732
  0.6 61.4 %copy-start.1 = (bf16[128,256]{1,0:T(8,128)(2,1)S(1)}, bf16[128,256]{1,0:T(8,128)(2,1)}, u32[]{:S(2)}) copy-start(bf16[128,256]{1,0:T(8,128)(2,1)} %param.8) | copy-start | bytes 196612
  0.7 8.8 %collective-permute-start = (bf16[128,256]{1,0:T(8,128)(2,1)}, bf16[128,256]{1,0:T(8,128)(2,1)S(1)}, u32[]{:S(2)}, u32[]{:S(2)}) collective-permute-start(bf16[128,256]{1,0:T(8,128)(2,1)} %param.8), channel_id=1, source_target_pairs={{0,128},{128,256},{256,384},{384,0},{1,129},{129,257},{257,385},{3... | collective-permute-start | bytes 196616 | tf_op jit(solution)/shard_map/ppermute | solution.py:26
  5.8 8.7 %collective-permute-start.2 = (bf16[128,256]{1,0:T(8,128)(2,1)}, bf16[128,256]{1,0:T(8,128)(2,1)S(1)}, u32[]{:S(2)}, u32[]{:S(2)}) collective-permute-start(bf16[128,256]{1,0:T(8,128)(2,1)} %param.8), channel_id=1, source_target_pairs={{0,384},{128,0},{256,128},{384,256},{1,385},{129,1},{257,129},{385... | collective-permute-start | bytes 196616 | tf_op jit(solution)/shard_map/ppermute | solution.py:29
  9.4 7.1 %collective-permute-start.1 = (bf16[128,256]{1,0:T(8,128)(2,1)S(1)}, bf16[128,256]{1,0:T(8,128)(2,1)S(1)}, u32[]{:S(2)}, u32[]{:S(2)}) collective-permute-start(bf16[128,256]{1,0:T(8,128)(2,1)S(1)} %collective-permute-done), channel_id=1, source_target_pairs={{0,128},{128,256},{256,384},{384,0},{1,129},{129,257},{257,385},{3... | collective-permute-start | bytes 196616 | tf_op jit(solution)/shard_map/ppermute | solution.py:26
  14.5 47.3 %copy-start.2 = (bf16[128,256]{1,0:T(8,128)(2,1)}, bf16[128,256]{1,0:T(8,128)(2,1)S(1)}, u32[]{:S(2)}) copy-start(bf16[128,256]{1,0:T(8,128)(2,1)S(1)} %collective-permute-done.2) | copy-start | bytes 196612
  17.5 15.2 %collective-permute-start.3 = (bf16[4,128,256]{2,1,0:T(8,128)(2,1)S(1)}, bf16[4,128,256]{2,1,0:T(8,128)(2,1)S(1)}, u32[]{:S(2)}, u32[]{:S(2)}) collective-permute-start(bf16[4,128,256]{2,1,0:T(8,128)(2,1)S(1)} %pad_maximum_fusion.2), channel_id=1, source_target_pairs={{0,4},{4,8},{8,12},{12,16},{16,20},{20,24},{24,28},{28,0},{1,5},{5... | collective-permute-start | bytes 786440 | tf_op jit(solution)/shard_map/ppermute | solution.py:26
  22.7 15.9 %collective-permute-start.12 = (s32[8]{0:T(128)S(1)}, s32[8]{0:T(128)S(1)}, u32[]{:S(2)}, u32[]{:S(2)}) collective-permute-start(s32[8]{0:T(128)S(1)} %get-tuple-element.7), channel_id=1, source_target_pairs={{0,64},{32,96},{64,0},{96,32},{1,65},{33,97},{65,1},{97,33},{2,66}... | collective-permute-start | bytes 104 | tf_op jit(solution)/shard_map/ppermute | solution.py:46
  27.4 19.8 %collective-permute-start.14 = (s32[8]{0:T(128)S(1)}, s32[8]{0:T(128)S(1)}, u32[]{:S(2)}, u32[]{:S(2)}) collective-permute-start(s32[8]{0:T(128)S(1)} %get-tuple-element.7), channel_id=1, source_target_pairs={{0,96},{32,0},{64,32},{96,64},{1,97},{33,1},{65,33},{97,65},{2,98}... | collective-permute-start | bytes 104 | tf_op jit(solution)/shard_map/ppermute | solution.py:46
  30.1 17.1 %collective-permute-start.10 = (s32[8]{0:T(128)S(1)}, s32[8]{0:T(128)S(1)}, u32[]{:S(2)}, u32[]{:S(2)}) collective-permute-start(s32[8]{0:T(128)S(1)} %get-tuple-element.7), channel_id=1, source_target_pairs={{0,32},{32,64},{64,96},{96,0},{1,33},{33,65},{65,97},{97,1},{2,34}... | collective-permute-start | bytes 104 | tf_op jit(solution)/shard_map/ppermute | solution.py:46
  32.7 12.5 %collective-permute-start.4 = (bf16[4,128,256]{2,1,0:T(8,128)(2,1)S(1)}, bf16[4,128,256]{2,1,0:T(8,128)(2,1)S(1)}, u32[]{:S(2)}, u32[]{:S(2)}) collective-permute-start(bf16[4,128,256]{2,1,0:T(8,128)(2,1)S(1)} %collective-permute-done.3), channel_id=1, source_target_pairs={{0,4},{4,8},{8,12},{12,16},{16,20},{20,24},{24,28},{28,0},{1,5},{5... | collective-permute-start | bytes 786440 | tf_op jit(solution)/shard_map/ppermute | solution.py:26
  38.7 9.8 %collective-permute-start.7 = (bf16[4,128,256]{2,1,0:T(8,128)(2,1)S(1)}, bf16[4,128,256]{2,1,0:T(8,128)(2,1)S(1)}, u32[]{:S(2)}, u32[]{:S(2)}) collective-permute-start(bf16[4,128,256]{2,1,0:T(8,128)(2,1)S(1)} %pad_maximum_fusion.2), channel_id=1, source_target_pairs={{0,28},{4,0},{8,4},{12,8},{16,12},{20,16},{24,20},{28,24},{1,29},{... | collective-permute-start | bytes 786440 | tf_op jit(solution)/shard_map/ppermute | solution.py:29
  45.2 8.3 %collective-permute-start.5 = (bf16[4,128,256]{2,1,0:T(8,128)(2,1)S(1)}, bf16[4,128,256]{2,1,0:T(8,128)(2,1)S(1)}, u32[]{:S(2)}, u32[]{:S(2)}) collective-permute-start(bf16[4,128,256]{2,1,0:T(8,128)(2,1)S(1)} %collective-permute-done.4), channel_id=1, source_target_pairs={{0,4},{4,8},{8,12},{12,16},{16,20},{20,24},{24,28},{28,0},{1,5},{5... | collective-permute-start | bytes 786440 | tf_op jit(solution)/shard_map/ppermute | solution.py:26
  48.5 8.3 %collective-permute-start.8 = (bf16[4,128,256]{2,1,0:T(8,128)(2,1)S(1)}, bf16[4,128,256]{2,1,0:T(8,128)(2,1)S(1)}, u32[]{:S(2)}, u32[]{:S(2)}) collective-permute-start(bf16[4,128,256]{2,1,0:T(8,128)(2,1)S(1)} %collective-permute-done.7), channel_id=1, source_target_pairs={{0,28},{4,0},{8,4},{12,8},{16,12},{20,16},{24,20},{28,24},{1,29},{... | collective-permute-start | bytes 786440 | tf_op jit(solution)/shard_map/ppermute | solution.py:29
  53.5 8.3 %collective-permute-start.6 = (bf16[4,128,256]{2,1,0:T(8,128)(2,1)S(1)}, bf16[4,128,256]{2,1,0:T(8,128)(2,1)S(1)}, u32[]{:S(2)}, u32[]{:S(2)}) collective-permute-start(bf16[4,128,256]{2,1,0:T(8,128)(2,1)S(1)} %collective-permute-done.5), channel_id=1, source_target_pairs={{0,4},{4,8},{8,12},{12,16},{16,20},{20,24},{24,28},{28,0},{1,5},{5... | collective-permute-start | bytes 786440 | tf_op jit(solution)/shard_map/ppermute | solution.py:26
  56.8 8.6 %collective-permute-start.9 = (bf16[4,128,256]{2,1,0:T(8,128)(2,1)S(1)}, bf16[4,128,256]{2,1,0:T(8,128)(2,1)S(1)}, u32[]{:S(2)}, u32[]{:S(2)}) collective-permute-start(bf16[4,128,256]{2,1,0:T(8,128)(2,1)S(1)} %collective-permute-done.8), channel_id=1, source_target_pairs={{0,28},{4,0},{8,4},{12,8},{16,12},{20,16},{24,20},{28,24},{1,29},{... | collective-permute-start | bytes 786440 | tf_op jit(solution)/shard_map/ppermute | solution.py:29
  66.8 14.2 %collective-permute-start.13 = (bf16[8,128,256]{2,1,0:T(8,128)(2,1)}, bf16[8,128,256]{2,1,0:T(8,128)(2,1)}, u32[]{:S(2)}, u32[]{:S(2)}) collective-permute-start(bf16[8,128,256]{2,1,0:T(8,128)(2,1)} %gather_fusion.1), channel_id=1, source_target_pairs={{0,64},{32,96},{64,0},{96,32},{1,65},{33,97},{65,1},{97,33},{2,66}... | collective-permute-start | bytes 1572872 | tf_op jit(solution)/shard_map/ppermute | solution.py:65
  70.5 21.4 %collective-permute-start.15 = (bf16[8,128,256]{2,1,0:T(8,128)(2,1)}, bf16[8,128,256]{2,1,0:T(8,128)(2,1)}, u32[]{:S(2)}, u32[]{:S(2)}) collective-permute-start(bf16[8,128,256]{2,1,0:T(8,128)(2,1)} %gather_fusion.2), channel_id=1, source_target_pairs={{0,32},{32,64},{64,96},{96,0},{1,33},{33,65},{65,97},{97,1},{2,34}... | collective-permute-start | bytes 1572872 | tf_op jit(solution)/shard_map/ppermute | solution.py:65
  76.0 16.1 %collective-permute-start.11 = (bf16[8,128,256]{2,1,0:T(8,128)(2,1)}, bf16[8,128,256]{2,1,0:T(8,128)(2,1)}, u32[]{:S(2)}, u32[]{:S(2)}) collective-permute-start(bf16[8,128,256]{2,1,0:T(8,128)(2,1)} %gather_fusion), channel_id=1, source_target_pairs={{0,96},{32,0},{64,32},{96,64},{1,97},{33,1},{65,33},{97,65},{2,98}... | collective-permute-start | bytes 1572872 | tf_op jit(solution)/shard_map/ppermute | solution.py:65
  94.7 9.3 %collective-permute-start.16 = (f32[512,256]{1,0:T(8,128)S(1)}, f32[512,256]{1,0:T(8,128)S(1)}, u32[]{:S(2)}, u32[]{:S(2)}) collective-permute-start(f32[512,256]{1,0:T(8,128)S(1)} %bitcast.67), channel_id=1, source_target_pairs={{0,1},{1,0},{2,3},{3,2},{4,5},{5,4},{6,7},{7,6},{8,9},{9,8},{10,11... | collective-permute-start | bytes 1572872 | tf_op jit(solution)/shard_map/ppermute | solution.py:137
  104.1 18.0 %collective-permute-start.17 = (f32[512,256]{1,0:T(8,128)S(1)}, f32[512,256]{1,0:T(8,128)S(1)}, u32[]{:S(2)}, u32[]{:S(2)}) collective-permute-start(f32[512,256]{1,0:T(8,128)S(1)} %bitcast_add_fusion), channel_id=1, source_target_pairs={{0,2},{2,0},{1,3},{3,1},{4,6},{6,4},{5,7},{7,5},{8,10},{10,8},{9,1... | collective-permute-start | bytes 1572872 | tf_op jit(solution)/shard_map/ppermute | solution.py:137
  107.6 3.5 %collective-permute-start.18 = (bf16[128,256]{1,0:T(8,128)(2,1)S(1)}, bf16[128,256]{1,0:T(8,128)(2,1)S(1)}, u32[]{:S(2)}, u32[]{:S(2)}) collective-permute-start(bf16[128,256]{1,0:T(8,128)(2,1)S(1)} %copy-done.6), channel_id=1, source_target_pairs={{0,1},{1,0},{2,3},{3,2},{4,5},{5,4},{6,7},{7,6},{8,9},{9,8},{10,11... | collective-permute-start | bytes 196616 | tf_op jit(solution)/shard_map/ppermute | solution.py:137
  111.0 11.1 %collective-permute-start.19 = (bf16[2,128,256]{2,1,0:T(8,128)(2,1)S(1)}, bf16[2,128,256]{2,1,0:T(8,128)(2,1)S(1)}, u32[]{:S(2)}, u32[]{:S(2)}) collective-permute-start(bf16[2,128,256]{2,1,0:T(8,128)(2,1)S(1)} %maximum_select_fusion.3), channel_id=1, source_target_pairs={{0,2},{2,0},{1,3},{3,1},{4,6},{6,4},{5,7},{7,5},{8,10},{10,8},{9,1... | collective-permute-start | bytes 393224 | tf_op jit(solution)/shard_map/ppermute | solution.py:137
  123.4 5.1 %collective-permute-start.20 = (f32[16896]{0:T(1024)S(1)}, f32[16896]{0:T(1024)S(1)}, u32[]{:S(2)}, u32[]{:S(2)}) collective-permute-start(f32[16896]{0:T(1024)S(1)} %dynamic-slice_reduce_fusion), channel_id=1, source_target_pairs={{0,4},{4,0},{8,12},{12,8},{16,20},{20,16},{24,28},{28,24},{1,5},{5... | collective-permute-start | bytes 202760 | tf_op jit(solution)/shard_map/ppermute | solution.py:194
  128.4 8.1 %collective-permute-start.21 = (f32[16896]{0:T(1024)S(1)}, f32[16896]{0:T(1024)S(1)}, u32[]{:S(2)}, u32[]{:S(2)}) collective-permute-start(f32[16896]{0:T(1024)S(1)} %add.315), channel_id=1, source_target_pairs={{0,8},{4,12},{8,0},{12,4},{16,24},{20,28},{24,16},{28,20},{1,9},{5... | collective-permute-start | bytes 202760 | tf_op jit(solution)/shard_map/ppermute | solution.py:194
  136.5 6.3 %collective-permute-start.22 = (f32[16896]{0:T(1024)S(1)}, f32[16896]{0:T(1024)S(1)}, u32[]{:S(2)}, u32[]{:S(2)}) collective-permute-start(f32[16896]{0:T(1024)S(1)} %add.316), channel_id=1, source_target_pairs={{0,28},{4,24},{8,20},{12,16},{16,12},{20,8},{24,4},{28,0},{1,29},{... | collective-permute-start | bytes 202760 | tf_op jit(solution)/shard_map/ppermute | solution.py:194
  142.8 5.1 %collective-permute-start.23 = (f32[16896]{0:T(1024)S(1)}, f32[16896]{0:T(1024)S(1)}, u32[]{:S(2)}, u32[]{:S(2)}) collective-permute-start(f32[16896]{0:T(1024)S(1)} %add.317), channel_id=1, source_target_pairs={{0,32},{32,0},{64,96},{96,64},{1,33},{33,1},{65,97},{97,65},{2,34}... | collective-permute-start | bytes 202760 | tf_op jit(solution)/shard_map/ppermute | solution.py:194
  147.9 6.3 %collective-permute-start.24 = (f32[16896]{0:T(1024)S(1)}, f32[16896]{0:T(1024)S(1)}, u32[]{:S(2)}, u32[]{:S(2)}) collective-permute-start(f32[16896]{0:T(1024)S(1)} %add.318), channel_id=1, source_target_pairs={{0,96},{32,64},{64,32},{96,0},{1,97},{33,65},{65,33},{97,1},{2,98}... | collective-permute-start | bytes 202760 | tf_op jit(solution)/shard_map/ppermute | solution.py:194
  154.2 6.0 %collective-permute-start.25 = (f32[16896]{0:T(1024)S(1)}, f32[16896]{0:T(1024)S(1)}, u32[]{:S(2)}, u32[]{:S(2)}) collective-permute-start(f32[16896]{0:T(1024)S(1)} %add.319), channel_id=1, source_target_pairs={{0,128},{128,0},{256,384},{384,256},{1,129},{129,1},{257,385},{385... | collective-permute-start | bytes 202760 | tf_op jit(solution)/shard_map/ppermute | solution.py:194
  160.1 7.7 %collective-permute-start.26 = (f32[16896]{0:T(1024)S(1)}, f32[16896]{0:T(1024)S(1)}, u32[]{:S(2)}, u32[]{:S(2)}) collective-permute-start(f32[16896]{0:T(1024)S(1)} %add.320), channel_id=1, source_target_pairs={{0,384},{128,256},{256,128},{384,0},{1,385},{129,257},{257,129},{3... | collective-permute-start | bytes 202760 | tf_op jit(solution)/shard_map/ppermute | solution.py:194
  167.8 5.5 %collective-permute-start.27 = (f32[16896]{0:T(1024)S(1)}, f32[16896]{0:T(1024)S(1)}, u32[]{:S(2)}, u32[]{:S(2)}) collective-permute-start(f32[16896]{0:T(1024)S(1)} %add.321), channel_id=1, source_target_pairs={{0,2},{2,0},{1,3},{3,1},{4,6},{6,4},{5,7},{7,5},{8,10},{10,8},{9,1... | collective-permute-start | bytes 202760 | tf_op jit(solution)/shard_map/ppermute | solution.py:106
  173.4 11.7 %collective-permute-start.28 = (f32[33792]{0:T(1024)S(1)}, f32[33792]{0:T(1024)S(1)}, u32[]{:S(2)}, u32[]{:S(2)}) collective-permute-start(f32[33792]{0:T(1024)S(1)} %maximum_select_fusion.2), channel_id=1, source_target_pairs={{0,1},{1,0},{2,3},{3,2},{4,5},{5,4},{6,7},{7,6},{8,9},{9,8},{10,11... | collective-permute-start | bytes 405512 | tf_op jit(solution)/shard_map/ppermute | solution.py:106
  (8 other events, 159.1 us)

commit v11 on v10

--- a/solution.py
+++ b/solution.py
@@ -40,14 +40,15 @@
     return coords
 
 
-def plane_blocks(features, cols, across="x", within=("y_hi", "z")):
+def plane_blocks(features, cols, extra, across="x", within=("y_hi", "z")):
     n_across = lax.axis_size(across)
     peer_cols = {
         s: lax.ppermute(cols, across, [(i, (i - s) % n_across) for i in range(n_across)])
         for s in range(1, n_across)
     }
-    stack = features
-    for a in within:
+    stack = ring_gather(features, within[0])
+    stack, peer_cols, extra = lax.optimization_barrier((stack, peer_cols, extra))
+    for a in within[1:]:
         stack = ring_gather(stack, a)
     plane = stack.reshape(-1, features.shape[0], features.shape[1])
 
@@ -67,7 +68,7 @@
     picked = copies[0]
     for s in range(1, n_across):
         picked = jnp.where((source == s)[:, None, None], copies[s], picked)
-    return picked
+    return picked, extra
 
 
 def halving_steps(axes):
@@ -164,7 +165,8 @@
     own_cols = lax.dynamic_index_in_dim(tile_col[0], rep_index, 0, keepdims=False)
     own_count = lax.dynamic_index_in_dim(tile_count[0], rep_index, 0, keepdims=False)
     capacity = own_rows.shape[0]
-    picked = plane_blocks(features, own_cols)
+    group_grad_out = gather_over_rep(grad_out)
+    picked, group_grad_out = plane_blocks(features, own_cols, group_grad_out)
     product = jnp.einsum("tij,tjf->tif", own_tiles, picked, preferred_element_type=jnp.float32)
     live = jnp.arange(capacity, dtype=jnp.int32) < own_count
     local_ids = jnp.arange(row_count, dtype=jnp.int32)
@@ -172,7 +174,6 @@
     partial_value = jnp.einsum("bt,tif->bif", select, product)
     partial_value = partial_value.reshape(row_count * block_size, feature_width)
     propagated = sum_over_rep(partial_value).astype(jnp.bfloat16)
-    group_grad_out = gather_over_rep(grad_out)
     preact = jnp.dot(propagated, weight, preferred_element_type=jnp.float32) + bias_terms
     sigma = jax.nn.sigmoid(preact)
     layer_out = (preact * sigma).astype(jnp.bfloat16)

time: 190 us -> 197 us (1.037)
  waiting for transfers between devices: 49.2 us -> 62.8 us
  starting transfers between devices: 118 us -> 111 us
    ppermute x6, waiting for transfers between devices: 2.09 us -> 10.8 us  [ring_gather(): left = lax.ppermute(left, axis, fwd)]
    ppermute x6, starting transfers between devices: 21.2 us -> 12.7 us  [ring_gather(): left = lax.ppermute(left, axis, fwd)]
    ppermute x4, starting transfers between devices: 15.8 us -> 21 us  [swap(): return lax.ppermute(x, axis, [(0, 1), (1, 0)])]
    ppermute x3, starting transfers between devices: 9.92 us -> 7.2 us  [plane_blocks(): lax.ppermute(cols, across, [(i, (i - s) % n_across) for i in range(n_acro...]
    ppermute x4, waiting for transfers between devices: 6.03 us -> 3.75 us  [ring_gather(): right = lax.ppermute(right, axis, bwd)]
    ppermute x3, waiting for transfers between devices: 11.2 us -> 13.2 us  [plane_blocks(): lax.ppermute(sent, across, [(i, (i + s) % n_across) for i in range(n_acro...]
    ppermute x4, waiting for transfers between devices: 11.4 us -> 13.4 us  [swap(): return lax.ppermute(x, axis, [(0, 1), (1, 0)])]
  transfers between devices with their start and end apart: 29 -> 29, of which waited for: 19 -> 18; matrix products, arithmetic and copies ran while one was open for 5% -> 7% of each run, Pallas kernels for 0% -> 0%
where the time goes in v11:
time: 197 us; the launch traced here: 195 us
  starting transfers between devices  111 us (56%)
  waiting for transfers between devices  62.8 us (32%)
  local copies, waits for them, and re-layouts  10.1 us (5%)
  other arithmetic  7.27 us (4%)
  matrix products  2.85 us (1%)
    ppermute x7, starting transfers between devices, shards(): flat = flat + lax.ppermute(flat, a, perm)  26.2 us
    ppermute x4, starting transfers between devices, swap(): return lax.ppermute(x, axis, [(0, 1), (1, 0)])  21 us
    ppermute x4, starting transfers between devices, ring_gather(): right = lax.ppermute(right, axis, bwd)  20.1 us
    ppermute x7, waiting for transfers between devices, shards(): flat = flat + lax.ppermute(flat, a, perm)  18 us
    ppermute x2, starting transfers between devices, all_gather_flat(): other = lax.ppermute(flat, a, perm)  14.8 us
    ppermute x4, waiting for transfers between devices, swap(): return lax.ppermute(x, axis, [(0, 1), (1, 0)])  13.4 us
    ppermute x3, waiting for transfers between devices, plane_blocks(): lax.ppermute(sent, across, [(i, (i + s) % n_across) for i in range(n_acro...  13.2 us
    ppermute x6, starting transfers between devices, ring_gather(): left = lax.ppermute(left, axis, fwd)  12.7 us
  transfers between devices with their start and end apart: 29, of which 18 were waited for; matrix products, arithmetic and copies ran while one was open for 7% of the time, Pallas kernels for 0%

profile of v11, /device:TPU:1, one launch (start us, length us, event | category | flops | bytes accessed | tf_op | source)
XLA Modules:
  0.0 195.2 jit_solution(8777815670502274561)
XLA Ops:
  0.6 8.9 %collective-permute-start.6 = (bf16[128,256]{1,0:T(8,128)(2,1)}, bf16[128,256]{1,0:T(8,128)(2,1)S(1)}, u32[]{:S(2)}, u32[]{:S(2)}) collective-permute-start(bf16[128,256]{1,0:T(8,128)(2,1)} %param.15), channel_id=1, source_target_pairs={{0,1},{1,0},{2,3},{3,2},{4,5},{5,4},{6,7},{7,6},{8,9},{9,8},{10,11... | collective-permute-start | bytes 196616 | tf_op jit(solution)/shard_map/ppermute | solution.py:138
  11.5 5.5 %collective-permute-start.2 = (bf16[128,256]{1,0:T(8,128)(2,1)}, bf16[128,256]{1,0:T(8,128)(2,1)S(1)}, u32[]{:S(2)}, u32[]{:S(2)}) collective-permute-start(bf16[128,256]{1,0:T(8,128)(2,1)} %param.8), channel_id=1, source_target_pairs={{0,384},{128,0},{256,128},{384,256},{1,385},{129,1},{257,129},{385... | collective-permute-start | bytes 196616 | tf_op jit(solution)/shard_map/ppermute | solution.py:29
  24.4 2.2 %collective-permute-start.4 = (s32[8]{0:T(128)S(1)}, s32[8]{0:T(128)S(1)}, u32[]{:S(2)}, u32[]{:S(2)}) collective-permute-start(s32[8]{0:T(128)S(1)} %get-tuple-element.17), channel_id=1, source_target_pairs={{0,64},{32,96},{64,0},{96,32},{1,65},{33,97},{65,1},{97,33},{2,66}... | collective-permute-start | bytes 104 | tf_op jit(solution)/shard_map/ppermute | solution.py:46
  26.6 3.1 %collective-permute-start.5 = (s32[8]{0:T(128)S(1)}, s32[8]{0:T(128)S(1)}, u32[]{:S(2)}, u32[]{:S(2)}) collective-permute-start(s32[8]{0:T(128)S(1)} %get-tuple-element.17), channel_id=1, source_target_pairs={{0,32},{32,64},{64,96},{96,0},{1,33},{33,65},{65,97},{97,1},{2,34}... | collective-permute-start | bytes 104 | tf_op jit(solution)/shard_map/ppermute | solution.py:46
  33.1 3.1 %collective-permute-start.8 = (bf16[4,128,256]{2,1,0:T(8,128)(2,1)S(1)}, bf16[4,128,256]{2,1,0:T(8,128)(2,1)S(1)}, u32[]{:S(2)}, u32[]{:S(2)}) collective-permute-start(bf16[4,128,256]{2,1,0:T(8,128)(2,1)S(1)} %pad_maximum_fusion.2), channel_id=1, source_target_pairs={{0,4},{4,8},{8,12},{12,16},{16,20},{20,24},{24,28},{28,0},{1,5},{5... | collective-permute-start | bytes 786440 | tf_op jit(solution)/shard_map/ppermute | solution.py:26
  36.1 10.8 %collective-permute-done.8 = bf16[4,128,256]{2,1,0:T(8,128)(2,1)S(1)} collective-permute-done((bf16[4,128,256]{2,1,0:T(8,128)(2,1)S(1)}, bf16[4,128,256]{2,1,0:T(8,128)(2,1)S(1)}, u32[]{:S(2)}, u32[]{:S(2)}) %collective-permute-start.8) | collective-permute-done | bytes 262176 | tf_op jit(solution)/shard_map/ppermute | solution.py:26
  50.8 4.6 %collective-permute-start.12 = (bf16[4,128,256]{2,1,0:T(8,128)(2,1)S(1)}, bf16[4,128,256]{2,1,0:T(8,128)(2,1)S(1)}, u32[]{:S(2)}, u32[]{:S(2)}) collective-permute-start(bf16[4,128,256]{2,1,0:T(8,128)(2,1)S(1)} %pad_maximum_fusion.2), channel_id=1, source_target_pairs={{0,28},{4,0},{8,4},{12,8},{16,12},{20,16},{24,20},{28,24},{1,29},{... | collective-permute-start | bytes 786440 | tf_op jit(solution)/shard_map/ppermute | solution.py:29
  58.7 5.0 %collective-permute-start.13 = (bf16[4,128,256]{2,1,0:T(8,128)(2,1)S(1)}, bf16[4,128,256]{2,1,0:T(8,128)(2,1)S(1)}, u32[]{:S(2)}, u32[]{:S(2)}) collective-permute-start(bf16[4,128,256]{2,1,0:T(8,128)(2,1)S(1)} %collective-permute-done.12), channel_id=1, source_target_pairs={{0,28},{4,0},{8,4},{12,8},{16,12},{20,16},{24,20},{28,24},{1,29},{... | collective-permute-start | bytes 786440 | tf_op jit(solution)/shard_map/ppermute | solution.py:29
  67.0 5.0 %collective-permute-start.14 = (bf16[4,128,256]{2,1,0:T(8,128)(2,1)S(1)}, bf16[4,128,256]{2,1,0:T(8,128)(2,1)S(1)}, u32[]{:S(2)}, u32[]{:S(2)}) collective-permute-start(bf16[4,128,256]{2,1,0:T(8,128)(2,1)S(1)} %collective-permute-done.13), channel_id=1, source_target_pairs={{0,28},{4,0},{8,4},{12,8},{16,12},{20,16},{24,20},{28,24},{1,29},{... | collective-permute-start | bytes 786440 | tf_op jit(solution)/shard_map/ppermute | solution.py:29
  76.7 2.8 %collective-permute-start.17 = (bf16[8,128,256]{2,1,0:T(8,128)(2,1)}, bf16[8,128,256]{2,1,0:T(8,128)(2,1)}, u32[]{:S(2)}, u32[]{:S(2)}) collective-permute-start(bf16[8,128,256]{2,1,0:T(8,128)(2,1)} %gather_fusion.2), channel_id=1, source_target_pairs={{0,32},{32,64},{64,96},{96,0},{1,33},{33,65},{65,97},{97,1},{2,34}... | collective-permute-start | bytes 1572872 | tf_op jit(solution)/shard_map/ppermute | solution.py:66
  80.9 3.7 %collective-permute-start.16 = (bf16[8,128,256]{2,1,0:T(8,128)(2,1)}, bf16[8,128,256]{2,1,0:T(8,128)(2,1)}, u32[]{:S(2)}, u32[]{:S(2)}) collective-permute-start(bf16[8,128,256]{2,1,0:T(8,128)(2,1)} %gather_fusion.1), channel_id=1, source_target_pairs={{0,64},{32,96},{64,0},{96,32},{1,65},{33,97},{65,1},{97,33},{2,66}... | collective-permute-start | bytes 1572872 | tf_op jit(solution)/shard_map/ppermute | solution.py:66
  86.0 2.5 %collective-permute-start.15 = (bf16[8,128,256]{2,1,0:T(8,128)(2,1)}, bf16[8,128,256]{2,1,0:T(8,128)(2,1)}, u32[]{:S(2)}, u32[]{:S(2)}) collective-permute-start(bf16[8,128,256]{2,1,0:T(8,128)(2,1)} %gather_fusion), channel_id=1, source_target_pairs={{0,96},{32,0},{64,32},{96,64},{1,97},{33,1},{65,33},{97,65},{2,98}... | collective-permute-start | bytes 1572872 | tf_op jit(solution)/shard_map/ppermute | solution.py:66
  91.3 7.6 %collective-permute-done.16 = bf16[8,128,256]{2,1,0:T(8,128)(2,1)} collective-permute-done((bf16[8,128,256]{2,1,0:T(8,128)(2,1)}, bf16[8,128,256]{2,1,0:T(8,128)(2,1)}, u32[]{:S(2)}, u32[]{:S(2)}) %collective-permute-start.16) | collective-permute-done | bytes 524320 | tf_op jit(solution)/shard_map/ppermute | solution.py:66
  98.9 5.6 %collective-permute-done.15 = bf16[8,128,256]{2,1,0:T(8,128)(2,1)} collective-permute-done((bf16[8,128,256]{2,1,0:T(8,128)(2,1)}, bf16[8,128,256]{2,1,0:T(8,128)(2,1)}, u32[]{:S(2)}, u32[]{:S(2)}) %collective-permute-start.15) | collective-permute-done | bytes 524320 | tf_op jit(solution)/shard_map/ppermute | solution.py:66
  104.5 1.9 fusion.2
  106.9 7.2 %collective-permute-start.18 = (f32[512,256]{1,0:T(8,128)S(1)}, f32[512,256]{1,0:T(8,128)S(1)}, u32[]{:S(2)}, u32[]{:S(2)}) collective-permute-start(f32[512,256]{1,0:T(8,128)S(1)} %bitcast.64), channel_id=1, source_target_pairs={{0,1},{1,0},{2,3},{3,2},{4,5},{5,4},{6,7},{7,6},{8,9},{9,8},{10,11... | collective-permute-start | bytes 1572872 | tf_op jit(solution)/shard_map/ppermute | solution.py:138
  115.7 3.0 %collective-permute-start.19 = (f32[512,256]{1,0:T(8,128)S(1)}, f32[512,256]{1,0:T(8,128)S(1)}, u32[]{:S(2)}, u32[]{:S(2)}) collective-permute-start(f32[512,256]{1,0:T(8,128)S(1)} %bitcast_add_fusion), channel_id=1, source_target_pairs={{0,2},{2,0},{1,3},{3,1},{4,6},{6,4},{5,7},{7,5},{8,10},{10,8},{9,1... | collective-permute-start | bytes 1572872 | tf_op jit(solution)/shard_map/ppermute | solution.py:138
  118.8 11.9 %collective-permute-done.19 = f32[512,256]{1,0:T(8,128)S(1)} collective-permute-done((f32[512,256]{1,0:T(8,128)S(1)}, f32[512,256]{1,0:T(8,128)S(1)}, u32[]{:S(2)}, u32[]{:S(2)}) %collective-permute-start.19) | collective-permute-done | bytes 524320 | tf_op jit(solution)/shard_map/ppermute | solution.py:138
  134.0 3.1 %collective-permute-done.20 = f32[16896]{0:T(1024)S(1)} collective-permute-done((f32[16896]{0:T(1024)S(1)}, f32[16896]{0:T(1024)S(1)}, u32[]{:S(2)}, u32[]{:S(2)}) %collective-permute-start.20) | collective-permute-done | bytes 67616 | tf_op jit(solution)/shard_map/ppermute | solution.py:195
  137.1 3.8 %collective-permute-start.21 = (f32[16896]{0:T(1024)S(1)}, f32[16896]{0:T(1024)S(1)}, u32[]{:S(2)}, u32[]{:S(2)}) collective-permute-start(f32[16896]{0:T(1024)S(1)} %add.315), channel_id=1, source_target_pairs={{0,8},{4,12},{8,0},{12,4},{16,24},{20,28},{24,16},{28,20},{1,9},{5... | collective-permute-start | bytes 202760 | tf_op jit(solution)/shard_map/ppermute | solution.py:195
  141.0 2.1 %collective-permute-done.21 = f32[16896]{0:T(1024)S(1)} collective-permute-done((f32[16896]{0:T(1024)S(1)}, f32[16896]{0:T(1024)S(1)}, u32[]{:S(2)}, u32[]{:S(2)}) %collective-permute-start.21) | collective-permute-done | bytes 67616 | tf_op jit(solution)/shard_map/ppermute | solution.py:195
  143.1 5.5 %collective-permute-start.22 = (f32[16896]{0:T(1024)S(1)}, f32[16896]{0:T(1024)S(1)}, u32[]{:S(2)}, u32[]{:S(2)}) collective-permute-start(f32[16896]{0:T(1024)S(1)} %add.316), channel_id=1, source_target_pairs={{0,28},{4,24},{8,20},{12,16},{16,12},{20,8},{24,4},{28,0},{1,29},{... | collective-permute-start | bytes 202760 | tf_op jit(solution)/shard_map/ppermute | solution.py:195
  148.6 2.0 %collective-permute-done.22 = f32[16896]{0:T(1024)S(1)} collective-permute-done((f32[16896]{0:T(1024)S(1)}, f32[16896]{0:T(1024)S(1)}, u32[]{:S(2)}, u32[]{:S(2)}) %collective-permute-start.22) | collective-permute-done | bytes 67616 | tf_op jit(solution)/shard_map/ppermute | solution.py:195
  150.6 2.5 %collective-permute-start.23 = (f32[16896]{0:T(1024)S(1)}, f32[16896]{0:T(1024)S(1)}, u32[]{:S(2)}, u32[]{:S(2)}) collective-permute-start(f32[16896]{0:T(1024)S(1)} %add.317), channel_id=1, source_target_pairs={{0,32},{32,0},{64,96},{96,64},{1,33},{33,1},{65,97},{97,65},{2,34}... | collective-permute-start | bytes 202760 | tf_op jit(solution)/shard_map/ppermute | solution.py:195
  153.1 2.6 %collective-permute-done.23 = f32[16896]{0:T(1024)S(1)} collective-permute-done((f32[16896]{0:T(1024)S(1)}, f32[16896]{0:T(1024)S(1)}, u32[]{:S(2)}, u32[]{:S(2)}) %collective-permute-start.23) | collective-permute-done | bytes 67616 | tf_op jit(solution)/shard_map/ppermute | solution.py:195
  155.6 4.2 %collective-permute-start.24 = (f32[16896]{0:T(1024)S(1)}, f32[16896]{0:T(1024)S(1)}, u32[]{:S(2)}, u32[]{:S(2)}) collective-permute-start(f32[16896]{0:T(1024)S(1)} %add.318), channel_id=1, source_target_pairs={{0,96},{32,64},{64,32},{96,0},{1,97},{33,65},{65,33},{97,1},{2,98}... | collective-permute-start | bytes 202760 | tf_op jit(solution)/shard_map/ppermute | solution.py:195
  159.9 2.0 %collective-permute-done.24 = f32[16896]{0:T(1024)S(1)} collective-permute-done((f32[16896]{0:T(1024)S(1)}, f32[16896]{0:T(1024)S(1)}, u32[]{:S(2)}, u32[]{:S(2)}) %collective-permute-start.24) | collective-permute-done | bytes 67616 | tf_op jit(solution)/shard_map/ppermute | solution.py:195
  161.9 5.2 %collective-permute-start.25 = (f32[16896]{0:T(1024)S(1)}, f32[16896]{0:T(1024)S(1)}, u32[]{:S(2)}, u32[]{:S(2)}) collective-permute-start(f32[16896]{0:T(1024)S(1)} %add.319), channel_id=1, source_target_pairs={{0,128},{128,0},{256,384},{384,256},{1,129},{129,1},{257,385},{385... | collective-permute-start | bytes 202760 | tf_op jit(solution)/shard_map/ppermute | solution.py:195
  168.8 3.0 %collective-permute-start.26 = (f32[16896]{0:T(1024)S(1)}, f32[16896]{0:T(1024)S(1)}, u32[]{:S(2)}, u32[]{:S(2)}) collective-permute-start(f32[16896]{0:T(1024)S(1)} %add.320), channel_id=1, source_target_pairs={{0,384},{128,256},{256,128},{384,0},{1,385},{129,257},{257,129},{3... | collective-permute-start | bytes 202760 | tf_op jit(solution)/shard_map/ppermute | solution.py:195
  171.8 4.5 %collective-permute-done.26 = f32[16896]{0:T(1024)S(1)} collective-permute-done((f32[16896]{0:T(1024)S(1)}, f32[16896]{0:T(1024)S(1)}, u32[]{:S(2)}, u32[]{:S(2)}) %collective-permute-start.26) | collective-permute-done | bytes 67616 | tf_op jit(solution)/shard_map/ppermute | solution.py:195
  176.4 3.5 %collective-permute-start.27 = (f32[16896]{0:T(1024)S(1)}, f32[16896]{0:T(1024)S(1)}, u32[]{:S(2)}, u32[]{:S(2)}) collective-permute-start(f32[16896]{0:T(1024)S(1)} %add.321), channel_id=1, source_target_pairs={{0,2},{2,0},{1,3},{3,1},{4,6},{6,4},{5,7},{7,5},{8,10},{10,8},{9,1... | collective-permute-start | bytes 202760 | tf_op jit(solution)/shard_map/ppermute | solution.py:107
  181.6 11.3 %collective-permute-start.28 = (f32[33792]{0:T(1024)S(1)}, f32[33792]{0:T(1024)S(1)}, u32[]{:S(2)}, u32[]{:S(2)}) collective-permute-start(f32[33792]{0:T(1024)S(1)} %maximum_select_fusion.2), channel_id=1, source_target_pairs={{0,1},{1,0},{2,3},{3,2},{4,5},{5,4},{6,7},{7,6},{8,9},{9,8},{10,11... | collective-permute-start | bytes 405512 | tf_op jit(solution)/shard_map/ppermute | solution.py:107
  (93 shorter events, 44.2 us)
Async XLA Ops:
  0.6 103.8 %copy-start = (bf16[1,4,8,128,128]{4,3,2,1,0:T(8,128)(2,1)S(1)}, bf16[1,4,8,128,128]{4,3,2,1,0:T(8,128)(2,1)}, u32[]{:S(2)}) copy-start(bf16[1,4,8,128,128]{4,3,2,1,0:T(8,128)(2,1)} %param.11) | copy-start | bytes 3145732
  0.6 16.3 %collective-permute-start.6 = (bf16[128,256]{1,0:T(8,128)(2,1)}, bf16[128,256]{1,0:T(8,128)(2,1)S(1)}, u32[]{:S(2)}, u32[]{:S(2)}) collective-permute-start(bf16[128,256]{1,0:T(8,128)(2,1)} %param.15), channel_id=1, source_target_pairs={{0,1},{1,0},{2,3},{3,2},{4,5},{5,4},{6,7},{7,6},{8,9},{9,8},{10,11... | collective-permute-start | bytes 196616 | tf_op jit(solution)/shard_map/ppermute | solution.py:138
  9.5 10.3 %collective-permute-start = (bf16[128,256]{1,0:T(8,128)(2,1)}, bf16[128,256]{1,0:T(8,128)(2,1)S(1)}, u32[]{:S(2)}, u32[]{:S(2)}) collective-permute-start(bf16[128,256]{1,0:T(8,128)(2,1)} %param.8), channel_id=1, source_target_pairs={{0,128},{128,256},{256,384},{384,0},{1,129},{129,257},{257,385},{3... | collective-permute-start | bytes 196616 | tf_op jit(solution)/shard_map/ppermute | solution.py:26
  11.5 15.2 %collective-permute-start.2 = (bf16[128,256]{1,0:T(8,128)(2,1)}, bf16[128,256]{1,0:T(8,128)(2,1)S(1)}, u32[]{:S(2)}, u32[]{:S(2)}) collective-permute-start(bf16[128,256]{1,0:T(8,128)(2,1)} %param.8), channel_id=1, source_target_pairs={{0,384},{128,0},{256,128},{384,256},{1,385},{129,1},{257,129},{385... | collective-permute-start | bytes 196616 | tf_op jit(solution)/shard_map/ppermute | solution.py:29
  17.9 12.7 %collective-permute-start.7 = (bf16[2,128,256]{2,1,0:T(8,128)(2,1)S(1)}, bf16[2,128,256]{2,1,0:T(8,128)(2,1)S(1)}, u32[]{:S(2)}, u32[]{:S(2)}) collective-permute-start(bf16[2,128,256]{2,1,0:T(8,128)(2,1)S(1)} %maximum_select_fusion.3), channel_id=1, source_target_pairs={{0,2},{2,0},{1,3},{3,1},{4,6},{6,4},{5,7},{7,5},{8,10},{10,8},{9,1... | collective-permute-start | bytes 393224 | tf_op jit(solution)/shard_map/ppermute | solution.py:138
  19.8 9.9 %collective-permute-start.1 = (bf16[128,256]{1,0:T(8,128)(2,1)S(1)}, bf16[128,256]{1,0:T(8,128)(2,1)S(1)}, u32[]{:S(2)}, u32[]{:S(2)}) collective-permute-start(bf16[128,256]{1,0:T(8,128)(2,1)S(1)} %collective-permute-done), channel_id=1, source_target_pairs={{0,128},{128,256},{256,384},{384,0},{1,129},{129,257},{257,385},{3... | collective-permute-start | bytes 196616 | tf_op jit(solution)/shard_map/ppermute | solution.py:26
  22.5 8.9 %collective-permute-start.3 = (s32[8]{0:T(128)S(1)}, s32[8]{0:T(128)S(1)}, u32[]{:S(2)}, u32[]{:S(2)}) collective-permute-start(s32[8]{0:T(128)S(1)} %get-tuple-element.17), channel_id=1, source_target_pairs={{0,96},{32,0},{64,32},{96,64},{1,97},{33,1},{65,33},{97,65},{2,98}... | collective-permute-start | bytes 104 | tf_op jit(solution)/shard_map/ppermute | solution.py:46
  24.4 6.9 %collective-permute-start.4 = (s32[8]{0:T(128)S(1)}, s32[8]{0:T(128)S(1)}, u32[]{:S(2)}, u32[]{:S(2)}) collective-permute-start(s32[8]{0:T(128)S(1)} %get-tuple-element.17), channel_id=1, source_target_pairs={{0,64},{32,96},{64,0},{96,32},{1,65},{33,97},{65,1},{97,33},{2,66}... | collective-permute-start | bytes 104 | tf_op jit(solution)/shard_map/ppermute | solution.py:46
  26.6 6.4 %collective-permute-start.5 = (s32[8]{0:T(128)S(1)}, s32[8]{0:T(128)S(1)}, u32[]{:S(2)}, u32[]{:S(2)}) collective-permute-start(s32[8]{0:T(128)S(1)} %get-tuple-element.17), channel_id=1, source_target_pairs={{0,32},{32,64},{64,96},{96,0},{1,33},{33,65},{65,97},{97,1},{2,34}... | collective-permute-start | bytes 104 | tf_op jit(solution)/shard_map/ppermute | solution.py:46
  33.1 13.9 %collective-permute-start.8 = (bf16[4,128,256]{2,1,0:T(8,128)(2,1)S(1)}, bf16[4,128,256]{2,1,0:T(8,128)(2,1)S(1)}, u32[]{:S(2)}, u32[]{:S(2)}) collective-permute-start(bf16[4,128,256]{2,1,0:T(8,128)(2,1)S(1)} %pad_maximum_fusion.2), channel_id=1, source_target_pairs={{0,4},{4,8},{8,12},{12,16},{16,20},{20,24},{24,28},{28,0},{1,5},{5... | collective-permute-start | bytes 786440 | tf_op jit(solution)/shard_map/ppermute | solution.py:26
  46.9 25.1 %copy-start.2 = (bf16[4,128,256]{2,1,0:T(8,128)(2,1)}, bf16[4,128,256]{2,1,0:T(8,128)(2,1)S(1)}, u32[]{:S(2)}) copy-start(bf16[4,128,256]{2,1,0:T(8,128)(2,1)S(1)} %collective-permute-done.8) | copy-start | bytes 786436
  46.9 8.5 %collective-permute-start.9 = (bf16[4,128,256]{2,1,0:T(8,128)(2,1)S(1)}, bf16[4,128,256]{2,1,0:T(8,128)(2,1)S(1)}, u32[]{:S(2)}, u32[]{:S(2)}) collective-permute-start(bf16[4,128,256]{2,1,0:T(8,128)(2,1)S(1)} %collective-permute-done.8), channel_id=1, source_target_pairs={{0,4},{4,8},{8,12},{12,16},{16,20},{20,24},{24,28},{28,0},{1,5},{5... | collective-permute-start | bytes 786440 | tf_op jit(solution)/shard_map/ppermute | solution.py:26
  50.8 7.9 %collective-permute-start.12 = (bf16[4,128,256]{2,1,0:T(8,128)(2,1)S(1)}, bf16[4,128,256]{2,1,0:T(8,128)(2,1)S(1)}, u32[]{:S(2)}, u32[]{:S(2)}) collective-permute-start(bf16[4,128,256]{2,1,0:T(8,128)(2,1)S(1)} %pad_maximum_fusion.2), channel_id=1, source_target_pairs={{0,28},{4,0},{8,4},{12,8},{16,12},{20,16},{24,20},{28,24},{1,29},{... | collective-permute-start | bytes 786440 | tf_op jit(solution)/shard_map/ppermute | solution.py:29
  55.4 8.3 %collective-permute-start.10 = (bf16[4,128,256]{2,1,0:T(8,128)(2,1)S(1)}, bf16[4,128,256]{2,1,0:T(8,128)(2,1)S(1)}, u32[]{:S(2)}, u32[]{:S(2)}) collective-permute-start(bf16[4,128,256]{2,1,0:T(8,128)(2,1)S(1)} %collective-permute-done.9), channel_id=1, source_target_pairs={{0,4},{4,8},{8,12},{12,16},{16,20},{20,24},{24,28},{28,0},{1,5},{5... | collective-permute-start | bytes 786440 | tf_op jit(solution)/shard_map/ppermute | solution.py:26
  58.7 8.3 %collective-permute-start.13 = (bf16[4,128,256]{2,1,0:T(8,128)(2,1)S(1)}, bf16[4,128,256]{2,1,0:T(8,128)(2,1)S(1)}, u32[]{:S(2)}, u32[]{:S(2)}) collective-permute-start(bf16[4,128,256]{2,1,0:T(8,128)(2,1)S(1)} %collective-permute-done.12), channel_id=1, source_target_pairs={{0,28},{4,0},{8,4},{12,8},{16,12},{20,16},{24,20},{28,24},{1,29},{... | collective-permute-start | bytes 786440 | tf_op jit(solution)/shard_map/ppermute | solution.py:29
  63.7 8.3 %collective-permute-start.11 = (bf16[4,128,256]{2,1,0:T(8,128)(2,1)S(1)}, bf16[4,128,256]{2,1,0:T(8,128)(2,1)S(1)}, u32[]{:S(2)}, u32[]{:S(2)}) collective-permute-start(bf16[4,128,256]{2,1,0:T(8,128)(2,1)S(1)} %collective-permute-done.10), channel_id=1, source_target_pairs={{0,4},{4,8},{8,12},{12,16},{16,20},{20,24},{24,28},{28,0},{1,5},{5... | collective-permute-start | bytes 786440 | tf_op jit(solution)/shard_map/ppermute | solution.py:26
  67.0 8.3 %collective-permute-start.14 = (bf16[4,128,256]{2,1,0:T(8,128)(2,1)S(1)}, bf16[4,128,256]{2,1,0:T(8,128)(2,1)S(1)}, u32[]{:S(2)}, u32[]{:S(2)}) collective-permute-start(bf16[4,128,256]{2,1,0:T(8,128)(2,1)S(1)} %collective-permute-done.13), channel_id=1, source_target_pairs={{0,28},{4,0},{8,4},{12,8},{16,12},{20,16},{24,20},{28,24},{1,29},{... | collective-permute-start | bytes 786440 | tf_op jit(solution)/shard_map/ppermute | solution.py:29
  76.7 14.6 %collective-permute-start.17 = (bf16[8,128,256]{2,1,0:T(8,128)(2,1)}, bf16[8,128,256]{2,1,0:T(8,128)(2,1)}, u32[]{:S(2)}, u32[]{:S(2)}) collective-permute-start(bf16[8,128,256]{2,1,0:T(8,128)(2,1)} %gather_fusion.2), channel_id=1, source_target_pairs={{0,32},{32,64},{64,96},{96,0},{1,33},{33,65},{65,97},{97,1},{2,34}... | collective-permute-start | bytes 1572872 | tf_op jit(solution)/shard_map/ppermute | solution.py:66
  80.9 18.0 %collective-permute-start.16 = (bf16[8,128,256]{2,1,0:T(8,128)(2,1)}, bf16[8,128,256]{2,1,0:T(8,128)(2,1)}, u32[]{:S(2)}, u32[]{:S(2)}) collective-permute-start(bf16[8,128,256]{2,1,0:T(8,128)(2,1)} %gather_fusion.1), channel_id=1, source_target_pairs={{0,64},{32,96},{64,0},{96,32},{1,65},{33,97},{65,1},{97,33},{2,66}... | collective-permute-start | bytes 1572872 | tf_op jit(solution)/shard_map/ppermute | solution.py:66
  86.0 18.4 %collective-permute-start.15 = (bf16[8,128,256]{2,1,0:T(8,128)(2,1)}, bf16[8,128,256]{2,1,0:T(8,128)(2,1)}, u32[]{:S(2)}, u32[]{:S(2)}) collective-permute-start(bf16[8,128,256]{2,1,0:T(8,128)(2,1)} %gather_fusion), channel_id=1, source_target_pairs={{0,96},{32,0},{64,32},{96,64},{1,97},{33,1},{65,33},{97,65},{2,98}... | collective-permute-start | bytes 1572872 | tf_op jit(solution)/shard_map/ppermute | solution.py:66
  106.9 24.1 %copy-start.1 = (bf16[4,128,256]{2,1,0:T(8,128)(2,1)S(1)}, bf16[4,128,256]{2,1,0:T(8,128)(2,1)}, u32[]{:S(2)}) copy-start(bf16[4,128,256]{2,1,0:T(8,128)(2,1)} %maximum_select_fusion) | copy-start | bytes 786436
  106.9 8.7 %collective-permute-start.18 = (f32[512,256]{1,0:T(8,128)S(1)}, f32[512,256]{1,0:T(8,128)S(1)}, u32[]{:S(2)}, u32[]{:S(2)}) collective-permute-start(f32[512,256]{1,0:T(8,128)S(1)} %bitcast.64), channel_id=1, source_target_pairs={{0,1},{1,0},{2,3},{3,2},{4,5},{5,4},{6,7},{7,6},{8,9},{9,8},{10,11... | collective-permute-start | bytes 1572872 | tf_op jit(solution)/shard_map/ppermute | solution.py:138
  115.7 15.0 %collective-permute-start.19 = (f32[512,256]{1,0:T(8,128)S(1)}, f32[512,256]{1,0:T(8,128)S(1)}, u32[]{:S(2)}, u32[]{:S(2)}) collective-permute-start(f32[512,256]{1,0:T(8,128)S(1)} %bitcast_add_fusion), channel_id=1, source_target_pairs={{0,2},{2,0},{1,3},{3,1},{4,6},{6,4},{5,7},{7,5},{8,10},{10,8},{9,1... | collective-permute-start | bytes 1572872 | tf_op jit(solution)/shard_map/ppermute | solution.py:138
  132.0 5.1 %collective-permute-start.20 = (f32[16896]{0:T(1024)S(1)}, f32[16896]{0:T(1024)S(1)}, u32[]{:S(2)}, u32[]{:S(2)}) collective-permute-start(f32[16896]{0:T(1024)S(1)} %dynamic-slice_reduce_fusion), channel_id=1, source_target_pairs={{0,4},{4,0},{8,12},{12,8},{16,20},{20,16},{24,28},{28,24},{1,5},{5... | collective-permute-start | bytes 202760 | tf_op jit(solution)/shard_map/ppermute | solution.py:195
  137.1 6.0 %collective-permute-start.21 = (f32[16896]{0:T(1024)S(1)}, f32[16896]{0:T(1024)S(1)}, u32[]{:S(2)}, u32[]{:S(2)}) collective-permute-start(f32[16896]{0:T(1024)S(1)} %add.315), channel_id=1, source_target_pairs={{0,8},{4,12},{8,0},{12,4},{16,24},{20,28},{24,16},{28,20},{1,9},{5... | collective-permute-start | bytes 202760 | tf_op jit(solution)/shard_map/ppermute | solution.py:195
  143.1 7.5 %collective-permute-start.22 = (f32[16896]{0:T(1024)S(1)}, f32[16896]{0:T(1024)S(1)}, u32[]{:S(2)}, u32[]{:S(2)}) collective-permute-start(f32[16896]{0:T(1024)S(1)} %add.316), channel_id=1, source_target_pairs={{0,28},{4,24},{8,20},{12,16},{16,12},{20,8},{24,4},{28,0},{1,29},{... | collective-permute-start | bytes 202760 | tf_op jit(solution)/shard_map/ppermute | solution.py:195
  150.6 5.1 %collective-permute-start.23 = (f32[16896]{0:T(1024)S(1)}, f32[16896]{0:T(1024)S(1)}, u32[]{:S(2)}, u32[]{:S(2)}) collective-permute-start(f32[16896]{0:T(1024)S(1)} %add.317), channel_id=1, source_target_pairs={{0,32},{32,0},{64,96},{96,64},{1,33},{33,1},{65,97},{97,65},{2,34}... | collective-permute-start | bytes 202760 | tf_op jit(solution)/shard_map/ppermute | solution.py:195
  155.6 6.3 %collective-permute-start.24 = (f32[16896]{0:T(1024)S(1)}, f32[16896]{0:T(1024)S(1)}, u32[]{:S(2)}, u32[]{:S(2)}) collective-permute-start(f32[16896]{0:T(1024)S(1)} %add.318), channel_id=1, source_target_pairs={{0,96},{32,64},{64,32},{96,0},{1,97},{33,65},{65,33},{97,1},{2,98}... | collective-permute-start | bytes 202760 | tf_op jit(solution)/shard_map/ppermute | solution.py:195
  161.9 6.9 %collective-permute-start.25 = (f32[16896]{0:T(1024)S(1)}, f32[16896]{0:T(1024)S(1)}, u32[]{:S(2)}, u32[]{:S(2)}) collective-permute-start(f32[16896]{0:T(1024)S(1)} %add.319), channel_id=1, source_target_pairs={{0,128},{128,0},{256,384},{384,256},{1,129},{129,1},{257,385},{385... | collective-permute-start | bytes 202760 | tf_op jit(solution)/shard_map/ppermute | solution.py:195
  168.8 7.5 %collective-permute-start.26 = (f32[16896]{0:T(1024)S(1)}, f32[16896]{0:T(1024)S(1)}, u32[]{:S(2)}, u32[]{:S(2)}) collective-permute-start(f32[16896]{0:T(1024)S(1)} %add.320), channel_id=1, source_target_pairs={{0,384},{128,256},{256,128},{384,0},{1,385},{129,257},{257,129},{3... | collective-permute-start | bytes 202760 | tf_op jit(solution)/shard_map/ppermute | solution.py:195
  176.4 5.2 %collective-permute-start.27 = (f32[16896]{0:T(1024)S(1)}, f32[16896]{0:T(1024)S(1)}, u32[]{:S(2)}, u32[]{:S(2)}) collective-permute-start(f32[16896]{0:T(1024)S(1)} %add.321), channel_id=1, source_target_pairs={{0,2},{2,0},{1,3},{3,1},{4,6},{6,4},{5,7},{7,5},{8,10},{10,8},{9,1... | collective-permute-start | bytes 202760 | tf_op jit(solution)/shard_map/ppermute | solution.py:107
  181.6 12.3 %collective-permute-start.28 = (f32[33792]{0:T(1024)S(1)}, f32[33792]{0:T(1024)S(1)}, u32[]{:S(2)}, u32[]{:S(2)}) collective-permute-start(f32[33792]{0:T(1024)S(1)} %maximum_select_fusion.2), channel_id=1, source_target_pairs={{0,1},{1,0},{2,3},{3,2},{4,5},{5,4},{6,7},{7,6},{8,9},{9,8},{10,11... | collective-permute-start | bytes 405512 | tf_op jit(solution)/shard_map/ppermute | solution.py:107
  (3 other events, 64.6 us)

commit v12 on v10

--- a/solution.py
+++ b/solution.py
@@ -13,6 +13,32 @@
     rows, rep = mesh.devices.shape
     y_hi, x, y_lo = 4, 4, 2
     return Mesh(mesh.devices.reshape(y_hi, x, rows // (y_hi * x), y_lo, rep // y_lo), ALL_AXES)
+
+
+def round_gather(piece, axis):
+    n = lax.axis_size(axis)
+    pieces = []
+    for k in range(n):
+        d = k - n // 2
+        if d == 0:
+            pieces.append(piece)
+        else:
+            pieces.append(lax.ppermute(piece, axis, [(i, (i - d) % n) for i in range(n)]))
+    return jnp.stack(pieces)
+
+
+def round_sum(value, axis):
+    n = lax.axis_size(axis)
+    got = [value] + [
+        lax.ppermute(value, axis, [(i, (i - d) % n) for i in range(n)]) for d in range(1, n)
+    ]
+    by_position = jnp.take(
+        jnp.stack(got), (jnp.arange(n) - lax.axis_index(axis)) % n, axis=0, mode="clip"
+    )
+    total = by_position[0]
+    for p in range(1, n):
+        total = total + by_position[p]
+    return total
 
 
 def ring_gather(piece, axis):
@@ -48,7 +74,7 @@
     }
     stack = features
     for a in within:
-        stack = ring_gather(stack, a)
+        stack = round_gather(stack, a) if lax.axis_size(a) <= 4 else ring_gather(stack, a)
     plane = stack.reshape(-1, features.shape[0], features.shape[1])
 
     def in_plane(c):
@@ -190,8 +216,12 @@
     rep_steps = halving_steps(("core", "y_lo"))
     quarter = lax.axis_index("core") * lax.axis_size("y_lo") + lax.axis_index("y_lo")
     flat = lax.dynamic_index_in_dim(packed.reshape(row_count, -1), quarter, 0, keepdims=False)
-    for a, perm in doubling_steps(ROW_AXES[::-1]):
-        flat = flat + lax.ppermute(flat, a, perm)
+    for a in ROW_AXES[::-1]:
+        if lax.axis_size(a) <= 4:
+            flat = round_sum(flat, a)
+        else:
+            for _, perm in doubling_steps((a,)):
+                flat = flat + lax.ppermute(flat, a, perm)
     packed = all_gather_flat(flat, rep_steps).reshape(packed.shape)
     weight_grad = packed[:feature_width]
     bias_grad = packed[feature_width]

time: 190 us -> 194 us (1.021)
  starting transfers between devices: 118 us -> 122 us
    ppermute x0 -> x9, starting transfers between devices: none -> 36.3 us  [the longest x6 20.5 us: round_sum(): lax.ppermute(value, axis, [(i, (i - d) % n) for i in range(n)])]
    ppermute x7 -> x3, starting transfers between devices: 27.8 us -> 12 us  [shards(): flat = flat + lax.ppermute(flat, a, perm)]
    ppermute x0 -> x9, waiting for transfers between devices: none -> 10.4 us  [the longest x6 7.74 us: round_sum(): lax.ppermute(value, axis, [(i, (i - d) % n) for i in range(n)])]
    ppermute x6 -> x4, starting transfers between devices: 21.2 us -> 11.2 us  [ring_gather(): left = lax.ppermute(left, axis, fwd)]
    ppermute x7 -> x3, waiting for transfers between devices: 16.5 us -> 7.05 us  [shards(): flat = flat + lax.ppermute(flat, a, perm)]
    ppermute x4 -> x3, starting transfers between devices: 20.1 us -> 16.5 us  [ring_gather(): right = lax.ppermute(right, axis, bwd)]
    ppermute x6 -> x4, waiting for transfers between devices: 2.09 us -> 0.03 us  [ring_gather(): left = lax.ppermute(left, axis, fwd)]
    ppermute x4 -> x3, waiting for transfers between devices: 6.03 us -> 4.88 us  [ring_gather(): right = lax.ppermute(right, axis, bwd)]
  transfers between devices with their start and end apart: 29 -> 31, of which waited for: 19 -> 17; matrix products, arithmetic and copies ran while one was open for 5% -> 5% of each run, Pallas kernels for 0% -> 0%
where the time goes in v12:
time: 194 us; the launch traced here: 192 us
  starting transfers between devices  122 us (63%)
  waiting for transfers between devices  47.6 us (25%)
  local copies, waits for them, and re-layouts  10.7 us (6%)
  other arithmetic  7.13 us (4%)
  matrix products  3.04 us (2%)
    ppermute x6, starting transfers between devices, round_sum(): lax.ppermute(value, axis, [(i, (i - d) % n) for i in range(n)])  20.5 us
    ppermute x3, starting transfers between devices, ring_gather(): right = lax.ppermute(right, axis, bwd)  16.5 us
    ppermute x3, starting transfers between devices, round_gather(): lax.ppermute(piece, axis, [(i, (i - d) % n) for i in range(n)])  15.8 us
    ppermute x4, starting transfers between devices, swap(): return lax.ppermute(x, axis, [(0, 1), (1, 0)])  13.8 us
    ppermute x2, starting transfers between devices, all_gather_flat(): other = lax.ppermute(flat, a, perm)  13.3 us
    ppermute x3, starting transfers between devices, shards(): flat = flat + lax.ppermute(flat, a, perm)  12 us
    ppermute x3, waiting for transfers between devices, plane_blocks(): lax.ppermute(sent, across, [(i, (i + s) % n_across) for i in range(n_acro...  11.5 us
    ppermute x4, waiting for transfers between devices, swap(): return lax.ppermute(x, axis, [(0, 1), (1, 0)])  11.3 us
  transfers between devices with their start and end apart: 31, of which 17 were waited for; matrix products, arithmetic and copies ran while one was open for 5% of the time, Pallas kernels for 0%

profile of v12, /device:TPU:1, one launch (start us, length us, event | category | flops | bytes accessed | tf_op | source)
XLA Modules:
  0.0 192.0 jit_solution(5469829867667848180)
XLA Ops:
  0.7 8.4 %collective-permute-start = (bf16[128,256]{1,0:T(8,128)(2,1)}, bf16[128,256]{1,0:T(8,128)(2,1)S(1)}, u32[]{:S(2)}, u32[]{:S(2)}) collective-permute-start(bf16[128,256]{1,0:T(8,128)(2,1)} %param.8), channel_id=1, source_target_pairs={{0,256},{128,384},{256,0},{384,128},{1,257},{129,385},{257,1},{385... | collective-permute-start | bytes 196616 | tf_op jit(solution)/shard_map/ppermute | solution.py:26
  9.1 2.4 %collective-permute-start.1 = (bf16[128,256]{1,0:T(8,128)(2,1)}, bf16[128,256]{1,0:T(8,128)(2,1)S(1)}, u32[]{:S(2)}, u32[]{:S(2)}) collective-permute-start(bf16[128,256]{1,0:T(8,128)(2,1)} %param.8), channel_id=1, source_target_pairs={{0,128},{128,256},{256,384},{384,0},{1,129},{129,257},{257,385},{3... | collective-permute-start | bytes 196616 | tf_op jit(solution)/shard_map/ppermute | solution.py:26
  11.5 5.0 %collective-permute-start.2 = (bf16[128,256]{1,0:T(8,128)(2,1)}, bf16[128,256]{1,0:T(8,128)(2,1)S(1)}, u32[]{:S(2)}, u32[]{:S(2)}) collective-permute-start(bf16[128,256]{1,0:T(8,128)(2,1)} %param.8), channel_id=1, source_target_pairs={{0,384},{128,0},{256,128},{384,256},{1,385},{129,1},{257,129},{385... | collective-permute-start | bytes 196616 | tf_op jit(solution)/shard_map/ppermute | solution.py:26
  16.5 2.7 %collective-permute-done.1 = bf16[128,256]{1,0:T(8,128)(2,1)S(1)} collective-permute-done((bf16[128,256]{1,0:T(8,128)(2,1)}, bf16[128,256]{1,0:T(8,128)(2,1)S(1)}, u32[]{:S(2)}, u32[]{:S(2)}) %collective-permute-start.1) | collective-permute-done | bytes 65568 | tf_op jit(solution)/shard_map/ppermute | solution.py:26
  20.1 3.4 %collective-permute-start.3 = (bf16[4,128,256]{2,1,0:T(8,128)(2,1)S(1)}, bf16[4,128,256]{2,1,0:T(8,128)(2,1)S(1)}, u32[]{:S(2)}, u32[]{:S(2)}) collective-permute-start(bf16[4,128,256]{2,1,0:T(8,128)(2,1)S(1)} %pad_maximum_fusion.4), channel_id=1, source_target_pairs={{0,4},{4,8},{8,12},{12,16},{16,20},{20,24},{24,28},{28,0},{1,5},{5... | collective-permute-start | bytes 786440 | tf_op jit(solution)/shard_map/ppermute | solution.py:52
  24.8 4.6 %collective-permute-start.12 = (s32[8]{0:T(128)S(1)}, s32[8]{0:T(128)S(1)}, u32[]{:S(2)}, u32[]{:S(2)}) collective-permute-start(s32[8]{0:T(128)S(1)} %get-tuple-element.9), channel_id=1, source_target_pairs={{0,64},{32,96},{64,0},{96,32},{1,65},{33,97},{65,1},{97,33},{2,66}... | collective-permute-start | bytes 104 | tf_op jit(solution)/shard_map/ppermute | solution.py:72
  29.4 2.8 %collective-permute-start.14 = (s32[8]{0:T(128)S(1)}, s32[8]{0:T(128)S(1)}, u32[]{:S(2)}, u32[]{:S(2)}) collective-permute-start(s32[8]{0:T(128)S(1)} %get-tuple-element.9), channel_id=1, source_target_pairs={{0,96},{32,0},{64,32},{96,64},{1,97},{33,1},{65,33},{97,65},{2,98}... | collective-permute-start | bytes 104 | tf_op jit(solution)/shard_map/ppermute | solution.py:72
  32.2 2.5 %collective-permute-start.10 = (s32[8]{0:T(128)S(1)}, s32[8]{0:T(128)S(1)}, u32[]{:S(2)}, u32[]{:S(2)}) collective-permute-start(s32[8]{0:T(128)S(1)} %get-tuple-element.9), channel_id=1, source_target_pairs={{0,32},{32,64},{64,96},{96,0},{1,33},{33,65},{65,97},{97,1},{2,34}... | collective-permute-start | bytes 104 | tf_op jit(solution)/shard_map/ppermute | solution.py:72
  34.7 4.0 %collective-permute-start.4 = (bf16[4,128,256]{2,1,0:T(8,128)(2,1)S(1)}, bf16[4,128,256]{2,1,0:T(8,128)(2,1)S(1)}, u32[]{:S(2)}, u32[]{:S(2)}) collective-permute-start(bf16[4,128,256]{2,1,0:T(8,128)(2,1)S(1)} %collective-permute-done.3), channel_id=1, source_target_pairs={{0,4},{4,8},{8,12},{12,16},{16,20},{20,24},{24,28},{28,0},{1,5},{5... | collective-permute-start | bytes 786440 | tf_op jit(solution)/shard_map/ppermute | solution.py:52
  40.8 6.5 %collective-permute-start.7 = (bf16[4,128,256]{2,1,0:T(8,128)(2,1)S(1)}, bf16[4,128,256]{2,1,0:T(8,128)(2,1)S(1)}, u32[]{:S(2)}, u32[]{:S(2)}) collective-permute-start(bf16[4,128,256]{2,1,0:T(8,128)(2,1)S(1)} %pad_maximum_fusion.4), channel_id=1, source_target_pairs={{0,28},{4,0},{8,4},{12,8},{16,12},{20,16},{24,20},{28,24},{1,29},{... | collective-permute-start | bytes 786440 | tf_op jit(solution)/shard_map/ppermute | solution.py:55
  50.6 5.0 %collective-permute-start.8 = (bf16[4,128,256]{2,1,0:T(8,128)(2,1)S(1)}, bf16[4,128,256]{2,1,0:T(8,128)(2,1)S(1)}, u32[]{:S(2)}, u32[]{:S(2)}) collective-permute-start(bf16[4,128,256]{2,1,0:T(8,128)(2,1)S(1)} %collective-permute-done.7), channel_id=1, source_target_pairs={{0,28},{4,0},{8,4},{12,8},{16,12},{20,16},{24,20},{28,24},{1,29},{... | collective-permute-start | bytes 786440 | tf_op jit(solution)/shard_map/ppermute | solution.py:55
  58.9 5.0 %collective-permute-start.9 = (bf16[4,128,256]{2,1,0:T(8,128)(2,1)S(1)}, bf16[4,128,256]{2,1,0:T(8,128)(2,1)S(1)}, u32[]{:S(2)}, u32[]{:S(2)}) collective-permute-start(bf16[4,128,256]{2,1,0:T(8,128)(2,1)S(1)} %collective-permute-done.8), channel_id=1, source_target_pairs={{0,28},{4,0},{8,4},{12,8},{16,12},{20,16},{24,20},{28,24},{1,29},{... | collective-permute-start | bytes 786440 | tf_op jit(solution)/shard_map/ppermute | solution.py:55
  64.9 2.3 %collective-permute-done.9 = bf16[4,128,256]{2,1,0:T(8,128)(2,1)S(1)} collective-permute-done((bf16[4,128,256]{2,1,0:T(8,128)(2,1)S(1)}, bf16[4,128,256]{2,1,0:T(8,128)(2,1)S(1)}, u32[]{:S(2)}, u32[]{:S(2)}) %collective-permute-start.9) | collective-permute-done | bytes 262176 | tf_op jit(solution)/shard_map/ppermute | solution.py:55
  68.6 2.5 %collective-permute-start.13 = (bf16[8,128,256]{2,1,0:T(8,128)(2,1)}, bf16[8,128,256]{2,1,0:T(8,128)(2,1)}, u32[]{:S(2)}, u32[]{:S(2)}) collective-permute-start(bf16[8,128,256]{2,1,0:T(8,128)(2,1)} %gather_fusion.1), channel_id=1, source_target_pairs={{0,64},{32,96},{64,0},{96,32},{1,65},{33,97},{65,1},{97,33},{2,66}... | collective-permute-start | bytes 1572872 | tf_op jit(solution)/shard_map/ppermute | solution.py:91
  72.6 3.9 %collective-permute-start.15 = (bf16[8,128,256]{2,1,0:T(8,128)(2,1)}, bf16[8,128,256]{2,1,0:T(8,128)(2,1)}, u32[]{:S(2)}, u32[]{:S(2)}) collective-permute-start(bf16[8,128,256]{2,1,0:T(8,128)(2,1)} %gather_fusion.2), channel_id=1, source_target_pairs={{0,32},{32,64},{64,96},{96,0},{1,33},{33,65},{65,97},{97,1},{2,34}... | collective-permute-start | bytes 1572872 | tf_op jit(solution)/shard_map/ppermute | solution.py:91
  77.9 2.6 %collective-permute-start.11 = (bf16[8,128,256]{2,1,0:T(8,128)(2,1)}, bf16[8,128,256]{2,1,0:T(8,128)(2,1)}, u32[]{:S(2)}, u32[]{:S(2)}) collective-permute-start(bf16[8,128,256]{2,1,0:T(8,128)(2,1)} %gather_fusion), channel_id=1, source_target_pairs={{0,96},{32,0},{64,32},{96,64},{1,97},{33,1},{65,33},{97,65},{2,98}... | collective-permute-start | bytes 1572872 | tf_op jit(solution)/shard_map/ppermute | solution.py:91
  83.2 11.5 %collective-permute-done.15 = bf16[8,128,256]{2,1,0:T(8,128)(2,1)} collective-permute-done((bf16[8,128,256]{2,1,0:T(8,128)(2,1)}, bf16[8,128,256]{2,1,0:T(8,128)(2,1)}, u32[]{:S(2)}, u32[]{:S(2)}) %collective-permute-start.15) | collective-permute-done | bytes 524320 | tf_op jit(solution)/shard_map/ppermute | solution.py:91
  97.2 6.0 %collective-permute-start.16 = (f32[512,256]{1,0:T(8,128)S(1)}, f32[512,256]{1,0:T(8,128)S(1)}, u32[]{:S(2)}, u32[]{:S(2)}) collective-permute-start(f32[512,256]{1,0:T(8,128)S(1)} %bitcast.71), channel_id=1, source_target_pairs={{0,1},{1,0},{2,3},{3,2},{4,5},{5,4},{6,7},{7,6},{8,9},{9,8},{10,11... | collective-permute-start | bytes 1572872 | tf_op jit(solution)/shard_map/ppermute | solution.py:163
  107.0 2.6 %collective-permute-start.18 = (bf16[128,256]{1,0:T(8,128)(2,1)S(1)}, bf16[128,256]{1,0:T(8,128)(2,1)S(1)}, u32[]{:S(2)}, u32[]{:S(2)}) collective-permute-start(bf16[128,256]{1,0:T(8,128)(2,1)S(1)} %copy-done.6), channel_id=1, source_target_pairs={{0,1},{1,0},{2,3},{3,2},{4,5},{5,4},{6,7},{7,6},{8,9},{9,8},{10,11... | collective-permute-start | bytes 196616 | tf_op jit(solution)/shard_map/ppermute | solution.py:163
  110.5 3.1 %collective-permute-start.19 = (bf16[2,128,256]{2,1,0:T(8,128)(2,1)S(1)}, bf16[2,128,256]{2,1,0:T(8,128)(2,1)S(1)}, u32[]{:S(2)}, u32[]{:S(2)}) collective-permute-start(bf16[2,128,256]{2,1,0:T(8,128)(2,1)S(1)} %maximum_select_fusion.3), channel_id=1, source_target_pairs={{0,2},{2,0},{1,3},{3,1},{4,6},{6,4},{5,7},{7,5},{8,10},{10,8},{9,1... | collective-permute-start | bytes 393224 | tf_op jit(solution)/shard_map/ppermute | solution.py:163
  113.6 8.9 %collective-permute-done.19 = bf16[2,128,256]{2,1,0:T(8,128)(2,1)S(1)} collective-permute-done((bf16[2,128,256]{2,1,0:T(8,128)(2,1)S(1)}, bf16[2,128,256]{2,1,0:T(8,128)(2,1)S(1)}, u32[]{:S(2)}, u32[]{:S(2)}) %collective-permute-start.19) | collective-permute-done | bytes 131104 | tf_op jit(solution)/shard_map/ppermute | solution.py:163
  125.8 3.1 %collective-permute-done.20 = f32[16896]{0:T(1024)S(1)} collective-permute-done((f32[16896]{0:T(1024)S(1)}, f32[16896]{0:T(1024)S(1)}, u32[]{:S(2)}, u32[]{:S(2)}) %collective-permute-start.20) | collective-permute-done | bytes 67616 | tf_op jit(solution)/shard_map/ppermute | solution.py:224
  128.9 6.1 %collective-permute-start.21 = (f32[16896]{0:T(1024)S(1)}, f32[16896]{0:T(1024)S(1)}, u32[]{:S(2)}, u32[]{:S(2)}) collective-permute-start(f32[16896]{0:T(1024)S(1)} %add.366), channel_id=1, source_target_pairs={{0,8},{4,12},{8,0},{12,4},{16,24},{20,28},{24,16},{28,20},{1,9},{5... | collective-permute-start | bytes 202760 | tf_op jit(solution)/shard_map/ppermute | solution.py:224
  136.8 3.9 %collective-permute-start.22 = (f32[16896]{0:T(1024)S(1)}, f32[16896]{0:T(1024)S(1)}, u32[]{:S(2)}, u32[]{:S(2)}) collective-permute-start(f32[16896]{0:T(1024)S(1)} %add.367), channel_id=1, source_target_pairs={{0,28},{4,24},{8,20},{12,16},{16,12},{20,8},{24,4},{28,0},{1,29},{... | collective-permute-start | bytes 202760 | tf_op jit(solution)/shard_map/ppermute | solution.py:224
  140.7 2.3 %collective-permute-done.22 = f32[16896]{0:T(1024)S(1)} collective-permute-done((f32[16896]{0:T(1024)S(1)}, f32[16896]{0:T(1024)S(1)}, u32[]{:S(2)}, u32[]{:S(2)}) %collective-permute-start.22) | collective-permute-done | bytes 67616 | tf_op jit(solution)/shard_map/ppermute | solution.py:224
  143.0 4.3 %collective-permute-start.23 = (f32[16896]{0:T(1024)S(1)}, f32[16896]{0:T(1024)S(1)}, u32[]{:S(2)}, u32[]{:S(2)}) collective-permute-start(f32[16896]{0:T(1024)S(1)} %add.368), channel_id=1, source_target_pairs={{0,96},{32,0},{64,32},{96,64},{1,97},{33,1},{65,33},{97,65},{2,98}... | collective-permute-start | bytes 202760 | tf_op jit(solution)/shard_map/ppermute | solution.py:33
  149.3 2.5 %collective-permute-start.25 = (f32[16896]{0:T(1024)S(1)}, f32[16896]{0:T(1024)S(1)}, u32[]{:S(2)}, u32[]{:S(2)}) collective-permute-start(f32[16896]{0:T(1024)S(1)} %add.368), channel_id=1, source_target_pairs={{0,32},{32,64},{64,96},{96,0},{1,33},{33,65},{65,97},{97,1},{2,34}... | collective-permute-start | bytes 202760 | tf_op jit(solution)/shard_map/ppermute | solution.py:33
  156.9 5.9 %collective-permute-start.26 = (f32[16896]{0:T(1024)S(1)}, f32[16896]{0:T(1024)S(1)}, u32[]{:S(2)}, u32[]{:S(2)}) collective-permute-start(f32[16896]{0:T(1024)S(1)} %get-tuple-element.3), channel_id=1, source_target_pairs={{0,384},{128,0},{256,128},{384,256},{1,385},{129,1},{257,129},{385... | collective-permute-start | bytes 202760 | tf_op jit(solution)/shard_map/ppermute | solution.py:33
  164.7 4.0 %collective-permute-start.28 = (f32[16896]{0:T(1024)S(1)}, f32[16896]{0:T(1024)S(1)}, u32[]{:S(2)}, u32[]{:S(2)}) collective-permute-start(f32[16896]{0:T(1024)S(1)} %get-tuple-element.3), channel_id=1, source_target_pairs={{0,128},{128,256},{256,384},{384,0},{1,129},{129,257},{257,385},{3... | collective-permute-start | bytes 202760 | tf_op jit(solution)/shard_map/ppermute | solution.py:33
  168.8 3.7 %collective-permute-done.27 = f32[16896]{0:T(1024)S(1)} collective-permute-done((f32[16896]{0:T(1024)S(1)}, f32[16896]{0:T(1024)S(1)}, u32[]{:S(2)}, u32[]{:S(2)}) %collective-permute-start.27) | collective-permute-done | bytes 67616 | tf_op jit(solution)/shard_map/ppermute | solution.py:33
  174.3 3.2 %collective-permute-start.29 = (f32[16896]{0:T(1024)S(1)}, f32[16896]{0:T(1024)S(1)}, u32[]{:S(2)}, u32[]{:S(2)}) collective-permute-start(f32[16896]{0:T(1024)S(1)} %fusion.14), channel_id=1, source_target_pairs={{0,2},{2,0},{1,3},{3,1},{4,6},{6,4},{5,7},{7,5},{8,10},{10,8},{9,1... | collective-permute-start | bytes 202760 | tf_op jit(solution)/shard_map/ppermute | solution.py:132
  179.7 10.0 %collective-permute-start.30 = (f32[33792]{0:T(1024)S(1)}, f32[33792]{0:T(1024)S(1)}, u32[]{:S(2)}, u32[]{:S(2)}) collective-permute-start(f32[33792]{0:T(1024)S(1)} %maximum_select_fusion.2), channel_id=1, source_target_pairs={{0,1},{1,0},{2,3},{3,2},{4,5},{5,4},{6,7},{7,6},{8,9},{9,8},{10,11... | collective-permute-start | bytes 405512 | tf_op jit(solution)/shard_map/ppermute | solution.py:132
  (120 shorter events, 45.7 us)
Async XLA Ops:
  0.6 94.1 %copy-start = (bf16[1,4,8,128,128]{4,3,2,1,0:T(8,128)(2,1)S(1)}, bf16[1,4,8,128,128]{4,3,2,1,0:T(8,128)(2,1)}, u32[]{:S(2)}) copy-start(bf16[1,4,8,128,128]{4,3,2,1,0:T(8,128)(2,1)} %param.11) | copy-start | bytes 3145732
  0.7 15.8 %collective-permute-start = (bf16[128,256]{1,0:T(8,128)(2,1)}, bf16[128,256]{1,0:T(8,128)(2,1)S(1)}, u32[]{:S(2)}, u32[]{:S(2)}) collective-permute-start(bf16[128,256]{1,0:T(8,128)(2,1)} %param.8), channel_id=1, source_target_pairs={{0,256},{128,384},{256,0},{384,128},{1,257},{129,385},{257,1},{385... | collective-permute-start | bytes 196616 | tf_op jit(solution)/shard_map/ppermute | solution.py:26
  9.1 10.1 %collective-permute-start.1 = (bf16[128,256]{1,0:T(8,128)(2,1)}, bf16[128,256]{1,0:T(8,128)(2,1)S(1)}, u32[]{:S(2)}, u32[]{:S(2)}) collective-permute-start(bf16[128,256]{1,0:T(8,128)(2,1)} %param.8), channel_id=1, source_target_pairs={{0,128},{128,256},{256,384},{384,0},{1,129},{129,257},{257,385},{3... | collective-permute-start | bytes 196616 | tf_op jit(solution)/shard_map/ppermute | solution.py:26
  11.5 7.7 %collective-permute-start.2 = (bf16[128,256]{1,0:T(8,128)(2,1)}, bf16[128,256]{1,0:T(8,128)(2,1)S(1)}, u32[]{:S(2)}, u32[]{:S(2)}) collective-permute-start(bf16[128,256]{1,0:T(8,128)(2,1)} %param.8), channel_id=1, source_target_pairs={{0,384},{128,0},{256,128},{384,256},{1,385},{129,1},{257,129},{385... | collective-permute-start | bytes 196616 | tf_op jit(solution)/shard_map/ppermute | solution.py:26
  20.1 14.6 %collective-permute-start.3 = (bf16[4,128,256]{2,1,0:T(8,128)(2,1)S(1)}, bf16[4,128,256]{2,1,0:T(8,128)(2,1)S(1)}, u32[]{:S(2)}, u32[]{:S(2)}) collective-permute-start(bf16[4,128,256]{2,1,0:T(8,128)(2,1)S(1)} %pad_maximum_fusion.4), channel_id=1, source_target_pairs={{0,4},{4,8},{8,12},{12,16},{16,20},{20,24},{24,28},{28,0},{1,5},{5... | collective-permute-start | bytes 786440 | tf_op jit(solution)/shard_map/ppermute | solution.py:52
  24.8 16.0 %collective-permute-start.12 = (s32[8]{0:T(128)S(1)}, s32[8]{0:T(128)S(1)}, u32[]{:S(2)}, u32[]{:S(2)}) collective-permute-start(s32[8]{0:T(128)S(1)} %get-tuple-element.9), channel_id=1, source_target_pairs={{0,64},{32,96},{64,0},{96,32},{1,65},{33,97},{65,1},{97,33},{2,66}... | collective-permute-start | bytes 104 | tf_op jit(solution)/shard_map/ppermute | solution.py:72
  29.4 19.8 %collective-permute-start.14 = (s32[8]{0:T(128)S(1)}, s32[8]{0:T(128)S(1)}, u32[]{:S(2)}, u32[]{:S(2)}) collective-permute-start(s32[8]{0:T(128)S(1)} %get-tuple-element.9), channel_id=1, source_target_pairs={{0,96},{32,0},{64,32},{96,64},{1,97},{33,1},{65,33},{97,65},{2,98}... | collective-permute-start | bytes 104 | tf_op jit(solution)/shard_map/ppermute | solution.py:72
  32.2 17.1 %collective-permute-start.10 = (s32[8]{0:T(128)S(1)}, s32[8]{0:T(128)S(1)}, u32[]{:S(2)}, u32[]{:S(2)}) collective-permute-start(s32[8]{0:T(128)S(1)} %get-tuple-element.9), channel_id=1, source_target_pairs={{0,32},{32,64},{64,96},{96,0},{1,33},{33,65},{65,97},{97,1},{2,34}... | collective-permute-start | bytes 104 | tf_op jit(solution)/shard_map/ppermute | solution.py:72
  34.7 12.6 %collective-permute-start.4 = (bf16[4,128,256]{2,1,0:T(8,128)(2,1)S(1)}, bf16[4,128,256]{2,1,0:T(8,128)(2,1)S(1)}, u32[]{:S(2)}, u32[]{:S(2)}) collective-permute-start(bf16[4,128,256]{2,1,0:T(8,128)(2,1)S(1)} %collective-permute-done.3), channel_id=1, source_target_pairs={{0,4},{4,8},{8,12},{12,16},{16,20},{20,24},{24,28},{28,0},{1,5},{5... | collective-permute-start | bytes 786440 | tf_op jit(solution)/shard_map/ppermute | solution.py:52
  40.8 9.8 %collective-permute-start.7 = (bf16[4,128,256]{2,1,0:T(8,128)(2,1)S(1)}, bf16[4,128,256]{2,1,0:T(8,128)(2,1)S(1)}, u32[]{:S(2)}, u32[]{:S(2)}) collective-permute-start(bf16[4,128,256]{2,1,0:T(8,128)(2,1)S(1)} %pad_maximum_fusion.4), channel_id=1, source_target_pairs={{0,28},{4,0},{8,4},{12,8},{16,12},{20,16},{24,20},{28,24},{1,29},{... | collective-permute-start | bytes 786440 | tf_op jit(solution)/shard_map/ppermute | solution.py:55
  47.3 8.3 %collective-permute-start.5 = (bf16[4,128,256]{2,1,0:T(8,128)(2,1)S(1)}, bf16[4,128,256]{2,1,0:T(8,128)(2,1)S(1)}, u32[]{:S(2)}, u32[]{:S(2)}) collective-permute-start(bf16[4,128,256]{2,1,0:T(8,128)(2,1)S(1)} %collective-permute-done.4), channel_id=1, source_target_pairs={{0,4},{4,8},{8,12},{12,16},{16,20},{20,24},{24,28},{28,0},{1,5},{5... | collective-permute-start | bytes 786440 | tf_op jit(solution)/shard_map/ppermute | solution.py:52
  50.6 8.3 %collective-permute-start.8 = (bf16[4,128,256]{2,1,0:T(8,128)(2,1)S(1)}, bf16[4,128,256]{2,1,0:T(8,128)(2,1)S(1)}, u32[]{:S(2)}, u32[]{:S(2)}) collective-permute-start(bf16[4,128,256]{2,1,0:T(8,128)(2,1)S(1)} %collective-permute-done.7), channel_id=1, source_target_pairs={{0,28},{4,0},{8,4},{12,8},{16,12},{20,16},{24,20},{28,24},{1,29},{... | collective-permute-start | bytes 786440 | tf_op jit(solution)/shard_map/ppermute | solution.py:55
  55.7 8.3 %collective-permute-start.6 = (bf16[4,128,256]{2,1,0:T(8,128)(2,1)S(1)}, bf16[4,128,256]{2,1,0:T(8,128)(2,1)S(1)}, u32[]{:S(2)}, u32[]{:S(2)}) collective-permute-start(bf16[4,128,256]{2,1,0:T(8,128)(2,1)S(1)} %collective-permute-done.5), channel_id=1, source_target_pairs={{0,4},{4,8},{8,12},{12,16},{16,20},{20,24},{24,28},{28,0},{1,5},{5... | collective-permute-start | bytes 786440 | tf_op jit(solution)/shard_map/ppermute | solution.py:52
  58.9 8.3 %collective-permute-start.9 = (bf16[4,128,256]{2,1,0:T(8,128)(2,1)S(1)}, bf16[4,128,256]{2,1,0:T(8,128)(2,1)S(1)}, u32[]{:S(2)}, u32[]{:S(2)}) collective-permute-start(bf16[4,128,256]{2,1,0:T(8,128)(2,1)S(1)} %collective-permute-done.8), channel_id=1, source_target_pairs={{0,28},{4,0},{8,4},{12,8},{16,12},{20,16},{24,20},{28,24},{1,29},{... | collective-permute-start | bytes 786440 | tf_op jit(solution)/shard_map/ppermute | solution.py:55
  68.6 14.5 %collective-permute-start.13 = (bf16[8,128,256]{2,1,0:T(8,128)(2,1)}, bf16[8,128,256]{2,1,0:T(8,128)(2,1)}, u32[]{:S(2)}, u32[]{:S(2)}) collective-permute-start(bf16[8,128,256]{2,1,0:T(8,128)(2,1)} %gather_fusion.1), channel_id=1, source_target_pairs={{0,64},{32,96},{64,0},{96,32},{1,65},{33,97},{65,1},{97,33},{2,66}... | collective-permute-start | bytes 1572872 | tf_op jit(solution)/shard_map/ppermute | solution.py:91
  72.6 22.1 %collective-permute-start.15 = (bf16[8,128,256]{2,1,0:T(8,128)(2,1)}, bf16[8,128,256]{2,1,0:T(8,128)(2,1)}, u32[]{:S(2)}, u32[]{:S(2)}) collective-permute-start(bf16[8,128,256]{2,1,0:T(8,128)(2,1)} %gather_fusion.2), channel_id=1, source_target_pairs={{0,32},{32,64},{64,96},{96,0},{1,33},{33,65},{65,97},{97,1},{2,34}... | collective-permute-start | bytes 1572872 | tf_op jit(solution)/shard_map/ppermute | solution.py:91
  77.9 16.8 %collective-permute-start.11 = (bf16[8,128,256]{2,1,0:T(8,128)(2,1)}, bf16[8,128,256]{2,1,0:T(8,128)(2,1)}, u32[]{:S(2)}, u32[]{:S(2)}) collective-permute-start(bf16[8,128,256]{2,1,0:T(8,128)(2,1)} %gather_fusion), channel_id=1, source_target_pairs={{0,96},{32,0},{64,32},{96,64},{1,97},{33,1},{65,33},{97,65},{2,98}... | collective-permute-start | bytes 1572872 | tf_op jit(solution)/shard_map/ppermute | solution.py:91
  97.2 7.5 %collective-permute-start.16 = (f32[512,256]{1,0:T(8,128)S(1)}, f32[512,256]{1,0:T(8,128)S(1)}, u32[]{:S(2)}, u32[]{:S(2)}) collective-permute-start(f32[512,256]{1,0:T(8,128)S(1)} %bitcast.71), channel_id=1, source_target_pairs={{0,1},{1,0},{2,3},{3,2},{4,5},{5,4},{6,7},{7,6},{8,9},{9,8},{10,11... | collective-permute-start | bytes 1572872 | tf_op jit(solution)/shard_map/ppermute | solution.py:163
  104.8 17.8 %collective-permute-start.17 = (f32[512,256]{1,0:T(8,128)S(1)}, f32[512,256]{1,0:T(8,128)S(1)}, u32[]{:S(2)}, u32[]{:S(2)}) collective-permute-start(f32[512,256]{1,0:T(8,128)S(1)} %bitcast_add_fusion), channel_id=1, source_target_pairs={{0,2},{2,0},{1,3},{3,1},{4,6},{6,4},{5,7},{7,5},{8,10},{10,8},{9,1... | collective-permute-start | bytes 1572872 | tf_op jit(solution)/shard_map/ppermute | solution.py:163
  107.0 3.5 %collective-permute-start.18 = (bf16[128,256]{1,0:T(8,128)(2,1)S(1)}, bf16[128,256]{1,0:T(8,128)(2,1)S(1)}, u32[]{:S(2)}, u32[]{:S(2)}) collective-permute-start(bf16[128,256]{1,0:T(8,128)(2,1)S(1)} %copy-done.6), channel_id=1, source_target_pairs={{0,1},{1,0},{2,3},{3,2},{4,5},{5,4},{6,7},{7,6},{8,9},{9,8},{10,11... | collective-permute-start | bytes 196616 | tf_op jit(solution)/shard_map/ppermute | solution.py:163
  110.5 12.1 %collective-permute-start.19 = (bf16[2,128,256]{2,1,0:T(8,128)(2,1)S(1)}, bf16[2,128,256]{2,1,0:T(8,128)(2,1)S(1)}, u32[]{:S(2)}, u32[]{:S(2)}) collective-permute-start(bf16[2,128,256]{2,1,0:T(8,128)(2,1)S(1)} %maximum_select_fusion.3), channel_id=1, source_target_pairs={{0,2},{2,0},{1,3},{3,1},{4,6},{6,4},{5,7},{7,5},{8,10},{10,8},{9,1... | collective-permute-start | bytes 393224 | tf_op jit(solution)/shard_map/ppermute | solution.py:163
  123.9 5.1 %collective-permute-start.20 = (f32[16896]{0:T(1024)S(1)}, f32[16896]{0:T(1024)S(1)}, u32[]{:S(2)}, u32[]{:S(2)}) collective-permute-start(f32[16896]{0:T(1024)S(1)} %dynamic-slice_reduce_fusion), channel_id=1, source_target_pairs={{0,4},{4,0},{8,12},{12,8},{16,20},{20,16},{24,28},{28,24},{1,5},{5... | collective-permute-start | bytes 202760 | tf_op jit(solution)/shard_map/ppermute | solution.py:224
  128.9 7.8 %collective-permute-start.21 = (f32[16896]{0:T(1024)S(1)}, f32[16896]{0:T(1024)S(1)}, u32[]{:S(2)}, u32[]{:S(2)}) collective-permute-start(f32[16896]{0:T(1024)S(1)} %add.366), channel_id=1, source_target_pairs={{0,8},{4,12},{8,0},{12,4},{16,24},{20,28},{24,16},{28,20},{1,9},{5... | collective-permute-start | bytes 202760 | tf_op jit(solution)/shard_map/ppermute | solution.py:224
  136.8 6.3 %collective-permute-start.22 = (f32[16896]{0:T(1024)S(1)}, f32[16896]{0:T(1024)S(1)}, u32[]{:S(2)}, u32[]{:S(2)}) collective-permute-start(f32[16896]{0:T(1024)S(1)} %add.367), channel_id=1, source_target_pairs={{0,28},{4,24},{8,20},{12,16},{16,12},{20,8},{24,4},{28,0},{1,29},{... | collective-permute-start | bytes 202760 | tf_op jit(solution)/shard_map/ppermute | solution.py:224
  143.0 8.8 %collective-permute-start.23 = (f32[16896]{0:T(1024)S(1)}, f32[16896]{0:T(1024)S(1)}, u32[]{:S(2)}, u32[]{:S(2)}) collective-permute-start(f32[16896]{0:T(1024)S(1)} %add.368), channel_id=1, source_target_pairs={{0,96},{32,0},{64,32},{96,64},{1,97},{33,1},{65,33},{97,65},{2,98}... | collective-permute-start | bytes 202760 | tf_op jit(solution)/shard_map/ppermute | solution.py:33
  147.3 6.6 %collective-permute-start.24 = (f32[16896]{0:T(1024)S(1)}, f32[16896]{0:T(1024)S(1)}, u32[]{:S(2)}, u32[]{:S(2)}) collective-permute-start(f32[16896]{0:T(1024)S(1)} %add.368), channel_id=1, source_target_pairs={{0,64},{32,96},{64,0},{96,32},{1,65},{33,97},{65,1},{97,33},{2,66}... | collective-permute-start | bytes 202760 | tf_op jit(solution)/shard_map/ppermute | solution.py:33
  149.3 6.3 %collective-permute-start.25 = (f32[16896]{0:T(1024)S(1)}, f32[16896]{0:T(1024)S(1)}, u32[]{:S(2)}, u32[]{:S(2)}) collective-permute-start(f32[16896]{0:T(1024)S(1)} %add.368), channel_id=1, source_target_pairs={{0,32},{32,64},{64,96},{96,0},{1,33},{33,65},{65,97},{97,1},{2,34}... | collective-permute-start | bytes 202760 | tf_op jit(solution)/shard_map/ppermute | solution.py:33
  156.9 11.9 %collective-permute-start.26 = (f32[16896]{0:T(1024)S(1)}, f32[16896]{0:T(1024)S(1)}, u32[]{:S(2)}, u32[]{:S(2)}) collective-permute-start(f32[16896]{0:T(1024)S(1)} %get-tuple-element.3), channel_id=1, source_target_pairs={{0,384},{128,0},{256,128},{384,256},{1,385},{129,1},{257,129},{385... | collective-permute-start | bytes 202760 | tf_op jit(solution)/shard_map/ppermute | solution.py:33
  162.8 9.8 %collective-permute-start.27 = (f32[16896]{0:T(1024)S(1)}, f32[16896]{0:T(1024)S(1)}, u32[]{:S(2)}, u32[]{:S(2)}) collective-permute-start(f32[16896]{0:T(1024)S(1)} %get-tuple-element.3), channel_id=1, source_target_pairs={{0,256},{128,384},{256,0},{384,128},{1,257},{129,385},{257,1},{385... | collective-permute-start | bytes 202760 | tf_op jit(solution)/shard_map/ppermute | solution.py:33
  164.7 8.3 %collective-permute-start.28 = (f32[16896]{0:T(1024)S(1)}, f32[16896]{0:T(1024)S(1)}, u32[]{:S(2)}, u32[]{:S(2)}) collective-permute-start(f32[16896]{0:T(1024)S(1)} %get-tuple-element.3), channel_id=1, source_target_pairs={{0,128},{128,256},{256,384},{384,0},{1,129},{129,257},{257,385},{3... | collective-permute-start | bytes 202760 | tf_op jit(solution)/shard_map/ppermute | solution.py:33
  174.3 5.3 %collective-permute-start.29 = (f32[16896]{0:T(1024)S(1)}, f32[16896]{0:T(1024)S(1)}, u32[]{:S(2)}, u32[]{:S(2)}) collective-permute-start(f32[16896]{0:T(1024)S(1)} %fusion.14), channel_id=1, source_target_pairs={{0,2},{2,0},{1,3},{3,1},{4,6},{6,4},{5,7},{7,5},{8,10},{10,8},{9,1... | collective-permute-start | bytes 202760 | tf_op jit(solution)/shard_map/ppermute | solution.py:132
  179.7 11.0 %collective-permute-start.30 = (f32[33792]{0:T(1024)S(1)}, f32[33792]{0:T(1024)S(1)}, u32[]{:S(2)}, u32[]{:S(2)}) collective-permute-start(f32[33792]{0:T(1024)S(1)} %maximum_select_fusion.2), channel_id=1, source_target_pairs={{0,1},{1,0},{2,3},{3,2},{4,5},{5,4},{6,7},{7,6},{8,9},{9,8},{10,11... | collective-permute-start | bytes 405512 | tf_op jit(solution)/shard_map/ppermute | solution.py:132
  (10 other events, 260.4 us)

commit v13 on v10

--- a/solution.py
+++ b/solution.py
@@ -13,6 +13,18 @@
     rows, rep = mesh.devices.shape
     y_hi, x, y_lo = 4, 4, 2
     return Mesh(mesh.devices.reshape(y_hi, x, rows // (y_hi * x), y_lo, rep // y_lo), ALL_AXES)
+
+
+def round_gather(piece, axis):
+    n = lax.axis_size(axis)
+    pieces = []
+    for k in range(n):
+        d = k - n // 2
+        if d == 0:
+            pieces.append(piece)
+        else:
+            pieces.append(lax.ppermute(piece, axis, [(i, (i - d) % n) for i in range(n)]))
+    return jnp.stack(pieces)
 
 
 def ring_gather(piece, axis):
@@ -48,7 +60,7 @@
     }
     stack = features
     for a in within:
-        stack = ring_gather(stack, a)
+        stack = round_gather(stack, a) if lax.axis_size(a) <= 4 else ring_gather(stack, a)
     plane = stack.reshape(-1, features.shape[0], features.shape[1])
 
     def in_plane(c):

time: 190 us -> 190 us (level)
    ppermute x0 -> x3, starting transfers between devices: none -> 15.8 us  [round_gather(): lax.ppermute(piece, axis, [(i, (i - d) % n) for i in range(n)])]
    ppermute x6 -> x4, starting transfers between devices: 21.2 us -> 11.2 us  [ring_gather(): left = lax.ppermute(left, axis, fwd)]
    ppermute x4 -> x3, starting transfers between devices: 20.1 us -> 16.5 us  [ring_gather(): right = lax.ppermute(right, axis, bwd)]
    ppermute x0 -> x3, waiting for transfers between devices: none -> 2.69 us  [round_gather(): lax.ppermute(piece, axis, [(i, (i - d) % n) for i in range(n)])]
    ppermute x6 -> x4, waiting for transfers between devices: 2.09 us -> 0.03 us  [ring_gather(): left = lax.ppermute(left, axis, fwd)]
    ppermute x4, starting transfers between devices: 15.8 us -> 13.8 us  [swap(): return lax.ppermute(x, axis, [(0, 1), (1, 0)])]
    ppermute x4 -> x3, waiting for transfers between devices: 6.03 us -> 4.88 us  [ring_gather(): right = lax.ppermute(right, axis, bwd)]
  transfers between devices with their start and end apart: 29 -> 29, of which waited for: 19 -> 17; matrix products, arithmetic and copies ran while one was open for 5% -> 5% of each run, Pallas kernels for 0% -> 0%
where the time goes in v13:
time: 190 us; the launch traced here: 188 us
  starting transfers between devices  118 us (62%)
  waiting for transfers between devices  51.1 us (27%)
  local copies, waits for them, and re-layouts  8.95 us (5%)
  other arithmetic  5.96 us (3%)
  matrix products  3.04 us (2%)
    ppermute x7, starting transfers between devices, shards(): flat = flat + lax.ppermute(flat, a, perm)  27.2 us
    ppermute x7, waiting for transfers between devices, shards(): flat = flat + lax.ppermute(flat, a, perm)  17.3 us
    ppermute x3, starting transfers between devices, ring_gather(): right = lax.ppermute(right, axis, bwd)  16.5 us
    ppermute x3, starting transfers between devices, round_gather(): lax.ppermute(piece, axis, [(i, (i - d) % n) for i in range(n)])  15.8 us
    ppermute x2, starting transfers between devices, all_gather_flat(): other = lax.ppermute(flat, a, perm)  14 us
    ppermute x4, starting transfers between devices, swap(): return lax.ppermute(x, axis, [(0, 1), (1, 0)])  13.8 us
    ppermute x3, waiting for transfers between devices, plane_blocks(): lax.ppermute(sent, across, [(i, (i + s) % n_across) for i in range(n_acro...  11.6 us
    ppermute x4, waiting for transfers between devices, swap(): return lax.ppermute(x, axis, [(0, 1), (1, 0)])  11.3 us
  transfers between devices with their start and end apart: 29, of which 17 were waited for; matrix products, arithmetic and copies ran while one was open for 5% of the time, Pallas kernels for 0%

profile of v13, /device:TPU:1, one launch (start us, length us, event | category | flops | bytes accessed | tf_op | source)
XLA Modules:
  0.0 187.9 jit_solution(10778533068804762638)
XLA Ops:
  0.7 8.4 %collective-permute-start = (bf16[128,256]{1,0:T(8,128)(2,1)}, bf16[128,256]{1,0:T(8,128)(2,1)S(1)}, u32[]{:S(2)}, u32[]{:S(2)}) collective-permute-start(bf16[128,256]{1,0:T(8,128)(2,1)} %param.8), channel_id=1, source_target_pairs={{0,256},{128,384},{256,0},{384,128},{1,257},{129,385},{257,1},{385... | collective-permute-start | bytes 196616 | tf_op jit(solution)/shard_map/ppermute | solution.py:26
  9.1 2.4 %collective-permute-start.1 = (bf16[128,256]{1,0:T(8,128)(2,1)}, bf16[128,256]{1,0:T(8,128)(2,1)S(1)}, u32[]{:S(2)}, u32[]{:S(2)}) collective-permute-start(bf16[128,256]{1,0:T(8,128)(2,1)} %param.8), channel_id=1, source_target_pairs={{0,128},{128,256},{256,384},{384,0},{1,129},{129,257},{257,385},{3... | collective-permute-start | bytes 196616 | tf_op jit(solution)/shard_map/ppermute | solution.py:26
  11.5 5.0 %collective-permute-start.2 = (bf16[128,256]{1,0:T(8,128)(2,1)}, bf16[128,256]{1,0:T(8,128)(2,1)S(1)}, u32[]{:S(2)}, u32[]{:S(2)}) collective-permute-start(bf16[128,256]{1,0:T(8,128)(2,1)} %param.8), channel_id=1, source_target_pairs={{0,384},{128,0},{256,128},{384,256},{1,385},{129,1},{257,129},{385... | collective-permute-start | bytes 196616 | tf_op jit(solution)/shard_map/ppermute | solution.py:26
  16.5 2.7 %collective-permute-done.1 = bf16[128,256]{1,0:T(8,128)(2,1)S(1)} collective-permute-done((bf16[128,256]{1,0:T(8,128)(2,1)}, bf16[128,256]{1,0:T(8,128)(2,1)S(1)}, u32[]{:S(2)}, u32[]{:S(2)}) %collective-permute-start.1) | collective-permute-done | bytes 65568 | tf_op jit(solution)/shard_map/ppermute | solution.py:26
  20.1 3.4 %collective-permute-start.3 = (bf16[4,128,256]{2,1,0:T(8,128)(2,1)S(1)}, bf16[4,128,256]{2,1,0:T(8,128)(2,1)S(1)}, u32[]{:S(2)}, u32[]{:S(2)}) collective-permute-start(bf16[4,128,256]{2,1,0:T(8,128)(2,1)S(1)} %pad_maximum_fusion.2), channel_id=1, source_target_pairs={{0,4},{4,8},{8,12},{12,16},{16,20},{20,24},{24,28},{28,0},{1,5},{5... | collective-permute-start | bytes 786440 | tf_op jit(solution)/shard_map/ppermute | solution.py:38
  24.8 4.6 %collective-permute-start.12 = (s32[8]{0:T(128)S(1)}, s32[8]{0:T(128)S(1)}, u32[]{:S(2)}, u32[]{:S(2)}) collective-permute-start(s32[8]{0:T(128)S(1)} %get-tuple-element.7), channel_id=1, source_target_pairs={{0,64},{32,96},{64,0},{96,32},{1,65},{33,97},{65,1},{97,33},{2,66}... | collective-permute-start | bytes 104 | tf_op jit(solution)/shard_map/ppermute | solution.py:58
  29.4 2.8 %collective-permute-start.14 = (s32[8]{0:T(128)S(1)}, s32[8]{0:T(128)S(1)}, u32[]{:S(2)}, u32[]{:S(2)}) collective-permute-start(s32[8]{0:T(128)S(1)} %get-tuple-element.7), channel_id=1, source_target_pairs={{0,96},{32,0},{64,32},{96,64},{1,97},{33,1},{65,33},{97,65},{2,98}... | collective-permute-start | bytes 104 | tf_op jit(solution)/shard_map/ppermute | solution.py:58
  32.2 2.5 %collective-permute-start.10 = (s32[8]{0:T(128)S(1)}, s32[8]{0:T(128)S(1)}, u32[]{:S(2)}, u32[]{:S(2)}) collective-permute-start(s32[8]{0:T(128)S(1)} %get-tuple-element.7), channel_id=1, source_target_pairs={{0,32},{32,64},{64,96},{96,0},{1,33},{33,65},{65,97},{97,1},{2,34}... | collective-permute-start | bytes 104 | tf_op jit(solution)/shard_map/ppermute | solution.py:58
  34.7 4.0 %collective-permute-start.4 = (bf16[4,128,256]{2,1,0:T(8,128)(2,1)S(1)}, bf16[4,128,256]{2,1,0:T(8,128)(2,1)S(1)}, u32[]{:S(2)}, u32[]{:S(2)}) collective-permute-start(bf16[4,128,256]{2,1,0:T(8,128)(2,1)S(1)} %collective-permute-done.3), channel_id=1, source_target_pairs={{0,4},{4,8},{8,12},{12,16},{16,20},{20,24},{24,28},{28,0},{1,5},{5... | collective-permute-start | bytes 786440 | tf_op jit(solution)/shard_map/ppermute | solution.py:38
  40.7 6.5 %collective-permute-start.7 = (bf16[4,128,256]{2,1,0:T(8,128)(2,1)S(1)}, bf16[4,128,256]{2,1,0:T(8,128)(2,1)S(1)}, u32[]{:S(2)}, u32[]{:S(2)}) collective-permute-start(bf16[4,128,256]{2,1,0:T(8,128)(2,1)S(1)} %pad_maximum_fusion.2), channel_id=1, source_target_pairs={{0,28},{4,0},{8,4},{12,8},{16,12},{20,16},{24,20},{28,24},{1,29},{... | collective-permute-start | bytes 786440 | tf_op jit(solution)/shard_map/ppermute | solution.py:41
  50.5 5.0 %collective-permute-start.8 = (bf16[4,128,256]{2,1,0:T(8,128)(2,1)S(1)}, bf16[4,128,256]{2,1,0:T(8,128)(2,1)S(1)}, u32[]{:S(2)}, u32[]{:S(2)}) collective-permute-start(bf16[4,128,256]{2,1,0:T(8,128)(2,1)S(1)} %collective-permute-done.7), channel_id=1, source_target_pairs={{0,28},{4,0},{8,4},{12,8},{16,12},{20,16},{24,20},{28,24},{1,29},{... | collective-permute-start | bytes 786440 | tf_op jit(solution)/shard_map/ppermute | solution.py:41
  58.9 5.0 %collective-permute-start.9 = (bf16[4,128,256]{2,1,0:T(8,128)(2,1)S(1)}, bf16[4,128,256]{2,1,0:T(8,128)(2,1)S(1)}, u32[]{:S(2)}, u32[]{:S(2)}) collective-permute-start(bf16[4,128,256]{2,1,0:T(8,128)(2,1)S(1)} %collective-permute-done.8), channel_id=1, source_target_pairs={{0,28},{4,0},{8,4},{12,8},{16,12},{20,16},{24,20},{28,24},{1,29},{... | collective-permute-start | bytes 786440 | tf_op jit(solution)/shard_map/ppermute | solution.py:41
  68.6 2.5 %collective-permute-start.13 = (bf16[8,128,256]{2,1,0:T(8,128)(2,1)}, bf16[8,128,256]{2,1,0:T(8,128)(2,1)}, u32[]{:S(2)}, u32[]{:S(2)}) collective-permute-start(bf16[8,128,256]{2,1,0:T(8,128)(2,1)} %gather_fusion.1), channel_id=1, source_target_pairs={{0,64},{32,96},{64,0},{96,32},{1,65},{33,97},{65,1},{97,33},{2,66}... | collective-permute-start | bytes 1572872 | tf_op jit(solution)/shard_map/ppermute | solution.py:77
  72.5 3.9 %collective-permute-start.15 = (bf16[8,128,256]{2,1,0:T(8,128)(2,1)}, bf16[8,128,256]{2,1,0:T(8,128)(2,1)}, u32[]{:S(2)}, u32[]{:S(2)}) collective-permute-start(bf16[8,128,256]{2,1,0:T(8,128)(2,1)} %gather_fusion.2), channel_id=1, source_target_pairs={{0,32},{32,64},{64,96},{96,0},{1,33},{33,65},{65,97},{97,1},{2,34}... | collective-permute-start | bytes 1572872 | tf_op jit(solution)/shard_map/ppermute | solution.py:77
  77.8 2.6 %collective-permute-start.11 = (bf16[8,128,256]{2,1,0:T(8,128)(2,1)}, bf16[8,128,256]{2,1,0:T(8,128)(2,1)}, u32[]{:S(2)}, u32[]{:S(2)}) collective-permute-start(bf16[8,128,256]{2,1,0:T(8,128)(2,1)} %gather_fusion), channel_id=1, source_target_pairs={{0,96},{32,0},{64,32},{96,64},{1,97},{33,1},{65,33},{97,65},{2,98}... | collective-permute-start | bytes 1572872 | tf_op jit(solution)/shard_map/ppermute | solution.py:77
  83.1 11.6 %collective-permute-done.15 = bf16[8,128,256]{2,1,0:T(8,128)(2,1)} collective-permute-done((bf16[8,128,256]{2,1,0:T(8,128)(2,1)}, bf16[8,128,256]{2,1,0:T(8,128)(2,1)}, u32[]{:S(2)}, u32[]{:S(2)}) %collective-permute-start.15) | collective-permute-done | bytes 524320 | tf_op jit(solution)/shard_map/ppermute | solution.py:77
  97.1 6.0 %collective-permute-start.16 = (f32[512,256]{1,0:T(8,128)S(1)}, f32[512,256]{1,0:T(8,128)S(1)}, u32[]{:S(2)}, u32[]{:S(2)}) collective-permute-start(f32[512,256]{1,0:T(8,128)S(1)} %bitcast.67), channel_id=1, source_target_pairs={{0,1},{1,0},{2,3},{3,2},{4,5},{5,4},{6,7},{7,6},{8,9},{9,8},{10,11... | collective-permute-start | bytes 1572872 | tf_op jit(solution)/shard_map/ppermute | solution.py:149
  106.9 2.6 %collective-permute-start.18 = (bf16[128,256]{1,0:T(8,128)(2,1)S(1)}, bf16[128,256]{1,0:T(8,128)(2,1)S(1)}, u32[]{:S(2)}, u32[]{:S(2)}) collective-permute-start(bf16[128,256]{1,0:T(8,128)(2,1)S(1)} %copy-done.6), channel_id=1, source_target_pairs={{0,1},{1,0},{2,3},{3,2},{4,5},{5,4},{6,7},{7,6},{8,9},{9,8},{10,11... | collective-permute-start | bytes 196616 | tf_op jit(solution)/shard_map/ppermute | solution.py:149
  110.4 3.1 %collective-permute-start.19 = (bf16[2,128,256]{2,1,0:T(8,128)(2,1)S(1)}, bf16[2,128,256]{2,1,0:T(8,128)(2,1)S(1)}, u32[]{:S(2)}, u32[]{:S(2)}) collective-permute-start(bf16[2,128,256]{2,1,0:T(8,128)(2,1)S(1)} %maximum_select_fusion.3), channel_id=1, source_target_pairs={{0,2},{2,0},{1,3},{3,1},{4,6},{6,4},{5,7},{7,5},{8,10},{10,8},{9,1... | collective-permute-start | bytes 393224 | tf_op jit(solution)/shard_map/ppermute | solution.py:149
  113.6 8.9 %collective-permute-done.19 = bf16[2,128,256]{2,1,0:T(8,128)(2,1)S(1)} collective-permute-done((bf16[2,128,256]{2,1,0:T(8,128)(2,1)S(1)}, bf16[2,128,256]{2,1,0:T(8,128)(2,1)S(1)}, u32[]{:S(2)}, u32[]{:S(2)}) %collective-permute-start.19) | collective-permute-done | bytes 131104 | tf_op jit(solution)/shard_map/ppermute | solution.py:149
  125.8 3.1 %collective-permute-done.20 = f32[16896]{0:T(1024)S(1)} collective-permute-done((f32[16896]{0:T(1024)S(1)}, f32[16896]{0:T(1024)S(1)}, u32[]{:S(2)}, u32[]{:S(2)}) %collective-permute-start.20) | collective-permute-done | bytes 67616 | tf_op jit(solution)/shard_map/ppermute | solution.py:206
  128.9 6.1 %collective-permute-start.21 = (f32[16896]{0:T(1024)S(1)}, f32[16896]{0:T(1024)S(1)}, u32[]{:S(2)}, u32[]{:S(2)}) collective-permute-start(f32[16896]{0:T(1024)S(1)} %add.315), channel_id=1, source_target_pairs={{0,8},{4,12},{8,0},{12,4},{16,24},{20,28},{24,16},{28,20},{1,9},{5... | collective-permute-start | bytes 202760 | tf_op jit(solution)/shard_map/ppermute | solution.py:206
  136.7 3.9 %collective-permute-start.22 = (f32[16896]{0:T(1024)S(1)}, f32[16896]{0:T(1024)S(1)}, u32[]{:S(2)}, u32[]{:S(2)}) collective-permute-start(f32[16896]{0:T(1024)S(1)} %add.316), channel_id=1, source_target_pairs={{0,28},{4,24},{8,20},{12,16},{16,12},{20,8},{24,4},{28,0},{1,29},{... | collective-permute-start | bytes 202760 | tf_op jit(solution)/shard_map/ppermute | solution.py:206
  140.6 2.3 %collective-permute-done.22 = f32[16896]{0:T(1024)S(1)} collective-permute-done((f32[16896]{0:T(1024)S(1)}, f32[16896]{0:T(1024)S(1)}, u32[]{:S(2)}, u32[]{:S(2)}) %collective-permute-start.22) | collective-permute-done | bytes 67616 | tf_op jit(solution)/shard_map/ppermute | solution.py:206
  143.0 2.5 %collective-permute-start.23 = (f32[16896]{0:T(1024)S(1)}, f32[16896]{0:T(1024)S(1)}, u32[]{:S(2)}, u32[]{:S(2)}) collective-permute-start(f32[16896]{0:T(1024)S(1)} %add.317), channel_id=1, source_target_pairs={{0,32},{32,0},{64,96},{96,64},{1,33},{33,1},{65,97},{97,65},{2,34}... | collective-permute-start | bytes 202760 | tf_op jit(solution)/shard_map/ppermute | solution.py:206
  145.4 2.6 %collective-permute-done.23 = f32[16896]{0:T(1024)S(1)} collective-permute-done((f32[16896]{0:T(1024)S(1)}, f32[16896]{0:T(1024)S(1)}, u32[]{:S(2)}, u32[]{:S(2)}) %collective-permute-start.23) | collective-permute-done | bytes 67616 | tf_op jit(solution)/shard_map/ppermute | solution.py:206
  148.0 4.3 %collective-permute-start.24 = (f32[16896]{0:T(1024)S(1)}, f32[16896]{0:T(1024)S(1)}, u32[]{:S(2)}, u32[]{:S(2)}) collective-permute-start(f32[16896]{0:T(1024)S(1)} %add.318), channel_id=1, source_target_pairs={{0,96},{32,64},{64,32},{96,0},{1,97},{33,65},{65,33},{97,1},{2,98}... | collective-permute-start | bytes 202760 | tf_op jit(solution)/shard_map/ppermute | solution.py:206
  154.3 3.0 %collective-permute-start.25 = (f32[16896]{0:T(1024)S(1)}, f32[16896]{0:T(1024)S(1)}, u32[]{:S(2)}, u32[]{:S(2)}) collective-permute-start(f32[16896]{0:T(1024)S(1)} %add.319), channel_id=1, source_target_pairs={{0,128},{128,0},{256,384},{384,256},{1,129},{129,1},{257,385},{385... | collective-permute-start | bytes 202760 | tf_op jit(solution)/shard_map/ppermute | solution.py:206
  157.3 3.7 %collective-permute-done.25 = f32[16896]{0:T(1024)S(1)} collective-permute-done((f32[16896]{0:T(1024)S(1)}, f32[16896]{0:T(1024)S(1)}, u32[]{:S(2)}, u32[]{:S(2)}) %collective-permute-start.25) | collective-permute-done | bytes 67616 | tf_op jit(solution)/shard_map/ppermute | solution.py:206
  161.0 5.4 %collective-permute-start.26 = (f32[16896]{0:T(1024)S(1)}, f32[16896]{0:T(1024)S(1)}, u32[]{:S(2)}, u32[]{:S(2)}) collective-permute-start(f32[16896]{0:T(1024)S(1)} %add.320), channel_id=1, source_target_pairs={{0,384},{128,256},{256,128},{384,0},{1,385},{129,257},{257,129},{3... | collective-permute-start | bytes 202760 | tf_op jit(solution)/shard_map/ppermute | solution.py:206
  170.3 3.1 %collective-permute-done.27 = f32[16896]{0:T(1024)S(1)} collective-permute-done((f32[16896]{0:T(1024)S(1)}, f32[16896]{0:T(1024)S(1)}, u32[]{:S(2)}, u32[]{:S(2)}) %collective-permute-start.27) | collective-permute-done | bytes 67616 | tf_op jit(solution)/shard_map/ppermute | solution.py:118
  173.5 12.1 %collective-permute-start.28 = (f32[33792]{0:T(1024)S(1)}, f32[33792]{0:T(1024)S(1)}, u32[]{:S(2)}, u32[]{:S(2)}) collective-permute-start(f32[33792]{0:T(1024)S(1)} %maximum_select_fusion.2), channel_id=1, source_target_pairs={{0,1},{1,0},{2,3},{3,2},{4,5},{5,4},{6,7},{7,6},{8,9},{9,8},{10,11... | collective-permute-start | bytes 405512 | tf_op jit(solution)/shard_map/ppermute | solution.py:118
  (103 shorter events, 41.0 us)
Async XLA Ops:
  0.6 94.0 %copy-start = (bf16[1,4,8,128,128]{4,3,2,1,0:T(8,128)(2,1)S(1)}, bf16[1,4,8,128,128]{4,3,2,1,0:T(8,128)(2,1)}, u32[]{:S(2)}) copy-start(bf16[1,4,8,128,128]{4,3,2,1,0:T(8,128)(2,1)} %param.11) | copy-start | bytes 3145732
  0.6 63.4 %copy-start.1 = (bf16[128,256]{1,0:T(8,128)(2,1)S(1)}, bf16[128,256]{1,0:T(8,128)(2,1)}, u32[]{:S(2)}) copy-start(bf16[128,256]{1,0:T(8,128)(2,1)} %param.8) | copy-start | bytes 196612
  0.7 15.8 %collective-permute-start = (bf16[128,256]{1,0:T(8,128)(2,1)}, bf16[128,256]{1,0:T(8,128)(2,1)S(1)}, u32[]{:S(2)}, u32[]{:S(2)}) collective-permute-start(bf16[128,256]{1,0:T(8,128)(2,1)} %param.8), channel_id=1, source_target_pairs={{0,256},{128,384},{256,0},{384,128},{1,257},{129,385},{257,1},{385... | collective-permute-start | bytes 196616 | tf_op jit(solution)/shard_map/ppermute | solution.py:26
  9.1 10.1 %collective-permute-start.1 = (bf16[128,256]{1,0:T(8,128)(2,1)}, bf16[128,256]{1,0:T(8,128)(2,1)S(1)}, u32[]{:S(2)}, u32[]{:S(2)}) collective-permute-start(bf16[128,256]{1,0:T(8,128)(2,1)} %param.8), channel_id=1, source_target_pairs={{0,128},{128,256},{256,384},{384,0},{1,129},{129,257},{257,385},{3... | collective-permute-start | bytes 196616 | tf_op jit(solution)/shard_map/ppermute | solution.py:26
  11.5 7.7 %collective-permute-start.2 = (bf16[128,256]{1,0:T(8,128)(2,1)}, bf16[128,256]{1,0:T(8,128)(2,1)S(1)}, u32[]{:S(2)}, u32[]{:S(2)}) collective-permute-start(bf16[128,256]{1,0:T(8,128)(2,1)} %param.8), channel_id=1, source_target_pairs={{0,384},{128,0},{256,128},{384,256},{1,385},{129,1},{257,129},{385... | collective-permute-start | bytes 196616 | tf_op jit(solution)/shard_map/ppermute | solution.py:26
  19.2 44.7 %copy-start.4 = (bf16[128,256]{1,0:T(8,128)(2,1)}, bf16[128,256]{1,0:T(8,128)(2,1)S(1)}, u32[]{:S(2)}) copy-start(bf16[128,256]{1,0:T(8,128)(2,1)S(1)} %collective-permute-done.2) | copy-start | bytes 196612
  20.1 14.6 %collective-permute-start.3 = (bf16[4,128,256]{2,1,0:T(8,128)(2,1)S(1)}, bf16[4,128,256]{2,1,0:T(8,128)(2,1)S(1)}, u32[]{:S(2)}, u32[]{:S(2)}) collective-permute-start(bf16[4,128,256]{2,1,0:T(8,128)(2,1)S(1)} %pad_maximum_fusion.2), channel_id=1, source_target_pairs={{0,4},{4,8},{8,12},{12,16},{16,20},{20,24},{24,28},{28,0},{1,5},{5... | collective-permute-start | bytes 786440 | tf_op jit(solution)/shard_map/ppermute | solution.py:38
  24.8 15.9 %collective-permute-start.12 = (s32[8]{0:T(128)S(1)}, s32[8]{0:T(128)S(1)}, u32[]{:S(2)}, u32[]{:S(2)}) collective-permute-start(s32[8]{0:T(128)S(1)} %get-tuple-element.7), channel_id=1, source_target_pairs={{0,64},{32,96},{64,0},{96,32},{1,65},{33,97},{65,1},{97,33},{2,66}... | collective-permute-start | bytes 104 | tf_op jit(solution)/shard_map/ppermute | solution.py:58
  29.4 19.8 %collective-permute-start.14 = (s32[8]{0:T(128)S(1)}, s32[8]{0:T(128)S(1)}, u32[]{:S(2)}, u32[]{:S(2)}) collective-permute-start(s32[8]{0:T(128)S(1)} %get-tuple-element.7), channel_id=1, source_target_pairs={{0,96},{32,0},{64,32},{96,64},{1,97},{33,1},{65,33},{97,65},{2,98}... | collective-permute-start | bytes 104 | tf_op jit(solution)/shard_map/ppermute | solution.py:58
  32.2 17.1 %collective-permute-start.10 = (s32[8]{0:T(128)S(1)}, s32[8]{0:T(128)S(1)}, u32[]{:S(2)}, u32[]{:S(2)}) collective-permute-start(s32[8]{0:T(128)S(1)} %get-tuple-element.7), channel_id=1, source_target_pairs={{0,32},{32,64},{64,96},{96,0},{1,33},{33,65},{65,97},{97,1},{2,34}... | collective-permute-start | bytes 104 | tf_op jit(solution)/shard_map/ppermute | solution.py:58
  34.7 12.5 %collective-permute-start.4 = (bf16[4,128,256]{2,1,0:T(8,128)(2,1)S(1)}, bf16[4,128,256]{2,1,0:T(8,128)(2,1)S(1)}, u32[]{:S(2)}, u32[]{:S(2)}) collective-permute-start(bf16[4,128,256]{2,1,0:T(8,128)(2,1)S(1)} %collective-permute-done.3), channel_id=1, source_target_pairs={{0,4},{4,8},{8,12},{12,16},{16,20},{20,24},{24,28},{28,0},{1,5},{5... | collective-permute-start | bytes 786440 | tf_op jit(solution)/shard_map/ppermute | solution.py:38
  40.7 9.8 %collective-permute-start.7 = (bf16[4,128,256]{2,1,0:T(8,128)(2,1)S(1)}, bf16[4,128,256]{2,1,0:T(8,128)(2,1)S(1)}, u32[]{:S(2)}, u32[]{:S(2)}) collective-permute-start(bf16[4,128,256]{2,1,0:T(8,128)(2,1)S(1)} %pad_maximum_fusion.2), channel_id=1, source_target_pairs={{0,28},{4,0},{8,4},{12,8},{16,12},{20,16},{24,20},{28,24},{1,29},{... | collective-permute-start | bytes 786440 | tf_op jit(solution)/shard_map/ppermute | solution.py:41
  47.3 8.3 %collective-permute-start.5 = (bf16[4,128,256]{2,1,0:T(8,128)(2,1)S(1)}, bf16[4,128,256]{2,1,0:T(8,128)(2,1)S(1)}, u32[]{:S(2)}, u32[]{:S(2)}) collective-permute-start(bf16[4,128,256]{2,1,0:T(8,128)(2,1)S(1)} %collective-permute-done.4), channel_id=1, source_target_pairs={{0,4},{4,8},{8,12},{12,16},{16,20},{20,24},{24,28},{28,0},{1,5},{5... | collective-permute-start | bytes 786440 | tf_op jit(solution)/shard_map/ppermute | solution.py:38
  50.5 8.3 %collective-permute-start.8 = (bf16[4,128,256]{2,1,0:T(8,128)(2,1)S(1)}, bf16[4,128,256]{2,1,0:T(8,128)(2,1)S(1)}, u32[]{:S(2)}, u32[]{:S(2)}) collective-permute-start(bf16[4,128,256]{2,1,0:T(8,128)(2,1)S(1)} %collective-permute-done.7), channel_id=1, source_target_pairs={{0,28},{4,0},{8,4},{12,8},{16,12},{20,16},{24,20},{28,24},{1,29},{... | collective-permute-start | bytes 786440 | tf_op jit(solution)/shard_map/ppermute | solution.py:41
  55.6 8.3 %collective-permute-start.6 = (bf16[4,128,256]{2,1,0:T(8,128)(2,1)S(1)}, bf16[4,128,256]{2,1,0:T(8,128)(2,1)S(1)}, u32[]{:S(2)}, u32[]{:S(2)}) collective-permute-start(bf16[4,128,256]{2,1,0:T(8,128)(2,1)S(1)} %collective-permute-done.5), channel_id=1, source_target_pairs={{0,4},{4,8},{8,12},{12,16},{16,20},{20,24},{24,28},{28,0},{1,5},{5... | collective-permute-start | bytes 786440 | tf_op jit(solution)/shard_map/ppermute | solution.py:38
  58.9 8.3 %collective-permute-start.9 = (bf16[4,128,256]{2,1,0:T(8,128)(2,1)S(1)}, bf16[4,128,256]{2,1,0:T(8,128)(2,1)S(1)}, u32[]{:S(2)}, u32[]{:S(2)}) collective-permute-start(bf16[4,128,256]{2,1,0:T(8,128)(2,1)S(1)} %collective-permute-done.8), channel_id=1, source_target_pairs={{0,28},{4,0},{8,4},{12,8},{16,12},{20,16},{24,20},{28,24},{1,29},{... | collective-permute-start | bytes 786440 | tf_op jit(solution)/shard_map/ppermute | solution.py:41
  68.6 14.5 %collective-permute-start.13 = (bf16[8,128,256]{2,1,0:T(8,128)(2,1)}, bf16[8,128,256]{2,1,0:T(8,128)(2,1)}, u32[]{:S(2)}, u32[]{:S(2)}) collective-permute-start(bf16[8,128,256]{2,1,0:T(8,128)(2,1)} %gather_fusion.1), channel_id=1, source_target_pairs={{0,64},{32,96},{64,0},{96,32},{1,65},{33,97},{65,1},{97,33},{2,66}... | collective-permute-start | bytes 1572872 | tf_op jit(solution)/shard_map/ppermute | solution.py:77
  72.5 22.1 %collective-permute-start.15 = (bf16[8,128,256]{2,1,0:T(8,128)(2,1)}, bf16[8,128,256]{2,1,0:T(8,128)(2,1)}, u32[]{:S(2)}, u32[]{:S(2)}) collective-permute-start(bf16[8,128,256]{2,1,0:T(8,128)(2,1)} %gather_fusion.2), channel_id=1, source_target_pairs={{0,32},{32,64},{64,96},{96,0},{1,33},{33,65},{65,97},{97,1},{2,34}... | collective-permute-start | bytes 1572872 | tf_op jit(solution)/shard_map/ppermute | solution.py:77
  77.8 16.8 %collective-permute-start.11 = (bf16[8,128,256]{2,1,0:T(8,128)(2,1)}, bf16[8,128,256]{2,1,0:T(8,128)(2,1)}, u32[]{:S(2)}, u32[]{:S(2)}) collective-permute-start(bf16[8,128,256]{2,1,0:T(8,128)(2,1)} %gather_fusion), channel_id=1, source_target_pairs={{0,96},{32,0},{64,32},{96,64},{1,97},{33,1},{65,33},{97,65},{2,98}... | collective-permute-start | bytes 1572872 | tf_op jit(solution)/shard_map/ppermute | solution.py:77
  97.1 7.5 %collective-permute-start.16 = (f32[512,256]{1,0:T(8,128)S(1)}, f32[512,256]{1,0:T(8,128)S(1)}, u32[]{:S(2)}, u32[]{:S(2)}) collective-permute-start(f32[512,256]{1,0:T(8,128)S(1)} %bitcast.67), channel_id=1, source_target_pairs={{0,1},{1,0},{2,3},{3,2},{4,5},{5,4},{6,7},{7,6},{8,9},{9,8},{10,11... | collective-permute-start | bytes 1572872 | tf_op jit(solution)/shard_map/ppermute | solution.py:149
  104.7 17.8 %collective-permute-start.17 = (f32[512,256]{1,0:T(8,128)S(1)}, f32[512,256]{1,0:T(8,128)S(1)}, u32[]{:S(2)}, u32[]{:S(2)}) collective-permute-start(f32[512,256]{1,0:T(8,128)S(1)} %bitcast_add_fusion), channel_id=1, source_target_pairs={{0,2},{2,0},{1,3},{3,1},{4,6},{6,4},{5,7},{7,5},{8,10},{10,8},{9,1... | collective-permute-start | bytes 1572872 | tf_op jit(solution)/shard_map/ppermute | solution.py:149
  106.9 3.5 %collective-permute-start.18 = (bf16[128,256]{1,0:T(8,128)(2,1)S(1)}, bf16[128,256]{1,0:T(8,128)(2,1)S(1)}, u32[]{:S(2)}, u32[]{:S(2)}) collective-permute-start(bf16[128,256]{1,0:T(8,128)(2,1)S(1)} %copy-done.6), channel_id=1, source_target_pairs={{0,1},{1,0},{2,3},{3,2},{4,5},{5,4},{6,7},{7,6},{8,9},{9,8},{10,11... | collective-permute-start | bytes 196616 | tf_op jit(solution)/shard_map/ppermute | solution.py:149
  110.4 12.1 %collective-permute-start.19 = (bf16[2,128,256]{2,1,0:T(8,128)(2,1)S(1)}, bf16[2,128,256]{2,1,0:T(8,128)(2,1)S(1)}, u32[]{:S(2)}, u32[]{:S(2)}) collective-permute-start(bf16[2,128,256]{2,1,0:T(8,128)(2,1)S(1)} %maximum_select_fusion.3), channel_id=1, source_target_pairs={{0,2},{2,0},{1,3},{3,1},{4,6},{6,4},{5,7},{7,5},{8,10},{10,8},{9,1... | collective-permute-start | bytes 393224 | tf_op jit(solution)/shard_map/ppermute | solution.py:149
  123.8 5.1 %collective-permute-start.20 = (f32[16896]{0:T(1024)S(1)}, f32[16896]{0:T(1024)S(1)}, u32[]{:S(2)}, u32[]{:S(2)}) collective-permute-start(f32[16896]{0:T(1024)S(1)} %dynamic-slice_reduce_fusion), channel_id=1, source_target_pairs={{0,4},{4,0},{8,12},{12,8},{16,20},{20,16},{24,28},{28,24},{1,5},{5... | collective-permute-start | bytes 202760 | tf_op jit(solution)/shard_map/ppermute | solution.py:206
  128.9 7.8 %collective-permute-start.21 = (f32[16896]{0:T(1024)S(1)}, f32[16896]{0:T(1024)S(1)}, u32[]{:S(2)}, u32[]{:S(2)}) collective-permute-start(f32[16896]{0:T(1024)S(1)} %add.315), channel_id=1, source_target_pairs={{0,8},{4,12},{8,0},{12,4},{16,24},{20,28},{24,16},{28,20},{1,9},{5... | collective-permute-start | bytes 202760 | tf_op jit(solution)/shard_map/ppermute | solution.py:206
  136.7 6.3 %collective-permute-start.22 = (f32[16896]{0:T(1024)S(1)}, f32[16896]{0:T(1024)S(1)}, u32[]{:S(2)}, u32[]{:S(2)}) collective-permute-start(f32[16896]{0:T(1024)S(1)} %add.316), channel_id=1, source_target_pairs={{0,28},{4,24},{8,20},{12,16},{16,12},{20,8},{24,4},{28,0},{1,29},{... | collective-permute-start | bytes 202760 | tf_op jit(solution)/shard_map/ppermute | solution.py:206
  143.0 5.1 %collective-permute-start.23 = (f32[16896]{0:T(1024)S(1)}, f32[16896]{0:T(1024)S(1)}, u32[]{:S(2)}, u32[]{:S(2)}) collective-permute-start(f32[16896]{0:T(1024)S(1)} %add.317), channel_id=1, source_target_pairs={{0,32},{32,0},{64,96},{96,64},{1,33},{33,1},{65,97},{97,65},{2,34}... | collective-permute-start | bytes 202760 | tf_op jit(solution)/shard_map/ppermute | solution.py:206
  148.0 6.3 %collective-permute-start.24 = (f32[16896]{0:T(1024)S(1)}, f32[16896]{0:T(1024)S(1)}, u32[]{:S(2)}, u32[]{:S(2)}) collective-permute-start(f32[16896]{0:T(1024)S(1)} %add.318), channel_id=1, source_target_pairs={{0,96},{32,64},{64,32},{96,0},{1,97},{33,65},{65,33},{97,1},{2,98}... | collective-permute-start | bytes 202760 | tf_op jit(solution)/shard_map/ppermute | solution.py:206
  154.3 6.7 %collective-permute-start.25 = (f32[16896]{0:T(1024)S(1)}, f32[16896]{0:T(1024)S(1)}, u32[]{:S(2)}, u32[]{:S(2)}) collective-permute-start(f32[16896]{0:T(1024)S(1)} %add.319), channel_id=1, source_target_pairs={{0,128},{128,0},{256,384},{384,256},{1,129},{129,1},{257,385},{385... | collective-permute-start | bytes 202760 | tf_op jit(solution)/shard_map/ppermute | solution.py:206
  161.0 7.4 %collective-permute-start.26 = (f32[16896]{0:T(1024)S(1)}, f32[16896]{0:T(1024)S(1)}, u32[]{:S(2)}, u32[]{:S(2)}) collective-permute-start(f32[16896]{0:T(1024)S(1)} %add.320), channel_id=1, source_target_pairs={{0,384},{128,256},{256,128},{384,0},{1,385},{129,257},{257,129},{3... | collective-permute-start | bytes 202760 | tf_op jit(solution)/shard_map/ppermute | solution.py:206
  168.4 5.1 %collective-permute-start.27 = (f32[16896]{0:T(1024)S(1)}, f32[16896]{0:T(1024)S(1)}, u32[]{:S(2)}, u32[]{:S(2)}) collective-permute-start(f32[16896]{0:T(1024)S(1)} %add.321), channel_id=1, source_target_pairs={{0,2},{2,0},{1,3},{3,1},{4,6},{6,4},{5,7},{7,5},{8,10},{10,8},{9,1... | collective-permute-start | bytes 202760 | tf_op jit(solution)/shard_map/ppermute | solution.py:118
  173.5 13.1 %collective-permute-start.28 = (f32[33792]{0:T(1024)S(1)}, f32[33792]{0:T(1024)S(1)}, u32[]{:S(2)}, u32[]{:S(2)}) collective-permute-start(f32[33792]{0:T(1024)S(1)} %maximum_select_fusion.2), channel_id=1, source_target_pairs={{0,1},{1,0},{2,3},{3,2},{4,5},{5,4},{6,7},{7,6},{8,9},{9,8},{10,11... | collective-permute-start | bytes 405512 | tf_op jit(solution)/shard_map/ppermute | solution.py:118
  (8 other events, 152.0 us)

commit v14 on v13

--- a/solution.py
+++ b/solution.py
@@ -25,6 +25,22 @@
         else:
             pieces.append(lax.ppermute(piece, axis, [(i, (i - d) % n) for i in range(n)]))
     return jnp.stack(pieces)
+
+
+def doubling_gather(piece, axis):
+    n = lax.axis_size(axis)
+    idx = lax.axis_index(axis)
+    stack = piece[None]
+    for b in range(n.bit_length() - 1):
+        if (1 << b) < n // 2:
+            perm = [(i, i ^ (1 << b)) for i in range(n)]
+            later = ((idx >> b) & 1) == 1
+        else:
+            perm = [(i, n - 1 - i) for i in range(n)]
+            later = idx >= n // 2
+        other = lax.ppermute(stack, axis, perm)
+        stack = jnp.where(later, jnp.concatenate([other, stack]), jnp.concatenate([stack, other]))
+    return stack
 
 
 def ring_gather(piece, axis):
@@ -60,7 +76,7 @@
     }
     stack = features
     for a in within:
-        stack = round_gather(stack, a) if lax.axis_size(a) <= 4 else ring_gather(stack, a)
+        stack = round_gather(stack, a) if lax.axis_size(a) <= 4 else doubling_gather(stack, a)
     plane = stack.reshape(-1, features.shape[0], features.shape[1])
 
     def in_plane(c):
@@ -68,7 +84,11 @@
         flat = jnp.zeros_like(c)
         for a in reversed(within):
             size = lax.axis_size(a)
-            flat = flat * size + (coords[a] - lax.axis_index(a) + size // 2) % size
+            if size <= 4:
+                k = (coords[a] - lax.axis_index(a) + size // 2) % size
+            else:
+                k = coords[a]
+            flat = flat * size + k
         return flat
 
     copies = [jnp.take(plane, in_plane(cols), axis=0, mode="clip")]

time: 190 us -> 237 us (1.25)
  waiting for transfers between devices: 51.1 us -> 111 us
  starting transfers between devices: 118 us -> 105 us
    ppermute x7 -> x3, waiting for transfers between devices: 4.91 us -> 58.5 us  [doubling_gather(): other = lax.ppermute(stack, axis, perm)]
    ppermute x7 -> x3, starting transfers between devices: 27.8 us -> 19.1 us  [doubling_gather(): other = lax.ppermute(stack, axis, perm)]
    ppermute x7, starting transfers between devices: 27.2 us -> 22.9 us  [shards(): flat = flat + lax.ppermute(flat, a, perm)]
    ppermute x7, waiting for transfers between devices: 17.3 us -> 21.5 us  [shards(): flat = flat + lax.ppermute(flat, a, perm)]
    ppermute x3, waiting for transfers between devices: 11.6 us -> 15.3 us  [plane_blocks(): lax.ppermute(sent, across, [(i, (i + s) % n_across) for i in range(n_acro...]
    select_n x0 -> x3, other arithmetic: none -> 2.77 us  [doubling_gather(): jnp.where(later, jnp.concatenate([other, stack]), jnp.concatenate([stack,...]
    ppermute x4, starting transfers between devices: 13.8 us -> 11.4 us  [swap(): return lax.ppermute(x, axis, [(0, 1), (1, 0)])]
  transfers between devices with their start and end apart: 29 -> 25, of which waited for: 17 -> 19; matrix products, arithmetic and copies ran while one was open for 5% -> 4% of each run, Pallas kernels for 0% -> 0%
where the time goes in v14:
time: 237 us; the launch traced here: 236 us
  waiting for transfers between devices  111 us (47%)
  starting transfers between devices  105 us (44%)
  other arithmetic  8.23 us (3%)
  local copies, waits for them, and re-layouts  7.44 us (3%)
  matrix products  3.03 us (1%)
    ppermute x3, waiting for transfers between devices, doubling_gather(): other = lax.ppermute(stack, axis, perm)  58.5 us
    ppermute x7, starting transfers between devices, shards(): flat = flat + lax.ppermute(flat, a, perm)  22.9 us
    ppermute x7, waiting for transfers between devices, shards(): flat = flat + lax.ppermute(flat, a, perm)  21.5 us
    ppermute x3, starting transfers between devices, doubling_gather(): other = lax.ppermute(stack, axis, perm)  19.1 us
    ppermute x3, starting transfers between devices, round_gather(): lax.ppermute(piece, axis, [(i, (i - d) % n) for i in range(n)])  15.8 us
    ppermute x2, starting transfers between devices, all_gather_flat(): other = lax.ppermute(flat, a, perm)  15.5 us
    ppermute x3, waiting for transfers between devices, plane_blocks(): lax.ppermute(sent, across, [(i, (i + s) % n_across) for i in range(n_acro...  15.3 us
    ppermute x4, starting transfers between devices, swap(): return lax.ppermute(x, axis, [(0, 1), (1, 0)])  11.4 us
  transfers between devices with their start and end apart: 25, of which 19 were waited for; matrix products, arithmetic and copies ran while one was open for 4% of the time, Pallas kernels for 0%

profile of v14, /device:TPU:1, one launch (start us, length us, event | category | flops | bytes accessed | tf_op | source)
XLA Modules:
  0.0 235.7 jit_solution(12563588579012953300)
XLA Ops:
  0.7 8.4 %collective-permute-start = (bf16[128,256]{1,0:T(8,128)(2,1)}, bf16[128,256]{1,0:T(8,128)(2,1)S(1)}, u32[]{:S(2)}, u32[]{:S(2)}) collective-permute-start(bf16[128,256]{1,0:T(8,128)(2,1)} %param.8), channel_id=1, source_target_pairs={{0,256},{128,384},{256,0},{384,128},{1,257},{129,385},{257,1},{385... | collective-permute-start | bytes 196616 | tf_op jit(solution)/shard_map/ppermute | solution.py:26
  11.5 5.0 %collective-permute-start.2 = (bf16[128,256]{1,0:T(8,128)(2,1)}, bf16[128,256]{1,0:T(8,128)(2,1)S(1)}, u32[]{:S(2)}, u32[]{:S(2)}) collective-permute-start(bf16[128,256]{1,0:T(8,128)(2,1)} %param.8), channel_id=1, source_target_pairs={{0,384},{128,0},{256,128},{384,256},{1,385},{129,1},{257,129},{385... | collective-permute-start | bytes 196616 | tf_op jit(solution)/shard_map/ppermute | solution.py:26
  16.5 2.7 %collective-permute-done.1 = bf16[128,256]{1,0:T(8,128)(2,1)S(1)} collective-permute-done((bf16[128,256]{1,0:T(8,128)(2,1)}, bf16[128,256]{1,0:T(8,128)(2,1)S(1)}, u32[]{:S(2)}, u32[]{:S(2)}) %collective-permute-start.1) | collective-permute-done | bytes 65568 | tf_op jit(solution)/shard_map/ppermute | solution.py:26
  20.0 3.4 %collective-permute-start.3 = (bf16[1,4,128,256]{3,2,1,0:T(8,128)(2,1)S(1)}, bf16[1,4,128,256]{3,2,1,0:T(8,128)(2,1)S(1)}, u32[]{:S(2)}, u32[]{:S(2)}) collective-permute-start(bf16[1,4,128,256]{3,2,1,0:T(8,128)(2,1)S(1)} %maximum_bitcast_fusion), channel_id=1, source_target_pairs={{0,4},{4,0},{8,12},{12,8},{16,20},{20,16},{24,28},{28,24},{1,5},{5... | collective-permute-start | bytes 786440 | tf_op jit(solution)/shard_map/ppermute | solution.py:41
  23.5 3.7 %collective-permute-done.3 = bf16[1,4,128,256]{3,2,1,0:T(8,128)(2,1)S(1)} collective-permute-done((bf16[1,4,128,256]{3,2,1,0:T(8,128)(2,1)S(1)}, bf16[1,4,128,256]{3,2,1,0:T(8,128)(2,1)S(1)}, u32[]{:S(2)}, u32[]{:S(2)}) %collective-permute-start.3) | collective-permute-done | bytes 262176 | tf_op jit(solution)/shard_map/ppermute | solution.py:41
  27.3 6.5 %collective-permute-start.4 = (bf16[2,4,128,256]{3,2,1,0:T(8,128)(2,1)S(1)}, bf16[2,4,128,256]{3,2,1,0:T(8,128)(2,1)S(1)}, u32[]{:S(2)}, u32[]{:S(2)}) collective-permute-start(bf16[2,4,128,256]{3,2,1,0:T(8,128)(2,1)S(1)} %maximum_select_fusion.2), channel_id=1, source_target_pairs={{0,8},{4,12},{8,0},{12,4},{16,24},{20,28},{24,16},{28,20},{1,9},{5... | collective-permute-start | bytes 1572872 | tf_op jit(solution)/shard_map/ppermute | solution.py:41
  34.6 4.4 %collective-permute-start.10 = (s32[8]{0:T(128)S(1)}, s32[8]{0:T(128)S(1)}, u32[]{:S(2)}, u32[]{:S(2)}) collective-permute-start(s32[8]{0:T(128)S(1)} %get-tuple-element.7), channel_id=1, source_target_pairs={{0,96},{32,0},{64,32},{96,64},{1,97},{33,1},{65,33},{97,65},{2,98}... | collective-permute-start | bytes 104 | tf_op jit(solution)/shard_map/ppermute | solution.py:74
  44.0 12.6 %collective-permute-done.4 = bf16[2,4,128,256]{3,2,1,0:T(8,128)(2,1)S(1)} collective-permute-done((bf16[2,4,128,256]{3,2,1,0:T(8,128)(2,1)S(1)}, bf16[2,4,128,256]{3,2,1,0:T(8,128)(2,1)S(1)}, u32[]{:S(2)}, u32[]{:S(2)}) %collective-permute-start.4) | collective-permute-done | bytes 524320 | tf_op jit(solution)/shard_map/ppermute | solution.py:41
  56.8 9.1 %collective-permute-start.5 = (bf16[4,4,128,256]{3,2,1,0:T(8,128)(2,1)S(1)}, bf16[4,4,128,256]{3,2,1,0:T(8,128)(2,1)}, u32[]{:S(2)}, u32[]{:S(2)}) collective-permute-start(bf16[4,4,128,256]{3,2,1,0:T(8,128)(2,1)S(1)} %maximum_select_fusion.1), channel_id=1, source_target_pairs={{0,28},{4,24},{8,20},{12,16},{16,12},{20,8},{24,4},{28,0},{1,29},{... | collective-permute-start | bytes 3145736 | tf_op jit(solution)/shard_map/ppermute | solution.py:41
  67.3 42.1 %collective-permute-done.5 = bf16[4,4,128,256]{3,2,1,0:T(8,128)(2,1)} collective-permute-done((bf16[4,4,128,256]{3,2,1,0:T(8,128)(2,1)S(1)}, bf16[4,4,128,256]{3,2,1,0:T(8,128)(2,1)}, u32[]{:S(2)}, u32[]{:S(2)}) %collective-permute-start.5) | collective-permute-done | bytes 1048608 | tf_op jit(solution)/shard_map/ppermute | solution.py:41
  109.5 2.5 %maximum_select_fusion = bf16[8,4,128,256]{3,2,1,0:T(8,128)(2,1)S(1)} fusion(bf16[4,4,128,256]{3,2,1,0:T(8,128)(2,1)} %copy-done.1, bf16[4,4,128,256]{3,2,1,0:T(8,128)(2,1)} %collective-permute-done.5, pred[]{:T(512)S(6)} %ge.3), kind=kLoop, calls=%fused_computation.4 | loop fusion | flops 3145728 | bytes 4194305 | tf_op jit(solution)/shard_map/jit(_where)/select_n | solution.py:42
  113.4 3.1 %collective-permute-start.11 = (bf16[8,128,256]{2,1,0:T(8,128)(2,1)}, bf16[8,128,256]{2,1,0:T(8,128)(2,1)}, u32[]{:S(2)}, u32[]{:S(2)}) collective-permute-start(bf16[8,128,256]{2,1,0:T(8,128)(2,1)} %gather_fusion.2), channel_id=1, source_target_pairs={{0,32},{32,64},{64,96},{96,0},{1,33},{33,65},{65,97},{97,1},{2,34}... | collective-permute-start | bytes 1572872 | tf_op jit(solution)/shard_map/ppermute | solution.py:97
  117.9 4.3 %collective-permute-start.9 = (bf16[8,128,256]{2,1,0:T(8,128)(2,1)}, bf16[8,128,256]{2,1,0:T(8,128)(2,1)}, u32[]{:S(2)}, u32[]{:S(2)}) collective-permute-start(bf16[8,128,256]{2,1,0:T(8,128)(2,1)} %gather_fusion.1), channel_id=1, source_target_pairs={{0,64},{32,96},{64,0},{96,32},{1,65},{33,97},{65,1},{97,33},{2,66}... | collective-permute-start | bytes 1572872 | tf_op jit(solution)/shard_map/ppermute | solution.py:97
  123.6 3.1 %collective-permute-start.7 = (bf16[8,128,256]{2,1,0:T(8,128)(2,1)}, bf16[8,128,256]{2,1,0:T(8,128)(2,1)}, u32[]{:S(2)}, u32[]{:S(2)}) collective-permute-start(bf16[8,128,256]{2,1,0:T(8,128)(2,1)} %gather_fusion), channel_id=1, source_target_pairs={{0,96},{32,0},{64,32},{96,64},{1,97},{33,1},{65,33},{97,65},{2,98}... | collective-permute-start | bytes 1572872 | tf_op jit(solution)/shard_map/ppermute | solution.py:97
  129.8 12.2 %collective-permute-done.9 = bf16[8,128,256]{2,1,0:T(8,128)(2,1)} collective-permute-done((bf16[8,128,256]{2,1,0:T(8,128)(2,1)}, bf16[8,128,256]{2,1,0:T(8,128)(2,1)}, u32[]{:S(2)}, u32[]{:S(2)}) %collective-permute-start.9) | collective-permute-done | bytes 524320 | tf_op jit(solution)/shard_map/ppermute | solution.py:97
  142.0 2.7 %collective-permute-done.7 = bf16[8,128,256]{2,1,0:T(8,128)(2,1)} collective-permute-done((bf16[8,128,256]{2,1,0:T(8,128)(2,1)}, bf16[8,128,256]{2,1,0:T(8,128)(2,1)}, u32[]{:S(2)}, u32[]{:S(2)}) %collective-permute-start.7) | collective-permute-done | bytes 524320 | tf_op jit(solution)/shard_map/ppermute | solution.py:97
  147.2 3.6 %collective-permute-start.12 = (f32[512,256]{1,0:T(8,128)S(1)}, f32[512,256]{1,0:T(8,128)S(1)}, u32[]{:S(2)}, u32[]{:S(2)}) collective-permute-start(f32[512,256]{1,0:T(8,128)S(1)} %bitcast.53), channel_id=1, source_target_pairs={{0,1},{1,0},{2,3},{3,2},{4,5},{5,4},{6,7},{7,6},{8,9},{9,8},{10,11... | collective-permute-start | bytes 1572872 | tf_op jit(solution)/shard_map/ppermute | solution.py:169
  154.7 2.6 %collective-permute-start.14 = (bf16[128,256]{1,0:T(8,128)(2,1)S(1)}, bf16[128,256]{1,0:T(8,128)(2,1)S(1)}, u32[]{:S(2)}, u32[]{:S(2)}) collective-permute-start(bf16[128,256]{1,0:T(8,128)(2,1)S(1)} %copy-done.2), channel_id=1, source_target_pairs={{0,1},{1,0},{2,3},{3,2},{4,5},{5,4},{6,7},{7,6},{8,9},{9,8},{10,11... | collective-permute-start | bytes 196616 | tf_op jit(solution)/shard_map/ppermute | solution.py:169
  158.1 3.0 %collective-permute-start.15 = (bf16[2,128,256]{2,1,0:T(8,128)(2,1)S(1)}, bf16[2,128,256]{2,1,0:T(8,128)(2,1)S(1)}, u32[]{:S(2)}, u32[]{:S(2)}) collective-permute-start(bf16[2,128,256]{2,1,0:T(8,128)(2,1)S(1)} %maximum_select_fusion.6), channel_id=1, source_target_pairs={{0,2},{2,0},{1,3},{3,1},{4,6},{6,4},{5,7},{7,5},{8,10},{10,8},{9,1... | collective-permute-start | bytes 393224 | tf_op jit(solution)/shard_map/ppermute | solution.py:169
  161.3 8.9 %collective-permute-done.15 = bf16[2,128,256]{2,1,0:T(8,128)(2,1)S(1)} collective-permute-done((bf16[2,128,256]{2,1,0:T(8,128)(2,1)S(1)}, bf16[2,128,256]{2,1,0:T(8,128)(2,1)S(1)}, u32[]{:S(2)}, u32[]{:S(2)}) %collective-permute-start.15) | collective-permute-done | bytes 131104 | tf_op jit(solution)/shard_map/ppermute | solution.py:169
  173.4 3.1 %collective-permute-done.16 = f32[16896]{0:T(1024)S(1)} collective-permute-done((f32[16896]{0:T(1024)S(1)}, f32[16896]{0:T(1024)S(1)}, u32[]{:S(2)}, u32[]{:S(2)}) %collective-permute-start.16) | collective-permute-done | bytes 67616 | tf_op jit(solution)/shard_map/ppermute | solution.py:226
  178.9 4.1 %collective-permute-done.17 = f32[16896]{0:T(1024)S(1)} collective-permute-done((f32[16896]{0:T(1024)S(1)}, f32[16896]{0:T(1024)S(1)}, u32[]{:S(2)}, u32[]{:S(2)}) %collective-permute-start.17) | collective-permute-done | bytes 67616 | tf_op jit(solution)/shard_map/ppermute | solution.py:226
  183.0 4.3 %collective-permute-start.18 = (f32[16896]{0:T(1024)S(1)}, f32[16896]{0:T(1024)S(1)}, u32[]{:S(2)}, u32[]{:S(2)}) collective-permute-start(f32[16896]{0:T(1024)S(1)} %add.266), channel_id=1, source_target_pairs={{0,28},{4,24},{8,20},{12,16},{16,12},{20,8},{24,4},{28,0},{1,29},{... | collective-permute-start | bytes 202760 | tf_op jit(solution)/shard_map/ppermute | solution.py:226
  187.3 2.7 %collective-permute-done.18 = f32[16896]{0:T(1024)S(1)} collective-permute-done((f32[16896]{0:T(1024)S(1)}, f32[16896]{0:T(1024)S(1)}, u32[]{:S(2)}, u32[]{:S(2)}) %collective-permute-start.18) | collective-permute-done | bytes 67616 | tf_op jit(solution)/shard_map/ppermute | solution.py:226
  190.0 4.0 %collective-permute-start.19 = (f32[16896]{0:T(1024)S(1)}, f32[16896]{0:T(1024)S(1)}, u32[]{:S(2)}, u32[]{:S(2)}) collective-permute-start(f32[16896]{0:T(1024)S(1)} %add.267), channel_id=1, source_target_pairs={{0,32},{32,0},{64,96},{96,64},{1,33},{33,1},{65,97},{97,65},{2,34}... | collective-permute-start | bytes 202760 | tf_op jit(solution)/shard_map/ppermute | solution.py:226
  195.7 3.6 %collective-permute-start.20 = (f32[16896]{0:T(1024)S(1)}, f32[16896]{0:T(1024)S(1)}, u32[]{:S(2)}, u32[]{:S(2)}) collective-permute-start(f32[16896]{0:T(1024)S(1)} %add.268), channel_id=1, source_target_pairs={{0,96},{32,64},{64,32},{96,0},{1,97},{33,65},{65,33},{97,1},{2,98}... | collective-permute-start | bytes 202760 | tf_op jit(solution)/shard_map/ppermute | solution.py:226
  199.4 2.6 %collective-permute-done.20 = f32[16896]{0:T(1024)S(1)} collective-permute-done((f32[16896]{0:T(1024)S(1)}, f32[16896]{0:T(1024)S(1)}, u32[]{:S(2)}, u32[]{:S(2)}) %collective-permute-start.20) | collective-permute-done | bytes 67616 | tf_op jit(solution)/shard_map/ppermute | solution.py:226
  204.2 4.5 %collective-permute-done.21 = f32[16896]{0:T(1024)S(1)} collective-permute-done((f32[16896]{0:T(1024)S(1)}, f32[16896]{0:T(1024)S(1)}, u32[]{:S(2)}, u32[]{:S(2)}) %collective-permute-start.21) | collective-permute-done | bytes 67616 | tf_op jit(solution)/shard_map/ppermute | solution.py:226
  208.7 4.5 %collective-permute-start.22 = (f32[16896]{0:T(1024)S(1)}, f32[16896]{0:T(1024)S(1)}, u32[]{:S(2)}, u32[]{:S(2)}) collective-permute-start(f32[16896]{0:T(1024)S(1)} %add.270), channel_id=1, source_target_pairs={{0,384},{128,256},{256,128},{384,0},{1,385},{129,257},{257,129},{3... | collective-permute-start | bytes 202760 | tf_op jit(solution)/shard_map/ppermute | solution.py:226
  213.3 2.7 %collective-permute-done.22 = f32[16896]{0:T(1024)S(1)} collective-permute-done((f32[16896]{0:T(1024)S(1)}, f32[16896]{0:T(1024)S(1)}, u32[]{:S(2)}, u32[]{:S(2)}) %collective-permute-start.22) | collective-permute-done | bytes 67616 | tf_op jit(solution)/shard_map/ppermute | solution.py:226
  216.0 3.3 %collective-permute-start.23 = (f32[16896]{0:T(1024)S(1)}, f32[16896]{0:T(1024)S(1)}, u32[]{:S(2)}, u32[]{:S(2)}) collective-permute-start(f32[16896]{0:T(1024)S(1)} %add.271), channel_id=1, source_target_pairs={{0,2},{2,0},{1,3},{3,1},{4,6},{6,4},{5,7},{7,5},{8,10},{10,8},{9,1... | collective-permute-start | bytes 202760 | tf_op jit(solution)/shard_map/ppermute | solution.py:138
  221.1 12.3 %collective-permute-start.24 = (f32[33792]{0:T(1024)S(1)}, f32[33792]{0:T(1024)S(1)}, u32[]{:S(2)}, u32[]{:S(2)}) collective-permute-start(f32[33792]{0:T(1024)S(1)} %maximum_select_fusion.5), channel_id=1, source_target_pairs={{0,1},{1,0},{2,3},{3,2},{4,5},{5,4},{6,7},{7,6},{8,9},{9,8},{10,11... | collective-permute-start | bytes 405512 | tf_op jit(solution)/shard_map/ppermute | solution.py:138
  (80 shorter events, 38.7 us)
Async XLA Ops:
  0.6 144.1 %copy-start = (bf16[1,4,8,128,128]{4,3,2,1,0:T(8,128)(2,1)S(1)}, bf16[1,4,8,128,128]{4,3,2,1,0:T(8,128)(2,1)}, u32[]{:S(2)}) copy-start(bf16[1,4,8,128,128]{4,3,2,1,0:T(8,128)(2,1)} %param.11) | copy-start | bytes 3145732
  0.6 65.9 %copy-start.5 = (s32[1,4]{1,0:T(1,128)S(1)}, s32[1,4]{1,0:T(1,128)}, u32[]{:S(2)}) copy-start(s32[1,4]{1,0:T(1,128)} %param.14) | copy-start | bytes 52
  0.7 15.8 %collective-permute-start = (bf16[128,256]{1,0:T(8,128)(2,1)}, bf16[128,256]{1,0:T(8,128)(2,1)S(1)}, u32[]{:S(2)}, u32[]{:S(2)}) collective-permute-start(bf16[128,256]{1,0:T(8,128)(2,1)} %param.8), channel_id=1, source_target_pairs={{0,256},{128,384},{256,0},{384,128},{1,257},{129,385},{257,1},{385... | collective-permute-start | bytes 196616 | tf_op jit(solution)/shard_map/ppermute | solution.py:26
  9.1 10.1 %collective-permute-start.1 = (bf16[128,256]{1,0:T(8,128)(2,1)}, bf16[128,256]{1,0:T(8,128)(2,1)S(1)}, u32[]{:S(2)}, u32[]{:S(2)}) collective-permute-start(bf16[128,256]{1,0:T(8,128)(2,1)} %param.8), channel_id=1, source_target_pairs={{0,128},{128,256},{256,384},{384,0},{1,129},{129,257},{257,385},{3... | collective-permute-start | bytes 196616 | tf_op jit(solution)/shard_map/ppermute | solution.py:26
  11.5 7.7 %collective-permute-start.2 = (bf16[128,256]{1,0:T(8,128)(2,1)}, bf16[128,256]{1,0:T(8,128)(2,1)S(1)}, u32[]{:S(2)}, u32[]{:S(2)}) collective-permute-start(bf16[128,256]{1,0:T(8,128)(2,1)} %param.8), channel_id=1, source_target_pairs={{0,384},{128,0},{256,128},{384,256},{1,385},{129,1},{257,129},{385... | collective-permute-start | bytes 196616 | tf_op jit(solution)/shard_map/ppermute | solution.py:26
  20.0 7.2 %collective-permute-start.3 = (bf16[1,4,128,256]{3,2,1,0:T(8,128)(2,1)S(1)}, bf16[1,4,128,256]{3,2,1,0:T(8,128)(2,1)S(1)}, u32[]{:S(2)}, u32[]{:S(2)}) collective-permute-start(bf16[1,4,128,256]{3,2,1,0:T(8,128)(2,1)S(1)} %maximum_bitcast_fusion), channel_id=1, source_target_pairs={{0,4},{4,0},{8,12},{12,8},{16,20},{20,16},{24,28},{28,24},{1,5},{5... | collective-permute-start | bytes 786440 | tf_op jit(solution)/shard_map/ppermute | solution.py:41
  27.3 29.3 %collective-permute-start.4 = (bf16[2,4,128,256]{3,2,1,0:T(8,128)(2,1)S(1)}, bf16[2,4,128,256]{3,2,1,0:T(8,128)(2,1)S(1)}, u32[]{:S(2)}, u32[]{:S(2)}) collective-permute-start(bf16[2,4,128,256]{3,2,1,0:T(8,128)(2,1)S(1)} %maximum_select_fusion.2), channel_id=1, source_target_pairs={{0,8},{4,12},{8,0},{12,4},{16,24},{20,28},{24,16},{28,20},{1,9},{5... | collective-permute-start | bytes 1572872 | tf_op jit(solution)/shard_map/ppermute | solution.py:41
  34.6 32.6 %collective-permute-start.10 = (s32[8]{0:T(128)S(1)}, s32[8]{0:T(128)S(1)}, u32[]{:S(2)}, u32[]{:S(2)}) collective-permute-start(s32[8]{0:T(128)S(1)} %get-tuple-element.7), channel_id=1, source_target_pairs={{0,96},{32,0},{64,32},{96,64},{1,97},{33,1},{65,33},{97,65},{2,98}... | collective-permute-start | bytes 104 | tf_op jit(solution)/shard_map/ppermute | solution.py:74
  39.0 28.2 %collective-permute-start.8 = (s32[8]{0:T(128)S(1)}, s32[8]{0:T(128)S(1)}, u32[]{:S(2)}, u32[]{:S(2)}) collective-permute-start(s32[8]{0:T(128)S(1)} %get-tuple-element.7), channel_id=1, source_target_pairs={{0,64},{32,96},{64,0},{96,32},{1,65},{33,97},{65,1},{97,33},{2,66}... | collective-permute-start | bytes 104 | tf_op jit(solution)/shard_map/ppermute | solution.py:74
  41.4 25.9 %collective-permute-start.6 = (s32[8]{0:T(128)S(1)}, s32[8]{0:T(128)S(1)}, u32[]{:S(2)}, u32[]{:S(2)}) collective-permute-start(s32[8]{0:T(128)S(1)} %get-tuple-element.7), channel_id=1, source_target_pairs={{0,32},{32,64},{64,96},{96,0},{1,33},{33,65},{65,97},{97,1},{2,34}... | collective-permute-start | bytes 104 | tf_op jit(solution)/shard_map/ppermute | solution.py:74
  56.7 10.6 %copy-start.1 = (bf16[4,4,128,256]{3,2,1,0:T(8,128)(2,1)}, bf16[4,4,128,256]{3,2,1,0:T(8,128)(2,1)S(1)}, u32[]{:S(2)}) copy-start(bf16[4,4,128,256]{3,2,1,0:T(8,128)(2,1)S(1)} %maximum_select_fusion.1) | copy-start | bytes 3145732
  56.8 52.7 %collective-permute-start.5 = (bf16[4,4,128,256]{3,2,1,0:T(8,128)(2,1)S(1)}, bf16[4,4,128,256]{3,2,1,0:T(8,128)(2,1)}, u32[]{:S(2)}, u32[]{:S(2)}) collective-permute-start(bf16[4,4,128,256]{3,2,1,0:T(8,128)(2,1)S(1)} %maximum_select_fusion.1), channel_id=1, source_target_pairs={{0,28},{4,24},{8,20},{12,16},{16,12},{20,8},{24,4},{28,0},{1,29},{... | collective-permute-start | bytes 3145736 | tf_op jit(solution)/shard_map/ppermute | solution.py:41
  113.4 16.4 %collective-permute-start.11 = (bf16[8,128,256]{2,1,0:T(8,128)(2,1)}, bf16[8,128,256]{2,1,0:T(8,128)(2,1)}, u32[]{:S(2)}, u32[]{:S(2)}) collective-permute-start(bf16[8,128,256]{2,1,0:T(8,128)(2,1)} %gather_fusion.2), channel_id=1, source_target_pairs={{0,32},{32,64},{64,96},{96,0},{1,33},{33,65},{65,97},{97,1},{2,34}... | collective-permute-start | bytes 1572872 | tf_op jit(solution)/shard_map/ppermute | solution.py:97
  117.9 24.1 %collective-permute-start.9 = (bf16[8,128,256]{2,1,0:T(8,128)(2,1)}, bf16[8,128,256]{2,1,0:T(8,128)(2,1)}, u32[]{:S(2)}, u32[]{:S(2)}) collective-permute-start(bf16[8,128,256]{2,1,0:T(8,128)(2,1)} %gather_fusion.1), channel_id=1, source_target_pairs={{0,64},{32,96},{64,0},{96,32},{1,65},{33,97},{65,1},{97,33},{2,66}... | collective-permute-start | bytes 1572872 | tf_op jit(solution)/shard_map/ppermute | solution.py:97
  123.6 21.1 %collective-permute-start.7 = (bf16[8,128,256]{2,1,0:T(8,128)(2,1)}, bf16[8,128,256]{2,1,0:T(8,128)(2,1)}, u32[]{:S(2)}, u32[]{:S(2)}) collective-permute-start(bf16[8,128,256]{2,1,0:T(8,128)(2,1)} %gather_fusion), channel_id=1, source_target_pairs={{0,96},{32,0},{64,32},{96,64},{1,97},{33,1},{65,33},{97,65},{2,98}... | collective-permute-start | bytes 1572872 | tf_op jit(solution)/shard_map/ppermute | solution.py:97
  146.7 8.0 %copy-start.2 = (bf16[128,256]{1,0:T(8,128)(2,1)S(1)}, bf16[128,256]{1,0:T(8,128)(2,1)}, u32[]{:S(2)}) copy-start(bf16[128,256]{1,0:T(8,128)(2,1)} %param.15) | copy-start | bytes 196612
  147.2 23.1 %copy-start.3 = (bf16[256,256]{1,0:T(8,128)(2,1)S(1)}, bf16[256,256]{1,0:T(8,128)(2,1)}, u32[]{:S(2)}) copy-start(bf16[256,256]{1,0:T(8,128)(2,1)} %param.9) | copy-start | bytes 393220
  147.2 23.1 %copy-start.4 = (f32[256]{0:T(256)S(1)}, f32[256]{0:T(256)}, u32[]{:S(2)}) copy-start(f32[256]{0:T(256)} %param.10) | copy-start | bytes 3076
  147.2 5.1 %collective-permute-start.12 = (f32[512,256]{1,0:T(8,128)S(1)}, f32[512,256]{1,0:T(8,128)S(1)}, u32[]{:S(2)}, u32[]{:S(2)}) collective-permute-start(f32[512,256]{1,0:T(8,128)S(1)} %bitcast.53), channel_id=1, source_target_pairs={{0,1},{1,0},{2,3},{3,2},{4,5},{5,4},{6,7},{7,6},{8,9},{9,8},{10,11... | collective-permute-start | bytes 1572872 | tf_op jit(solution)/shard_map/ppermute | solution.py:169
  152.4 17.8 %collective-permute-start.13 = (f32[512,256]{1,0:T(8,128)S(1)}, f32[512,256]{1,0:T(8,128)S(1)}, u32[]{:S(2)}, u32[]{:S(2)}) collective-permute-start(f32[512,256]{1,0:T(8,128)S(1)} %bitcast_add_fusion), channel_id=1, source_target_pairs={{0,2},{2,0},{1,3},{3,1},{4,6},{6,4},{5,7},{7,5},{8,10},{10,8},{9,1... | collective-permute-start | bytes 1572872 | tf_op jit(solution)/shard_map/ppermute | solution.py:169
  154.7 3.5 %collective-permute-start.14 = (bf16[128,256]{1,0:T(8,128)(2,1)S(1)}, bf16[128,256]{1,0:T(8,128)(2,1)S(1)}, u32[]{:S(2)}, u32[]{:S(2)}) collective-permute-start(bf16[128,256]{1,0:T(8,128)(2,1)S(1)} %copy-done.2), channel_id=1, source_target_pairs={{0,1},{1,0},{2,3},{3,2},{4,5},{5,4},{6,7},{7,6},{8,9},{9,8},{10,11... | collective-permute-start | bytes 196616 | tf_op jit(solution)/shard_map/ppermute | solution.py:169
  158.1 12.1 %collective-permute-start.15 = (bf16[2,128,256]{2,1,0:T(8,128)(2,1)S(1)}, bf16[2,128,256]{2,1,0:T(8,128)(2,1)S(1)}, u32[]{:S(2)}, u32[]{:S(2)}) collective-permute-start(bf16[2,128,256]{2,1,0:T(8,128)(2,1)S(1)} %maximum_select_fusion.6), channel_id=1, source_target_pairs={{0,2},{2,0},{1,3},{3,1},{4,6},{6,4},{5,7},{7,5},{8,10},{10,8},{9,1... | collective-permute-start | bytes 393224 | tf_op jit(solution)/shard_map/ppermute | solution.py:169
  171.5 5.1 %collective-permute-start.16 = (f32[16896]{0:T(1024)S(1)}, f32[16896]{0:T(1024)S(1)}, u32[]{:S(2)}, u32[]{:S(2)}) collective-permute-start(f32[16896]{0:T(1024)S(1)} %dynamic-slice_reduce_fusion), channel_id=1, source_target_pairs={{0,4},{4,0},{8,12},{12,8},{16,20},{20,16},{24,28},{28,24},{1,5},{5... | collective-permute-start | bytes 202760 | tf_op jit(solution)/shard_map/ppermute | solution.py:226
  176.6 6.4 %collective-permute-start.17 = (f32[16896]{0:T(1024)S(1)}, f32[16896]{0:T(1024)S(1)}, u32[]{:S(2)}, u32[]{:S(2)}) collective-permute-start(f32[16896]{0:T(1024)S(1)} %add.265), channel_id=1, source_target_pairs={{0,8},{4,12},{8,0},{12,4},{16,24},{20,28},{24,16},{28,20},{1,9},{5... | collective-permute-start | bytes 202760 | tf_op jit(solution)/shard_map/ppermute | solution.py:226
  183.0 7.0 %collective-permute-start.18 = (f32[16896]{0:T(1024)S(1)}, f32[16896]{0:T(1024)S(1)}, u32[]{:S(2)}, u32[]{:S(2)}) collective-permute-start(f32[16896]{0:T(1024)S(1)} %add.266), channel_id=1, source_target_pairs={{0,28},{4,24},{8,20},{12,16},{16,12},{20,8},{24,4},{28,0},{1,29},{... | collective-permute-start | bytes 202760 | tf_op jit(solution)/shard_map/ppermute | solution.py:226
  190.0 5.7 %collective-permute-start.19 = (f32[16896]{0:T(1024)S(1)}, f32[16896]{0:T(1024)S(1)}, u32[]{:S(2)}, u32[]{:S(2)}) collective-permute-start(f32[16896]{0:T(1024)S(1)} %add.267), channel_id=1, source_target_pairs={{0,32},{32,0},{64,96},{96,64},{1,33},{33,1},{65,97},{97,65},{2,34}... | collective-permute-start | bytes 202760 | tf_op jit(solution)/shard_map/ppermute | solution.py:226
  195.7 6.3 %collective-permute-start.20 = (f32[16896]{0:T(1024)S(1)}, f32[16896]{0:T(1024)S(1)}, u32[]{:S(2)}, u32[]{:S(2)}) collective-permute-start(f32[16896]{0:T(1024)S(1)} %add.268), channel_id=1, source_target_pairs={{0,96},{32,64},{64,32},{96,0},{1,97},{33,65},{65,33},{97,1},{2,98}... | collective-permute-start | bytes 202760 | tf_op jit(solution)/shard_map/ppermute | solution.py:226
  202.0 6.7 %collective-permute-start.21 = (f32[16896]{0:T(1024)S(1)}, f32[16896]{0:T(1024)S(1)}, u32[]{:S(2)}, u32[]{:S(2)}) collective-permute-start(f32[16896]{0:T(1024)S(1)} %add.269), channel_id=1, source_target_pairs={{0,128},{128,0},{256,384},{384,256},{1,129},{129,1},{257,385},{385... | collective-permute-start | bytes 202760 | tf_op jit(solution)/shard_map/ppermute | solution.py:226
  208.7 7.3 %collective-permute-start.22 = (f32[16896]{0:T(1024)S(1)}, f32[16896]{0:T(1024)S(1)}, u32[]{:S(2)}, u32[]{:S(2)}) collective-permute-start(f32[16896]{0:T(1024)S(1)} %add.270), channel_id=1, source_target_pairs={{0,384},{128,256},{256,128},{384,0},{1,385},{129,257},{257,129},{3... | collective-permute-start | bytes 202760 | tf_op jit(solution)/shard_map/ppermute | solution.py:226
  216.0 5.1 %collective-permute-start.23 = (f32[16896]{0:T(1024)S(1)}, f32[16896]{0:T(1024)S(1)}, u32[]{:S(2)}, u32[]{:S(2)}) collective-permute-start(f32[16896]{0:T(1024)S(1)} %add.271), channel_id=1, source_target_pairs={{0,2},{2,0},{1,3},{3,1},{4,6},{6,4},{5,7},{7,5},{8,10},{10,8},{9,1... | collective-permute-start | bytes 202760 | tf_op jit(solution)/shard_map/ppermute | solution.py:138
  221.1 13.3 %collective-permute-start.24 = (f32[33792]{0:T(1024)S(1)}, f32[33792]{0:T(1024)S(1)}, u32[]{:S(2)}, u32[]{:S(2)}) collective-permute-start(f32[33792]{0:T(1024)S(1)} %maximum_select_fusion.5), channel_id=1, source_target_pairs={{0,1},{1,0},{2,3},{3,2},{4,5},{5,4},{6,7},{7,6},{8,9},{9,8},{10,11... | collective-permute-start | bytes 405512 | tf_op jit(solution)/shard_map/ppermute | solution.py:138

commit v15 on v13

--- a/solution.py
+++ b/solution.py
@@ -52,7 +52,7 @@
     return coords
 
 
-def plane_blocks(features, cols, across="x", within=("y_hi", "z")):
+def plane_blocks(features, cols, extra, across="x", within=("y_hi", "z")):
     n_across = lax.axis_size(across)
     peer_cols = {
         s: lax.ppermute(cols, across, [(i, (i - s) % n_across) for i in range(n_across)])
@@ -75,11 +75,12 @@
     for s in range(1, n_across):
         sent = jnp.take(plane, in_plane(peer_cols[s]), axis=0, mode="clip")
         copies.append(lax.ppermute(sent, across, [(i, (i + s) % n_across) for i in range(n_across)]))
+    copies, extra = lax.optimization_barrier((copies, extra))
     source = (lax.axis_index(across) - row_coords(cols)[across]) % n_across
     picked = copies[0]
     for s in range(1, n_across):
         picked = jnp.where((source == s)[:, None, None], copies[s], picked)
-    return picked
+    return picked, extra
 
 
 def halving_steps(axes):
@@ -176,7 +177,7 @@
     own_cols = lax.dynamic_index_in_dim(tile_col[0], rep_index, 0, keepdims=False)
     own_count = lax.dynamic_index_in_dim(tile_count[0], rep_index, 0, keepdims=False)
     capacity = own_rows.shape[0]
-    picked = plane_blocks(features, own_cols)
+    picked, group_grad_out = plane_blocks(features, own_cols, gather_over_rep(grad_out))
     product = jnp.einsum("tij,tjf->tif", own_tiles, picked, preferred_element_type=jnp.float32)
     live = jnp.arange(capacity, dtype=jnp.int32) < own_count
     local_ids = jnp.arange(row_count, dtype=jnp.int32)
@@ -184,7 +185,6 @@
     partial_value = jnp.einsum("bt,tif->bif", select, product)
     partial_value = partial_value.reshape(row_count * block_size, feature_width)
     propagated = sum_over_rep(partial_value).astype(jnp.bfloat16)
-    group_grad_out = gather_over_rep(grad_out)
     preact = jnp.dot(propagated, weight, preferred_element_type=jnp.float32) + bias_terms
     sigma = jax.nn.sigmoid(preact)
     layer_out = (preact * sigma).astype(jnp.bfloat16)

time: 190 us -> 199 us (1.047)
  waiting for transfers between devices: 51.1 us -> 56.4 us
  other arithmetic: 5.96 us -> 8.63 us
    ppermute x4, waiting for transfers between devices: 0.03 us -> 6.36 us  [ring_gather(): left = lax.ppermute(left, axis, fwd)]
    ppermute x4, waiting for transfers between devices: 11.3 us -> 17.2 us  [swap(): return lax.ppermute(x, axis, [(0, 1), (1, 0)])]
    ppermute x7, waiting for transfers between devices: 17.3 us -> 14.6 us  [shards(): flat = flat + lax.ppermute(flat, a, perm)]
    ppermute x7, starting transfers between devices: 27.2 us -> 29.7 us  [shards(): flat = flat + lax.ppermute(flat, a, perm)]
    ppermute x3, waiting for transfers between devices: 11.6 us -> 9.09 us  [plane_blocks(): lax.ppermute(sent, across, [(i, (i + s) % n_across) for i in range(n_acro...]
    ppermute x3, waiting for transfers between devices: 4.88 us -> 2.8 us  [ring_gather(): right = lax.ppermute(right, axis, bwd)]
  transfers between devices with their start and end apart: 29 -> 29, of which waited for: 17 -> 21; matrix products, arithmetic and copies ran while one was open for 5% -> 7% of each run, Pallas kernels for 0% -> 0%
where the time goes in v15:
time: 199 us; the launch traced here: 198 us
  starting transfers between devices  119 us (60%)
  waiting for transfers between devices  56.4 us (28%)
  local copies, waits for them, and re-layouts  9.15 us (5%)
  other arithmetic  8.63 us (4%)
  matrix products  2.85 us (1%)
    ppermute x7, starting transfers between devices, shards(): flat = flat + lax.ppermute(flat, a, perm)  29.7 us
    ppermute x4, waiting for transfers between devices, swap(): return lax.ppermute(x, axis, [(0, 1), (1, 0)])  17.2 us
    ppermute x3, starting transfers between devices, ring_gather(): right = lax.ppermute(right, axis, bwd)  16.8 us
    ppermute x7, waiting for transfers between devices, shards(): flat = flat + lax.ppermute(flat, a, perm)  14.6 us
    ppermute x3, starting transfers between devices, round_gather(): lax.ppermute(piece, axis, [(i, (i - d) % n) for i in range(n)])  14.6 us
    ppermute x2, starting transfers between devices, all_gather_flat(): other = lax.ppermute(flat, a, perm)  14.5 us
    ppermute x4, starting transfers between devices, swap(): return lax.ppermute(x, axis, [(0, 1), (1, 0)])  12.6 us
    ppermute x4, starting transfers between devices, ring_gather(): left = lax.ppermute(left, axis, fwd)  12.1 us
  transfers between devices with their start and end apart: 29, of which 21 were waited for; matrix products, arithmetic and copies ran while one was open for 7% of the time, Pallas kernels for 0%

profile of v15, /device:TPU:1, one launch (start us, length us, event | category | flops | bytes accessed | tf_op | source)
XLA Modules:
  0.0 197.6 jit_solution(16369350039182785967)
XLA Ops:
  0.7 6.8 %collective-permute-start.2 = (bf16[128,256]{1,0:T(8,128)(2,1)}, bf16[128,256]{1,0:T(8,128)(2,1)S(1)}, u32[]{:S(2)}, u32[]{:S(2)}) collective-permute-start(bf16[128,256]{1,0:T(8,128)(2,1)} %param.8), channel_id=1, source_target_pairs={{0,384},{128,0},{256,128},{384,256},{1,385},{129,1},{257,129},{385... | collective-permute-start | bytes 196616 | tf_op jit(solution)/shard_map/ppermute | solution.py:26
  9.4 5.8 %collective-permute-start = (bf16[128,256]{1,0:T(8,128)(2,1)}, bf16[128,256]{1,0:T(8,128)(2,1)S(1)}, u32[]{:S(2)}, u32[]{:S(2)}) collective-permute-start(bf16[128,256]{1,0:T(8,128)(2,1)} %param.8), channel_id=1, source_target_pairs={{0,256},{128,384},{256,0},{384,128},{1,257},{129,385},{257,1},{385... | collective-permute-start | bytes 196616 | tf_op jit(solution)/shard_map/ppermute | solution.py:26
  15.3 3.5 %collective-permute-done = bf16[128,256]{1,0:T(8,128)(2,1)S(1)} collective-permute-done((bf16[128,256]{1,0:T(8,128)(2,1)}, bf16[128,256]{1,0:T(8,128)(2,1)S(1)}, u32[]{:S(2)}, u32[]{:S(2)}) %collective-permute-start) | collective-permute-done | bytes 65568 | tf_op jit(solution)/shard_map/ppermute | solution.py:26
  19.7 4.3 %collective-permute-start.3 = (bf16[4,128,256]{2,1,0:T(8,128)(2,1)S(1)}, bf16[4,128,256]{2,1,0:T(8,128)(2,1)S(1)}, u32[]{:S(2)}, u32[]{:S(2)}) collective-permute-start(bf16[4,128,256]{2,1,0:T(8,128)(2,1)S(1)} %pad_maximum_fusion.2), channel_id=1, source_target_pairs={{0,4},{4,8},{8,12},{12,16},{16,20},{20,24},{24,28},{28,0},{1,5},{5... | collective-permute-start | bytes 786440 | tf_op jit(solution)/shard_map/ppermute | solution.py:38
  25.2 4.4 %collective-permute-start.10 = (s32[8]{0:T(128)S(1)}, s32[8]{0:T(128)S(1)}, u32[]{:S(2)}, u32[]{:S(2)}) collective-permute-start(s32[8]{0:T(128)S(1)} %get-tuple-element.17), channel_id=1, source_target_pairs={{0,96},{32,0},{64,32},{96,64},{1,97},{33,1},{65,33},{97,65},{2,98}... | collective-permute-start | bytes 104 | tf_op jit(solution)/shard_map/ppermute | solution.py:58
  29.6 2.4 %collective-permute-start.12 = (s32[8]{0:T(128)S(1)}, s32[8]{0:T(128)S(1)}, u32[]{:S(2)}, u32[]{:S(2)}) collective-permute-start(s32[8]{0:T(128)S(1)} %get-tuple-element.17), channel_id=1, source_target_pairs={{0,64},{32,96},{64,0},{96,32},{1,65},{33,97},{65,1},{97,33},{2,66}... | collective-permute-start | bytes 104 | tf_op jit(solution)/shard_map/ppermute | solution.py:58
  32.0 2.5 %collective-permute-start.14 = (s32[8]{0:T(128)S(1)}, s32[8]{0:T(128)S(1)}, u32[]{:S(2)}, u32[]{:S(2)}) collective-permute-start(s32[8]{0:T(128)S(1)} %get-tuple-element.17), channel_id=1, source_target_pairs={{0,32},{32,64},{64,96},{96,0},{1,33},{33,65},{65,97},{97,1},{2,34}... | collective-permute-start | bytes 104 | tf_op jit(solution)/shard_map/ppermute | solution.py:58
  34.6 4.7 %collective-permute-start.16 = (bf16[128,256]{1,0:T(8,128)(2,1)}, bf16[128,256]{1,0:T(8,128)(2,1)}, u32[]{:S(2)}, u32[]{:S(2)}) collective-permute-start(bf16[128,256]{1,0:T(8,128)(2,1)} %param.15), channel_id=1, source_target_pairs={{0,1},{1,0},{2,3},{3,2},{4,5},{5,4},{6,7},{7,6},{8,9},{9,8},{10,11... | collective-permute-start | bytes 196616 | tf_op jit(solution)/shard_map/ppermute | solution.py:150
  39.8 4.0 %collective-permute-start.4 = (bf16[4,128,256]{2,1,0:T(8,128)(2,1)S(1)}, bf16[4,128,256]{2,1,0:T(8,128)(2,1)S(1)}, u32[]{:S(2)}, u32[]{:S(2)}) collective-permute-start(bf16[4,128,256]{2,1,0:T(8,128)(2,1)S(1)} %collective-permute-done.3), channel_id=1, source_target_pairs={{0,4},{4,8},{8,12},{12,16},{16,20},{20,24},{24,28},{28,0},{1,5},{5... | collective-permute-start | bytes 786440 | tf_op jit(solution)/shard_map/ppermute | solution.py:38
  45.9 6.2 %collective-permute-start.7 = (bf16[4,128,256]{2,1,0:T(8,128)(2,1)S(1)}, bf16[4,128,256]{2,1,0:T(8,128)(2,1)S(1)}, u32[]{:S(2)}, u32[]{:S(2)}) collective-permute-start(bf16[4,128,256]{2,1,0:T(8,128)(2,1)S(1)} %pad_maximum_fusion.2), channel_id=1, source_target_pairs={{0,28},{4,0},{8,4},{12,8},{16,12},{20,16},{24,20},{28,24},{1,29},{... | collective-permute-start | bytes 786440 | tf_op jit(solution)/shard_map/ppermute | solution.py:41
  52.1 2.7 %collective-permute-done.4 = bf16[4,128,256]{2,1,0:T(8,128)(2,1)S(1)} collective-permute-done((bf16[4,128,256]{2,1,0:T(8,128)(2,1)S(1)}, bf16[4,128,256]{2,1,0:T(8,128)(2,1)S(1)}, u32[]{:S(2)}, u32[]{:S(2)}) %collective-permute-start.4) | collective-permute-done | bytes 262176 | tf_op jit(solution)/shard_map/ppermute | solution.py:38
  57.7 5.3 %collective-permute-start.8 = (bf16[4,128,256]{2,1,0:T(8,128)(2,1)S(1)}, bf16[4,128,256]{2,1,0:T(8,128)(2,1)S(1)}, u32[]{:S(2)}, u32[]{:S(2)}) collective-permute-start(bf16[4,128,256]{2,1,0:T(8,128)(2,1)S(1)} %collective-permute-done.7), channel_id=1, source_target_pairs={{0,28},{4,0},{8,4},{12,8},{16,12},{20,16},{24,20},{28,24},{1,29},{... | collective-permute-start | bytes 786440 | tf_op jit(solution)/shard_map/ppermute | solution.py:41
  67.8 5.3 %collective-permute-start.9 = (bf16[4,128,256]{2,1,0:T(8,128)(2,1)S(1)}, bf16[4,128,256]{2,1,0:T(8,128)(2,1)S(1)}, u32[]{:S(2)}, u32[]{:S(2)}) collective-permute-start(bf16[4,128,256]{2,1,0:T(8,128)(2,1)S(1)} %collective-permute-done.8), channel_id=1, source_target_pairs={{0,28},{4,0},{8,4},{12,8},{16,12},{20,16},{24,20},{28,24},{1,29},{... | collective-permute-start | bytes 786440 | tf_op jit(solution)/shard_map/ppermute | solution.py:41
  78.4 3.4 %collective-permute-start.11 = (bf16[8,128,256]{2,1,0:T(8,128)(2,1)}, bf16[8,128,256]{2,1,0:T(8,128)(2,1)}, u32[]{:S(2)}, u32[]{:S(2)}) collective-permute-start(bf16[8,128,256]{2,1,0:T(8,128)(2,1)} %gather_fusion.1), channel_id=1, source_target_pairs={{0,32},{32,64},{64,96},{96,0},{1,33},{33,65},{65,97},{97,1},{2,34}... | collective-permute-start | bytes 1572872 | tf_op jit(solution)/shard_map/ppermute | solution.py:77
  83.3 3.6 %collective-permute-start.13 = (bf16[8,128,256]{2,1,0:T(8,128)(2,1)}, bf16[8,128,256]{2,1,0:T(8,128)(2,1)}, u32[]{:S(2)}, u32[]{:S(2)}) collective-permute-start(bf16[8,128,256]{2,1,0:T(8,128)(2,1)} %gather_fusion.2), channel_id=1, source_target_pairs={{0,64},{32,96},{64,0},{96,32},{1,65},{33,97},{65,1},{97,33},{2,66}... | collective-permute-start | bytes 1572872 | tf_op jit(solution)/shard_map/ppermute | solution.py:77
  88.3 2.6 %collective-permute-start.15 = (bf16[8,128,256]{2,1,0:T(8,128)(2,1)}, bf16[8,128,256]{2,1,0:T(8,128)(2,1)}, u32[]{:S(2)}, u32[]{:S(2)}) collective-permute-start(bf16[8,128,256]{2,1,0:T(8,128)(2,1)} %gather_fusion.3), channel_id=1, source_target_pairs={{0,96},{32,0},{64,32},{96,64},{1,97},{33,1},{65,33},{97,65},{2,98}... | collective-permute-start | bytes 1572872 | tf_op jit(solution)/shard_map/ppermute | solution.py:77
  95.3 3.0 %collective-permute-done.17 = bf16[2,128,256]{2,1,0:T(8,128)(2,1)} collective-permute-done((bf16[2,128,256]{2,1,0:T(8,128)(2,1)S(1)}, bf16[2,128,256]{2,1,0:T(8,128)(2,1)}, u32[]{:S(2)}, u32[]{:S(2)}) %collective-permute-start.17) | collective-permute-done | bytes 131104 | tf_op jit(solution)/shard_map/ppermute | solution.py:150
  100.7 3.9 %collective-permute-done.13 = bf16[8,128,256]{2,1,0:T(8,128)(2,1)} collective-permute-done((bf16[8,128,256]{2,1,0:T(8,128)(2,1)}, bf16[8,128,256]{2,1,0:T(8,128)(2,1)}, u32[]{:S(2)}, u32[]{:S(2)}) %collective-permute-start.13) | collective-permute-done | bytes 524320 | tf_op jit(solution)/shard_map/ppermute | solution.py:77
  104.6 5.2 %collective-permute-done.15 = bf16[8,128,256]{2,1,0:T(8,128)(2,1)} collective-permute-done((bf16[8,128,256]{2,1,0:T(8,128)(2,1)}, bf16[8,128,256]{2,1,0:T(8,128)(2,1)}, u32[]{:S(2)}, u32[]{:S(2)}) %collective-permute-start.15) | collective-permute-done | bytes 524320 | tf_op jit(solution)/shard_map/ppermute | solution.py:77
  112.3 3.5 %collective-permute-start.18 = (f32[512,256]{1,0:T(8,128)S(1)}, f32[512,256]{1,0:T(8,128)S(1)}, u32[]{:S(2)}, u32[]{:S(2)}) collective-permute-start(f32[512,256]{1,0:T(8,128)S(1)} %bitcast.64), channel_id=1, source_target_pairs={{0,1},{1,0},{2,3},{3,2},{4,5},{5,4},{6,7},{7,6},{8,9},{9,8},{10,11... | collective-permute-start | bytes 1572872 | tf_op jit(solution)/shard_map/ppermute | solution.py:150
  119.7 12.7 %collective-permute-done.19 = f32[512,256]{1,0:T(8,128)S(1)} collective-permute-done((f32[512,256]{1,0:T(8,128)S(1)}, f32[512,256]{1,0:T(8,128)S(1)}, u32[]{:S(2)}, u32[]{:S(2)}) %collective-permute-start.19) | collective-permute-done | bytes 524320 | tf_op jit(solution)/shard_map/ppermute | solution.py:150
  135.9 2.8 %collective-permute-done.20 = f32[16896]{0:T(1024)S(1)} collective-permute-done((f32[16896]{0:T(1024)S(1)}, f32[16896]{0:T(1024)S(1)}, u32[]{:S(2)}, u32[]{:S(2)}) %collective-permute-start.20) | collective-permute-done | bytes 67616 | tf_op jit(solution)/shard_map/ppermute | solution.py:206
  138.7 5.0 %collective-permute-start.21 = (f32[16896]{0:T(1024)S(1)}, f32[16896]{0:T(1024)S(1)}, u32[]{:S(2)}, u32[]{:S(2)}) collective-permute-start(f32[16896]{0:T(1024)S(1)} %add.315), channel_id=1, source_target_pairs={{0,8},{4,12},{8,0},{12,4},{16,24},{20,28},{24,16},{28,20},{1,9},{5... | collective-permute-start | bytes 202760 | tf_op jit(solution)/shard_map/ppermute | solution.py:206
  145.4 5.0 %collective-permute-start.22 = (f32[16896]{0:T(1024)S(1)}, f32[16896]{0:T(1024)S(1)}, u32[]{:S(2)}, u32[]{:S(2)}) collective-permute-start(f32[16896]{0:T(1024)S(1)} %add.316), channel_id=1, source_target_pairs={{0,28},{4,24},{8,20},{12,16},{16,12},{20,8},{24,4},{28,0},{1,29},{... | collective-permute-start | bytes 202760 | tf_op jit(solution)/shard_map/ppermute | solution.py:206
  152.4 3.1 %collective-permute-start.23 = (f32[16896]{0:T(1024)S(1)}, f32[16896]{0:T(1024)S(1)}, u32[]{:S(2)}, u32[]{:S(2)}) collective-permute-start(f32[16896]{0:T(1024)S(1)} %add.317), channel_id=1, source_target_pairs={{0,32},{32,0},{64,96},{96,64},{1,33},{33,1},{65,97},{97,65},{2,34}... | collective-permute-start | bytes 202760 | tf_op jit(solution)/shard_map/ppermute | solution.py:206
  157.5 4.3 %collective-permute-start.24 = (f32[16896]{0:T(1024)S(1)}, f32[16896]{0:T(1024)S(1)}, u32[]{:S(2)}, u32[]{:S(2)}) collective-permute-start(f32[16896]{0:T(1024)S(1)} %add.318), channel_id=1, source_target_pairs={{0,96},{32,64},{64,32},{96,0},{1,97},{33,65},{65,33},{97,1},{2,98}... | collective-permute-start | bytes 202760 | tf_op jit(solution)/shard_map/ppermute | solution.py:206
  163.8 4.6 %collective-permute-start.25 = (f32[16896]{0:T(1024)S(1)}, f32[16896]{0:T(1024)S(1)}, u32[]{:S(2)}, u32[]{:S(2)}) collective-permute-start(f32[16896]{0:T(1024)S(1)} %add.319), channel_id=1, source_target_pairs={{0,128},{128,0},{256,384},{384,256},{1,129},{129,1},{257,385},{385... | collective-permute-start | bytes 202760 | tf_op jit(solution)/shard_map/ppermute | solution.py:206
  168.4 2.4 %collective-permute-done.25 = f32[16896]{0:T(1024)S(1)} collective-permute-done((f32[16896]{0:T(1024)S(1)}, f32[16896]{0:T(1024)S(1)}, u32[]{:S(2)}, u32[]{:S(2)}) %collective-permute-start.25) | collective-permute-done | bytes 67616 | tf_op jit(solution)/shard_map/ppermute | solution.py:206
  170.9 5.3 %collective-permute-start.26 = (f32[16896]{0:T(1024)S(1)}, f32[16896]{0:T(1024)S(1)}, u32[]{:S(2)}, u32[]{:S(2)}) collective-permute-start(f32[16896]{0:T(1024)S(1)} %add.320), channel_id=1, source_target_pairs={{0,384},{128,256},{256,128},{384,0},{1,385},{129,257},{257,129},{3... | collective-permute-start | bytes 202760 | tf_op jit(solution)/shard_map/ppermute | solution.py:206
  178.1 2.4 %collective-permute-start.27 = (f32[16896]{0:T(1024)S(1)}, f32[16896]{0:T(1024)S(1)}, u32[]{:S(2)}, u32[]{:S(2)}) collective-permute-start(f32[16896]{0:T(1024)S(1)} %add.321), channel_id=1, source_target_pairs={{0,2},{2,0},{1,3},{3,1},{4,6},{6,4},{5,7},{7,5},{8,10},{10,8},{9,1... | collective-permute-start | bytes 202760 | tf_op jit(solution)/shard_map/ppermute | solution.py:119
  180.4 2.7 %collective-permute-done.27 = f32[16896]{0:T(1024)S(1)} collective-permute-done((f32[16896]{0:T(1024)S(1)}, f32[16896]{0:T(1024)S(1)}, u32[]{:S(2)}, u32[]{:S(2)}) %collective-permute-start.27) | collective-permute-done | bytes 67616 | tf_op jit(solution)/shard_map/ppermute | solution.py:119
  183.1 12.1 %collective-permute-start.28 = (f32[33792]{0:T(1024)S(1)}, f32[33792]{0:T(1024)S(1)}, u32[]{:S(2)}, u32[]{:S(2)}) collective-permute-start(f32[33792]{0:T(1024)S(1)} %maximum_select_fusion.2), channel_id=1, source_target_pairs={{0,1},{1,0},{2,3},{3,2},{4,5},{5,4},{6,7},{7,6},{8,9},{9,8},{10,11... | collective-permute-start | bytes 405512 | tf_op jit(solution)/shard_map/ppermute | solution.py:119
  (102 shorter events, 50.8 us)
Async XLA Ops:
  0.6 109.2 %copy-start = (bf16[1,4,8,128,128]{4,3,2,1,0:T(8,128)(2,1)S(1)}, bf16[1,4,8,128,128]{4,3,2,1,0:T(8,128)(2,1)}, u32[]{:S(2)}) copy-start(bf16[1,4,8,128,128]{4,3,2,1,0:T(8,128)(2,1)} %param.11) | copy-start | bytes 3145732
  0.6 75.1 %copy-start.2 = (bf16[128,256]{1,0:T(8,128)(2,1)S(1)}, bf16[128,256]{1,0:T(8,128)(2,1)}, u32[]{:S(2)}) copy-start(bf16[128,256]{1,0:T(8,128)(2,1)} %param.8) | copy-start | bytes 196612
  0.7 14.6 %collective-permute-start.2 = (bf16[128,256]{1,0:T(8,128)(2,1)}, bf16[128,256]{1,0:T(8,128)(2,1)S(1)}, u32[]{:S(2)}, u32[]{:S(2)}) collective-permute-start(bf16[128,256]{1,0:T(8,128)(2,1)} %param.8), channel_id=1, source_target_pairs={{0,384},{128,0},{256,128},{384,256},{1,385},{129,1},{257,129},{385... | collective-permute-start | bytes 196616 | tf_op jit(solution)/shard_map/ppermute | solution.py:26
  7.5 7.8 %collective-permute-start.1 = (bf16[128,256]{1,0:T(8,128)(2,1)}, bf16[128,256]{1,0:T(8,128)(2,1)S(1)}, u32[]{:S(2)}, u32[]{:S(2)}) collective-permute-start(bf16[128,256]{1,0:T(8,128)(2,1)} %param.8), channel_id=1, source_target_pairs={{0,128},{128,256},{256,384},{384,0},{1,129},{129,257},{257,385},{3... | collective-permute-start | bytes 196616 | tf_op jit(solution)/shard_map/ppermute | solution.py:26
  9.4 9.4 %collective-permute-start = (bf16[128,256]{1,0:T(8,128)(2,1)}, bf16[128,256]{1,0:T(8,128)(2,1)S(1)}, u32[]{:S(2)}, u32[]{:S(2)}) collective-permute-start(bf16[128,256]{1,0:T(8,128)(2,1)} %param.8), channel_id=1, source_target_pairs={{0,256},{128,384},{256,0},{384,128},{1,257},{129,385},{257,1},{385... | collective-permute-start | bytes 196616 | tf_op jit(solution)/shard_map/ppermute | solution.py:26
  19.7 20.2 %collective-permute-start.3 = (bf16[4,128,256]{2,1,0:T(8,128)(2,1)S(1)}, bf16[4,128,256]{2,1,0:T(8,128)(2,1)S(1)}, u32[]{:S(2)}, u32[]{:S(2)}) collective-permute-start(bf16[4,128,256]{2,1,0:T(8,128)(2,1)S(1)} %pad_maximum_fusion.2), channel_id=1, source_target_pairs={{0,4},{4,8},{8,12},{12,16},{16,20},{20,24},{24,28},{28,0},{1,5},{5... | collective-permute-start | bytes 786440 | tf_op jit(solution)/shard_map/ppermute | solution.py:38
  25.2 20.6 %collective-permute-start.10 = (s32[8]{0:T(128)S(1)}, s32[8]{0:T(128)S(1)}, u32[]{:S(2)}, u32[]{:S(2)}) collective-permute-start(s32[8]{0:T(128)S(1)} %get-tuple-element.17), channel_id=1, source_target_pairs={{0,96},{32,0},{64,32},{96,64},{1,97},{33,1},{65,33},{97,65},{2,98}... | collective-permute-start | bytes 104 | tf_op jit(solution)/shard_map/ppermute | solution.py:58
  29.6 27.1 %collective-permute-start.12 = (s32[8]{0:T(128)S(1)}, s32[8]{0:T(128)S(1)}, u32[]{:S(2)}, u32[]{:S(2)}) collective-permute-start(s32[8]{0:T(128)S(1)} %get-tuple-element.17), channel_id=1, source_target_pairs={{0,64},{32,96},{64,0},{96,32},{1,65},{33,97},{65,1},{97,33},{2,66}... | collective-permute-start | bytes 104 | tf_op jit(solution)/shard_map/ppermute | solution.py:58
  32.0 24.7 %collective-permute-start.14 = (s32[8]{0:T(128)S(1)}, s32[8]{0:T(128)S(1)}, u32[]{:S(2)}, u32[]{:S(2)}) collective-permute-start(s32[8]{0:T(128)S(1)} %get-tuple-element.17), channel_id=1, source_target_pairs={{0,32},{32,64},{64,96},{96,0},{1,33},{33,65},{65,97},{97,1},{2,34}... | collective-permute-start | bytes 104 | tf_op jit(solution)/shard_map/ppermute | solution.py:58
  34.6 57.0 %collective-permute-start.16 = (bf16[128,256]{1,0:T(8,128)(2,1)}, bf16[128,256]{1,0:T(8,128)(2,1)}, u32[]{:S(2)}, u32[]{:S(2)}) collective-permute-start(bf16[128,256]{1,0:T(8,128)(2,1)} %param.15), channel_id=1, source_target_pairs={{0,1},{1,0},{2,3},{3,2},{4,5},{5,4},{6,7},{7,6},{8,9},{9,8},{10,11... | collective-permute-start | bytes 196616 | tf_op jit(solution)/shard_map/ppermute | solution.py:150
  39.8 15.0 %collective-permute-start.4 = (bf16[4,128,256]{2,1,0:T(8,128)(2,1)S(1)}, bf16[4,128,256]{2,1,0:T(8,128)(2,1)S(1)}, u32[]{:S(2)}, u32[]{:S(2)}) collective-permute-start(bf16[4,128,256]{2,1,0:T(8,128)(2,1)S(1)} %collective-permute-done.3), channel_id=1, source_target_pairs={{0,4},{4,8},{8,12},{12,16},{16,20},{20,24},{24,28},{28,0},{1,5},{5... | collective-permute-start | bytes 786440 | tf_op jit(solution)/shard_map/ppermute | solution.py:38
  44.6 31.2 %copy-start.6 = (bf16[128,256]{1,0:T(8,128)(2,1)S(1)}, bf16[128,256]{1,0:T(8,128)(2,1)}, u32[]{:S(2)}) copy-start(bf16[128,256]{1,0:T(8,128)(2,1)} %copy-done.5) | copy-start | bytes 196612
  45.9 11.9 %collective-permute-start.7 = (bf16[4,128,256]{2,1,0:T(8,128)(2,1)S(1)}, bf16[4,128,256]{2,1,0:T(8,128)(2,1)S(1)}, u32[]{:S(2)}, u32[]{:S(2)}) collective-permute-start(bf16[4,128,256]{2,1,0:T(8,128)(2,1)S(1)} %pad_maximum_fusion.2), channel_id=1, source_target_pairs={{0,28},{4,0},{8,4},{12,8},{16,12},{20,16},{24,20},{28,24},{1,29},{... | collective-permute-start | bytes 786440 | tf_op jit(solution)/shard_map/ppermute | solution.py:41
  54.8 10.4 %collective-permute-start.5 = (bf16[4,128,256]{2,1,0:T(8,128)(2,1)S(1)}, bf16[4,128,256]{2,1,0:T(8,128)(2,1)S(1)}, u32[]{:S(2)}, u32[]{:S(2)}) collective-permute-start(bf16[4,128,256]{2,1,0:T(8,128)(2,1)S(1)} %collective-permute-done.4), channel_id=1, source_target_pairs={{0,4},{4,8},{8,12},{12,16},{16,20},{20,24},{24,28},{28,0},{1,5},{5... | collective-permute-start | bytes 786440 | tf_op jit(solution)/shard_map/ppermute | solution.py:38
  57.7 10.1 %collective-permute-start.8 = (bf16[4,128,256]{2,1,0:T(8,128)(2,1)S(1)}, bf16[4,128,256]{2,1,0:T(8,128)(2,1)S(1)}, u32[]{:S(2)}, u32[]{:S(2)}) collective-permute-start(bf16[4,128,256]{2,1,0:T(8,128)(2,1)S(1)} %collective-permute-done.7), channel_id=1, source_target_pairs={{0,28},{4,0},{8,4},{12,8},{16,12},{20,16},{24,20},{28,24},{1,29},{... | collective-permute-start | bytes 786440 | tf_op jit(solution)/shard_map/ppermute | solution.py:41
  65.2 9.5 %collective-permute-start.6 = (bf16[4,128,256]{2,1,0:T(8,128)(2,1)S(1)}, bf16[4,128,256]{2,1,0:T(8,128)(2,1)S(1)}, u32[]{:S(2)}, u32[]{:S(2)}) collective-permute-start(bf16[4,128,256]{2,1,0:T(8,128)(2,1)S(1)} %collective-permute-done.5), channel_id=1, source_target_pairs={{0,4},{4,8},{8,12},{12,16},{16,20},{20,24},{24,28},{28,0},{1,5},{5... | collective-permute-start | bytes 786440 | tf_op jit(solution)/shard_map/ppermute | solution.py:38
  67.8 9.2 %collective-permute-start.9 = (bf16[4,128,256]{2,1,0:T(8,128)(2,1)S(1)}, bf16[4,128,256]{2,1,0:T(8,128)(2,1)S(1)}, u32[]{:S(2)}, u32[]{:S(2)}) collective-permute-start(bf16[4,128,256]{2,1,0:T(8,128)(2,1)S(1)} %collective-permute-done.8), channel_id=1, source_target_pairs={{0,28},{4,0},{8,4},{12,8},{16,12},{20,16},{24,20},{28,24},{1,29},{... | collective-permute-start | bytes 786440 | tf_op jit(solution)/shard_map/ppermute | solution.py:41
  78.4 22.2 %collective-permute-start.11 = (bf16[8,128,256]{2,1,0:T(8,128)(2,1)}, bf16[8,128,256]{2,1,0:T(8,128)(2,1)}, u32[]{:S(2)}, u32[]{:S(2)}) collective-permute-start(bf16[8,128,256]{2,1,0:T(8,128)(2,1)} %gather_fusion.1), channel_id=1, source_target_pairs={{0,32},{32,64},{64,96},{96,0},{1,33},{33,65},{65,97},{97,1},{2,34}... | collective-permute-start | bytes 1572872 | tf_op jit(solution)/shard_map/ppermute | solution.py:77
  83.3 21.3 %collective-permute-start.13 = (bf16[8,128,256]{2,1,0:T(8,128)(2,1)}, bf16[8,128,256]{2,1,0:T(8,128)(2,1)}, u32[]{:S(2)}, u32[]{:S(2)}) collective-permute-start(bf16[8,128,256]{2,1,0:T(8,128)(2,1)} %gather_fusion.2), channel_id=1, source_target_pairs={{0,64},{32,96},{64,0},{96,32},{1,65},{33,97},{65,1},{97,33},{2,66}... | collective-permute-start | bytes 1572872 | tf_op jit(solution)/shard_map/ppermute | solution.py:77
  88.3 21.5 %collective-permute-start.15 = (bf16[8,128,256]{2,1,0:T(8,128)(2,1)}, bf16[8,128,256]{2,1,0:T(8,128)(2,1)}, u32[]{:S(2)}, u32[]{:S(2)}) collective-permute-start(bf16[8,128,256]{2,1,0:T(8,128)(2,1)} %gather_fusion.3), channel_id=1, source_target_pairs={{0,96},{32,0},{64,32},{96,64},{1,97},{33,1},{65,33},{97,65},{2,98}... | collective-permute-start | bytes 1572872 | tf_op jit(solution)/shard_map/ppermute | solution.py:77
  92.5 5.8 %collective-permute-start.17 = (bf16[2,128,256]{2,1,0:T(8,128)(2,1)S(1)}, bf16[2,128,256]{2,1,0:T(8,128)(2,1)}, u32[]{:S(2)}, u32[]{:S(2)}) collective-permute-start(bf16[2,128,256]{2,1,0:T(8,128)(2,1)S(1)} %maximum_select_fusion.3), channel_id=1, source_target_pairs={{0,2},{2,0},{1,3},{3,1},{4,6},{6,4},{5,7},{7,5},{8,10},{10,8},{9,1... | collective-permute-start | bytes 393224 | tf_op jit(solution)/shard_map/ppermute | solution.py:150
  112.3 5.0 %collective-permute-start.18 = (f32[512,256]{1,0:T(8,128)S(1)}, f32[512,256]{1,0:T(8,128)S(1)}, u32[]{:S(2)}, u32[]{:S(2)}) collective-permute-start(f32[512,256]{1,0:T(8,128)S(1)} %bitcast.64), channel_id=1, source_target_pairs={{0,1},{1,0},{2,3},{3,2},{4,5},{5,4},{6,7},{7,6},{8,9},{9,8},{10,11... | collective-permute-start | bytes 1572872 | tf_op jit(solution)/shard_map/ppermute | solution.py:150
  117.3 15.0 %collective-permute-start.19 = (f32[512,256]{1,0:T(8,128)S(1)}, f32[512,256]{1,0:T(8,128)S(1)}, u32[]{:S(2)}, u32[]{:S(2)}) collective-permute-start(f32[512,256]{1,0:T(8,128)S(1)} %bitcast_add_fusion), channel_id=1, source_target_pairs={{0,2},{2,0},{1,3},{3,1},{4,6},{6,4},{5,7},{7,5},{8,10},{10,8},{9,1... | collective-permute-start | bytes 1572872 | tf_op jit(solution)/shard_map/ppermute | solution.py:150
  133.6 5.1 %collective-permute-start.20 = (f32[16896]{0:T(1024)S(1)}, f32[16896]{0:T(1024)S(1)}, u32[]{:S(2)}, u32[]{:S(2)}) collective-permute-start(f32[16896]{0:T(1024)S(1)} %dynamic-slice_reduce_fusion), channel_id=1, source_target_pairs={{0,4},{4,0},{8,12},{12,8},{16,20},{20,16},{24,28},{28,24},{1,5},{5... | collective-permute-start | bytes 202760 | tf_op jit(solution)/shard_map/ppermute | solution.py:206
  138.7 6.7 %collective-permute-start.21 = (f32[16896]{0:T(1024)S(1)}, f32[16896]{0:T(1024)S(1)}, u32[]{:S(2)}, u32[]{:S(2)}) collective-permute-start(f32[16896]{0:T(1024)S(1)} %add.315), channel_id=1, source_target_pairs={{0,8},{4,12},{8,0},{12,4},{16,24},{20,28},{24,16},{28,20},{1,9},{5... | collective-permute-start | bytes 202760 | tf_op jit(solution)/shard_map/ppermute | solution.py:206
  145.4 7.0 %collective-permute-start.22 = (f32[16896]{0:T(1024)S(1)}, f32[16896]{0:T(1024)S(1)}, u32[]{:S(2)}, u32[]{:S(2)}) collective-permute-start(f32[16896]{0:T(1024)S(1)} %add.316), channel_id=1, source_target_pairs={{0,28},{4,24},{8,20},{12,16},{16,12},{20,8},{24,4},{28,0},{1,29},{... | collective-permute-start | bytes 202760 | tf_op jit(solution)/shard_map/ppermute | solution.py:206
  152.4 5.1 %collective-permute-start.23 = (f32[16896]{0:T(1024)S(1)}, f32[16896]{0:T(1024)S(1)}, u32[]{:S(2)}, u32[]{:S(2)}) collective-permute-start(f32[16896]{0:T(1024)S(1)} %add.317), channel_id=1, source_target_pairs={{0,32},{32,0},{64,96},{96,64},{1,33},{33,1},{65,97},{97,65},{2,34}... | collective-permute-start | bytes 202760 | tf_op jit(solution)/shard_map/ppermute | solution.py:206
  157.5 6.3 %collective-permute-start.24 = (f32[16896]{0:T(1024)S(1)}, f32[16896]{0:T(1024)S(1)}, u32[]{:S(2)}, u32[]{:S(2)}) collective-permute-start(f32[16896]{0:T(1024)S(1)} %add.318), channel_id=1, source_target_pairs={{0,96},{32,64},{64,32},{96,0},{1,97},{33,65},{65,33},{97,1},{2,98}... | collective-permute-start | bytes 202760 | tf_op jit(solution)/shard_map/ppermute | solution.py:206
  163.8 7.1 %collective-permute-start.25 = (f32[16896]{0:T(1024)S(1)}, f32[16896]{0:T(1024)S(1)}, u32[]{:S(2)}, u32[]{:S(2)}) collective-permute-start(f32[16896]{0:T(1024)S(1)} %add.319), channel_id=1, source_target_pairs={{0,128},{128,0},{256,384},{384,256},{1,129},{129,1},{257,385},{385... | collective-permute-start | bytes 202760 | tf_op jit(solution)/shard_map/ppermute | solution.py:206
  170.9 7.2 %collective-permute-start.26 = (f32[16896]{0:T(1024)S(1)}, f32[16896]{0:T(1024)S(1)}, u32[]{:S(2)}, u32[]{:S(2)}) collective-permute-start(f32[16896]{0:T(1024)S(1)} %add.320), channel_id=1, source_target_pairs={{0,384},{128,256},{256,128},{384,0},{1,385},{129,257},{257,129},{3... | collective-permute-start | bytes 202760 | tf_op jit(solution)/shard_map/ppermute | solution.py:206
  178.1 5.1 %collective-permute-start.27 = (f32[16896]{0:T(1024)S(1)}, f32[16896]{0:T(1024)S(1)}, u32[]{:S(2)}, u32[]{:S(2)}) collective-permute-start(f32[16896]{0:T(1024)S(1)} %add.321), channel_id=1, source_target_pairs={{0,2},{2,0},{1,3},{3,1},{4,6},{6,4},{5,7},{7,5},{8,10},{10,8},{9,1... | collective-permute-start | bytes 202760 | tf_op jit(solution)/shard_map/ppermute | solution.py:119
  183.1 13.1 %collective-permute-start.28 = (f32[33792]{0:T(1024)S(1)}, f32[33792]{0:T(1024)S(1)}, u32[]{:S(2)}, u32[]{:S(2)}) collective-permute-start(f32[33792]{0:T(1024)S(1)} %maximum_select_fusion.2), channel_id=1, source_target_pairs={{0,1},{1,0},{2,3},{3,2},{4,5},{5,4},{6,7},{7,6},{8,9},{9,8},{10,11... | collective-permute-start | bytes 405512 | tf_op jit(solution)/shard_map/ppermute | solution.py:119
  (7 other events, 151.3 us)

commit v16 on v13

--- a/solution.py
+++ b/solution.py
@@ -52,7 +52,7 @@
     return coords
 
 
-def plane_blocks(features, cols, across="x", within=("y_hi", "z")):
+def plane_blocks(features, cols, across="x", within=("z", "y_hi")):
     n_across = lax.axis_size(across)
     peer_cols = {
         s: lax.ppermute(cols, across, [(i, (i - s) % n_across) for i in range(n_across)])

time: 190 us -> 221 us (1.16)
  waiting for transfers between devices: 51.1 us -> 90.6 us
  starting transfers between devices: 118 us -> 112 us
    ppermute x3, waiting for transfers between devices: 2.69 us -> 39.4 us  [round_gather(): lax.ppermute(piece, axis, [(i, (i - d) % n) for i in range(n)])]
    ppermute x3, waiting for transfers between devices: 4.88 us -> 0.38 us  [ring_gather(): right = lax.ppermute(right, axis, bwd)]
    ppermute x4, waiting for transfers between devices: 0.03 us -> 3.57 us  [ring_gather(): left = lax.ppermute(left, axis, fwd)]
    ppermute x4, starting transfers between devices: 13.8 us -> 10.4 us  [swap(): return lax.ppermute(x, axis, [(0, 1), (1, 0)])]
    ppermute x3, waiting for transfers between devices: 11.6 us -> 14.2 us  [plane_blocks(): lax.ppermute(sent, across, [(i, (i + s) % n_across) for i in range(n_acro...]
  transfers between devices with their start and end apart: 29 -> 29, of which waited for: 17 -> 19; matrix products, arithmetic and copies ran while one was open for 5% -> 5% of each run, Pallas kernels for 0% -> 0%
where the time goes in v16:
time: 221 us; the launch traced here: 220 us
  starting transfers between devices  112 us (51%)
  waiting for transfers between devices  90.6 us (41%)
  local copies, waits for them, and re-layouts  8.98 us (4%)
  other arithmetic  4.84 us (2%)
  matrix products  3.02 us (1%)
    ppermute x3, waiting for transfers between devices, round_gather(): lax.ppermute(piece, axis, [(i, (i - d) % n) for i in range(n)])  39.4 us
    ppermute x7, starting transfers between devices, shards(): flat = flat + lax.ppermute(flat, a, perm)  25.2 us
    ppermute x7, waiting for transfers between devices, shards(): flat = flat + lax.ppermute(flat, a, perm)  18.4 us
    ppermute x3, starting transfers between devices, ring_gather(): right = lax.ppermute(right, axis, bwd)  17.7 us
    ppermute x3, starting transfers between devices, round_gather(): lax.ppermute(piece, axis, [(i, (i - d) % n) for i in range(n)])  14.8 us
    ppermute x3, waiting for transfers between devices, plane_blocks(): lax.ppermute(sent, across, [(i, (i + s) % n_across) for i in range(n_acro...  14.2 us
    ppermute x2, starting transfers between devices, all_gather_flat(): other = lax.ppermute(flat, a, perm)  13.9 us
    ppermute x4, waiting for transfers between devices, swap(): return lax.ppermute(x, axis, [(0, 1), (1, 0)])  11.3 us
  transfers between devices with their start and end apart: 29, of which 19 were waited for; matrix products, arithmetic and copies ran while one was open for 5% of the time, Pallas kernels for 0%

profile of v16, /device:TPU:1, one launch (start us, length us, event | category | flops | bytes accessed | tf_op | source)
XLA Modules:
  0.0 220.3 jit_solution(15955179822785901651)
XLA Ops:
  0.6 5.0 %collective-permute-start = (bf16[128,256]{1,0:T(8,128)(2,1)}, bf16[128,256]{1,0:T(8,128)(2,1)S(1)}, u32[]{:S(2)}, u32[]{:S(2)}) collective-permute-start(bf16[128,256]{1,0:T(8,128)(2,1)} %param.8), channel_id=1, source_target_pairs={{0,4},{4,8},{8,12},{12,16},{16,20},{20,24},{24,28},{28,0},{1,5},{5... | collective-permute-start | bytes 196616 | tf_op jit(solution)/shard_map/ppermute | solution.py:38
  5.6 8.6 %collective-permute-start.4 = (bf16[128,256]{1,0:T(8,128)(2,1)}, bf16[128,256]{1,0:T(8,128)(2,1)S(1)}, u32[]{:S(2)}, u32[]{:S(2)}) collective-permute-start(bf16[128,256]{1,0:T(8,128)(2,1)} %param.8), channel_id=1, source_target_pairs={{0,28},{4,0},{8,4},{12,8},{16,12},{20,16},{24,20},{28,24},{1,29},{... | collective-permute-start | bytes 196616 | tf_op jit(solution)/shard_map/ppermute | solution.py:41
  14.9 4.7 %collective-permute-start.12 = (s32[8]{0:T(128)S(1)}, s32[8]{0:T(128)S(1)}, u32[]{:S(2)}, u32[]{:S(2)}) collective-permute-start(s32[8]{0:T(128)S(1)} %get-tuple-element.7), channel_id=1, source_target_pairs={{0,64},{32,96},{64,0},{96,32},{1,65},{33,97},{65,1},{97,33},{2,66}... | collective-permute-start | bytes 104 | tf_op jit(solution)/shard_map/ppermute | solution.py:58
  19.6 2.8 %collective-permute-start.14 = (s32[8]{0:T(128)S(1)}, s32[8]{0:T(128)S(1)}, u32[]{:S(2)}, u32[]{:S(2)}) collective-permute-start(s32[8]{0:T(128)S(1)} %get-tuple-element.7), channel_id=1, source_target_pairs={{0,96},{32,0},{64,32},{96,64},{1,97},{33,1},{65,33},{97,65},{2,98}... | collective-permute-start | bytes 104 | tf_op jit(solution)/shard_map/ppermute | solution.py:58
  22.4 2.5 %collective-permute-start.10 = (s32[8]{0:T(128)S(1)}, s32[8]{0:T(128)S(1)}, u32[]{:S(2)}, u32[]{:S(2)}) collective-permute-start(s32[8]{0:T(128)S(1)} %get-tuple-element.7), channel_id=1, source_target_pairs={{0,32},{32,64},{64,96},{96,0},{1,33},{33,65},{65,97},{97,1},{2,34}... | collective-permute-start | bytes 104 | tf_op jit(solution)/shard_map/ppermute | solution.py:58
  28.8 3.6 %collective-permute-done.1 = bf16[128,256]{1,0:T(8,128)(2,1)S(1)} collective-permute-done((bf16[128,256]{1,0:T(8,128)(2,1)S(1)}, bf16[128,256]{1,0:T(8,128)(2,1)S(1)}, u32[]{:S(2)}, u32[]{:S(2)}) %collective-permute-start.1) | collective-permute-done | bytes 65568 | tf_op jit(solution)/shard_map/ppermute | solution.py:38
  34.3 4.6 %collective-permute-start.5 = (bf16[128,256]{1,0:T(8,128)(2,1)S(1)}, bf16[128,256]{1,0:T(8,128)(2,1)S(1)}, u32[]{:S(2)}, u32[]{:S(2)}) collective-permute-start(bf16[128,256]{1,0:T(8,128)(2,1)S(1)} %collective-permute-done.4), channel_id=1, source_target_pairs={{0,28},{4,0},{8,4},{12,8},{16,12},{20,16},{24,20},{28,24},{1,29},{... | collective-permute-start | bytes 196616 | tf_op jit(solution)/shard_map/ppermute | solution.py:41
  40.9 4.6 %collective-permute-start.6 = (bf16[128,256]{1,0:T(8,128)(2,1)S(1)}, bf16[128,256]{1,0:T(8,128)(2,1)S(1)}, u32[]{:S(2)}, u32[]{:S(2)}) collective-permute-start(bf16[128,256]{1,0:T(8,128)(2,1)S(1)} %collective-permute-done.5), channel_id=1, source_target_pairs={{0,28},{4,0},{8,4},{12,8},{16,12},{20,16},{24,20},{28,24},{1,29},{... | collective-permute-start | bytes 196616 | tf_op jit(solution)/shard_map/ppermute | solution.py:41
  46.8 7.4 %collective-permute-start.7 = (bf16[8,128,256]{2,1,0:T(8,128)(2,1)S(1)}, bf16[8,128,256]{2,1,0:T(8,128)(2,1)S(1)}, u32[]{:S(2)}, u32[]{:S(2)}) collective-permute-start(bf16[8,128,256]{2,1,0:T(8,128)(2,1)S(1)} %bitcast_dynamic-update-slice_fusion), channel_id=1, source_target_pairs={{0,256},{128,384},{256,0},{384,128},{1,257},{129,385},{257,1},{385... | collective-permute-start | bytes 1572872 | tf_op jit(solution)/shard_map/ppermute | solution.py:26
  56.7 5.0 %collective-permute-start.9 = (bf16[8,128,256]{2,1,0:T(8,128)(2,1)S(1)}, bf16[8,128,256]{2,1,0:T(8,128)(2,1)S(1)}, u32[]{:S(2)}, u32[]{:S(2)}) collective-permute-start(bf16[8,128,256]{2,1,0:T(8,128)(2,1)S(1)} %bitcast_dynamic-update-slice_fusion), channel_id=1, source_target_pairs={{0,384},{128,0},{256,128},{384,256},{1,385},{129,1},{257,129},{385... | collective-permute-start | bytes 1572872 | tf_op jit(solution)/shard_map/ppermute | solution.py:26
  61.7 5.0 %collective-permute-done.7 = bf16[8,128,256]{2,1,0:T(8,128)(2,1)S(1)} collective-permute-done((bf16[8,128,256]{2,1,0:T(8,128)(2,1)S(1)}, bf16[8,128,256]{2,1,0:T(8,128)(2,1)S(1)}, u32[]{:S(2)}, u32[]{:S(2)}) %collective-permute-start.7) | collective-permute-done | bytes 524320 | tf_op jit(solution)/shard_map/ppermute | solution.py:26
  66.7 20.9 %collective-permute-done.8 = bf16[8,128,256]{2,1,0:T(8,128)(2,1)S(1)} collective-permute-done((bf16[8,128,256]{2,1,0:T(8,128)(2,1)S(1)}, bf16[8,128,256]{2,1,0:T(8,128)(2,1)S(1)}, u32[]{:S(2)}, u32[]{:S(2)}) %collective-permute-start.8) | collective-permute-done | bytes 524320 | tf_op jit(solution)/shard_map/ppermute | solution.py:26
  87.6 13.5 %collective-permute-done.9 = bf16[8,128,256]{2,1,0:T(8,128)(2,1)S(1)} collective-permute-done((bf16[8,128,256]{2,1,0:T(8,128)(2,1)S(1)}, bf16[8,128,256]{2,1,0:T(8,128)(2,1)S(1)}, u32[]{:S(2)}, u32[]{:S(2)}) %collective-permute-start.9) | collective-permute-done | bytes 524320 | tf_op jit(solution)/shard_map/ppermute | solution.py:26
  102.8 2.5 %collective-permute-start.13 = (bf16[8,128,256]{2,1,0:T(8,128)(2,1)}, bf16[8,128,256]{2,1,0:T(8,128)(2,1)}, u32[]{:S(2)}, u32[]{:S(2)}) collective-permute-start(bf16[8,128,256]{2,1,0:T(8,128)(2,1)} %gather_fusion.1), channel_id=1, source_target_pairs={{0,64},{32,96},{64,0},{96,32},{1,65},{33,97},{65,1},{97,33},{2,66}... | collective-permute-start | bytes 1572872 | tf_op jit(solution)/shard_map/ppermute | solution.py:77
  106.7 3.9 %collective-permute-start.15 = (bf16[8,128,256]{2,1,0:T(8,128)(2,1)}, bf16[8,128,256]{2,1,0:T(8,128)(2,1)}, u32[]{:S(2)}, u32[]{:S(2)}) collective-permute-start(bf16[8,128,256]{2,1,0:T(8,128)(2,1)} %gather_fusion.2), channel_id=1, source_target_pairs={{0,32},{32,64},{64,96},{96,0},{1,33},{33,65},{65,97},{97,1},{2,34}... | collective-permute-start | bytes 1572872 | tf_op jit(solution)/shard_map/ppermute | solution.py:77
  112.0 2.6 %collective-permute-start.11 = (bf16[8,128,256]{2,1,0:T(8,128)(2,1)}, bf16[8,128,256]{2,1,0:T(8,128)(2,1)}, u32[]{:S(2)}, u32[]{:S(2)}) collective-permute-start(bf16[8,128,256]{2,1,0:T(8,128)(2,1)} %gather_fusion), channel_id=1, source_target_pairs={{0,96},{32,0},{64,32},{96,64},{1,97},{33,1},{65,33},{97,65},{2,98}... | collective-permute-start | bytes 1572872 | tf_op jit(solution)/shard_map/ppermute | solution.py:77
  119.5 12.0 %collective-permute-done.15 = bf16[8,128,256]{2,1,0:T(8,128)(2,1)} collective-permute-done((bf16[8,128,256]{2,1,0:T(8,128)(2,1)}, bf16[8,128,256]{2,1,0:T(8,128)(2,1)}, u32[]{:S(2)}, u32[]{:S(2)}) %collective-permute-start.15) | collective-permute-done | bytes 524320 | tf_op jit(solution)/shard_map/ppermute | solution.py:77
  134.1 2.5 %collective-permute-start.16 = (f32[512,256]{1,0:T(8,128)S(1)}, f32[512,256]{1,0:T(8,128)S(1)}, u32[]{:S(2)}, u32[]{:S(2)}) collective-permute-start(f32[512,256]{1,0:T(8,128)S(1)} %bitcast.67), channel_id=1, source_target_pairs={{0,1},{1,0},{2,3},{3,2},{4,5},{5,4},{6,7},{7,6},{8,9},{9,8},{10,11... | collective-permute-start | bytes 1572872 | tf_op jit(solution)/shard_map/ppermute | solution.py:149
  140.6 2.6 %collective-permute-start.18 = (bf16[128,256]{1,0:T(8,128)(2,1)S(1)}, bf16[128,256]{1,0:T(8,128)(2,1)S(1)}, u32[]{:S(2)}, u32[]{:S(2)}) collective-permute-start(bf16[128,256]{1,0:T(8,128)(2,1)S(1)} %copy-done.1), channel_id=1, source_target_pairs={{0,1},{1,0},{2,3},{3,2},{4,5},{5,4},{6,7},{7,6},{8,9},{9,8},{10,11... | collective-permute-start | bytes 196616 | tf_op jit(solution)/shard_map/ppermute | solution.py:149
  144.1 2.9 %collective-permute-start.19 = (bf16[2,128,256]{2,1,0:T(8,128)(2,1)S(1)}, bf16[2,128,256]{2,1,0:T(8,128)(2,1)S(1)}, u32[]{:S(2)}, u32[]{:S(2)}) collective-permute-start(bf16[2,128,256]{2,1,0:T(8,128)(2,1)S(1)} %maximum_select_fusion.3), channel_id=1, source_target_pairs={{0,2},{2,0},{1,3},{3,1},{4,6},{6,4},{5,7},{7,5},{8,10},{10,8},{9,1... | collective-permute-start | bytes 393224 | tf_op jit(solution)/shard_map/ppermute | solution.py:149
  147.1 8.9 %collective-permute-done.19 = bf16[2,128,256]{2,1,0:T(8,128)(2,1)S(1)} collective-permute-done((bf16[2,128,256]{2,1,0:T(8,128)(2,1)S(1)}, bf16[2,128,256]{2,1,0:T(8,128)(2,1)S(1)}, u32[]{:S(2)}, u32[]{:S(2)}) %collective-permute-start.19) | collective-permute-done | bytes 131104 | tf_op jit(solution)/shard_map/ppermute | solution.py:149
  159.2 3.1 %collective-permute-done.20 = f32[16896]{0:T(1024)S(1)} collective-permute-done((f32[16896]{0:T(1024)S(1)}, f32[16896]{0:T(1024)S(1)}, u32[]{:S(2)}, u32[]{:S(2)}) %collective-permute-start.20) | collective-permute-done | bytes 67616 | tf_op jit(solution)/shard_map/ppermute | solution.py:206
  162.4 4.0 %collective-permute-start.21 = (f32[16896]{0:T(1024)S(1)}, f32[16896]{0:T(1024)S(1)}, u32[]{:S(2)}, u32[]{:S(2)}) collective-permute-start(f32[16896]{0:T(1024)S(1)} %add.315), channel_id=1, source_target_pairs={{0,8},{4,12},{8,0},{12,4},{16,24},{20,28},{24,16},{28,20},{1,9},{5... | collective-permute-start | bytes 202760 | tf_op jit(solution)/shard_map/ppermute | solution.py:206
  168.3 5.4 %collective-permute-start.22 = (f32[16896]{0:T(1024)S(1)}, f32[16896]{0:T(1024)S(1)}, u32[]{:S(2)}, u32[]{:S(2)}) collective-permute-start(f32[16896]{0:T(1024)S(1)} %add.316), channel_id=1, source_target_pairs={{0,28},{4,24},{8,20},{12,16},{16,12},{20,8},{24,4},{28,0},{1,29},{... | collective-permute-start | bytes 202760 | tf_op jit(solution)/shard_map/ppermute | solution.py:206
  177.9 2.8 %collective-permute-done.23 = f32[16896]{0:T(1024)S(1)} collective-permute-done((f32[16896]{0:T(1024)S(1)}, f32[16896]{0:T(1024)S(1)}, u32[]{:S(2)}, u32[]{:S(2)}) %collective-permute-start.23) | collective-permute-done | bytes 67616 | tf_op jit(solution)/shard_map/ppermute | solution.py:206
  180.8 4.0 %collective-permute-start.24 = (f32[16896]{0:T(1024)S(1)}, f32[16896]{0:T(1024)S(1)}, u32[]{:S(2)}, u32[]{:S(2)}) collective-permute-start(f32[16896]{0:T(1024)S(1)} %add.318), channel_id=1, source_target_pairs={{0,96},{32,64},{64,32},{96,0},{1,97},{33,65},{65,33},{97,1},{2,98}... | collective-permute-start | bytes 202760 | tf_op jit(solution)/shard_map/ppermute | solution.py:206
  187.0 3.3 %collective-permute-start.25 = (f32[16896]{0:T(1024)S(1)}, f32[16896]{0:T(1024)S(1)}, u32[]{:S(2)}, u32[]{:S(2)}) collective-permute-start(f32[16896]{0:T(1024)S(1)} %add.319), channel_id=1, source_target_pairs={{0,128},{128,0},{256,384},{384,256},{1,129},{129,1},{257,385},{385... | collective-permute-start | bytes 202760 | tf_op jit(solution)/shard_map/ppermute | solution.py:206
  190.3 3.4 %collective-permute-done.25 = f32[16896]{0:T(1024)S(1)} collective-permute-done((f32[16896]{0:T(1024)S(1)}, f32[16896]{0:T(1024)S(1)}, u32[]{:S(2)}, u32[]{:S(2)}) %collective-permute-start.25) | collective-permute-done | bytes 67616 | tf_op jit(solution)/shard_map/ppermute | solution.py:206
  193.8 4.4 %collective-permute-start.26 = (f32[16896]{0:T(1024)S(1)}, f32[16896]{0:T(1024)S(1)}, u32[]{:S(2)}, u32[]{:S(2)}) collective-permute-start(f32[16896]{0:T(1024)S(1)} %add.320), channel_id=1, source_target_pairs={{0,384},{128,256},{256,128},{384,0},{1,385},{129,257},{257,129},{3... | collective-permute-start | bytes 202760 | tf_op jit(solution)/shard_map/ppermute | solution.py:206
  198.2 2.8 %collective-permute-done.26 = f32[16896]{0:T(1024)S(1)} collective-permute-done((f32[16896]{0:T(1024)S(1)}, f32[16896]{0:T(1024)S(1)}, u32[]{:S(2)}, u32[]{:S(2)}) %collective-permute-start.26) | collective-permute-done | bytes 67616 | tf_op jit(solution)/shard_map/ppermute | solution.py:206
  202.9 3.1 %collective-permute-done.27 = f32[16896]{0:T(1024)S(1)} collective-permute-done((f32[16896]{0:T(1024)S(1)}, f32[16896]{0:T(1024)S(1)}, u32[]{:S(2)}, u32[]{:S(2)}) %collective-permute-start.27) | collective-permute-done | bytes 67616 | tf_op jit(solution)/shard_map/ppermute | solution.py:118
  206.0 12.0 %collective-permute-start.28 = (f32[33792]{0:T(1024)S(1)}, f32[33792]{0:T(1024)S(1)}, u32[]{:S(2)}, u32[]{:S(2)}) collective-permute-start(f32[33792]{0:T(1024)S(1)} %maximum_select_fusion.2), channel_id=1, source_target_pairs={{0,1},{1,0},{2,3},{3,2},{4,5},{5,4},{6,7},{7,6},{8,9},{9,8},{10,11... | collective-permute-start | bytes 405512 | tf_op jit(solution)/shard_map/ppermute | solution.py:118
  (89 shorter events, 44.9 us)
Async XLA Ops:
  0.6 130.9 %copy-start = (bf16[1,4,8,128,128]{4,3,2,1,0:T(8,128)(2,1)S(1)}, bf16[1,4,8,128,128]{4,3,2,1,0:T(8,128)(2,1)}, u32[]{:S(2)}) copy-start(bf16[1,4,8,128,128]{4,3,2,1,0:T(8,128)(2,1)} %param.11) | copy-start | bytes 3145732
  0.6 25.5 %collective-permute-start = (bf16[128,256]{1,0:T(8,128)(2,1)}, bf16[128,256]{1,0:T(8,128)(2,1)S(1)}, u32[]{:S(2)}, u32[]{:S(2)}) collective-permute-start(bf16[128,256]{1,0:T(8,128)(2,1)} %param.8), channel_id=1, source_target_pairs={{0,4},{4,8},{8,12},{12,16},{16,20},{20,24},{24,28},{28,0},{1,5},{5... | collective-permute-start | bytes 196616 | tf_op jit(solution)/shard_map/ppermute | solution.py:38
  5.6 28.7 %collective-permute-start.4 = (bf16[128,256]{1,0:T(8,128)(2,1)}, bf16[128,256]{1,0:T(8,128)(2,1)S(1)}, u32[]{:S(2)}, u32[]{:S(2)}) collective-permute-start(bf16[128,256]{1,0:T(8,128)(2,1)} %param.8), channel_id=1, source_target_pairs={{0,28},{4,0},{8,4},{12,8},{16,12},{20,16},{24,20},{28,24},{1,29},{... | collective-permute-start | bytes 196616 | tf_op jit(solution)/shard_map/ppermute | solution.py:41
  14.9 19.3 %collective-permute-start.12 = (s32[8]{0:T(128)S(1)}, s32[8]{0:T(128)S(1)}, u32[]{:S(2)}, u32[]{:S(2)}) collective-permute-start(s32[8]{0:T(128)S(1)} %get-tuple-element.7), channel_id=1, source_target_pairs={{0,64},{32,96},{64,0},{96,32},{1,65},{33,97},{65,1},{97,33},{2,66}... | collective-permute-start | bytes 104 | tf_op jit(solution)/shard_map/ppermute | solution.py:58
  19.6 21.3 %collective-permute-start.14 = (s32[8]{0:T(128)S(1)}, s32[8]{0:T(128)S(1)}, u32[]{:S(2)}, u32[]{:S(2)}) collective-permute-start(s32[8]{0:T(128)S(1)} %get-tuple-element.7), channel_id=1, source_target_pairs={{0,96},{32,0},{64,32},{96,64},{1,97},{33,1},{65,33},{97,65},{2,98}... | collective-permute-start | bytes 104 | tf_op jit(solution)/shard_map/ppermute | solution.py:58
  22.4 39.3 %collective-permute-start.10 = (s32[8]{0:T(128)S(1)}, s32[8]{0:T(128)S(1)}, u32[]{:S(2)}, u32[]{:S(2)}) collective-permute-start(s32[8]{0:T(128)S(1)} %get-tuple-element.7), channel_id=1, source_target_pairs={{0,32},{32,64},{64,96},{96,0},{1,33},{33,65},{65,97},{97,1},{2,34}... | collective-permute-start | bytes 104 | tf_op jit(solution)/shard_map/ppermute | solution.py:58
  26.1 6.2 %collective-permute-start.1 = (bf16[128,256]{1,0:T(8,128)(2,1)S(1)}, bf16[128,256]{1,0:T(8,128)(2,1)S(1)}, u32[]{:S(2)}, u32[]{:S(2)}) collective-permute-start(bf16[128,256]{1,0:T(8,128)(2,1)S(1)} %collective-permute-done), channel_id=1, source_target_pairs={{0,4},{4,8},{8,12},{12,16},{16,20},{20,24},{24,28},{28,0},{1,5},{5... | collective-permute-start | bytes 196616 | tf_op jit(solution)/shard_map/ppermute | solution.py:38
  32.4 6.6 %collective-permute-start.2 = (bf16[128,256]{1,0:T(8,128)(2,1)S(1)}, bf16[128,256]{1,0:T(8,128)(2,1)S(1)}, u32[]{:S(2)}, u32[]{:S(2)}) collective-permute-start(bf16[128,256]{1,0:T(8,128)(2,1)S(1)} %collective-permute-done.1), channel_id=1, source_target_pairs={{0,4},{4,8},{8,12},{12,16},{16,20},{20,24},{24,28},{28,0},{1,5},{5... | collective-permute-start | bytes 196616 | tf_op jit(solution)/shard_map/ppermute | solution.py:38
  34.3 6.6 %collective-permute-start.5 = (bf16[128,256]{1,0:T(8,128)(2,1)S(1)}, bf16[128,256]{1,0:T(8,128)(2,1)S(1)}, u32[]{:S(2)}, u32[]{:S(2)}) collective-permute-start(bf16[128,256]{1,0:T(8,128)(2,1)S(1)} %collective-permute-done.4), channel_id=1, source_target_pairs={{0,28},{4,0},{8,4},{12,8},{16,12},{20,16},{24,20},{28,24},{1,29},{... | collective-permute-start | bytes 196616 | tf_op jit(solution)/shard_map/ppermute | solution.py:41
  38.9 6.6 %collective-permute-start.3 = (bf16[128,256]{1,0:T(8,128)(2,1)S(1)}, bf16[128,256]{1,0:T(8,128)(2,1)S(1)}, u32[]{:S(2)}, u32[]{:S(2)}) collective-permute-start(bf16[128,256]{1,0:T(8,128)(2,1)S(1)} %collective-permute-done.2), channel_id=1, source_target_pairs={{0,4},{4,8},{8,12},{12,16},{16,20},{20,24},{24,28},{28,0},{1,5},{5... | collective-permute-start | bytes 196616 | tf_op jit(solution)/shard_map/ppermute | solution.py:38
  40.9 5.9 %collective-permute-start.6 = (bf16[128,256]{1,0:T(8,128)(2,1)S(1)}, bf16[128,256]{1,0:T(8,128)(2,1)S(1)}, u32[]{:S(2)}, u32[]{:S(2)}) collective-permute-start(bf16[128,256]{1,0:T(8,128)(2,1)S(1)} %collective-permute-done.5), channel_id=1, source_target_pairs={{0,28},{4,0},{8,4},{12,8},{16,12},{20,16},{24,20},{28,24},{1,29},{... | collective-permute-start | bytes 196616 | tf_op jit(solution)/shard_map/ppermute | solution.py:41
  46.8 19.9 %collective-permute-start.7 = (bf16[8,128,256]{2,1,0:T(8,128)(2,1)S(1)}, bf16[8,128,256]{2,1,0:T(8,128)(2,1)S(1)}, u32[]{:S(2)}, u32[]{:S(2)}) collective-permute-start(bf16[8,128,256]{2,1,0:T(8,128)(2,1)S(1)} %bitcast_dynamic-update-slice_fusion), channel_id=1, source_target_pairs={{0,256},{128,384},{256,0},{384,128},{1,257},{129,385},{257,1},{385... | collective-permute-start | bytes 1572872 | tf_op jit(solution)/shard_map/ppermute | solution.py:26
  54.2 33.4 %collective-permute-start.8 = (bf16[8,128,256]{2,1,0:T(8,128)(2,1)S(1)}, bf16[8,128,256]{2,1,0:T(8,128)(2,1)S(1)}, u32[]{:S(2)}, u32[]{:S(2)}) collective-permute-start(bf16[8,128,256]{2,1,0:T(8,128)(2,1)S(1)} %bitcast_dynamic-update-slice_fusion), channel_id=1, source_target_pairs={{0,128},{128,256},{256,384},{384,0},{1,129},{129,257},{257,385},{3... | collective-permute-start | bytes 1572872 | tf_op jit(solution)/shard_map/ppermute | solution.py:26
  56.7 44.5 %collective-permute-start.9 = (bf16[8,128,256]{2,1,0:T(8,128)(2,1)S(1)}, bf16[8,128,256]{2,1,0:T(8,128)(2,1)S(1)}, u32[]{:S(2)}, u32[]{:S(2)}) collective-permute-start(bf16[8,128,256]{2,1,0:T(8,128)(2,1)S(1)} %bitcast_dynamic-update-slice_fusion), channel_id=1, source_target_pairs={{0,384},{128,0},{256,128},{384,256},{1,385},{129,1},{257,129},{385... | collective-permute-start | bytes 1572872 | tf_op jit(solution)/shard_map/ppermute | solution.py:26
  102.8 16.7 %collective-permute-start.13 = (bf16[8,128,256]{2,1,0:T(8,128)(2,1)}, bf16[8,128,256]{2,1,0:T(8,128)(2,1)}, u32[]{:S(2)}, u32[]{:S(2)}) collective-permute-start(bf16[8,128,256]{2,1,0:T(8,128)(2,1)} %gather_fusion.1), channel_id=1, source_target_pairs={{0,64},{32,96},{64,0},{96,32},{1,65},{33,97},{65,1},{97,33},{2,66}... | collective-permute-start | bytes 1572872 | tf_op jit(solution)/shard_map/ppermute | solution.py:77
  106.7 24.9 %collective-permute-start.15 = (bf16[8,128,256]{2,1,0:T(8,128)(2,1)}, bf16[8,128,256]{2,1,0:T(8,128)(2,1)}, u32[]{:S(2)}, u32[]{:S(2)}) collective-permute-start(bf16[8,128,256]{2,1,0:T(8,128)(2,1)} %gather_fusion.2), channel_id=1, source_target_pairs={{0,32},{32,64},{64,96},{96,0},{1,33},{33,65},{65,97},{97,1},{2,34}... | collective-permute-start | bytes 1572872 | tf_op jit(solution)/shard_map/ppermute | solution.py:77
  112.0 19.6 %collective-permute-start.11 = (bf16[8,128,256]{2,1,0:T(8,128)(2,1)}, bf16[8,128,256]{2,1,0:T(8,128)(2,1)}, u32[]{:S(2)}, u32[]{:S(2)}) collective-permute-start(bf16[8,128,256]{2,1,0:T(8,128)(2,1)} %gather_fusion), channel_id=1, source_target_pairs={{0,96},{32,0},{64,32},{96,64},{1,97},{33,1},{65,33},{97,65},{2,98}... | collective-permute-start | bytes 1572872 | tf_op jit(solution)/shard_map/ppermute | solution.py:77
  134.0 22.1 %copy-start.2 = (bf16[256,256]{1,0:T(8,128)(2,1)S(1)}, bf16[256,256]{1,0:T(8,128)(2,1)}, u32[]{:S(2)}) copy-start(bf16[256,256]{1,0:T(8,128)(2,1)} %param.9) | copy-start | bytes 393220
  134.1 22.1 %copy-start.3 = (f32[256]{0:T(256)S(1)}, f32[256]{0:T(256)}, u32[]{:S(2)}) copy-start(f32[256]{0:T(256)} %param.10) | copy-start | bytes 3076
  134.1 4.1 %collective-permute-start.16 = (f32[512,256]{1,0:T(8,128)S(1)}, f32[512,256]{1,0:T(8,128)S(1)}, u32[]{:S(2)}, u32[]{:S(2)}) collective-permute-start(f32[512,256]{1,0:T(8,128)S(1)} %bitcast.67), channel_id=1, source_target_pairs={{0,1},{1,0},{2,3},{3,2},{4,5},{5,4},{6,7},{7,6},{8,9},{9,8},{10,11... | collective-permute-start | bytes 1572872 | tf_op jit(solution)/shard_map/ppermute | solution.py:149
  138.2 17.8 %collective-permute-start.17 = (f32[512,256]{1,0:T(8,128)S(1)}, f32[512,256]{1,0:T(8,128)S(1)}, u32[]{:S(2)}, u32[]{:S(2)}) collective-permute-start(f32[512,256]{1,0:T(8,128)S(1)} %bitcast_add_fusion), channel_id=1, source_target_pairs={{0,2},{2,0},{1,3},{3,1},{4,6},{6,4},{5,7},{7,5},{8,10},{10,8},{9,1... | collective-permute-start | bytes 1572872 | tf_op jit(solution)/shard_map/ppermute | solution.py:149
  140.6 3.5 %collective-permute-start.18 = (bf16[128,256]{1,0:T(8,128)(2,1)S(1)}, bf16[128,256]{1,0:T(8,128)(2,1)S(1)}, u32[]{:S(2)}, u32[]{:S(2)}) collective-permute-start(bf16[128,256]{1,0:T(8,128)(2,1)S(1)} %copy-done.1), channel_id=1, source_target_pairs={{0,1},{1,0},{2,3},{3,2},{4,5},{5,4},{6,7},{7,6},{8,9},{9,8},{10,11... | collective-permute-start | bytes 196616 | tf_op jit(solution)/shard_map/ppermute | solution.py:149
  144.1 12.0 %collective-permute-start.19 = (bf16[2,128,256]{2,1,0:T(8,128)(2,1)S(1)}, bf16[2,128,256]{2,1,0:T(8,128)(2,1)S(1)}, u32[]{:S(2)}, u32[]{:S(2)}) collective-permute-start(bf16[2,128,256]{2,1,0:T(8,128)(2,1)S(1)} %maximum_select_fusion.3), channel_id=1, source_target_pairs={{0,2},{2,0},{1,3},{3,1},{4,6},{6,4},{5,7},{7,5},{8,10},{10,8},{9,1... | collective-permute-start | bytes 393224 | tf_op jit(solution)/shard_map/ppermute | solution.py:149
  157.3 5.1 %collective-permute-start.20 = (f32[16896]{0:T(1024)S(1)}, f32[16896]{0:T(1024)S(1)}, u32[]{:S(2)}, u32[]{:S(2)}) collective-permute-start(f32[16896]{0:T(1024)S(1)} %dynamic-slice_reduce_fusion), channel_id=1, source_target_pairs={{0,4},{4,0},{8,12},{12,8},{16,20},{20,16},{24,28},{28,24},{1,5},{5... | collective-permute-start | bytes 202760 | tf_op jit(solution)/shard_map/ppermute | solution.py:206
  162.4 6.0 %collective-permute-start.21 = (f32[16896]{0:T(1024)S(1)}, f32[16896]{0:T(1024)S(1)}, u32[]{:S(2)}, u32[]{:S(2)}) collective-permute-start(f32[16896]{0:T(1024)S(1)} %add.315), channel_id=1, source_target_pairs={{0,8},{4,12},{8,0},{12,4},{16,24},{20,28},{24,16},{28,20},{1,9},{5... | collective-permute-start | bytes 202760 | tf_op jit(solution)/shard_map/ppermute | solution.py:206
  168.3 7.4 %collective-permute-start.22 = (f32[16896]{0:T(1024)S(1)}, f32[16896]{0:T(1024)S(1)}, u32[]{:S(2)}, u32[]{:S(2)}) collective-permute-start(f32[16896]{0:T(1024)S(1)} %add.316), channel_id=1, source_target_pairs={{0,28},{4,24},{8,20},{12,16},{16,12},{20,8},{24,4},{28,0},{1,29},{... | collective-permute-start | bytes 202760 | tf_op jit(solution)/shard_map/ppermute | solution.py:206
  175.7 5.1 %collective-permute-start.23 = (f32[16896]{0:T(1024)S(1)}, f32[16896]{0:T(1024)S(1)}, u32[]{:S(2)}, u32[]{:S(2)}) collective-permute-start(f32[16896]{0:T(1024)S(1)} %add.317), channel_id=1, source_target_pairs={{0,32},{32,0},{64,96},{96,64},{1,33},{33,1},{65,97},{97,65},{2,34}... | collective-permute-start | bytes 202760 | tf_op jit(solution)/shard_map/ppermute | solution.py:206
  180.8 6.3 %collective-permute-start.24 = (f32[16896]{0:T(1024)S(1)}, f32[16896]{0:T(1024)S(1)}, u32[]{:S(2)}, u32[]{:S(2)}) collective-permute-start(f32[16896]{0:T(1024)S(1)} %add.318), channel_id=1, source_target_pairs={{0,96},{32,64},{64,32},{96,0},{1,97},{33,65},{65,33},{97,1},{2,98}... | collective-permute-start | bytes 202760 | tf_op jit(solution)/shard_map/ppermute | solution.py:206
  187.0 6.7 %collective-permute-start.25 = (f32[16896]{0:T(1024)S(1)}, f32[16896]{0:T(1024)S(1)}, u32[]{:S(2)}, u32[]{:S(2)}) collective-permute-start(f32[16896]{0:T(1024)S(1)} %add.319), channel_id=1, source_target_pairs={{0,128},{128,0},{256,384},{384,256},{1,129},{129,1},{257,385},{385... | collective-permute-start | bytes 202760 | tf_op jit(solution)/shard_map/ppermute | solution.py:206
  193.8 7.2 %collective-permute-start.26 = (f32[16896]{0:T(1024)S(1)}, f32[16896]{0:T(1024)S(1)}, u32[]{:S(2)}, u32[]{:S(2)}) collective-permute-start(f32[16896]{0:T(1024)S(1)} %add.320), channel_id=1, source_target_pairs={{0,384},{128,256},{256,128},{384,0},{1,385},{129,257},{257,129},{3... | collective-permute-start | bytes 202760 | tf_op jit(solution)/shard_map/ppermute | solution.py:206
  200.9 5.1 %collective-permute-start.27 = (f32[16896]{0:T(1024)S(1)}, f32[16896]{0:T(1024)S(1)}, u32[]{:S(2)}, u32[]{:S(2)}) collective-permute-start(f32[16896]{0:T(1024)S(1)} %add.321), channel_id=1, source_target_pairs={{0,2},{2,0},{1,3},{3,1},{4,6},{6,4},{5,7},{7,5},{8,10},{10,8},{9,1... | collective-permute-start | bytes 202760 | tf_op jit(solution)/shard_map/ppermute | solution.py:118
  206.0 12.9 %collective-permute-start.28 = (f32[33792]{0:T(1024)S(1)}, f32[33792]{0:T(1024)S(1)}, u32[]{:S(2)}, u32[]{:S(2)}) collective-permute-start(f32[33792]{0:T(1024)S(1)} %maximum_select_fusion.2), channel_id=1, source_target_pairs={{0,1},{1,0},{2,3},{3,2},{4,5},{5,4},{6,7},{7,6},{8,9},{9,8},{10,11... | collective-permute-start | bytes 405512 | tf_op jit(solution)/shard_map/ppermute | solution.py:118
  (1 other events, 7.1 us)

commit v17 on v13

--- a/solution.py
+++ b/solution.py
@@ -163,7 +163,9 @@
 
 def sum_over_rep(value):
     value = value + swap(value, "core")
-    return value + swap(value, "y_lo")
+    half = value.shape[0] // 2
+    other = jnp.concatenate([swap(value[:half], "y_lo"), swap(value[half:], "y_lo")])
+    return value + other
 
 
 def shards(features, weight, bias_terms, tile_data, tile_row, tile_col, tile_count, grad_out):

time: 190 us -> 190 us (level)
    ppermute x4 -> x5, starting transfers between devices: 13.8 us -> 15.2 us  [swap(): return lax.ppermute(x, axis, [(0, 1), (1, 0)])]
    ppermute x4 -> x5, waiting for transfers between devices: 11.3 us -> 10.1 us  [swap(): return lax.ppermute(x, axis, [(0, 1), (1, 0)])]
  transfers between devices with their start and end apart: 29 -> 30, of which waited for: 17 -> 15; matrix products, arithmetic and copies ran while one was open for 5% -> 5% of each run, Pallas kernels for 0% -> 0%
where the time goes in v17:
time: 190 us; the launch traced here: 188 us
  starting transfers between devices  119 us (63%)
  waiting for transfers between devices  49.9 us (26%)
  local copies, waits for them, and re-layouts  8.98 us (5%)
  other arithmetic  6.05 us (3%)
  matrix products  3.07 us (2%)
    ppermute x7, starting transfers between devices, shards(): flat = flat + lax.ppermute(flat, a, perm)  27.3 us
    ppermute x7, waiting for transfers between devices, shards(): flat = flat + lax.ppermute(flat, a, perm)  17.3 us
    ppermute x3, starting transfers between devices, ring_gather(): right = lax.ppermute(right, axis, bwd)  16.5 us
    ppermute x3, starting transfers between devices, round_gather(): lax.ppermute(piece, axis, [(i, (i - d) % n) for i in range(n)])  15.8 us
    ppermute x5, starting transfers between devices, swap(): return lax.ppermute(x, axis, [(0, 1), (1, 0)])  15.2 us
    ppermute x2, starting transfers between devices, all_gather_flat(): other = lax.ppermute(flat, a, perm)  14 us
    ppermute x3, waiting for transfers between devices, plane_blocks(): lax.ppermute(sent, across, [(i, (i + s) % n_across) for i in range(n_acro...  11.5 us
    ppermute x4, starting transfers between devices, ring_gather(): left = lax.ppermute(left, axis, fwd)  11.2 us
  transfers between devices with their start and end apart: 30, of which 15 were waited for; matrix products, arithmetic and copies ran while one was open for 5% of the time, Pallas kernels for 0%

profile of v17, /device:TPU:1, one launch (start us, length us, event | category | flops | bytes accessed | tf_op | source)
XLA Modules:
  0.0 188.4 jit_solution(10560306615148565080)
XLA Ops:
  0.7 8.4 %collective-permute-start = (bf16[128,256]{1,0:T(8,128)(2,1)}, bf16[128,256]{1,0:T(8,128)(2,1)S(1)}, u32[]{:S(2)}, u32[]{:S(2)}) collective-permute-start(bf16[128,256]{1,0:T(8,128)(2,1)} %param.8), channel_id=1, source_target_pairs={{0,256},{128,384},{256,0},{384,128},{1,257},{129,385},{257,1},{385... | collective-permute-start | bytes 196616 | tf_op jit(solution)/shard_map/ppermute | solution.py:26
  9.1 2.4 %collective-permute-start.1 = (bf16[128,256]{1,0:T(8,128)(2,1)}, bf16[128,256]{1,0:T(8,128)(2,1)S(1)}, u32[]{:S(2)}, u32[]{:S(2)}) collective-permute-start(bf16[128,256]{1,0:T(8,128)(2,1)} %param.8), channel_id=1, source_target_pairs={{0,128},{128,256},{256,384},{384,0},{1,129},{129,257},{257,385},{3... | collective-permute-start | bytes 196616 | tf_op jit(solution)/shard_map/ppermute | solution.py:26
  11.5 5.0 %collective-permute-start.2 = (bf16[128,256]{1,0:T(8,128)(2,1)}, bf16[128,256]{1,0:T(8,128)(2,1)S(1)}, u32[]{:S(2)}, u32[]{:S(2)}) collective-permute-start(bf16[128,256]{1,0:T(8,128)(2,1)} %param.8), channel_id=1, source_target_pairs={{0,384},{128,0},{256,128},{384,256},{1,385},{129,1},{257,129},{385... | collective-permute-start | bytes 196616 | tf_op jit(solution)/shard_map/ppermute | solution.py:26
  16.5 2.7 %collective-permute-done.1 = bf16[128,256]{1,0:T(8,128)(2,1)S(1)} collective-permute-done((bf16[128,256]{1,0:T(8,128)(2,1)}, bf16[128,256]{1,0:T(8,128)(2,1)S(1)}, u32[]{:S(2)}, u32[]{:S(2)}) %collective-permute-start.1) | collective-permute-done | bytes 65568 | tf_op jit(solution)/shard_map/ppermute | solution.py:26
  20.1 3.4 %collective-permute-start.3 = (bf16[4,128,256]{2,1,0:T(8,128)(2,1)S(1)}, bf16[4,128,256]{2,1,0:T(8,128)(2,1)S(1)}, u32[]{:S(2)}, u32[]{:S(2)}) collective-permute-start(bf16[4,128,256]{2,1,0:T(8,128)(2,1)S(1)} %pad_maximum_fusion.2), channel_id=1, source_target_pairs={{0,4},{4,8},{8,12},{12,16},{16,20},{20,24},{24,28},{28,0},{1,5},{5... | collective-permute-start | bytes 786440 | tf_op jit(solution)/shard_map/ppermute | solution.py:38
  24.8 4.6 %collective-permute-start.12 = (s32[8]{0:T(128)S(1)}, s32[8]{0:T(128)S(1)}, u32[]{:S(2)}, u32[]{:S(2)}) collective-permute-start(s32[8]{0:T(128)S(1)} %get-tuple-element.7), channel_id=1, source_target_pairs={{0,64},{32,96},{64,0},{96,32},{1,65},{33,97},{65,1},{97,33},{2,66}... | collective-permute-start | bytes 104 | tf_op jit(solution)/shard_map/ppermute | solution.py:58
  29.5 2.8 %collective-permute-start.14 = (s32[8]{0:T(128)S(1)}, s32[8]{0:T(128)S(1)}, u32[]{:S(2)}, u32[]{:S(2)}) collective-permute-start(s32[8]{0:T(128)S(1)} %get-tuple-element.7), channel_id=1, source_target_pairs={{0,96},{32,0},{64,32},{96,64},{1,97},{33,1},{65,33},{97,65},{2,98}... | collective-permute-start | bytes 104 | tf_op jit(solution)/shard_map/ppermute | solution.py:58
  32.2 2.5 %collective-permute-start.10 = (s32[8]{0:T(128)S(1)}, s32[8]{0:T(128)S(1)}, u32[]{:S(2)}, u32[]{:S(2)}) collective-permute-start(s32[8]{0:T(128)S(1)} %get-tuple-element.7), channel_id=1, source_target_pairs={{0,32},{32,64},{64,96},{96,0},{1,33},{33,65},{65,97},{97,1},{2,34}... | collective-permute-start | bytes 104 | tf_op jit(solution)/shard_map/ppermute | solution.py:58
  34.8 4.0 %collective-permute-start.4 = (bf16[4,128,256]{2,1,0:T(8,128)(2,1)S(1)}, bf16[4,128,256]{2,1,0:T(8,128)(2,1)S(1)}, u32[]{:S(2)}, u32[]{:S(2)}) collective-permute-start(bf16[4,128,256]{2,1,0:T(8,128)(2,1)S(1)} %collective-permute-done.3), channel_id=1, source_target_pairs={{0,4},{4,8},{8,12},{12,16},{16,20},{20,24},{24,28},{28,0},{1,5},{5... | collective-permute-start | bytes 786440 | tf_op jit(solution)/shard_map/ppermute | solution.py:38
  40.8 6.5 %collective-permute-start.7 = (bf16[4,128,256]{2,1,0:T(8,128)(2,1)S(1)}, bf16[4,128,256]{2,1,0:T(8,128)(2,1)S(1)}, u32[]{:S(2)}, u32[]{:S(2)}) collective-permute-start(bf16[4,128,256]{2,1,0:T(8,128)(2,1)S(1)} %pad_maximum_fusion.2), channel_id=1, source_target_pairs={{0,28},{4,0},{8,4},{12,8},{16,12},{20,16},{24,20},{28,24},{1,29},{... | collective-permute-start | bytes 786440 | tf_op jit(solution)/shard_map/ppermute | solution.py:41
  50.6 5.0 %collective-permute-start.8 = (bf16[4,128,256]{2,1,0:T(8,128)(2,1)S(1)}, bf16[4,128,256]{2,1,0:T(8,128)(2,1)S(1)}, u32[]{:S(2)}, u32[]{:S(2)}) collective-permute-start(bf16[4,128,256]{2,1,0:T(8,128)(2,1)S(1)} %collective-permute-done.7), channel_id=1, source_target_pairs={{0,28},{4,0},{8,4},{12,8},{16,12},{20,16},{24,20},{28,24},{1,29},{... | collective-permute-start | bytes 786440 | tf_op jit(solution)/shard_map/ppermute | solution.py:41
  58.9 5.0 %collective-permute-start.9 = (bf16[4,128,256]{2,1,0:T(8,128)(2,1)S(1)}, bf16[4,128,256]{2,1,0:T(8,128)(2,1)S(1)}, u32[]{:S(2)}, u32[]{:S(2)}) collective-permute-start(bf16[4,128,256]{2,1,0:T(8,128)(2,1)S(1)} %collective-permute-done.8), channel_id=1, source_target_pairs={{0,28},{4,0},{8,4},{12,8},{16,12},{20,16},{24,20},{28,24},{1,29},{... | collective-permute-start | bytes 786440 | tf_op jit(solution)/shard_map/ppermute | solution.py:41
  64.9 2.3 %collective-permute-done.9 = bf16[4,128,256]{2,1,0:T(8,128)(2,1)S(1)} collective-permute-done((bf16[4,128,256]{2,1,0:T(8,128)(2,1)S(1)}, bf16[4,128,256]{2,1,0:T(8,128)(2,1)S(1)}, u32[]{:S(2)}, u32[]{:S(2)}) %collective-permute-start.9) | collective-permute-done | bytes 262176 | tf_op jit(solution)/shard_map/ppermute | solution.py:41
  68.6 2.5 %collective-permute-start.13 = (bf16[8,128,256]{2,1,0:T(8,128)(2,1)}, bf16[8,128,256]{2,1,0:T(8,128)(2,1)}, u32[]{:S(2)}, u32[]{:S(2)}) collective-permute-start(bf16[8,128,256]{2,1,0:T(8,128)(2,1)} %gather_fusion.1), channel_id=1, source_target_pairs={{0,64},{32,96},{64,0},{96,32},{1,65},{33,97},{65,1},{97,33},{2,66}... | collective-permute-start | bytes 1572872 | tf_op jit(solution)/shard_map/ppermute | solution.py:77
  72.6 3.9 %collective-permute-start.15 = (bf16[8,128,256]{2,1,0:T(8,128)(2,1)}, bf16[8,128,256]{2,1,0:T(8,128)(2,1)}, u32[]{:S(2)}, u32[]{:S(2)}) collective-permute-start(bf16[8,128,256]{2,1,0:T(8,128)(2,1)} %gather_fusion.2), channel_id=1, source_target_pairs={{0,32},{32,64},{64,96},{96,0},{1,33},{33,65},{65,97},{97,1},{2,34}... | collective-permute-start | bytes 1572872 | tf_op jit(solution)/shard_map/ppermute | solution.py:77
  77.9 2.6 %collective-permute-start.11 = (bf16[8,128,256]{2,1,0:T(8,128)(2,1)}, bf16[8,128,256]{2,1,0:T(8,128)(2,1)}, u32[]{:S(2)}, u32[]{:S(2)}) collective-permute-start(bf16[8,128,256]{2,1,0:T(8,128)(2,1)} %gather_fusion), channel_id=1, source_target_pairs={{0,96},{32,0},{64,32},{96,64},{1,97},{33,1},{65,33},{97,65},{2,98}... | collective-permute-start | bytes 1572872 | tf_op jit(solution)/shard_map/ppermute | solution.py:77
  83.1 11.5 %collective-permute-done.15 = bf16[8,128,256]{2,1,0:T(8,128)(2,1)} collective-permute-done((bf16[8,128,256]{2,1,0:T(8,128)(2,1)}, bf16[8,128,256]{2,1,0:T(8,128)(2,1)}, u32[]{:S(2)}, u32[]{:S(2)}) %collective-permute-start.15) | collective-permute-done | bytes 524320 | tf_op jit(solution)/shard_map/ppermute | solution.py:77
  97.2 5.8 %collective-permute-start.16 = (f32[512,256]{1,0:T(8,128)S(1)}, f32[512,256]{1,0:T(8,128)S(1)}, u32[]{:S(2)}, u32[]{:S(2)}) collective-permute-start(f32[512,256]{1,0:T(8,128)S(1)} %bitcast.67), channel_id=1, source_target_pairs={{0,1},{1,0},{2,3},{3,2},{4,5},{5,4},{6,7},{7,6},{8,9},{9,8},{10,11... | collective-permute-start | bytes 1572872 | tf_op jit(solution)/shard_map/ppermute | solution.py:149
  107.3 3.1 %collective-permute-start.18 = (f32[256,256]{1,0:T(8,128)S(1)}, f32[256,256]{1,0:T(8,128)S(1)}, u32[]{:S(2)}, u32[]{:S(2)}) collective-permute-start(f32[256,256]{1,0:T(8,128)S(1)} %get-tuple-element.10), channel_id=1, source_target_pairs={{0,2},{2,0},{1,3},{3,1},{4,6},{6,4},{5,7},{7,5},{8,10},{10,8},{9,1... | collective-permute-start | bytes 786440 | tf_op jit(solution)/shard_map/ppermute | solution.py:149
  112.8 10.0 %collective-permute-done.20 = bf16[2,128,256]{2,1,0:T(8,128)(2,1)S(1)} collective-permute-done((bf16[2,128,256]{2,1,0:T(8,128)(2,1)S(1)}, bf16[2,128,256]{2,1,0:T(8,128)(2,1)S(1)}, u32[]{:S(2)}, u32[]{:S(2)}) %collective-permute-start.20) | collective-permute-done | bytes 131104 | tf_op jit(solution)/shard_map/ppermute | solution.py:149
  126.1 3.1 %collective-permute-done.21 = f32[16896]{0:T(1024)S(1)} collective-permute-done((f32[16896]{0:T(1024)S(1)}, f32[16896]{0:T(1024)S(1)}, u32[]{:S(2)}, u32[]{:S(2)}) %collective-permute-start.21) | collective-permute-done | bytes 67616 | tf_op jit(solution)/shard_map/ppermute | solution.py:208
  129.2 6.1 %collective-permute-start.22 = (f32[16896]{0:T(1024)S(1)}, f32[16896]{0:T(1024)S(1)}, u32[]{:S(2)}, u32[]{:S(2)}) collective-permute-start(f32[16896]{0:T(1024)S(1)} %add.315), channel_id=1, source_target_pairs={{0,8},{4,12},{8,0},{12,4},{16,24},{20,28},{24,16},{28,20},{1,9},{5... | collective-permute-start | bytes 202760 | tf_op jit(solution)/shard_map/ppermute | solution.py:208
  137.0 3.9 %collective-permute-start.23 = (f32[16896]{0:T(1024)S(1)}, f32[16896]{0:T(1024)S(1)}, u32[]{:S(2)}, u32[]{:S(2)}) collective-permute-start(f32[16896]{0:T(1024)S(1)} %add.316), channel_id=1, source_target_pairs={{0,28},{4,24},{8,20},{12,16},{16,12},{20,8},{24,4},{28,0},{1,29},{... | collective-permute-start | bytes 202760 | tf_op jit(solution)/shard_map/ppermute | solution.py:208
  141.0 2.3 %collective-permute-done.23 = f32[16896]{0:T(1024)S(1)} collective-permute-done((f32[16896]{0:T(1024)S(1)}, f32[16896]{0:T(1024)S(1)}, u32[]{:S(2)}, u32[]{:S(2)}) %collective-permute-start.23) | collective-permute-done | bytes 67616 | tf_op jit(solution)/shard_map/ppermute | solution.py:208
  143.3 2.4 %collective-permute-start.24 = (f32[16896]{0:T(1024)S(1)}, f32[16896]{0:T(1024)S(1)}, u32[]{:S(2)}, u32[]{:S(2)}) collective-permute-start(f32[16896]{0:T(1024)S(1)} %add.317), channel_id=1, source_target_pairs={{0,32},{32,0},{64,96},{96,64},{1,33},{33,1},{65,97},{97,65},{2,34}... | collective-permute-start | bytes 202760 | tf_op jit(solution)/shard_map/ppermute | solution.py:208
  145.8 2.6 %collective-permute-done.24 = f32[16896]{0:T(1024)S(1)} collective-permute-done((f32[16896]{0:T(1024)S(1)}, f32[16896]{0:T(1024)S(1)}, u32[]{:S(2)}, u32[]{:S(2)}) %collective-permute-start.24) | collective-permute-done | bytes 67616 | tf_op jit(solution)/shard_map/ppermute | solution.py:208
  148.4 4.3 %collective-permute-start.25 = (f32[16896]{0:T(1024)S(1)}, f32[16896]{0:T(1024)S(1)}, u32[]{:S(2)}, u32[]{:S(2)}) collective-permute-start(f32[16896]{0:T(1024)S(1)} %add.318), channel_id=1, source_target_pairs={{0,96},{32,64},{64,32},{96,0},{1,97},{33,65},{65,33},{97,1},{2,98}... | collective-permute-start | bytes 202760 | tf_op jit(solution)/shard_map/ppermute | solution.py:208
  154.6 3.0 %collective-permute-start.26 = (f32[16896]{0:T(1024)S(1)}, f32[16896]{0:T(1024)S(1)}, u32[]{:S(2)}, u32[]{:S(2)}) collective-permute-start(f32[16896]{0:T(1024)S(1)} %add.319), channel_id=1, source_target_pairs={{0,128},{128,0},{256,384},{384,256},{1,129},{129,1},{257,385},{385... | collective-permute-start | bytes 202760 | tf_op jit(solution)/shard_map/ppermute | solution.py:208
  157.6 3.7 %collective-permute-done.26 = f32[16896]{0:T(1024)S(1)} collective-permute-done((f32[16896]{0:T(1024)S(1)}, f32[16896]{0:T(1024)S(1)}, u32[]{:S(2)}, u32[]{:S(2)}) %collective-permute-start.26) | collective-permute-done | bytes 67616 | tf_op jit(solution)/shard_map/ppermute | solution.py:208
  161.4 5.5 %collective-permute-start.27 = (f32[16896]{0:T(1024)S(1)}, f32[16896]{0:T(1024)S(1)}, u32[]{:S(2)}, u32[]{:S(2)}) collective-permute-start(f32[16896]{0:T(1024)S(1)} %add.320), channel_id=1, source_target_pairs={{0,384},{128,256},{256,128},{384,0},{1,385},{129,257},{257,129},{3... | collective-permute-start | bytes 202760 | tf_op jit(solution)/shard_map/ppermute | solution.py:208
  170.8 3.1 %collective-permute-done.28 = f32[16896]{0:T(1024)S(1)} collective-permute-done((f32[16896]{0:T(1024)S(1)}, f32[16896]{0:T(1024)S(1)}, u32[]{:S(2)}, u32[]{:S(2)}) %collective-permute-start.28) | collective-permute-done | bytes 67616 | tf_op jit(solution)/shard_map/ppermute | solution.py:118
  173.9 12.1 %collective-permute-start.29 = (f32[33792]{0:T(1024)S(1)}, f32[33792]{0:T(1024)S(1)}, u32[]{:S(2)}, u32[]{:S(2)}) collective-permute-start(f32[33792]{0:T(1024)S(1)} %maximum_select_fusion.2), channel_id=1, source_target_pairs={{0,1},{1,0},{2,3},{3,2},{4,5},{5,4},{6,7},{7,6},{8,9},{9,8},{10,11... | collective-permute-start | bytes 405512 | tf_op jit(solution)/shard_map/ppermute | solution.py:118
  (106 shorter events, 40.6 us)
Async XLA Ops:
  0.6 94.0 %copy-start = (bf16[1,4,8,128,128]{4,3,2,1,0:T(8,128)(2,1)S(1)}, bf16[1,4,8,128,128]{4,3,2,1,0:T(8,128)(2,1)}, u32[]{:S(2)}) copy-start(bf16[1,4,8,128,128]{4,3,2,1,0:T(8,128)(2,1)} %param.11) | copy-start | bytes 3145732
  0.6 63.5 %copy-start.1 = (bf16[128,256]{1,0:T(8,128)(2,1)S(1)}, bf16[128,256]{1,0:T(8,128)(2,1)}, u32[]{:S(2)}) copy-start(bf16[128,256]{1,0:T(8,128)(2,1)} %param.8) | copy-start | bytes 196612
  0.7 15.8 %collective-permute-start = (bf16[128,256]{1,0:T(8,128)(2,1)}, bf16[128,256]{1,0:T(8,128)(2,1)S(1)}, u32[]{:S(2)}, u32[]{:S(2)}) collective-permute-start(bf16[128,256]{1,0:T(8,128)(2,1)} %param.8), channel_id=1, source_target_pairs={{0,256},{128,384},{256,0},{384,128},{1,257},{129,385},{257,1},{385... | collective-permute-start | bytes 196616 | tf_op jit(solution)/shard_map/ppermute | solution.py:26
  9.1 10.1 %collective-permute-start.1 = (bf16[128,256]{1,0:T(8,128)(2,1)}, bf16[128,256]{1,0:T(8,128)(2,1)S(1)}, u32[]{:S(2)}, u32[]{:S(2)}) collective-permute-start(bf16[128,256]{1,0:T(8,128)(2,1)} %param.8), channel_id=1, source_target_pairs={{0,128},{128,256},{256,384},{384,0},{1,129},{129,257},{257,385},{3... | collective-permute-start | bytes 196616 | tf_op jit(solution)/shard_map/ppermute | solution.py:26
  11.5 7.7 %collective-permute-start.2 = (bf16[128,256]{1,0:T(8,128)(2,1)}, bf16[128,256]{1,0:T(8,128)(2,1)S(1)}, u32[]{:S(2)}, u32[]{:S(2)}) collective-permute-start(bf16[128,256]{1,0:T(8,128)(2,1)} %param.8), channel_id=1, source_target_pairs={{0,384},{128,0},{256,128},{384,256},{1,385},{129,1},{257,129},{385... | collective-permute-start | bytes 196616 | tf_op jit(solution)/shard_map/ppermute | solution.py:26
  20.1 14.7 %collective-permute-start.3 = (bf16[4,128,256]{2,1,0:T(8,128)(2,1)S(1)}, bf16[4,128,256]{2,1,0:T(8,128)(2,1)S(1)}, u32[]{:S(2)}, u32[]{:S(2)}) collective-permute-start(bf16[4,128,256]{2,1,0:T(8,128)(2,1)S(1)} %pad_maximum_fusion.2), channel_id=1, source_target_pairs={{0,4},{4,8},{8,12},{12,16},{16,20},{20,24},{24,28},{28,0},{1,5},{5... | collective-permute-start | bytes 786440 | tf_op jit(solution)/shard_map/ppermute | solution.py:38
  24.8 15.9 %collective-permute-start.12 = (s32[8]{0:T(128)S(1)}, s32[8]{0:T(128)S(1)}, u32[]{:S(2)}, u32[]{:S(2)}) collective-permute-start(s32[8]{0:T(128)S(1)} %get-tuple-element.7), channel_id=1, source_target_pairs={{0,64},{32,96},{64,0},{96,32},{1,65},{33,97},{65,1},{97,33},{2,66}... | collective-permute-start | bytes 104 | tf_op jit(solution)/shard_map/ppermute | solution.py:58
  29.5 19.8 %collective-permute-start.14 = (s32[8]{0:T(128)S(1)}, s32[8]{0:T(128)S(1)}, u32[]{:S(2)}, u32[]{:S(2)}) collective-permute-start(s32[8]{0:T(128)S(1)} %get-tuple-element.7), channel_id=1, source_target_pairs={{0,96},{32,0},{64,32},{96,64},{1,97},{33,1},{65,33},{97,65},{2,98}... | collective-permute-start | bytes 104 | tf_op jit(solution)/shard_map/ppermute | solution.py:58
  32.2 17.1 %collective-permute-start.10 = (s32[8]{0:T(128)S(1)}, s32[8]{0:T(128)S(1)}, u32[]{:S(2)}, u32[]{:S(2)}) collective-permute-start(s32[8]{0:T(128)S(1)} %get-tuple-element.7), channel_id=1, source_target_pairs={{0,32},{32,64},{64,96},{96,0},{1,33},{33,65},{65,97},{97,1},{2,34}... | collective-permute-start | bytes 104 | tf_op jit(solution)/shard_map/ppermute | solution.py:58
  34.8 12.5 %collective-permute-start.4 = (bf16[4,128,256]{2,1,0:T(8,128)(2,1)S(1)}, bf16[4,128,256]{2,1,0:T(8,128)(2,1)S(1)}, u32[]{:S(2)}, u32[]{:S(2)}) collective-permute-start(bf16[4,128,256]{2,1,0:T(8,128)(2,1)S(1)} %collective-permute-done.3), channel_id=1, source_target_pairs={{0,4},{4,8},{8,12},{12,16},{16,20},{20,24},{24,28},{28,0},{1,5},{5... | collective-permute-start | bytes 786440 | tf_op jit(solution)/shard_map/ppermute | solution.py:38
  40.8 9.8 %collective-permute-start.7 = (bf16[4,128,256]{2,1,0:T(8,128)(2,1)S(1)}, bf16[4,128,256]{2,1,0:T(8,128)(2,1)S(1)}, u32[]{:S(2)}, u32[]{:S(2)}) collective-permute-start(bf16[4,128,256]{2,1,0:T(8,128)(2,1)S(1)} %pad_maximum_fusion.2), channel_id=1, source_target_pairs={{0,28},{4,0},{8,4},{12,8},{16,12},{20,16},{24,20},{28,24},{1,29},{... | collective-permute-start | bytes 786440 | tf_op jit(solution)/shard_map/ppermute | solution.py:41
  47.3 8.3 %collective-permute-start.5 = (bf16[4,128,256]{2,1,0:T(8,128)(2,1)S(1)}, bf16[4,128,256]{2,1,0:T(8,128)(2,1)S(1)}, u32[]{:S(2)}, u32[]{:S(2)}) collective-permute-start(bf16[4,128,256]{2,1,0:T(8,128)(2,1)S(1)} %collective-permute-done.4), channel_id=1, source_target_pairs={{0,4},{4,8},{8,12},{12,16},{16,20},{20,24},{24,28},{28,0},{1,5},{5... | collective-permute-start | bytes 786440 | tf_op jit(solution)/shard_map/ppermute | solution.py:38
  50.6 8.3 %collective-permute-start.8 = (bf16[4,128,256]{2,1,0:T(8,128)(2,1)S(1)}, bf16[4,128,256]{2,1,0:T(8,128)(2,1)S(1)}, u32[]{:S(2)}, u32[]{:S(2)}) collective-permute-start(bf16[4,128,256]{2,1,0:T(8,128)(2,1)S(1)} %collective-permute-done.7), channel_id=1, source_target_pairs={{0,28},{4,0},{8,4},{12,8},{16,12},{20,16},{24,20},{28,24},{1,29},{... | collective-permute-start | bytes 786440 | tf_op jit(solution)/shard_map/ppermute | solution.py:41
  55.6 8.3 %collective-permute-start.6 = (bf16[4,128,256]{2,1,0:T(8,128)(2,1)S(1)}, bf16[4,128,256]{2,1,0:T(8,128)(2,1)S(1)}, u32[]{:S(2)}, u32[]{:S(2)}) collective-permute-start(bf16[4,128,256]{2,1,0:T(8,128)(2,1)S(1)} %collective-permute-done.5), channel_id=1, source_target_pairs={{0,4},{4,8},{8,12},{12,16},{16,20},{20,24},{24,28},{28,0},{1,5},{5... | collective-permute-start | bytes 786440 | tf_op jit(solution)/shard_map/ppermute | solution.py:38
  58.9 8.3 %collective-permute-start.9 = (bf16[4,128,256]{2,1,0:T(8,128)(2,1)S(1)}, bf16[4,128,256]{2,1,0:T(8,128)(2,1)S(1)}, u32[]{:S(2)}, u32[]{:S(2)}) collective-permute-start(bf16[4,128,256]{2,1,0:T(8,128)(2,1)S(1)} %collective-permute-done.8), channel_id=1, source_target_pairs={{0,28},{4,0},{8,4},{12,8},{16,12},{20,16},{24,20},{28,24},{1,29},{... | collective-permute-start | bytes 786440 | tf_op jit(solution)/shard_map/ppermute | solution.py:41
  68.6 14.5 %collective-permute-start.13 = (bf16[8,128,256]{2,1,0:T(8,128)(2,1)}, bf16[8,128,256]{2,1,0:T(8,128)(2,1)}, u32[]{:S(2)}, u32[]{:S(2)}) collective-permute-start(bf16[8,128,256]{2,1,0:T(8,128)(2,1)} %gather_fusion.1), channel_id=1, source_target_pairs={{0,64},{32,96},{64,0},{96,32},{1,65},{33,97},{65,1},{97,33},{2,66}... | collective-permute-start | bytes 1572872 | tf_op jit(solution)/shard_map/ppermute | solution.py:77
  72.6 22.1 %collective-permute-start.15 = (bf16[8,128,256]{2,1,0:T(8,128)(2,1)}, bf16[8,128,256]{2,1,0:T(8,128)(2,1)}, u32[]{:S(2)}, u32[]{:S(2)}) collective-permute-start(bf16[8,128,256]{2,1,0:T(8,128)(2,1)} %gather_fusion.2), channel_id=1, source_target_pairs={{0,32},{32,64},{64,96},{96,0},{1,33},{33,65},{65,97},{97,1},{2,34}... | collective-permute-start | bytes 1572872 | tf_op jit(solution)/shard_map/ppermute | solution.py:77
  77.9 16.8 %collective-permute-start.11 = (bf16[8,128,256]{2,1,0:T(8,128)(2,1)}, bf16[8,128,256]{2,1,0:T(8,128)(2,1)}, u32[]{:S(2)}, u32[]{:S(2)}) collective-permute-start(bf16[8,128,256]{2,1,0:T(8,128)(2,1)} %gather_fusion), channel_id=1, source_target_pairs={{0,96},{32,0},{64,32},{96,64},{1,97},{33,1},{65,33},{97,65},{2,98}... | collective-permute-start | bytes 1572872 | tf_op jit(solution)/shard_map/ppermute | solution.py:77
  97.2 7.8 %collective-permute-start.16 = (f32[512,256]{1,0:T(8,128)S(1)}, f32[512,256]{1,0:T(8,128)S(1)}, u32[]{:S(2)}, u32[]{:S(2)}) collective-permute-start(f32[512,256]{1,0:T(8,128)S(1)} %bitcast.67), channel_id=1, source_target_pairs={{0,1},{1,0},{2,3},{3,2},{4,5},{5,4},{6,7},{7,6},{8,9},{9,8},{10,11... | collective-permute-start | bytes 1572872 | tf_op jit(solution)/shard_map/ppermute | solution.py:149
  103.1 7.4 %collective-permute-start.19 = (bf16[128,256]{1,0:T(8,128)(2,1)S(1)}, bf16[128,256]{1,0:T(8,128)(2,1)S(1)}, u32[]{:S(2)}, u32[]{:S(2)}) collective-permute-start(bf16[128,256]{1,0:T(8,128)(2,1)S(1)} %copy-done.6), channel_id=1, source_target_pairs={{0,1},{1,0},{2,3},{3,2},{4,5},{5,4},{6,7},{7,6},{8,9},{9,8},{10,11... | collective-permute-start | bytes 196616 | tf_op jit(solution)/shard_map/ppermute | solution.py:149
  105.1 17.7 %collective-permute-start.17 = (f32[256,256]{1,0:T(8,128)S(1)}, f32[256,256]{1,0:T(8,128)S(1)}, u32[]{:S(2)}, u32[]{:S(2)}) collective-permute-start(f32[256,256]{1,0:T(8,128)S(1)} %get-tuple-element.9), channel_id=1, source_target_pairs={{0,2},{2,0},{1,3},{3,1},{4,6},{6,4},{5,7},{7,5},{8,10},{10,8},{9,1... | collective-permute-start | bytes 786440 | tf_op jit(solution)/shard_map/ppermute | solution.py:149
  107.3 15.5 %collective-permute-start.18 = (f32[256,256]{1,0:T(8,128)S(1)}, f32[256,256]{1,0:T(8,128)S(1)}, u32[]{:S(2)}, u32[]{:S(2)}) collective-permute-start(f32[256,256]{1,0:T(8,128)S(1)} %get-tuple-element.10), channel_id=1, source_target_pairs={{0,2},{2,0},{1,3},{3,1},{4,6},{6,4},{5,7},{7,5},{8,10},{10,8},{9,1... | collective-permute-start | bytes 786440 | tf_op jit(solution)/shard_map/ppermute | solution.py:149
  110.5 12.4 %collective-permute-start.20 = (bf16[2,128,256]{2,1,0:T(8,128)(2,1)S(1)}, bf16[2,128,256]{2,1,0:T(8,128)(2,1)S(1)}, u32[]{:S(2)}, u32[]{:S(2)}) collective-permute-start(bf16[2,128,256]{2,1,0:T(8,128)(2,1)S(1)} %maximum_select_fusion.3), channel_id=1, source_target_pairs={{0,2},{2,0},{1,3},{3,1},{4,6},{6,4},{5,7},{7,5},{8,10},{10,8},{9,1... | collective-permute-start | bytes 393224 | tf_op jit(solution)/shard_map/ppermute | solution.py:149
  124.1 5.1 %collective-permute-start.21 = (f32[16896]{0:T(1024)S(1)}, f32[16896]{0:T(1024)S(1)}, u32[]{:S(2)}, u32[]{:S(2)}) collective-permute-start(f32[16896]{0:T(1024)S(1)} %dynamic-slice_reduce_fusion), channel_id=1, source_target_pairs={{0,4},{4,0},{8,12},{12,8},{16,20},{20,16},{24,28},{28,24},{1,5},{5... | collective-permute-start | bytes 202760 | tf_op jit(solution)/shard_map/ppermute | solution.py:208
  129.2 7.8 %collective-permute-start.22 = (f32[16896]{0:T(1024)S(1)}, f32[16896]{0:T(1024)S(1)}, u32[]{:S(2)}, u32[]{:S(2)}) collective-permute-start(f32[16896]{0:T(1024)S(1)} %add.315), channel_id=1, source_target_pairs={{0,8},{4,12},{8,0},{12,4},{16,24},{20,28},{24,16},{28,20},{1,9},{5... | collective-permute-start | bytes 202760 | tf_op jit(solution)/shard_map/ppermute | solution.py:208
  137.0 6.3 %collective-permute-start.23 = (f32[16896]{0:T(1024)S(1)}, f32[16896]{0:T(1024)S(1)}, u32[]{:S(2)}, u32[]{:S(2)}) collective-permute-start(f32[16896]{0:T(1024)S(1)} %add.316), channel_id=1, source_target_pairs={{0,28},{4,24},{8,20},{12,16},{16,12},{20,8},{24,4},{28,0},{1,29},{... | collective-permute-start | bytes 202760 | tf_op jit(solution)/shard_map/ppermute | solution.py:208
  143.3 5.1 %collective-permute-start.24 = (f32[16896]{0:T(1024)S(1)}, f32[16896]{0:T(1024)S(1)}, u32[]{:S(2)}, u32[]{:S(2)}) collective-permute-start(f32[16896]{0:T(1024)S(1)} %add.317), channel_id=1, source_target_pairs={{0,32},{32,0},{64,96},{96,64},{1,33},{33,1},{65,97},{97,65},{2,34}... | collective-permute-start | bytes 202760 | tf_op jit(solution)/shard_map/ppermute | solution.py:208
  148.4 6.3 %collective-permute-start.25 = (f32[16896]{0:T(1024)S(1)}, f32[16896]{0:T(1024)S(1)}, u32[]{:S(2)}, u32[]{:S(2)}) collective-permute-start(f32[16896]{0:T(1024)S(1)} %add.318), channel_id=1, source_target_pairs={{0,96},{32,64},{64,32},{96,0},{1,97},{33,65},{65,33},{97,1},{2,98}... | collective-permute-start | bytes 202760 | tf_op jit(solution)/shard_map/ppermute | solution.py:208
  154.6 6.7 %collective-permute-start.26 = (f32[16896]{0:T(1024)S(1)}, f32[16896]{0:T(1024)S(1)}, u32[]{:S(2)}, u32[]{:S(2)}) collective-permute-start(f32[16896]{0:T(1024)S(1)} %add.319), channel_id=1, source_target_pairs={{0,128},{128,0},{256,384},{384,256},{1,129},{129,1},{257,385},{385... | collective-permute-start | bytes 202760 | tf_op jit(solution)/shard_map/ppermute | solution.py:208
  161.4 7.5 %collective-permute-start.27 = (f32[16896]{0:T(1024)S(1)}, f32[16896]{0:T(1024)S(1)}, u32[]{:S(2)}, u32[]{:S(2)}) collective-permute-start(f32[16896]{0:T(1024)S(1)} %add.320), channel_id=1, source_target_pairs={{0,384},{128,256},{256,128},{384,0},{1,385},{129,257},{257,129},{3... | collective-permute-start | bytes 202760 | tf_op jit(solution)/shard_map/ppermute | solution.py:208
  168.8 5.1 %collective-permute-start.28 = (f32[16896]{0:T(1024)S(1)}, f32[16896]{0:T(1024)S(1)}, u32[]{:S(2)}, u32[]{:S(2)}) collective-permute-start(f32[16896]{0:T(1024)S(1)} %add.321), channel_id=1, source_target_pairs={{0,2},{2,0},{1,3},{3,1},{4,6},{6,4},{5,7},{7,5},{8,10},{10,8},{9,1... | collective-permute-start | bytes 202760 | tf_op jit(solution)/shard_map/ppermute | solution.py:118
  173.9 13.1 %collective-permute-start.29 = (f32[33792]{0:T(1024)S(1)}, f32[33792]{0:T(1024)S(1)}, u32[]{:S(2)}, u32[]{:S(2)}) collective-permute-start(f32[33792]{0:T(1024)S(1)} %maximum_select_fusion.2), channel_id=1, source_target_pairs={{0,1},{1,0},{2,3},{3,2},{4,5},{5,4},{6,7},{7,6},{8,9},{9,8},{10,11... | collective-permute-start | bytes 405512 | tf_op jit(solution)/shard_map/ppermute | solution.py:118
  (9 other events, 179.9 us)
